TPU v7x, 128 devices: a whole 4x4x4 slice. The times are simulated.
128 devices in a mesh: row: 8 (over z, core), col: 16 (over x, y).
Axes of the slice: x: 4, y: 4, z: 4, core: 2. Of those that a mesh axis runs over, the one named last changes fastest.
Arguments:
- tokens: bfloat16 [4096, 2048], P('col', 'row'), may hold values from -6 to 6
- router: bfloat16 [2048, 32], replicated, may hold values from -0.125 to 0.125
- shared_gate_vector: bfloat16 [2048], replicated, may hold values from -0.125 to 0.125
- shared_gate_weight: bfloat16 [2048, 5632], P('col', 'row'), may hold values from -0.125 to 0.125
- shared_up_weight: bfloat16 [2048, 5632], P('col', 'row'), may hold values from -0.125 to 0.125
- shared_down_weight: bfloat16 [5632, 2048], P('row', 'col'), may hold values from -0.078125 to 0.078125
- routed_gate_weight: bfloat16 [32, 2048, 1408], P('col', None, 'row'), may hold values from -0.125 to 0.125
- routed_up_weight: bfloat16 [32, 2048, 1408], P('col', None, 'row'), may hold values from -0.125 to 0.125
- routed_down_weight: bfloat16 [32, 1408, 2048], P('col', 'row'), may hold values from -0.15625 to 0.15625
- adapter_input_factor: bfloat16 [64, 16, 2048], P(None, None, 'row'), may hold values from -0.125 to 0.125
- adapter_output_factor: bfloat16 [64, 16, 5632], P(None, None, 'row'), may hold values from -0.29882812 to 0.29882812
- routes: int32 [4096, 4], P('col'), may hold values from 0 to 31, all different within a row; in each aligned block of 256 rows (0 to 255, 256 to 511, ...) at most 64 rows name the same one
- lengths: int32 [16, 16], P('col'), may hold values from 1 to 128, 256 in all within a row
- prompt_adapter_index: int32 [16, 16], P('col'), may hold values from 0 to 15
- active_adapter_index: int32 [16], replicated, may hold values from 0 to 63, as said below
Outputs:
- moe_out: float32 [4096, 2048], P('col', 'row')
Inputs may be any that keep to these rules, and one draw needn't show every extreme that they name: `routes`: in each group of 256 consecutive tokens no expert is named by more than 64 tokens, a bound that some block reaches. Each group's 16 lengths sum to 256; the longest is exactly 128. `active_adapter_index`: the 16 entries are distinct.
All inputs are finite; a program needn't handle non-finite values.
Results may differ from a plain program's by a relative error of at most 0.003.
Values may be sent and summed in bfloat16 or wider, within the bound.
No kernel may reach another device: no remote copies, remote signals or barrier semaphores. Data moves between devices by JAX's collectives and lax.ppermute only.
A program may use at most 128 MiB of HBM per device.

v0:
```python
import jax
import jax.numpy as jnp
from jax import lax
from jax.sharding import PartitionSpec as P

ADAPTER_SCALE = 2.0


def on_device(
    tokens,
    router,
    shared_gate_vector,
    shared_gate_weight,
    shared_up_weight,
    shared_down_weight,
    routed_gate_weight,
    routed_up_weight,
    routed_down_weight,
    adapter_input_factor,
    adapter_output_factor,
    routes,
    lengths,
    prompt_adapter_index,
    active_adapter_index,
):
    all_features = lax.all_gather(tokens, "row", axis=1, tiled=True)
    token_count = all_features.shape[0]
    full_width = all_features.shape[1]
    local_width = tokens.shape[1]
    col_count = lax.axis_size("col")
    local_experts = routed_gate_weight.shape[0]
    expert_count = local_experts * col_count
    route_count = routes.shape[1]
    capacity = 2 * token_count * route_count // expert_count
    logits = jnp.dot(all_features, router, preferred_element_type=jnp.float32)
    onehot = routes[:, :, None] == jnp.arange(expert_count, dtype=jnp.int32)[None, None, :]
    picked = jnp.sum(jnp.where(onehot, logits[:, None, :], 0.0), axis=2)
    raw_exp = jnp.exp(picked)
    gate_weights = raw_exp / jnp.sum(raw_exp, axis=1, keepdims=True)
    share = jax.nn.sigmoid(
        jnp.dot(all_features, shared_gate_vector, preferred_element_type=jnp.float32)
    )
    hit_table = jnp.any(onehot, axis=1).astype(jnp.int32)
    running_count = jnp.cumsum(hit_table, axis=0)
    slot_rank = running_count - hit_table
    route_rank = jnp.sum(jnp.where(onehot, slot_rank[:, None, :], 0), axis=2)
    row_index = routes * capacity + route_rank
    request_ends = jnp.cumsum(lengths[0])
    request_count = lengths.shape[1]
    token_position = jnp.arange(token_count, dtype=jnp.int32)
    request_of = jnp.sum(
        (token_position[:, None] >= request_ends[None, :]).astype(jnp.int32), axis=1
    )
    request_match = request_of[:, None] == jnp.arange(request_count, dtype=jnp.int32)[None, :]
    adapter_of = jnp.sum(jnp.where(request_match, prompt_adapter_index[0][None, :], 0), axis=1)
    picked_input_factor = jnp.take(adapter_input_factor, active_adapter_index, axis=0)
    rank_width = picked_input_factor.shape[1]
    reduced_rank_value = picked_input_factor.shape[0] * rank_width
    full_in = lax.all_gather(picked_input_factor, "row", axis=2, tiled=True).reshape(
        reduced_rank_value, full_width
    )
    low_rank = lax.dot_general(
        all_features, full_in, (((1,), (1,)), ((), ())), preferred_element_type=jnp.float32
    )
    owner = jnp.arange(reduced_rank_value, dtype=jnp.int32) // rank_width
    adapter_mask = adapter_of[:, None] == owner[None, :]
    low_masked = jnp.where(adapter_mask, low_rank.astype(jnp.bfloat16), jnp.zeros((), jnp.bfloat16))
    picked_output_factor = jnp.take(adapter_output_factor, active_adapter_index, axis=0).reshape(
        reduced_rank_value, adapter_output_factor.shape[2]
    )
    adapter_update = jnp.dot(low_masked, picked_output_factor, preferred_element_type=jnp.float32)
    shared_gate_value = jnp.dot(
        all_features,
        lax.all_gather(shared_gate_weight, "col", axis=0, tiled=True),
        preferred_element_type=jnp.float32,
    )
    shared_up_value = jnp.dot(
        all_features,
        lax.all_gather(shared_up_weight, "col", axis=0, tiled=True),
        preferred_element_type=jnp.float32,
    )
    shared_hidden_units = (
        jax.nn.silu(shared_gate_value) * (shared_up_value + ADAPTER_SCALE * adapter_update)
    ).astype(jnp.bfloat16)
    shared_part = jnp.dot(
        shared_hidden_units,
        lax.all_gather(shared_down_weight, "col", axis=1, tiled=True),
        preferred_element_type=jnp.float32,
    )
    shared_part = shared_part * share[:, None]
    positions = jnp.arange(capacity, dtype=jnp.int32)
    slot_token = jnp.sum(
        (running_count.T[:, None, :] <= positions[None, :, None]).astype(jnp.int32), axis=2
    )
    slot_valid = positions[None, :] < running_count[-1][:, None]
    picked_rows = jnp.take(all_features, jnp.minimum(slot_token, token_count - 1), axis=0)
    chosen = jnp.where(slot_valid[:, :, None], picked_rows, jnp.zeros((), jnp.bfloat16))
    outgoing = chosen.reshape(col_count, local_experts, capacity, full_width)
    slot_block = lax.all_to_all(outgoing, "col", split_axis=0, concat_axis=0, tiled=True)
    gate_part = jnp.einsum(
        "sexd,edf->sexf", slot_block, routed_gate_weight, preferred_element_type=jnp.float32
    )
    up_part = jnp.einsum(
        "sexd,edf->sexf", slot_block, routed_up_weight, preferred_element_type=jnp.float32
    )
    hidden = (jax.nn.silu(gate_part) * up_part).astype(jnp.bfloat16)
    partial_value = jnp.einsum(
        "sexf,efd->sexd", hidden, routed_down_weight, preferred_element_type=jnp.float32
    )
    summed, shared_sum = (
        lax.psum_scatter(partial_value, "row", scatter_dimension=3, tiled=True),
        lax.psum_scatter(shared_part, "row", scatter_dimension=1, tiled=True),
    )
    returned = lax.all_to_all(summed, "col", split_axis=0, concat_axis=0, tiled=True)
    flat_rows = returned.reshape(expert_count * capacity, local_width)
    routed_rows = jnp.take(flat_rows, row_index, axis=0)
    routed = jnp.sum(gate_weights[:, :, None] * routed_rows, axis=1)
    return routed + shared_sum


def solution(mesh):
    return jax.shard_map(
        on_device,
        mesh=mesh,
        in_specs=(
            P("col", "row"),
            P(),
            P(),
            P("col", "row"),
            P("col", "row"),
            P("row", "col"),
            P("col", None, "row"),
            P("col", None, "row"),
            P("col", "row", None),
            P(None, None, "row"),
            P(None, None, "row"),
            P("col", None),
            P("col", None),
            P("col", None),
            P(),
        ),
        out_specs=P("col", "row"),
        check_vma=False,
    )
```

profile of v0, /device:TPU:0, one launch (start us, length us, event | category | flops | bytes accessed | tf_op | source)
XLA Modules:
  0.0 487.8 jit_solution(12929686134690936716)
XLA Ops:
  6.5 0.7 all-gather.6.cloned.1.call-update
  7.3 0.0 all-gather.12.cloned.1.call-start
  7.3 0.7 compare_select_fusion.3
  8.0 1.6 gather_fusion.2
  9.6 0.7 compare_and_fusion.2
  10.2 0.7 broadcast_select_fusion
  11.0 0.0 all-gather.8.cloned.1.call-start
  11.1 0.7 all-gather.8.cloned.1.call-update
  11.8 0.0 all-gather.10.cloned.1.call-start
  11.8 0.5 all-gather.10.cloned.1.call-update
  12.3 0.7 fusion.29
  13.1 0.6 reduce-window.18
  13.7 0.2 slice_reduce_fusion
  13.9 0.1 fusion.33
  14.0 0.6 convert_reduce_fusion
  14.6 0.2 slice_reduce_fusion.1
  14.8 0.1 lt.58
  14.9 0.1 reshape.157
  15.0 0.1 compare_and_fusion
  15.1 20.0 %all-gather.6.cloned.1.call-done = bf16[256,2048]{1,0:T(8,128)(2,1)} async-done(((bf16[256,256]{1,0:T(8,128)(2,1)}), bf16[256,2048]{1,0:T(8,128)(2,1)}) %all-gather.6.cloned.1.call-update) | async-done | bytes 1048592 | tf_op jit(solution)/shard_map/all_gather | solution.py:26
  35.0 17.7 %gather_fusion = bf16[2048,2048]{1,0:T(8,128)(2,1)} fusion(bf16[256,2048]{1,0:T(8,128)(2,1)} %all-gather.6.cloned.1.call-done, s32[2048]{0:T(1024)S(1)} %broadcast_clamp_fusion), kind=kCustom, calls=%fused_computation | custom fusion | bytes 16785408 | tf_op jit(solution)/shard_map/jit(_take)/gather | solution.py:96
  52.7 7.5 %select_select_fusion = bf16[16,2,64,2048]{3,2,1,0:T(8,128)(2,1)} fusion(bf16[16,2,64,2048]{3,2,1,0:T(8,128)(2,1)} %bitcast.88, pred[16,2,64]{2,1,0:T(4,128)(4,1)S(1)} %get-tuple-element.9, pred[16,2,64]{2,1,0:T(4,128)(4,1)S(1)} %get-tuple-element.10), kind=kLoop, calls=%fused_computation.4 | loop fusion | flops 8388608 | bytes 16781312 | tf_op jit(solution)/shard_map/jit(_where)/select_n | solution.py:97
  60.2 7.0 %all-to-all-start = ((bf16[16,2,64,2048]{3,2,1,0:T(8,128)(2,1)}), bf16[16,2,64,2048]{3,2,1,0:T(8,128)(2,1)}, u32[]{:S(2)}, u32[]{:S(2)}) async-start(bf16[16,2,64,2048]{3,2,1,0:T(8,128)(2,1)} %select_select_fusion), calls=%async_computation | async-start | bytes 16777216 | tf_op jit(solution)/shard_map/all_to_all | solution.py:99
  67.2 0.0 all-gather.14.cloned.1.call-start
  67.3 0.5 all-gather.14.cloned.1.call-update
  67.8 0.0 reduce-scatter.3.cloned.1.call-start
  67.9 152.1 %all-to-all-done = bf16[16,2,64,2048]{3,2,1,0:T(8,128)(2,1)} async-done(((bf16[16,2,64,2048]{3,2,1,0:T(8,128)(2,1)}), bf16[16,2,64,2048]{3,2,1,0:T(8,128)(2,1)}, u32[]{:S(2)}, u32[]{:S(2)}) %all-to-all-start) | async-done | bytes 8388640 | tf_op jit(solution)/shard_map/all_to_all | solution.py:99
  219.9 7.0 %fusion.2 = f32[2,16,64,176]{3,2,1,0:T(8,128)} fusion(bf16[16,2,64,2048]{3,2,1,0:T(8,128)(2,1)} %all-to-all-done, bf16[2,2048,176]{1,2,0:T(8,128)(2,1)S(1)} %copy-done.7), kind=kOutput, calls=%fused_computation.7 | convolution fusion | flops 1476395008 | bytes 11272192 | tf_op jit(solution)/shard_map/sexd,edf->sexf/dot_general | solution.py:100
  227.0 15.2 %convolution_bitcast_fusion = f32[16,2,64,2048]{3,2,0,1:T(8,128)} fusion(f32[2,16,64,176]{3,2,1,0:T(8,128)} %fusion.2, bf16[16,2,64,2048]{3,2,1,0:T(8,128)(2,1)} %all-to-all-done, bf16[2,176,2048]{2,1,0:T(8,128)(2,1)} %param.23, bf16[2,2048,176]{1,2,0:T(8,128)(2,1)} %param.22), kind=kOutput, calls=%fused_computation.9 | convolution fusion | flops 2954952704 | bytes 29491200 | tf_op jit(solution)/shard_map/sexf,efd->sexd/dot_general | solution.py:107
  242.2 0.0 reduce-scatter.3.cloned.1.call-update
  242.2 0.2 reduce-scatter.5.cloned.1.call-start
  242.4 0.1 broadcast_in_dim.137
  242.5 0.1 broadcast_in_dim.138
  242.6 0.3 copy-done.4
  242.9 0.1 copy.54
  243.0 0.1 reduce.2
  243.1 0.6 gather_fusion.3
  243.7 0.1 convert_reduce_fusion.1
  243.8 0.1 select_reduce_fusion.2
  243.9 0.1 bitcast_select_fusion
  244.0 0.4 fusion.37
  244.4 0.0 all-gather.12.cloned.1.call-done
  244.4 1.7 fusion.20
  246.2 0.0 all-gather.8.cloned.1.call-done
  246.2 3.6 fusion.35
  249.8 35.6 %all-gather.10.cloned.1.call-done = bf16[2048,704]{0,1:T(8,128)(2,1)} async-done(((bf16[128,704]{0,1:T(8,128)(2,1)}), bf16[2048,704]{0,1:T(8,128)(2,1)}) %all-gather.10.cloned.1.call-update) | async-done | bytes 2883600 | tf_op jit(solution)/shard_map/all_gather | solution.py:79
  285.5 3.6 fusion.36
  289.1 48.2 %all-gather.14.cloned.1.call-done = bf16[704,2048]{1,0:T(8,128)(2,1)} async-done(((bf16[704,128]{1,0:T(8,128)(2,1)}), bf16[704,2048]{1,0:T(8,128)(2,1)}) %all-gather.14.cloned.1.call-update) | async-done | bytes 2883600 | tf_op jit(solution)/shard_map/all_gather | solution.py:87
  337.3 4.9 %convolution_multiply_fusion = f32[256,2048]{1,0:T(8,128)} fusion(bf16[704,2048]{1,0:T(8,128)(2,1)} %all-gather.14.cloned.1.call-done, f32[256,704]{0,1:T(8,128)} %fusion.36, bf16[256,256]{0,1:T(8,128)(2,1)S(1)} %fusion.20, bf16[256,704]{1,0:T(8,128)(2,1)S(1)} %bitcast_select_fusion, f32[256]{0:T(256)S(1)} %add_divide_fusion, f32[256,704]{0,1:T(8,128)} %fusion.35), kind=kOutput, calls=%fused_computation.10 | convolution fusion | flops 832438272 | bytes 6915072 | tf_op jit(solution)/shard_map/dot_general | solution.py:85
  342.2 88.8 %reduce-scatter.3.cloned.1.call-done = f32[16,2,64,256]{3,2,0,1:T(8,128)} async-done(((f32[16,2,64,2048]{3,2,0,1:T(8,128)}), f32[16,2,64,256]{3,2,0,1:T(8,128)}) %reduce-scatter.3.cloned.1.call-update) | async-done | bytes 2097168 | tf_op jit(solution)/shard_map/reduce_scatter | solution.py:111
  431.0 3.2 copy.52
  434.2 7.0 %all-to-all-start.1 = ((f32[16,2,64,256]{3,2,1,0:T(8,128)}), f32[16,2,64,256]{3,2,1,0:T(8,128)}, u32[]{:S(2)}, u32[]{:S(2)}) async-start(f32[16,2,64,256]{3,2,1,0:T(8,128)} %copy.52), calls=%async_computation.2 | async-start | bytes 4194304 | tf_op jit(solution)/shard_map/all_to_all | solution.py:114
  441.2 0.1 convert_subtract_fusion
  441.3 0.2 copy.49
  441.5 0.1 copy.53
  441.7 0.1 reshape.165
  441.8 0.4 fusion.34
  442.3 0.1 copy.46
  442.5 27.9 %all-to-all-done.1 = f32[16,2,64,256]{3,2,1,0:T(8,128)} async-done(((f32[16,2,64,256]{3,2,1,0:T(8,128)}), f32[16,2,64,256]{3,2,1,0:T(8,128)}, u32[]{:S(2)}, u32[]{:S(2)}) %all-to-all-start.1) | async-done | bytes 2097184 | tf_op jit(solution)/shard_map/all_to_all | solution.py:114
  470.3 5.1 %gather_fusion.1 = f32[1024,256]{1,0:T(8,128)S(1)} fusion(f32[2048,256]{1,0:T(8,128)} %bitcast.14, s32[1024]{0:T(1024)S(1)} %broadcast_clamp_fusion.1), kind=kCustom, calls=%fused_computation.1 | custom fusion | bytes 2101248 | tf_op jit(solution)/shard_map/jit(_take)/gather | solution.py:116
  475.4 1.3 reshape.164
  476.7 2.5 multiply_reduce_fusion
  479.2 0.0 reduce-scatter.5.cloned.1.call-done
  479.2 1.7 add.77
  (35 shorter events, 0.3 us)
Async XLA Ops:
  6.5 236.6 %copy-start = (bf16[64,16,704]{2,1,0:T(8,128)(2,1)S(1)}, bf16[64,16,704]{2,1,0:T(8,128)(2,1)}, u32[]{:S(2)}) copy-start(bf16[64,16,704]{2,1,0:T(8,128)(2,1)} %param.25) | copy-start | bytes 4325380
  6.5 28.5 %all-gather.6.cloned.1.call-start = ((), (), s32[]{:S(2)}) async-start(), calls=%async_computation.4 | async-start | bytes 1179648 | tf_op jit(solution)/shard_map/all_gather | solution.py:26
  7.3 237.2 %all-gather.12.cloned.1.call-start = ((), (), s32[]{:S(2)}) async-start(), calls=%async_computation.8 | async-start | bytes 1179648 | tf_op jit(solution)/shard_map/all_gather | solution.py:59
  11.0 235.2 %all-gather.8.cloned.1.call-start = ((), (), s32[]{:S(2)}) async-start(), calls=%async_computation.6 | async-start | bytes 3063808 | tf_op jit(solution)/shard_map/all_gather | solution.py:74
  11.8 273.7 %all-gather.10.cloned.1.call-start = ((), (), s32[]{:S(2)}) async-start(), calls=%async_computation.7 | async-start | bytes 3063808 | tf_op jit(solution)/shard_map/all_gather | solution.py:79
  60.2 159.7 %copy-start.7 = (bf16[2,2048,176]{1,2,0:T(8,128)(2,1)S(1)}, bf16[2,2048,176]{1,2,0:T(8,128)(2,1)}, u32[]{:S(2)}) copy-start(bf16[2,2048,176]{1,2,0:T(8,128)(2,1)} %param.21) | copy-start | bytes 4325380
  60.2 159.7 %all-to-all-start = ((bf16[16,2,64,2048]{3,2,1,0:T(8,128)(2,1)}), bf16[16,2,64,2048]{3,2,1,0:T(8,128)(2,1)}, u32[]{:S(2)}, u32[]{:S(2)}) async-start(bf16[16,2,64,2048]{3,2,1,0:T(8,128)(2,1)} %select_select_fusion), calls=%async_computation | async-start | bytes 16777216 | tf_op jit(solution)/shard_map/all_to_all | solution.py:99
  67.2 270.1 %all-gather.14.cloned.1.call-start = ((), (), s32[]{:S(2)}) async-start(), calls=%async_computation.9 | async-start | bytes 3063808 | tf_op jit(solution)/shard_map/all_gather | solution.py:87
  67.8 363.2 %reduce-scatter.3.cloned.1.call-start = ((), (), s32[]{:S(2)}) async-start(), calls=%async_computation.5 | async-start | bytes 18874368 | tf_op jit(solution)/shard_map/reduce_scatter | solution.py:111
  242.2 0.7 copy-start.4
  242.2 0.7 copy-start.5
  242.2 1.6 copy-start.6
  242.2 1.8 copy-start.1
  242.2 237.0 %reduce-scatter.5.cloned.1.call-start = ((), (), s32[]{:S(2)}) async-start(), calls=%async_computation.10 | async-start | bytes 2359296 | tf_op jit(solution)/shard_map/reduce_scatter | solution.py:112
  434.2 7.1 %copy-start.3 = (s32[256,4]{0,1:T(4,128)S(1)}, s32[256,4]{0,1:T(4,128)}, u32[]{:S(2)}) copy-start(s32[256,4]{0,1:T(4,128)} %param.26) | copy-start | bytes 12292
  434.2 7.6 %copy-start.2 = (bf16[2048,32]{0,1:T(8,128)(2,1)S(1)}, bf16[2048,32]{0,1:T(8,128)(2,1)}, u32[]{:S(2)}) copy-start(bf16[2048,32]{0,1:T(8,128)(2,1)} %param.16) | copy-start | bytes 393220
  434.2 36.1 %all-to-all-start.1 = ((f32[16,2,64,256]{3,2,1,0:T(8,128)}), f32[16,2,64,256]{3,2,1,0:T(8,128)}, u32[]{:S(2)}, u32[]{:S(2)}) async-start(f32[16,2,64,256]{3,2,1,0:T(8,128)} %copy.52), calls=%async_computation.2 | async-start | bytes 4194304 | tf_op jit(solution)/shard_map/all_to_all | solution.py:114
Sparse Core Ops, SparseCore 0:
  9.0 25.9 all-gather.5
  36.7 24.2 all-gather.11
  63.1 155.2 all-gather.7
  220.5 64.9 all-gather.9
  287.4 49.8 all-gather.13
  339.6 91.3 reduce-scatter.2
  433.4 34.4 reduce-scatter.4
where the time goes:
time: 488 us
  waiting for transfers between devices  375 us (77%)
  matrix products  36.9 us (8%)
  local copies, waits for them, and re-layouts  31 us (6%)
  other arithmetic  16.6 us (3%)
  starting transfers between devices  14.4 us (3%)
  between operations  13.7 us (3%)
    all_to_all x1, waiting for transfers between devices, on_device(): lax.all_to_all(outgoing, 'col', split_axis=0, concat_axis=0, tiled=True)  152 us
    reduce_scatter x1, waiting for transfers between devices, on_device(): lax.psum_scatter(partial_value, 'row', scatter_dimension=3, tiled=True)  88.8 us
    all_gather x1, waiting for transfers between devices, on_device(): lax.all_gather(shared_down_weight, 'col', axis=1, tiled=True)  48.2 us
    all_gather x1, waiting for transfers between devices, on_device(): lax.all_gather(shared_up_weight, 'col', axis=0, tiled=True)  35.6 us
    all_to_all x1, waiting for transfers between devices, on_device(): lax.all_to_all(summed, 'col', split_axis=0, concat_axis=0, tiled=True)  27.9 us
    all_gather x1, waiting for transfers between devices, on_device(): all_features = lax.all_gather(tokens, 'row', axis=1, tiled=True)  20 us
    gather x1, local copies, waits for them, and re-layouts, on_device(): jnp.take(all_features, jnp.minimum(slot_token, token_count - 1), axis=0)  17.7 us
    dot_general x1, matrix products, on_device(): jnp.einsum('sexf,efd->sexd', hidden, routed_down_weight, preferred_elemen...  15.2 us
  transfers between devices with their start and end apart: 9, of which 6 were waited for; matrix products, arithmetic and copies ran while one was open for 17% of the time, Pallas kernels for 0%

commit v1 on v0

v1 whole, which is shorter than its diff:
```python
import jax
import jax.numpy as jnp
from jax import lax
from jax.sharding import PartitionSpec as P

ADAPTER_SCALE = 2.0


def on_device(
    tokens,
    router,
    shared_gate_vector,
    shared_gate_weight,
    shared_up_weight,
    shared_down_weight,
    routed_gate_weight,
    routed_up_weight,
    routed_down_weight,
    adapter_input_factor,
    adapter_output_factor,
    routes,
    lengths,
    prompt_adapter_index,
    active_adapter_index,
):
    row_count = lax.axis_size("row")
    col_count = lax.axis_size("col")
    row_id = lax.axis_index("row")
    token_count = tokens.shape[0]
    local_width = tokens.shape[1]
    picked_input_factor = jnp.take(adapter_input_factor, active_adapter_index, axis=0)
    rank_width = picked_input_factor.shape[1]
    reduced_rank_value = picked_input_factor.shape[0] * rank_width
    gathered = lax.all_gather(
        jnp.concatenate(
            [tokens, picked_input_factor.reshape(reduced_rank_value, local_width)], axis=0
        ),
        "row",
        axis=1,
        tiled=True,
    )
    all_features = gathered[:token_count]
    full_in = gathered[token_count:]
    full_width = all_features.shape[1]
    local_experts = routed_gate_weight.shape[0]
    expert_count = local_experts * col_count
    route_count = routes.shape[1]
    capacity = 2 * token_count * route_count // expert_count

    shared_stack = jnp.stack(
        [shared_gate_weight, shared_up_weight, shared_down_weight.T], axis=0
    )
    shared_full = lax.all_gather(shared_stack, "col", axis=1, tiled=True)

    down_by_feature = lax.all_to_all(
        routed_down_weight, "row", split_axis=2, concat_axis=1, tiled=True
    )

    logits = jnp.dot(all_features, router, preferred_element_type=jnp.float32)
    onehot = routes[:, :, None] == jnp.arange(expert_count, dtype=jnp.int32)[None, None, :]
    picked = jnp.sum(jnp.where(onehot, logits[:, None, :], 0.0), axis=2)
    raw_exp = jnp.exp(picked)
    gate_weights = raw_exp / jnp.sum(raw_exp, axis=1, keepdims=True)
    share = jax.nn.sigmoid(
        jnp.dot(all_features, shared_gate_vector, preferred_element_type=jnp.float32)
    )
    hit_table = jnp.any(onehot, axis=1).astype(jnp.int32)
    running_count = jnp.cumsum(hit_table, axis=0)
    slot_rank = running_count - hit_table
    route_rank = jnp.sum(jnp.where(onehot, slot_rank[:, None, :], 0), axis=2)
    row_index = routes * capacity + route_rank

    request_ends = jnp.cumsum(lengths[0])
    request_count = lengths.shape[1]
    token_position = jnp.arange(token_count, dtype=jnp.int32)
    request_of = jnp.sum(
        (token_position[:, None] >= request_ends[None, :]).astype(jnp.int32), axis=1
    )
    request_match = request_of[:, None] == jnp.arange(request_count, dtype=jnp.int32)[None, :]
    adapter_of = jnp.sum(jnp.where(request_match, prompt_adapter_index[0][None, :], 0), axis=1)
    low_rank = lax.dot_general(
        all_features, full_in, (((1,), (1,)), ((), ())), preferred_element_type=jnp.float32
    )
    owner = jnp.arange(reduced_rank_value, dtype=jnp.int32) // rank_width
    adapter_mask = adapter_of[:, None] == owner[None, :]
    low_masked = jnp.where(adapter_mask, low_rank.astype(jnp.bfloat16), jnp.zeros((), jnp.bfloat16))
    picked_output_factor = jnp.take(adapter_output_factor, active_adapter_index, axis=0).reshape(
        reduced_rank_value, adapter_output_factor.shape[2]
    )
    adapter_update = jnp.dot(low_masked, picked_output_factor, preferred_element_type=jnp.float32)

    half_width = full_width // 2
    half = row_id % 2
    slot_count = expert_count * capacity
    slot_id = jnp.arange(slot_count, dtype=jnp.int32)
    selection = jnp.any(row_index[None, :, :] == slot_id[:, None, None], axis=2).astype(jnp.bfloat16)
    own_features = lax.dynamic_slice_in_dim(all_features, half * half_width, half_width, axis=1)
    chosen = jnp.dot(selection, own_features, preferred_element_type=jnp.float32).astype(jnp.bfloat16)
    outgoing = chosen.reshape(col_count, local_experts, capacity, half_width)
    own_half = lax.all_to_all(outgoing, "col", split_axis=0, concat_axis=0, tiled=True)
    other_half = lax.ppermute(own_half, "row", [(i, i ^ 1) for i in range(row_count)])

    def half_weights(w, which):
        return lax.dynamic_slice_in_dim(w, which * half_width, half_width, axis=1)

    def project(w):
        return jnp.einsum(
            "sexd,edf->sexf", own_half, half_weights(w, half), preferred_element_type=jnp.float32
        ) + jnp.einsum(
            "sexd,edf->sexf", other_half, half_weights(w, 1 - half), preferred_element_type=jnp.float32
        )

    gate_part = project(routed_gate_weight)
    up_part = project(routed_up_weight)
    hidden = (jax.nn.silu(gate_part) * up_part).astype(jnp.bfloat16)
    hidden_all = lax.all_gather(hidden, "row", axis=3, tiled=True)
    expert_value = jnp.einsum(
        "sexf,efd->sexd", hidden_all, down_by_feature, preferred_element_type=jnp.float32
    )
    returned = lax.all_to_all(expert_value, "col", split_axis=0, concat_axis=0, tiled=True)
    flat_rows = returned.reshape(expert_count * capacity, local_width)
    routed_rows = jnp.take(flat_rows, row_index, axis=0)
    routed = jnp.sum(gate_weights[:, :, None] * routed_rows, axis=1)

    shared_gate_value = jnp.dot(all_features, shared_full[0], preferred_element_type=jnp.float32)
    shared_up_value = jnp.dot(all_features, shared_full[1], preferred_element_type=jnp.float32)
    shared_hidden_units = (
        jax.nn.silu(shared_gate_value) * (shared_up_value + ADAPTER_SCALE * adapter_update)
    ).astype(jnp.bfloat16)
    shared_part = lax.dot_general(
        shared_hidden_units,
        shared_full[2],
        (((1,), (1,)), ((), ())),
        preferred_element_type=jnp.float32,
    )
    shared_part = shared_part * share[:, None]
    shared_sum = lax.psum_scatter(shared_part, "row", scatter_dimension=1, tiled=True)
    return routed + shared_sum


def solution(mesh):
    return jax.shard_map(
        on_device,
        mesh=mesh,
        in_specs=(
            P("col", "row"),
            P(),
            P(),
            P("col", "row"),
            P("col", "row"),
            P("row", "col"),
            P("col", None, "row"),
            P("col", None, "row"),
            P("col", "row", None),
            P(None, None, "row"),
            P(None, None, "row"),
            P("col", None),
            P("col", None),
            P("col", None),
            P(),
        ),
        out_specs=P("col", "row"),
        check_vma=False,
    )
```

time: 488 us -> 289 us (0.59)
  waiting for transfers between devices: 375 us -> 115 us
  blocking collectives: 0 us -> 66.5 us
    all_to_all x2, waiting for transfers between devices: 180 us -> 28.6 us  [the longest x1 28.6 us: on_device(): lax.all_to_all(expert_value, 'col', split_axis=0, concat_axis=0, tiled=True)]
    reduce_scatter x1 -> x0, waiting for transfers between devices: 88.8 us -> none  [on_device(): lax.psum_scatter(partial_value, 'row', scatter_dimension=3, tiled=True)]
    all_to_all x0 -> x1, blocking collectives: none -> 66.5 us  [on_device(): lax.all_to_all(outgoing, 'col', split_axis=0, concat_axis=0, tiled=True)]
    all_gather x5 -> x3, waiting for transfers between devices: 104 us -> 84.5 us  [the longest x1 47.7 us: on_device(): hidden_all = lax.all_gather(hidden, 'row', axis=3, tiled=True)]
    gather x1 -> x0, local copies, waits for them, and re-layouts: 17.7 us -> none  [on_device(): jnp.take(all_features, jnp.minimum(slot_token, token_count - 1), axis=0)]
    select_n x2 -> x1, other arithmetic: 7.52 us -> 0.01 us  [on_device(): routed_rows = jnp.take(flat_rows, row_index, axis=0)]
    all_to_all x0 -> x2, local copies, waits for them, and re-layouts: none -> 7.25 us  [the longest x1 4.8 us: on_device(): lax.all_to_all(routed_down_weight, 'row', split_axis=2, concat_axis=1, ti...]
    dot_general x5 -> x9, matrix products: 34.4 us -> 34.4 us  [the longest x1 8.42 us: on_device(): jnp.einsum('sexf,efd->sexd', hidden_all, down_by_feature, preferred_eleme...]
  transfers between devices with their start and end apart: 9 -> 7, of which waited for: 6 -> 5; matrix products, arithmetic and copies ran while one was open for 17% -> 25% of each run, Pallas kernels for 0% -> 0%
where the time goes in v1:
time: 289 us; the launch traced here: 288 us
  waiting for transfers between devices  115 us (40%)
  blocking collectives  66.5 us (23%)
  matrix products  39.7 us (14%)
  local copies, waits for them, and re-layouts  27.9 us (10%)
  between operations  13.5 us (5%)
  other arithmetic  13.3 us (5%)
  starting transfers between devices  11.8 us (4%)
    all_to_all x1, blocking collectives, on_device(): lax.all_to_all(outgoing, 'col', split_axis=0, concat_axis=0, tiled=True)  66.5 us
    all_gather x1, waiting for transfers between devices, on_device(): hidden_all = lax.all_gather(hidden, 'row', axis=3, tiled=True)  47.7 us
    all_to_all x1, waiting for transfers between devices, on_device(): lax.all_to_all(expert_value, 'col', split_axis=0, concat_axis=0, tiled=True)  28.6 us
    all_gather x1, waiting for transfers between devices, on_device(): lax.all_gather(jnp.concatenate([tokens, picked_input_factor.reshape(reduc...  23.9 us
    all_gather x1, waiting for transfers between devices, on_device(): shared_full = lax.all_gather(shared_stack, 'col', axis=1, tiled=True)  12.9 us
    dot_general x1, matrix products, on_device(): jnp.einsum('sexf,efd->sexd', hidden_all, down_by_feature, preferred_eleme...  8.42 us
    dot_general x2, matrix products, project(): jnp.einsum('sexd,edf->sexf', other_half, half_weights(w, 1 - half), prefe...  8.22 us
    all_to_all x1, starting transfers between devices, on_device(): lax.all_to_all(expert_value, 'col', split_axis=0, concat_axis=0, tiled=True)  6.99 us
  transfers between devices with their start and end apart: 7, of which 5 were waited for; matrix products, arithmetic and copies ran while one was open for 25% of the time, Pallas kernels for 0%

profile of v1, /device:TPU:0, one launch (start us, length us, event | category | flops | bytes accessed | tf_op | source)
XLA Modules:
  0.0 288.0 jit_solution(5609938968949109063)
XLA Ops:
  6.5 0.8 compare_and_fusion.1
  7.3 0.7 compare_select_fusion.1
  8.0 0.1 broadcast_in_dim.95
  8.1 0.1 broadcast_in_dim.96
  8.2 1.6 gather_fusion
  9.8 0.1 bitcast_select_fusion.1
  9.9 1.6 pad_maximum_fusion.1
  11.5 0.0 all-gather.4.cloned.1.call-update
  11.5 0.0 all-gather.8.cloned.1.call-start
  11.6 2.0 pad_maximum_fusion
  13.6 0.0 all-gather.8.cloned.1.call-update
  13.6 0.0 all-gather.6.cloned.1.call-start
  13.7 0.6 reduce-window.18
  14.3 0.2 slice_reduce_fusion
  14.5 0.1 convert_subtract_fusion
  14.7 2.6 fusion.2
  17.3 23.9 %all-gather.4.cloned.1.call-done = bf16[512,2048]{1,0:T(8,128)(2,1)} async-done(((bf16[512,256]{1,0:T(8,128)(2,1)}), bf16[512,2048]{1,0:T(8,128)(2,1)}) %all-gather.4.cloned.1.call-update) | async-done | bytes 2097168 | tf_op jit(solution)/shard_map/all_gather | solution.py:34
  41.2 1.2 slice-done
  42.4 1.3 convolution_convert_fusion
  43.7 66.5 %all_to_all.28 = bf16[16,2,64,1024]{3,2,1,0:T(8,128)(2,1)S(1)} all-to-all(bf16[16,2,64,1024]{3,2,1,0:T(8,128)(2,1)S(1)} %bitcast.97), channel_id=1, replica_groups=mesh['row'=8,'col'=16] {'col'}, dimensions={0} | all-to-all | bytes 8388608 | tf_op jit(solution)/shard_map/all_to_all | solution.py:100
  110.2 2.5 copy.56
  112.6 0.8 copy-done.1
  113.4 0.0 collective-permute-start
  113.4 3.6 %fusion.24 = f32[2,176,16,64]{1,3,2,0:T(8,128)S(1)} fusion(bf16[2,2048,176]{1,2,0:T(8,128)(2,1)S(1)} %copy-done.9, s32[]{:T(128)S(6)} %select_n.73, bf16[16,2,64,1024]{3,2,1,0:T(8,128)(2,1)} %copy-done.1), kind=kOutput, calls=%fused_computation.36 | convolution fusion | flops 738197504 | bytes 6356996 | tf_op jit(solution)/shard_map/sexd,edf->sexf/dot_general | solution.py:107
  117.1 0.5 copy-done.10
  117.5 1.3 fusion.20
  118.8 2.1 collective-permute-done
  120.9 3.5 %fusion.22 = f32[2,176,16,64]{1,3,2,0:T(8,128)S(1)} fusion(bf16[16,2,64,1024]{3,2,0,1:T(8,128)(2,1)} %collective-permute-done, bf16[2,2048,176]{1,2,0:T(8,128)(2,1)S(1)} %copy-done.9, s32[]{:T(128)S(6)} %select_n.74), kind=kOutput, calls=%fused_computation.34 | convolution fusion | flops 738197504 | bytes 6356996 | tf_op jit(solution)/shard_map/sexd,edf->sexf/dot_general | solution.py:109
  124.4 4.8 %fusion.7 = bf16[16,2,64,176]{3,2,0,1:T(8,128)(2,1)} fusion(f32[2,176,16,64]{1,3,2,0:T(8,128)S(1)} %fusion.20, f32[2,176,16,64]{1,3,2,0:T(8,128)S(1)} %fusion.24, f32[2,176,16,64]{1,3,2,0:T(8,128)S(1)} %fusion.22, bf16[16,2,64,1024]{3,2,0,1:T(8,128)(2,1)} %collective-permute-done, bf16[2,2048,176]{1,2,0:T(8,128)(2,1)S(1)} %copy-done.10, s32[]{:T(128)S(6)} %select_n.74), kind=kOutput, calls=%fused_computation.16 | convolution fusion | flops 741081088 | bytes 11927556 | tf_op jit(solution)/shard_map/sexd,edf->sexf/dot_general | solution.py:109
  129.1 3.2 %copy.59 = bf16[16,2,64,176]{2,0,1,3:T(8,128)(2,1)} copy(bf16[16,2,64,176]{3,2,0,1:T(8,128)(2,1)} %fusion.7) | data formatting | bytes 1441792 | tf_op jit(solution)/shard_map/convert_element_type | solution.py:115
  132.3 0.0 all-gather.6.cloned.1.call-update
  132.3 3.8 %copy.60 = bf16[2,176,2048]{1,0,2:T(2,128)(2,1)} copy(bf16[2,176,2048]{2,1,0:T(8,128)(2,1)S(1)} %copy-done.4) | data formatting | bytes 2883584 | tf_op args[8]
  136.2 4.7 %all-to-all-start.1 = ((bf16[2,176,2048]{1,0,2:T(2,128)(2,1)}), bf16[2,176,2048]{1,0,2:T(2,128)(2,1)}, u32[]{:S(2)}, u32[]{:S(2)}) async-start(bf16[2,176,2048]{1,0,2:T(2,128)(2,1)} %copy.60), calls=%async_computation.1 | async-start | bytes 4194304 | tf_op jit(solution)/shard_map/all_to_all | solution.py:55
  140.9 0.0 reduce-scatter.2.cloned.1.call-start
  140.9 0.1 copy.65
  141.1 0.1 reduce.1
  141.2 0.6 gather_fusion.2
  141.8 0.1 convert_reduce_fusion
  141.9 0.1 select_reduce_fusion.2
  142.0 0.1 bitcast_select_fusion
  142.1 1.6 fusion.46
  143.7 2.0 fusion.17
  145.7 12.9 %all-gather.8.cloned.1.call-done = bf16[3,2048,704]{1,2,0:T(8,128)(2,1)} async-done(((bf16[3,128,704]{1,2,0:T(8,128)(2,1)}), bf16[3,2048,704]{1,2,0:T(8,128)(2,1)}) %all-gather.8.cloned.1.call-update) | async-done | bytes 8650768 | tf_op jit(solution)/shard_map/all_gather | solution.py:53
  158.6 3.2 %fusion.4 = f32[256,704]{0,1:T(8,128)S(1)} fusion(bf16[3,2048,704]{1,2,0:T(8,128)(2,1)} %all-gather.8.cloned.1.call-done, bf16[512,2048]{1,0:T(8,128)(2,1)} %all-gather.4.cloned.1.call-done), kind=kOutput, calls=%fused_computation.11 | convolution fusion | flops 738197504 | bytes 4653056 | tf_op jit(solution)/shard_map/dot_general | solution.py:126
  161.8 3.7 %fusion.5 = f32[256,704]{0,1:T(8,128)} fusion(bf16[3,2048,704]{1,2,0:T(8,128)(2,1)} %all-gather.8.cloned.1.call-done, bf16[512,2048]{1,0:T(8,128)(2,1)S(1)} %copy-done.3), kind=kOutput, calls=%fused_computation.13 | convolution fusion | flops 738197504 | bytes 4653056 | tf_op jit(solution)/shard_map/dot_general | solution.py:125
  165.5 4.8 %fusion.6 = f32[256,2048]{1,0:T(8,128)} fusion(bf16[3,2048,704]{1,2,0:T(8,128)(2,1)} %all-gather.8.cloned.1.call-done, f32[256,704]{0,1:T(8,128)S(1)} %fusion.4, bf16[256,256]{1,0:T(8,128)(2,1)S(1)} %fusion.17, bf16[256,704]{1,0:T(8,128)(2,1)S(1)} %bitcast_select_fusion, f32[256]{0:T(256)S(1)} %add_divide_fusion, f32[256,704]{0,1:T(8,128)} %fusion.5), kind=kOutput, calls=%fused_computation.14 | convolution fusion | flops 832438272 | bytes 6915072 | tf_op jit(solution)/shard_map/dot_general | solution.py:130
  170.3 0.0 reduce-scatter.2.cloned.1.call-update
  170.3 0.0 all-to-all-done.1
  170.3 4.8 %copy.61 = bf16[2,176,8,256]{3,1,2,0:T(8,128)(2,1)S(1)} copy(bf16[2,176,8,256]{1,0,3,2:T(2,128)(2,1)} %bitcast.14) | data formatting | bytes 2883584 | tf_op jit(solution)/shard_map/all_to_all | solution.py:55
  175.1 47.7 %all-gather.6.cloned.1.call-done = bf16[16,2,64,1408]{2,0,1,3:T(8,128)(2,1)} async-done(((bf16[16,2,64,176]{2,0,1,3:T(8,128)(2,1)}), bf16[16,2,64,1408]{2,0,1,3:T(8,128)(2,1)}) %all-gather.6.cloned.1.call-update) | async-done | bytes 5767184 | tf_op jit(solution)/shard_map/all_gather | solution.py:116
  222.8 8.4 %fusion.11 = f32[16,2,64,256]{3,2,0,1:T(8,128)S(1)} fusion(bf16[2,1408,256,1]{2,1,3,0:T(8,128)(2,1)S(1)} %bitcast.98, bf16[16,2,64,1408]{2,0,1,3:T(8,128)(2,1)} %all-gather.6.cloned.1.call-done), kind=kOutput, calls=%fused_computation.22 | convolution fusion | flops 1476395008 | bytes 9306112 | tf_op jit(solution)/shard_map/sexf,efd->sexd/dot_general | solution.py:117
  231.2 1.6 copy.63
  232.8 7.0 %all-to-all-start.2 = ((f32[16,2,64,256]{3,2,1,0:T(8,128)}), f32[16,2,64,256]{3,2,1,0:T(8,128)}, u32[]{:S(2)}, u32[]{:S(2)}) async-start(f32[16,2,64,256]{3,2,1,0:T(8,128)} %copy.63), calls=%async_computation.2 | async-start | bytes 4194304 | tf_op jit(solution)/shard_map/all_to_all | solution.py:120
  239.8 0.2 copy.55
  240.0 0.1 copy.64
  240.2 0.1 reshape.113
  240.3 1.7 fusion.51
  242.1 0.1 copy.52
  242.2 28.6 %all-to-all-done.2 = f32[16,2,64,256]{3,2,1,0:T(8,128)} async-done(((f32[16,2,64,256]{3,2,1,0:T(8,128)}), f32[16,2,64,256]{3,2,1,0:T(8,128)}, u32[]{:S(2)}, u32[]{:S(2)}) %all-to-all-start.2) | async-done | bytes 2097184 | tf_op jit(solution)/shard_map/all_to_all | solution.py:120
  270.8 5.1 %gather_fusion.1 = f32[1024,256]{1,0:T(8,128)S(1)} fusion(f32[2048,256]{1,0:T(8,128)} %bitcast.20, s32[1024]{0:T(1024)S(1)} %broadcast_clamp_fusion), kind=kCustom, calls=%fused_computation.1 | custom fusion | bytes 2101248 | tf_op jit(solution)/shard_map/jit(_take)/gather | solution.py:122
  275.9 1.3 reshape.112
  277.2 2.5 multiply_reduce_fusion
  279.7 0.0 reduce-scatter.2.cloned.1.call-done
  279.8 1.7 add.81
  (40 shorter events, 0.3 us)
Async XLA Ops:
  6.5 134.7 %copy-start = (bf16[64,16,704]{2,1,0:T(8,128)(2,1)S(1)}, bf16[64,16,704]{2,1,0:T(8,128)(2,1)}, u32[]{:S(2)}) copy-start(bf16[64,16,704]{2,1,0:T(8,128)(2,1)} %param.25) | copy-start | bytes 4325380
  6.5 7.1 %copy-start.5 = (s32[256,4]{0,1:T(4,128)S(1)}, s32[256,4]{0,1:T(4,128)}, u32[]{:S(2)}) copy-start(s32[256,4]{0,1:T(4,128)} %param.26) | copy-start | bytes 12292
  6.5 34.6 %all-gather.4.cloned.1.call-start = ((), (), s32[]{:S(2)}) async-start(), calls=%async_computation.4 | async-start | bytes 2359296 | tf_op jit(solution)/shard_map/all_gather | solution.py:34
  11.5 147.1 %all-gather.8.cloned.1.call-start = ((), (), s32[]{:S(2)}) async-start(), calls=%async_computation.6 | async-start | bytes 9191424 | tf_op jit(solution)/shard_map/all_gather | solution.py:53
  13.6 209.2 %all-gather.6.cloned.1.call-start = ((), (), s32[]{:S(2)}) async-start(), calls=%async_computation.5 | async-start | bytes 12976128 | tf_op jit(solution)/shard_map/all_gather | solution.py:116
  41.2 1.2 slice-start
  110.2 3.2 %copy-start.1 = (bf16[16,2,64,1024]{3,2,1,0:T(8,128)(2,1)}, bf16[16,2,64,1024]{3,2,1,0:T(8,128)(2,1)S(1)}, u32[]{:S(2)}) copy-start(bf16[16,2,64,1024]{3,2,1,0:T(8,128)(2,1)S(1)} %all_to_all.28) | copy-start | bytes 12582916
  110.2 3.2 %copy-start.9 = (bf16[2,2048,176]{1,2,0:T(8,128)(2,1)S(1)}, bf16[2,2048,176]{1,2,0:T(8,128)(2,1)}, u32[]{:S(2)}) copy-start(bf16[2,2048,176]{1,2,0:T(8,128)(2,1)} %param.21) | copy-start | bytes 4325380
  113.4 7.5 %collective-permute-start = (bf16[16,2,64,1024]{3,2,0,1:T(8,128)(2,1)}, bf16[16,2,64,1024]{3,2,0,1:T(8,128)(2,1)}, u32[]{:S(2)}, u32[]{:S(2)}) collective-permute-start(bf16[16,2,64,1024]{3,2,0,1:T(8,128)(2,1)} %copy.56), channel_id=1, source_target_pairs={{0,16},{16,0},{32,48},{48,32},{64,80},{80,64},{96,112},{112,96},{1... | collective-permute-start | bytes 12582920 | tf_op jit(solution)/shard_map/ppermute | solution.py:101
  113.4 3.6 %copy-start.2 = (bf16[16,2,64,1024]{3,2,1,0:T(8,128)(2,1)S(1)}, bf16[16,2,64,1024]{3,2,1,0:T(8,128)(2,1)}, u32[]{:S(2)}) copy-start(bf16[16,2,64,1024]{3,2,1,0:T(8,128)(2,1)} %copy-done.1) | copy-start | bytes 12582916
  113.4 4.1 %copy-start.10 = (bf16[2,2048,176]{1,2,0:T(8,128)(2,1)S(1)}, bf16[2,2048,176]{1,2,0:T(8,128)(2,1)}, u32[]{:S(2)}) copy-start(bf16[2,2048,176]{1,2,0:T(8,128)(2,1)} %param.22) | copy-start | bytes 4325380
  129.1 3.2 %copy-start.4 = (bf16[2,176,2048]{2,1,0:T(8,128)(2,1)S(1)}, bf16[2,176,2048]{2,1,0:T(8,128)(2,1)}, u32[]{:S(2)}) copy-start(bf16[2,176,2048]{2,1,0:T(8,128)(2,1)} %param.23) | copy-start | bytes 4325380
  136.2 4.7 %copy-start.6 = (bf16[2048]{0:T(1024)(128)(2,1)S(1)}, bf16[2048]{0:T(1024)(128)(2,1)}, u32[]{:S(2)}) copy-start(bf16[2048]{0:T(1024)(128)(2,1)} %param.17) | copy-start | bytes 12292
  136.2 4.8 %copy-start.7 = (s32[1,16]{1,0:T(1,128)S(1)}, s32[1,16]{1,0:T(1,128)}, u32[]{:S(2)}) copy-start(s32[1,16]{1,0:T(1,128)} %param.27) | copy-start | bytes 196
  136.2 5.7 %copy-start.8 = (s32[1,16]{1,0:T(1,128)S(1)}, s32[1,16]{1,0:T(1,128)}, u32[]{:S(2)}) copy-start(s32[1,16]{1,0:T(1,128)} %param.28) | copy-start | bytes 196
  136.2 34.1 %all-to-all-start.1 = ((bf16[2,176,2048]{1,0,2:T(2,128)(2,1)}), bf16[2,176,2048]{1,0,2:T(2,128)(2,1)}, u32[]{:S(2)}, u32[]{:S(2)}) async-start(bf16[2,176,2048]{1,0,2:T(2,128)(2,1)} %copy.60), calls=%async_computation.1 | async-start | bytes 4194304 | tf_op jit(solution)/shard_map/all_to_all | solution.py:55
  140.9 138.9 %reduce-scatter.2.cloned.1.call-start = ((), (), s32[]{:S(2)}) async-start(), calls=%async_computation.7 | async-start | bytes 2359296 | tf_op jit(solution)/shard_map/reduce_scatter | solution.py:137
  158.6 3.2 %copy-start.3 = (bf16[512,2048]{1,0:T(8,128)(2,1)S(1)}, bf16[512,2048]{1,0:T(8,128)(2,1)}, u32[]{:S(2)}) copy-start(bf16[512,2048]{1,0:T(8,128)(2,1)} %all-gather.4.cloned.1.call-done) | copy-start | bytes 6291460
  232.8 7.5 %copy-start.11 = (bf16[2048,32]{0,1:T(8,128)(2,1)S(1)}, bf16[2048,32]{0,1:T(8,128)(2,1)}, u32[]{:S(2)}) copy-start(bf16[2048,32]{0,1:T(8,128)(2,1)} %param.16) | copy-start | bytes 393220
  232.8 38.0 %all-to-all-start.2 = ((f32[16,2,64,256]{3,2,1,0:T(8,128)}), f32[16,2,64,256]{3,2,1,0:T(8,128)}, u32[]{:S(2)}, u32[]{:S(2)}) async-start(f32[16,2,64,256]{3,2,1,0:T(8,128)} %copy.63), calls=%async_computation.2 | async-start | bytes 4194304 | tf_op jit(solution)/shard_map/all_to_all | solution.py:120
Sparse Core Ops, SparseCore 0:
  11.7 29.4 all-gather.3
  43.3 115.2 all-gather.7
  160.3 62.4 all-gather.5
  225.1 34.8 reduce-scatter.1

commit v2 on v1

--- a/solution.py
+++ b/solution.py
@@ -4,6 +4,20 @@
 from jax.sharding import PartitionSpec as P
 
 ADAPTER_SCALE = 2.0
+
+
+def row_blocks(x, row_count, row_id):
+    same_core = [x]
+    sources = [row_id]
+    for shift in range(2, row_count, 2):
+        same_core.append(
+            lax.ppermute(x, "row", [(i, (i + shift) % row_count) for i in range(row_count)])
+        )
+        sources.append((row_id - shift) % row_count)
+    own = jnp.stack(same_core)
+    other = lax.ppermute(own, "row", [(i, i ^ 1) for i in range(row_count)])
+    source = jnp.stack(sources).astype(jnp.int32)
+    return jnp.concatenate([own, other]), jnp.concatenate([source, source ^ 1])
 
 
 def on_device(
@@ -31,14 +45,19 @@
     picked_input_factor = jnp.take(adapter_input_factor, active_adapter_index, axis=0)
     rank_width = picked_input_factor.shape[1]
     reduced_rank_value = picked_input_factor.shape[0] * rank_width
-    gathered = lax.all_gather(
+    blocks, source = row_blocks(
         jnp.concatenate(
             [tokens, picked_input_factor.reshape(reduced_rank_value, local_width)], axis=0
         ),
-        "row",
-        axis=1,
-        tiled=True,
+        row_count,
+        row_id,
     )
+    row_ids = jnp.arange(row_count, dtype=jnp.int32)
+    position = jnp.sum(
+        jnp.where(source[None, :] == row_ids[:, None], row_ids[None, :], 0), axis=1
+    )
+    ordered = jnp.take(blocks, position, axis=0)
+    gathered = jnp.transpose(ordered, (1, 0, 2)).reshape(ordered.shape[1], row_count * local_width)
     all_features = gathered[:token_count]
     full_in = gathered[token_count:]
     full_width = all_features.shape[1]
@@ -113,9 +132,15 @@
     gate_part = project(routed_gate_weight)
     up_part = project(routed_up_weight)
     hidden = (jax.nn.silu(gate_part) * up_part).astype(jnp.bfloat16)
-    hidden_all = lax.all_gather(hidden, "row", axis=3, tiled=True)
+    hidden_blocks, hidden_source = row_blocks(hidden, row_count, row_id)
+    local_hidden = hidden.shape[3]
+    down_blocks = jnp.take(
+        down_by_feature.reshape(local_experts, row_count, local_hidden, local_width),
+        hidden_source,
+        axis=1,
+    )
     expert_value = jnp.einsum(
-        "sexf,efd->sexd", hidden_all, down_by_feature, preferred_element_type=jnp.float32
+        "isexf,eifd->sexd", hidden_blocks, down_blocks, preferred_element_type=jnp.float32
     )
     returned = lax.all_to_all(expert_value, "col", split_axis=0, concat_axis=0, tiled=True)
     flat_rows = returned.reshape(expert_count * capacity, local_width)

time: 289 us -> 308 us (1.066)
  waiting for transfers between devices: 115 us -> 86.4 us
  local copies, waits for them, and re-layouts: 27.9 us -> 54.8 us
  starting transfers between devices: 11.8 us -> 25.3 us
  other arithmetic: 13.3 us -> 20.7 us
  matrix products: 39.7 us -> 34 us
  blocking collectives: 66.5 us -> 71.5 us
    all_gather x2 -> x0, waiting for transfers between devices: 71.6 us -> none  [the longest x1 47.7 us: on_device(): hidden_all = lax.all_gather(hidden, 'row', axis=3, tiled=True)]
    ppermute x0 -> x8, waiting for transfers between devices: none -> 56.7 us  [the longest x6 56.6 us: row_blocks(): lax.ppermute(x, 'row', [(i, (i + shift) % row_count) for i in range(row_c...]
    unnamed x26 -> x44, local copies, waits for them, and re-layouts: 5.1 us -> 21.1 us
    all_gather x1, waiting for transfers between devices: 12.9 us -> 0.02 us  [on_device(): shared_full = lax.all_gather(shared_stack, 'col', axis=1, tiled=True)]
    ppermute x0 -> x8, starting transfers between devices: none -> 12 us  [the longest x6 11.9 us: row_blocks(): lax.ppermute(x, 'row', [(i, (i + shift) % row_count) for i in range(row_c...]
    concatenate x0 -> x4, local copies, waits for them, and re-layouts: none -> 7.36 us  [the longest x2 7.17 us: row_blocks(): jnp.concatenate([own, other])]
    another operation x5 -> x8, other arithmetic: 0.8 us -> 6.96 us  [the longest x3 6.17 us: row_blocks(): own = jnp.stack(same_core)]
    gather x0 -> x2, local copies, waits for them, and re-layouts: none -> 5.35 us  [the longest x1 3.59 us: on_device(): ordered = jnp.take(blocks, position, axis=0)]
  transfers between devices with their start and end apart: 7 -> 13, of which waited for: 5 -> 6; matrix products, arithmetic and copies ran while one was open for 25% -> 34% of each run, Pallas kernels for 0% -> 0%
where the time goes in v2:
time: 308 us; the launch traced here: 307 us
  waiting for transfers between devices  86.4 us (28%)
  blocking collectives  71.5 us (23%)
  local copies, waits for them, and re-layouts  54.8 us (18%)
  matrix products  34 us (11%)
  starting transfers between devices  25.3 us (8%)
  other arithmetic  20.7 us (7%)
  between operations  13.8 us (4%)
    all_to_all x1, blocking collectives, on_device(): lax.all_to_all(outgoing, 'col', split_axis=0, concat_axis=0, tiled=True)  71.5 us
    ppermute x6, waiting for transfers between devices, row_blocks(): lax.ppermute(x, 'row', [(i, (i + shift) % row_count) for i in range(row_c...  56.6 us
    all_to_all x1, waiting for transfers between devices, on_device(): lax.all_to_all(expert_value, 'col', split_axis=0, concat_axis=0, tiled=True)  29.7 us
    unnamed x44, local copies, waits for them, and re-layouts  21.1 us
    ppermute x6, starting transfers between devices, row_blocks(): lax.ppermute(x, 'row', [(i, (i + shift) % row_count) for i in range(row_c...  11.9 us
    dot_general x2, matrix products, project(): jnp.einsum('sexd,edf->sexf', other_half, half_weights(w, 1 - half), prefe...  8.79 us
    concatenate x2, local copies, waits for them, and re-layouts, row_blocks(): jnp.concatenate([own, other])  7.17 us
    dot_general x1, matrix products, on_device(): jnp.einsum('isexf,eifd->sexd', hidden_blocks, down_blocks, preferred_elem...  6.66 us
  transfers between devices with their start and end apart: 13, of which 6 were waited for; matrix products, arithmetic and copies ran while one was open for 34% of the time, Pallas kernels for 0%

profile of v2, /device:TPU:0, one launch (start us, length us, event | category | flops | bytes accessed | tf_op | source)
XLA Modules:
  0.0 306.5 jit_solution(4586298467919034229)
XLA Ops:
  6.5 2.1 pad_maximum_fusion.2
  8.7 0.7 compare_and_fusion.2
  9.5 0.7 compare_select_fusion.4
  10.2 1.6 gather_fusion
  11.9 0.7 fusion.51
  12.6 4.0 %collective-permute-start.1 = (bf16[512,256]{1,0:T(8,128)(2,1)}, bf16[512,256]{1,0:T(8,128)(2,1)S(1)}, u32[]{:S(2)}, u32[]{:S(2)}) collective-permute-start(bf16[512,256]{1,0:T(8,128)(2,1)} %get-tuple-element.8), channel_id=1, source_target_pairs={{0,64},{16,80},{32,96},{48,112},{64,0},{80,16},{96,32},{112,48},{1... | collective-permute-start | bytes 786440 | tf_op jit(solution)/shard_map/ppermute | solution.py:14
  16.6 1.0 collective-permute-start
  17.6 2.2 collective-permute-start.2
  20.1 0.6 reduce-window.18
  21.0 0.7 constant_dynamic-update-slice_fusion.4
  21.7 2.6 fusion.2
  24.5 4.2 %collective-permute-done = bf16[512,256]{1,0:T(8,128)(2,1)S(1)} collective-permute-done((bf16[512,256]{1,0:T(8,128)(2,1)}, bf16[512,256]{1,0:T(8,128)(2,1)S(1)}, u32[]{:S(2)}, u32[]{:S(2)}) %collective-permute-start) | collective-permute-done | bytes 262176 | tf_op jit(solution)/shard_map/ppermute | solution.py:14
  28.8 0.8 collective-permute-done.2
  29.5 0.7 copy-done.8
  30.2 1.3 pad_maximum_fusion.1
  31.6 1.7 constant_dynamic-update-slice_fusion.3
  33.3 1.7 constant_dynamic-update-slice_fusion.2
  35.0 1.7 constant_dynamic-update-slice_fusion.1
  36.7 2.3 constant_dynamic-update-slice_fusion
  39.0 3.6 %gather_fusion.1 = bf16[8,512,256]{2,1,0:T(8,128)(2,1)} fusion(bf16[8,512,256]{2,1,0:T(8,128)(2,1)} %constant_dynamic-update-slice_fusion, s32[1024]{0:T(1024)S(1)} %pad_clamp_fusion.1), kind=kCustom, calls=%fused_computation.1 | custom fusion | bytes 4194336 | tf_op jit(solution)/shard_map/jit(_take)/gather | solution.py:59
  42.6 1.9 select_bitcast_fusion
  44.5 1.4 copy-done.4
  45.8 1.1 slice.43
  46.9 1.5 copy.70
  48.4 1.3 convolution_convert_fusion
  49.7 71.5 %all_to_all.25 = bf16[16,2,64,1024]{3,2,1,0:T(8,128)(2,1)S(1)} all-to-all(bf16[16,2,64,1024]{3,2,1,0:T(8,128)(2,1)S(1)} %bitcast.147), channel_id=1, replica_groups=mesh['row'=8,'col'=16] {'col'}, dimensions={0} | all-to-all | bytes 8388608 | tf_op jit(solution)/shard_map/all_to_all | solution.py:119
  121.2 2.7 copy.78
  123.9 0.6 copy-done.2
  124.4 6.0 %copy.75 = bf16[2,176,2048]{1,0,2:T(2,128)(2,1)} copy(bf16[2,176,2048]{2,1,0:T(8,128)(2,1)} %param.23) | data formatting | bytes 2883584 | tf_op args[8]
  130.5 6.5 %all-to-all-start = ((bf16[2,176,2048]{1,0,2:T(2,128)(2,1)}), bf16[2,176,2048]{1,0,2:T(2,128)(2,1)}, u32[]{:S(2)}, u32[]{:S(2)}) async-start(bf16[2,176,2048]{1,0,2:T(2,128)(2,1)} %copy.75), calls=%async_computation | async-start | bytes 4194304 | tf_op jit(solution)/shard_map/all_to_all | solution.py:74
  136.9 0.2 reduce-scatter.2.cloned.1.call-start
  137.6 3.8 %fusion.26 = f32[2,176,16,64]{1,3,2,0:T(8,128)S(1)} fusion(bf16[2,2048,176]{1,2,0:T(8,128)(2,1)} %param.21, s32[]{:T(128)S(6)} %select_n.149, bf16[16,2,64,1024]{3,2,1,0:T(8,128)(2,1)} %copy-done.2), kind=kOutput, calls=%fused_computation.44 | convolution fusion | flops 738197504 | bytes 6356996 | tf_op jit(solution)/shard_map/sexd,edf->sexf/dot_general | solution.py:126
  141.5 0.2 copy-done.17
  141.7 1.3 fusion.22
  143.1 3.5 %fusion.24 = f32[2,176,16,64]{1,3,2,0:T(8,128)S(1)} fusion(bf16[16,2,64,1024]{3,2,0,1:T(8,128)(2,1)} %collective-permute-done.4, bf16[2,2048,176]{1,2,0:T(8,128)(2,1)S(1)} %copy-done.16, s32[]{:T(128)S(6)} %select_n.150), kind=kOutput, calls=%fused_computation.42 | convolution fusion | flops 738197504 | bytes 6356996 | tf_op jit(solution)/shard_map/sexd,edf->sexf/dot_general | solution.py:128
  146.5 5.3 %constant_dynamic-update-slice_fusion.9 = (bf16[8,16,2,64,176]{4,3,1,2,0:T(8,128)(2,1)}, bf16[16,2,64,176]{3,2,0,1:T(8,128)(2,1)}) fusion(f32[2,176,16,64]{1,3,2,0:T(8,128)S(1)} %fusion.22, bf16[16,2,64,1024]{3,2,0,1:T(8,128)(2,1)} %collective-permute-done.4, bf16[2,2048,176]{1,2,0:T(8,128)(2,1)S(1)} %copy-done.17, s32[]{:T(128)S(6)} %select_n.150, ...), kind=kOutput, calls=%fused_computation.81 | convolution fusion | flops 741081088 | bytes 13303812 | tf_op jit(solution)/shard_map/sexd,edf->sexf/dot_general | solution.py:128
  151.9 3.0 collective-permute-start.7
  154.9 0.9 collective-permute-start.6
  155.7 0.9 collective-permute-start.5
  156.7 0.6 gather_fusion.4
  157.5 28.3 %collective-permute-done.7 = bf16[16,2,64,176]{3,2,0,1:T(8,128)(2,1)} collective-permute-done((bf16[16,2,64,176]{3,2,0,1:T(8,128)(2,1)}, bf16[16,2,64,176]{3,2,0,1:T(8,128)(2,1)}, u32[]{:S(2)}, u32[]{:S(2)}) %collective-permute-start.7) | collective-permute-done | bytes 720928 | tf_op jit(solution)/shard_map/ppermute | solution.py:14
  185.8 1.5 collective-permute-done.6
  187.3 21.9 %collective-permute-done.5 = bf16[16,2,64,176]{3,2,0,1:T(8,128)(2,1)} collective-permute-done((bf16[16,2,64,176]{3,2,0,1:T(8,128)(2,1)}, bf16[16,2,64,176]{3,2,0,1:T(8,128)(2,1)}, u32[]{:S(2)}, u32[]{:S(2)}) %collective-permute-start.5) | collective-permute-done | bytes 720928 | tf_op jit(solution)/shard_map/ppermute | solution.py:14
  209.2 4.2 %pad_maximum_fusion = bf16[4,16,2,64,176]{4,3,1,2,0:T(8,128)(2,1)} fusion(bf16[1,16,2,64,176]{4,3,1,2,0:T(8,128)(2,1)} %bitcast.39, bf16[1,16,2,64,176]{4,3,1,2,0:T(8,128)(2,1)} %bitcast.38, bf16[1,16,2,64,176]{4,3,1,2,0:T(8,128)(2,1)} %bitcast.37, bf16[1,16,2,64,176]{4,3,1,2,0:T(8,128)(2,1)} %bitcast.36), kind=kLoop, calls=%fused_computation.9 | loop fusion | flops 4325376 | bytes 5767168 | tf_op jit(solution)/shard_map/stack | solution.py:17
  213.3 0.2 fusion.54
  213.6 0.5 fusion.19
  214.1 2.7 fusion.5
  216.8 3.6 %fusion.4 = f32[256,704]{0,1:T(8,128)} fusion(bf16[256,2048]{0,1:T(8,128)(2,1)S(1)} %bitcast.151, bf16[3,2048,704]{1,2,0:T(8,128)(2,1)} %all-gather.2.cloned.1.call-done), kind=kOutput, calls=%fused_computation.14 | convolution fusion | flops 738197504 | bytes 4653056 | tf_op jit(solution)/shard_map/dot_general | solution.py:151
  220.5 4.8 %fusion.6 = f32[256,2048]{1,0:T(8,128)} fusion(bf16[3,2048,704]{1,2,0:T(8,128)(2,1)} %all-gather.2.cloned.1.call-done, f32[256,704]{0,1:T(8,128)} %fusion.4, bf16[256,256]{1,0:T(8,128)(2,1)S(1)} %fusion.19, bf16[256,704]{1,0:T(8,128)(2,1)S(1)} %bitcast_select_fusion, f32[256]{0:T(256)S(1)} %add_divide_fusion, f32[256,704]{0,1:T(8,128)S(1)} %fusion.5), kind=kOutput, calls=%fused_computation.17 | convolution fusion | flops 832438272 | bytes 6915072 | tf_op jit(solution)/shard_map/dot_general | solution.py:155
  225.3 4.7 %copy.77 = bf16[2,176,8,256]{3,1,2,0:T(8,128)(2,1)S(1)} copy(bf16[2,176,8,256]{1,0,3,2:T(2,128)(2,1)} %bitcast.15) | data formatting | bytes 2883584 | tf_op jit(solution)/shard_map/all_to_all | solution.py:74
  230.0 1.8 gather_fusion.2
  231.7 2.3 constant_dynamic-update-slice_fusion.8
  234.0 2.3 constant_dynamic-update-slice_fusion.7
  236.4 2.3 constant_dynamic-update-slice_fusion.6
  238.7 4.9 %constant_dynamic-update-slice_fusion.5 = bf16[8,16,2,64,176]{4,3,1,2,0:T(8,128)(2,1)} fusion(bf16[8,16,2,64,176]{4,3,1,2,0:T(8,128)(2,1)} %constant_dynamic-update-slice_fusion.6, bf16[4,16,2,64,176]{4,3,1,2,0:T(8,128)(2,1)} %collective-permute-done.8), kind=kLoop, calls=%fused_computation.77 | loop fusion | bytes 8388608 | tf_op jit(solution)/shard_map/concatenate | solution.py:20
  243.6 6.7 %fusion.11 = f32[16,2,64,256]{3,2,0,1:T(8,128)S(1)} fusion(bf16[8,16,2,64,176]{4,3,1,2,0:T(8,128)(2,1)} %constant_dynamic-update-slice_fusion.5, bf16[8,2,176,256]{3,2,1,0:T(8,128)(2,1)S(1)} %copy-done.6, pred[8]{0:T(512)(128)(4,1)S(1)} %compare_and_fusion.1), kind=kOutput, calls=%fused_computation.26 | convolution fusion | flops 1477115904 | bytes 9306120 | tf_op jit(solution)/shard_map/isexf,eifd->sexd/dot_general | solution.py:142
  250.2 1.4 copy.83
  251.7 6.6 %all-to-all-start.2 = ((f32[16,2,64,256]{3,2,1,0:T(8,128)}), f32[16,2,64,256]{3,2,1,0:T(8,128)}, u32[]{:S(2)}, u32[]{:S(2)}) async-start(f32[16,2,64,256]{3,2,1,0:T(8,128)} %copy.83), calls=%async_computation.2 | async-start | bytes 4194304 | tf_op jit(solution)/shard_map/all_to_all | solution.py:145
  258.7 0.3 fusion.55
  259.3 29.7 %all-to-all-done.2 = f32[16,2,64,256]{3,2,1,0:T(8,128)} async-done(((f32[16,2,64,256]{3,2,1,0:T(8,128)}), f32[16,2,64,256]{3,2,1,0:T(8,128)}, u32[]{:S(2)}, u32[]{:S(2)}) %all-to-all-start.2) | async-done | bytes 2097184 | tf_op jit(solution)/shard_map/all_to_all | solution.py:145
  289.0 5.2 %gather_fusion.3 = f32[1024,256]{1,0:T(8,128)S(1)} fusion(f32[2048,256]{1,0:T(8,128)} %bitcast.43, s32[1024]{0:T(1024)S(1)} %broadcast_clamp_fusion), kind=kCustom, calls=%fused_computation.3 | custom fusion | bytes 2101248 | tf_op jit(solution)/shard_map/jit(_take)/gather | solution.py:147
  294.1 1.3 reshape.451
  295.4 2.5 multiply_reduce_fusion
  298.0 1.7 add.133
  (86 shorter events, 2.7 us)
Async XLA Ops:
  6.5 150.2 %copy-start = (bf16[64,16,704]{2,1,0:T(8,128)(2,1)S(1)}, bf16[64,16,704]{2,1,0:T(8,128)(2,1)}, u32[]{:S(2)}) copy-start(bf16[64,16,704]{2,1,0:T(8,128)(2,1)} %param.25) | copy-start | bytes 4325380
  6.5 5.3 %copy-start.10 = (bf16[256,256]{1,0:T(8,128)(2,1)S(1)}, bf16[256,256]{1,0:T(8,128)(2,1)}, u32[]{:S(2)}) copy-start(bf16[256,256]{1,0:T(8,128)(2,1)} %param.15) | copy-start | bytes 393220
  6.5 13.5 %copy-start.12 = (s32[256,4]{0,1:T(4,128)S(1)}, s32[256,4]{0,1:T(4,128)}, u32[]{:S(2)}) copy-start(s32[256,4]{0,1:T(4,128)} %param.26) | copy-start | bytes 12292
  6.5 207.6 %all-gather.2.cloned.1.call-start = ((), (), s32[]{:S(2)}) async-start(), calls=%async_computation.4 | async-start | bytes 9191424 | tf_op jit(solution)/shard_map/all_gather | solution.py:72
  12.6 11.9 %collective-permute-start.1 = (bf16[512,256]{1,0:T(8,128)(2,1)}, bf16[512,256]{1,0:T(8,128)(2,1)S(1)}, u32[]{:S(2)}, u32[]{:S(2)}) collective-permute-start(bf16[512,256]{1,0:T(8,128)(2,1)} %get-tuple-element.8), channel_id=1, source_target_pairs={{0,64},{16,80},{32,96},{48,112},{64,0},{80,16},{96,32},{112,48},{1... | collective-permute-start | bytes 786440 | tf_op jit(solution)/shard_map/ppermute | solution.py:14
  16.6 12.1 %collective-permute-start = (bf16[512,256]{1,0:T(8,128)(2,1)}, bf16[512,256]{1,0:T(8,128)(2,1)S(1)}, u32[]{:S(2)}, u32[]{:S(2)}) collective-permute-start(bf16[512,256]{1,0:T(8,128)(2,1)} %get-tuple-element.8), channel_id=1, source_target_pairs={{0,32},{16,48},{32,64},{48,80},{64,96},{80,112},{96,0},{112,16},{1... | collective-permute-start | bytes 786440 | tf_op jit(solution)/shard_map/ppermute | solution.py:14
  17.6 11.9 %collective-permute-start.2 = (bf16[512,256]{1,0:T(8,128)(2,1)}, bf16[512,256]{1,0:T(8,128)(2,1)S(1)}, u32[]{:S(2)}, u32[]{:S(2)}) collective-permute-start(bf16[512,256]{1,0:T(8,128)(2,1)} %get-tuple-element.8), channel_id=1, source_target_pairs={{0,96},{16,112},{32,0},{48,16},{64,32},{80,48},{96,64},{112,80},{1... | collective-permute-start | bytes 786440 | tf_op jit(solution)/shard_map/ppermute | solution.py:14
  24.5 5.0 %copy-start.7 = (bf16[512,256]{1,0:T(8,128)(2,1)}, bf16[512,256]{1,0:T(8,128)(2,1)S(1)}, u32[]{:S(2)}) copy-start(bf16[512,256]{1,0:T(8,128)(2,1)S(1)} %collective-permute-done.1) | copy-start | bytes 786436
  28.8 0.8 copy-start.9
  29.5 0.7 copy-start.8
  31.5 5.2 %collective-permute-start.3 = (bf16[4,512,256]{2,1,0:T(8,128)(2,1)S(1)}, bf16[4,512,256]{2,1,0:T(8,128)(2,1)}, u32[]{:S(2)}, u32[]{:S(2)}) collective-permute-start(bf16[4,512,256]{2,1,0:T(8,128)(2,1)S(1)} %pad_maximum_fusion.1), channel_id=1, source_target_pairs={{0,16},{16,0},{32,48},{48,32},{64,80},{80,64},{96,112},{112,96},{1... | collective-permute-start | bytes 3145736 | tf_op jit(solution)/shard_map/ppermute | solution.py:18
  44.4 1.4 copy-start.4
  121.2 3.2 %copy-start.2 = (bf16[16,2,64,1024]{3,2,1,0:T(8,128)(2,1)}, bf16[16,2,64,1024]{3,2,1,0:T(8,128)(2,1)S(1)}, u32[]{:S(2)}) copy-start(bf16[16,2,64,1024]{3,2,1,0:T(8,128)(2,1)S(1)} %all_to_all.25) | copy-start | bytes 12582916
  124.4 18.6 %collective-permute-start.4 = (bf16[16,2,64,1024]{3,2,0,1:T(8,128)(2,1)}, bf16[16,2,64,1024]{3,2,0,1:T(8,128)(2,1)}, u32[]{:S(2)}, u32[]{:S(2)}) collective-permute-start(bf16[16,2,64,1024]{3,2,0,1:T(8,128)(2,1)} %copy.78), channel_id=1, source_target_pairs={{0,16},{16,0},{32,48},{48,32},{64,80},{80,64},{96,112},{112,96},{1... | collective-permute-start | bytes 12582920 | tf_op jit(solution)/shard_map/ppermute | solution.py:120
  130.5 6.7 %copy-start.14 = (s32[1,16]{1,0:T(1,128)S(1)}, s32[1,16]{1,0:T(1,128)}, u32[]{:S(2)}) copy-start(s32[1,16]{1,0:T(1,128)} %param.27) | copy-start | bytes 196
  130.5 7.0 %copy-start.15 = (s32[1,16]{1,0:T(1,128)S(1)}, s32[1,16]{1,0:T(1,128)}, u32[]{:S(2)}) copy-start(s32[1,16]{1,0:T(1,128)} %param.28) | copy-start | bytes 196
  130.5 94.8 %all-to-all-start = ((bf16[2,176,2048]{1,0,2:T(2,128)(2,1)}), bf16[2,176,2048]{1,0,2:T(2,128)(2,1)}, u32[]{:S(2)}, u32[]{:S(2)}) async-start(bf16[2,176,2048]{1,0,2:T(2,128)(2,1)} %copy.75), calls=%async_computation | async-start | bytes 4194304 | tf_op jit(solution)/shard_map/all_to_all | solution.py:74
  136.9 161.1 %reduce-scatter.2.cloned.1.call-start = ((), (), s32[]{:S(2)}) async-start(), calls=%async_computation.5 | async-start | bytes 2359296 | tf_op jit(solution)/shard_map/reduce_scatter | solution.py:162
  137.6 3.8 %copy-start.3 = (bf16[16,2,64,1024]{3,2,1,0:T(8,128)(2,1)S(1)}, bf16[16,2,64,1024]{3,2,1,0:T(8,128)(2,1)}, u32[]{:S(2)}) copy-start(bf16[16,2,64,1024]{3,2,1,0:T(8,128)(2,1)} %copy-done.2) | copy-start | bytes 12582916
  137.6 4.1 %copy-start.17 = (bf16[2,2048,176]{1,2,0:T(8,128)(2,1)S(1)}, bf16[2,2048,176]{1,2,0:T(8,128)(2,1)}, u32[]{:S(2)}) copy-start(bf16[2,2048,176]{1,2,0:T(8,128)(2,1)} %param.22) | copy-start | bytes 4325380
  141.7 1.4 copy-start.16
  146.5 10.2 %copy-start.13 = (bf16[2048]{0:T(1024)(128)(2,1)S(1)}, bf16[2048]{0:T(1024)(128)(2,1)}, u32[]{:S(2)}) copy-start(bf16[2048]{0:T(1024)(128)(2,1)} %param.17) | copy-start | bytes 12292
  151.9 33.9 %collective-permute-start.7 = (bf16[16,2,64,176]{3,2,0,1:T(8,128)(2,1)}, bf16[16,2,64,176]{3,2,0,1:T(8,128)(2,1)}, u32[]{:S(2)}, u32[]{:S(2)}) collective-permute-start(bf16[16,2,64,176]{3,2,0,1:T(8,128)(2,1)} %get-tuple-element.10), channel_id=1, source_target_pairs={{0,96},{16,112},{32,0},{48,16},{64,32},{80,48},{96,64},{112,80},{1... | collective-permute-start | bytes 2162696 | tf_op jit(solution)/shard_map/ppermute | solution.py:14
  154.9 32.4 %collective-permute-start.6 = (bf16[16,2,64,176]{3,2,0,1:T(8,128)(2,1)}, bf16[16,2,64,176]{3,2,0,1:T(8,128)(2,1)}, u32[]{:S(2)}, u32[]{:S(2)}) collective-permute-start(bf16[16,2,64,176]{3,2,0,1:T(8,128)(2,1)} %get-tuple-element.10), channel_id=1, source_target_pairs={{0,64},{16,80},{32,96},{48,112},{64,0},{80,16},{96,32},{112,48},{1... | collective-permute-start | bytes 2162696 | tf_op jit(solution)/shard_map/ppermute | solution.py:14
  155.7 53.4 %collective-permute-start.5 = (bf16[16,2,64,176]{3,2,0,1:T(8,128)(2,1)}, bf16[16,2,64,176]{3,2,0,1:T(8,128)(2,1)}, u32[]{:S(2)}, u32[]{:S(2)}) collective-permute-start(bf16[16,2,64,176]{3,2,0,1:T(8,128)(2,1)} %get-tuple-element.10), channel_id=1, source_target_pairs={{0,32},{16,48},{32,64},{48,80},{64,96},{80,112},{96,0},{112,16},{1... | collective-permute-start | bytes 2162696 | tf_op jit(solution)/shard_map/ppermute | solution.py:14
  209.2 4.4 %copy-start.5 = (bf16[512,8,256]{2,0,1:T(8,128)(2,1)S(1)}, bf16[512,8,256]{2,0,1:T(8,128)(2,1)}, u32[]{:S(2)}) copy-start(bf16[512,8,256]{2,0,1:T(8,128)(2,1)} %copy-done.4) | copy-start | bytes 6291460
  213.3 25.4 %collective-permute-start.8 = (bf16[4,16,2,64,176]{4,3,1,2,0:T(8,128)(2,1)}, bf16[4,16,2,64,176]{4,3,1,2,0:T(8,128)(2,1)}, u32[]{:S(2)}, u32[]{:S(2)}) collective-permute-start(bf16[4,16,2,64,176]{4,3,1,2,0:T(8,128)(2,1)} %pad_maximum_fusion), channel_id=1, source_target_pairs={{0,16},{16,0},{32,48},{48,32},{64,80},{80,64},{96,112},{112,96},{1... | collective-permute-start | bytes 8650760 | tf_op jit(solution)/shard_map/ppermute | solution.py:18
  238.7 4.9 %copy-start.6 = (bf16[8,2,176,256]{3,2,1,0:T(8,128)(2,1)S(1)}, bf16[8,2,176,256]{3,2,1,0:T(8,128)(2,1)}, u32[]{:S(2)}) copy-start(bf16[8,2,176,256]{3,2,1,0:T(8,128)(2,1)} %gather_fusion.2) | copy-start | bytes 4325380
  251.7 7.1 %copy-start.11 = (bf16[2048,32]{0,1:T(8,128)(2,1)S(1)}, bf16[2048,32]{0,1:T(8,128)(2,1)}, u32[]{:S(2)}) copy-start(bf16[2048,32]{0,1:T(8,128)(2,1)} %param.16) | copy-start | bytes 393220
  251.7 37.3 %all-to-all-start.2 = ((f32[16,2,64,256]{3,2,1,0:T(8,128)}), f32[16,2,64,256]{3,2,1,0:T(8,128)}, u32[]{:S(2)}, u32[]{:S(2)}) async-start(f32[16,2,64,256]{3,2,1,0:T(8,128)} %copy.83), calls=%async_computation.2 | async-start | bytes 4194304 | tf_op jit(solution)/shard_map/all_to_all | solution.py:145
  289.0 10.7 %copy-start.1 = (bf16[64,16,704]{2,1,0:T(8,128)(2,1)S(1)}, bf16[64,16,704]{2,1,0:T(8,128)(2,1)}, u32[]{:S(2)}) copy-start(bf16[64,16,704]{2,1,0:T(8,128)(2,1)} %param.25) | copy-start | bytes 4325380
Sparse Core Ops, SparseCore 0:
  9.5 122.2 all-gather.1
  225.4 33.1 reduce-scatter.1

commit v3 on v1

--- a/solution.py
+++ b/solution.py
@@ -113,10 +113,37 @@
     gate_part = project(routed_gate_weight)
     up_part = project(routed_up_weight)
     hidden = (jax.nn.silu(gate_part) * up_part).astype(jnp.bfloat16)
-    hidden_all = lax.all_gather(hidden, "row", axis=3, tiled=True)
-    expert_value = jnp.einsum(
-        "sexf,efd->sexd", hidden_all, down_by_feature, preferred_element_type=jnp.float32
+    def shifted(x, shift):
+        return lax.ppermute(x, "row", [(i, (i + shift) % row_count) for i in range(row_count)])
+
+    def partner(x):
+        return lax.ppermute(x, "row", [(i, i ^ 1) for i in range(row_count)])
+
+    local_hidden = hidden.shape[3]
+    group_half = hidden.shape[0] // 2
+    from_below = shifted(hidden, 2)
+    from_above = shifted(hidden, -2)
+    far_low = shifted(from_below[:group_half], 2)
+    far_high = shifted(from_above[group_half:], -2)
+    far = (row_id + 4) % row_count
+
+    def down_of(block, source):
+        weight = lax.dynamic_slice_in_dim(down_by_feature, source * local_hidden, local_hidden, axis=1)
+        return jnp.einsum("sexf,efd->sexd", block, weight, preferred_element_type=jnp.float32)
+
+    whole_blocks = (
+        (hidden, row_id),
+        (from_below, (row_id - 2) % row_count),
+        (from_above, (row_id + 2) % row_count),
     )
+    expert_value = None
+    for block, source in whole_blocks:
+        for piece, piece_source in ((block, source), (partner(block), source ^ 1)):
+            term = down_of(piece, piece_source)
+            expert_value = term if expert_value is None else expert_value + term
+    low_part = down_of(far_low, far) + down_of(partner(far_low), far ^ 1)
+    high_part = down_of(far_high, far) + down_of(partner(far_high), far ^ 1)
+    expert_value = expert_value + jnp.concatenate([low_part, high_part], axis=0)
     returned = lax.all_to_all(expert_value, "col", split_axis=0, concat_axis=0, tiled=True)
     flat_rows = returned.reshape(expert_count * capacity, local_width)
     routed_rows = jnp.take(flat_rows, row_index, axis=0)

time: 289 us -> 282 us (0.976)
  waiting for transfers between devices: 115 us -> 99.2 us
  matrix products: 39.7 us -> 46.8 us
  starting transfers between devices: 11.8 us -> 15 us
    all_gather x1 -> x0, waiting for transfers between devices: 47.7 us -> none  [on_device(): hidden_all = lax.all_gather(hidden, 'row', axis=3, tiled=True)]
    all_to_all x1, waiting for transfers between devices: 0.01 us -> 25.7 us  [on_device(): lax.all_to_all(routed_down_weight, 'row', split_axis=2, concat_axis=1, ti...]
    ppermute x0 -> x9, waiting for transfers between devices: none -> 20.9 us  [the longest x4 20.9 us: shifted(): lax.ppermute(x, 'row', [(i, (i + shift) % row_count) for i in range(row_c...]
    all_gather x1, waiting for transfers between devices: 12.9 us -> 0.01 us  [on_device(): shared_full = lax.all_gather(shared_stack, 'col', axis=1, tiled=True)]
    dot_general x1 -> x10, matrix products: 8.42 us -> 15.8 us  [down_of(): jnp.einsum('sexf,efd->sexd', block, weight, preferred_element_type=jnp.fl...]
    ppermute x0 -> x9, starting transfers between devices: none -> 5.65 us  [the longest x4 4.55 us: shifted(): lax.ppermute(x, 'row', [(i, (i + shift) % row_count) for i in range(row_c...]
    convert_element_type x1 -> x0, local copies, waits for them, and re-layouts: 3.17 us -> none  [on_device(): hidden = (jax.nn.silu(gate_part) * up_part).astype(jnp.bfloat16)]
  transfers between devices with their start and end apart: 7 -> 15, of which waited for: 5 -> 5; matrix products, arithmetic and copies ran while one was open for 25% -> 28% of each run, Pallas kernels for 0% -> 0%
where the time goes in v3:
time: 282 us; the launch traced here: 281 us
  waiting for transfers between devices  99.2 us (35%)
  blocking collectives  66.5 us (24%)
  matrix products  46.8 us (17%)
  local copies, waits for them, and re-layouts  26.9 us (10%)
  starting transfers between devices  15 us (5%)
  between operations  13.7 us (5%)
  other arithmetic  13.3 us (5%)
    all_to_all x1, blocking collectives, on_device(): lax.all_to_all(outgoing, 'col', split_axis=0, concat_axis=0, tiled=True)  66.5 us
    all_to_all x1, waiting for transfers between devices, on_device(): lax.all_to_all(expert_value, 'col', split_axis=0, concat_axis=0, tiled=True)  28.5 us
    all_to_all x1, waiting for transfers between devices, on_device(): lax.all_to_all(routed_down_weight, 'row', split_axis=2, concat_axis=1, ti...  25.7 us
    all_gather x1, waiting for transfers between devices, on_device(): lax.all_gather(jnp.concatenate([tokens, picked_input_factor.reshape(reduc...  23.9 us
    ppermute x4, waiting for transfers between devices, shifted(): lax.ppermute(x, 'row', [(i, (i + shift) % row_count) for i in range(row_c...  20.9 us
    dot_general x10, matrix products, down_of(): jnp.einsum('sexf,efd->sexd', block, weight, preferred_element_type=jnp.fl...  15.8 us
    dot_general x2, matrix products, project(): jnp.einsum('sexd,edf->sexf', other_half, half_weights(w, 1 - half), prefe...  7.38 us
    gather x2, local copies, waits for them, and re-layouts, on_device(): routed_rows = jnp.take(flat_rows, row_index, axis=0)  6.45 us
  transfers between devices with their start and end apart: 15, of which 5 were waited for; matrix products, arithmetic and copies ran while one was open for 28% of the time, Pallas kernels for 0%

profile of v3, /device:TPU:0, one launch (start us, length us, event | category | flops | bytes accessed | tf_op | source)
XLA Modules:
  0.0 281.4 jit_solution(10815375648907549469)
XLA Ops:
  6.5 0.8 compare_and_fusion.1
  7.3 0.7 compare_select_fusion.1
  8.2 1.6 gather_fusion
  9.8 0.1 bitcast_select_fusion.1
  9.9 1.6 pad_maximum_fusion.1
  11.6 2.0 pad_maximum_fusion
  13.6 0.6 reduce-window.18
  14.2 0.2 slice_reduce_fusion
  14.6 2.6 fusion
  17.2 23.9 %all-gather.3.cloned.1.call-done = bf16[512,2048]{1,0:T(8,128)(2,1)} async-done(((bf16[512,256]{1,0:T(8,128)(2,1)}), bf16[512,2048]{1,0:T(8,128)(2,1)}) %all-gather.3.cloned.1.call-update) | async-done | bytes 2097168 | tf_op jit(solution)/shard_map/all_gather | solution.py:34
  41.2 1.2 slice-done
  42.4 1.3 convolution_convert_fusion
  43.7 66.5 %all_to_all.28 = bf16[16,2,64,1024]{3,2,1,0:T(8,128)(2,1)S(1)} all-to-all(bf16[16,2,64,1024]{3,2,1,0:T(8,128)(2,1)S(1)} %bitcast.150), channel_id=1, replica_groups=mesh['row'=8,'col'=16] {'col'}, dimensions={0} | all-to-all | bytes 8388608 | tf_op jit(solution)/shard_map/all_to_all | solution.py:100
  110.2 2.4 copy.56
  112.6 0.8 copy-done.2
  113.4 3.8 %copy.54 = bf16[2,176,2048]{1,0,2:T(2,128)(2,1)} copy(bf16[2,176,2048]{2,1,0:T(8,128)(2,1)S(1)} %copy-done.9) | data formatting | bytes 2883584 | tf_op args[8]
  117.3 4.5 %all-to-all-start = ((bf16[2,176,2048]{1,0,2:T(2,128)(2,1)}), bf16[2,176,2048]{1,0,2:T(2,128)(2,1)}, u32[]{:S(2)}, u32[]{:S(2)}) async-start(bf16[2,176,2048]{1,0,2:T(2,128)(2,1)} %copy.54), calls=%async_computation | async-start | bytes 4194304 | tf_op jit(solution)/shard_map/all_to_all | solution.py:55
  121.8 0.2 reduce-scatter.2.cloned.1.call-start
  122.2 0.1 reduce.1
  122.4 0.6 gather_fusion.2
  123.2 0.1 bitcast_select_fusion
  123.3 25.7 %all-to-all-done = bf16[2,176,2048]{1,0,2:T(2,128)(2,1)} async-done(((bf16[2,176,2048]{1,0,2:T(2,128)(2,1)}), bf16[2,176,2048]{1,0,2:T(2,128)(2,1)}, u32[]{:S(2)}, u32[]{:S(2)}) %all-to-all-start) | async-done | bytes 1441824 | tf_op jit(solution)/shard_map/all_to_all | solution.py:55
  148.9 4.7 %copy.55 = bf16[2,176,8,256]{3,1,2,0:T(8,128)(2,1)S(1)} copy(bf16[2,176,8,256]{1,0,3,2:T(2,128)(2,1)} %bitcast.3) | data formatting | bytes 2883584 | tf_op jit(solution)/shard_map/all_to_all | solution.py:55
  153.7 1.6 fusion.80
  155.3 3.8 %fusion.21 = f32[2,176,16,64]{1,3,2,0:T(8,128)S(1)} fusion(bf16[2,2048,176]{1,2,0:T(8,128)(2,1)} %param.21, s32[]{:T(128)S(6)} %select_n.112, bf16[16,2,64,1024]{3,2,1,0:T(8,128)(2,1)} %copy-done.2), kind=kOutput, calls=%fused_computation.38 | convolution fusion | flops 738197504 | bytes 6356996 | tf_op jit(solution)/shard_map/sexd,edf->sexf/dot_general | solution.py:107
  159.1 0.3 copy-done.15
  159.4 1.3 fusion.17
  160.7 3.4 %fusion.19 = f32[2,176,16,64]{1,3,2,0:T(8,128)S(1)} fusion(bf16[16,2,64,1024]{3,2,0,1:T(8,128)(2,1)} %collective-permute-done, bf16[2,2048,176]{1,2,0:T(8,128)(2,1)S(1)} %copy-done.14, s32[]{:T(128)S(6)} %select_n.113), kind=kOutput, calls=%fused_computation.36 | convolution fusion | flops 738197504 | bytes 6356996 | tf_op jit(solution)/shard_map/sexd,edf->sexf/dot_general | solution.py:109
  164.2 3.9 %fusion.5 = bf16[16,2,64,176]{3,2,0,1:T(8,128)(2,1)S(1)} fusion(f32[2,176,16,64]{1,3,2,0:T(8,128)S(1)} %fusion.17, f32[2,176,16,64]{1,3,2,0:T(8,128)S(1)} %fusion.21, f32[2,176,16,64]{1,3,2,0:T(8,128)S(1)} %fusion.19, bf16[16,2,64,1024]{3,2,0,1:T(8,128)(2,1)} %collective-permute-done, bf16[2,2048,176]{1,2,0:T(8,128)(2,1)S(1)} %copy-done.15, s32[]{:T(128)S(6)} %select_n.113), kind=kOutput, calls=%fused_computation.15 | convolution fusion | flops 741081088 | bytes 11927556 | tf_op jit(solution)/shard_map/sexd,edf->sexf/dot_general | solution.py:109
  168.1 1.2 collective-permute-start.4
  169.4 0.9 collective-permute-start.2
  170.2 1.1 fusion.14
  171.4 1.8 fusion.44
  173.2 19.6 %collective-permute-done.4 = bf16[16,2,64,176]{3,2,0,1:T(8,128)(2,1)S(1)} collective-permute-done((bf16[16,2,64,176]{3,2,0,1:T(8,128)(2,1)S(1)}, bf16[16,2,64,176]{3,2,0,1:T(8,128)(2,1)S(1)}, u32[]{:S(2)}, u32[]{:S(2)}) %collective-permute-start.4) | collective-permute-done | bytes 720928 | tf_op jit(solution)/shard_map/ppermute | solution.py:117
  192.9 2.4 collective-permute-start.8
  195.3 1.9 slice.44
  197.2 0.5 collective-permute-start.3
  197.7 3.0 %fusion.40 = f32[2,256,16,64]{1,3,2,0:T(8,128)} fusion(bf16[16,2,64,176]{3,2,0,1:T(8,128)(2,1)} %collective-permute-done.2, bf16[2,1408,256]{2,1,0:T(8,128)(2,1)S(1)} %bitcast.152, s32[]{:T(128)S(6)} %select_n.116), kind=kOutput, calls=%fused_computation.60 | convolution fusion | flops 184549376 | bytes 2998276 | tf_op jit(solution)/shard_map/sexf,efd->sexd/dot_general | solution.py:132
  200.7 1.7 fusion.36
  202.5 1.8 fusion.42
  204.2 1.3 collective-permute-done.8
  205.6 4.0 %fusion.2 = f32[256,704]{0,1:T(8,128)} fusion(bf16[3,2048,704]{1,2,0:T(8,128)(2,1)} %all-gather.5.cloned.1.call-done, bf16[512,2048]{1,0:T(8,128)(2,1)} %all-gather.3.cloned.1.call-done), kind=kOutput, calls=%fused_computation.9 | convolution fusion | flops 738197504 | bytes 4653056 | tf_op jit(solution)/shard_map/dot_general | solution.py:153
  209.5 4.0 %fusion.3 = f32[256,704]{0,1:T(8,128)} fusion(bf16[3,2048,704]{1,2,0:T(8,128)(2,1)} %all-gather.5.cloned.1.call-done, bf16[512,2048]{1,0:T(8,128)(2,1)} %all-gather.3.cloned.1.call-done), kind=kOutput, calls=%fused_computation.11 | convolution fusion | flops 738197504 | bytes 4653056 | tf_op jit(solution)/shard_map/dot_general | solution.py:152
  213.6 4.9 %fusion.4 = f32[256,2048]{1,0:T(8,128)} fusion(bf16[3,2048,704]{1,2,0:T(8,128)(2,1)} %all-gather.5.cloned.1.call-done, f32[256,704]{0,1:T(8,128)} %fusion.2, bf16[256,256]{1,0:T(8,128)(2,1)S(1)} %copy-done.17, bf16[256,704]{1,0:T(8,128)(2,1)S(1)} %bitcast_select_fusion, f32[256]{0:T(256)S(1)} %add_divide_fusion, f32[256,704]{0,1:T(8,128)} %fusion.3), kind=kOutput, calls=%fused_computation.12 | convolution fusion | flops 832438272 | bytes 6915072 | tf_op jit(solution)/shard_map/dot_general | solution.py:157
  218.5 0.3 fusion.48
  218.9 0.6 collective-permute-start.7
  219.5 1.3 fusion.50
  220.8 1.5 fusion.9
  222.4 0.3 fusion.10
  222.7 1.8 fusion.38
  224.6 0.5 copy-done.4
  225.0 2.2 maximum_add_fusion
  227.2 1.4 copy.59
  228.7 4.6 %all-to-all-start.2 = ((f32[16,2,64,256]{3,2,1,0:T(8,128)}), f32[16,2,64,256]{3,2,1,0:T(8,128)}, u32[]{:S(2)}, u32[]{:S(2)}) async-start(f32[16,2,64,256]{3,2,1,0:T(8,128)} %copy.59), calls=%async_computation.2 | async-start | bytes 4194304 | tf_op jit(solution)/shard_map/all_to_all | solution.py:147
  233.2 0.2 copy.53
  233.4 0.1 copy.60
  233.6 0.1 reshape.113
  233.7 1.6 fusion.85
  235.5 0.1 copy.50
  235.6 28.5 %all-to-all-done.2 = f32[16,2,64,256]{3,2,1,0:T(8,128)} async-done(((f32[16,2,64,256]{3,2,1,0:T(8,128)}), f32[16,2,64,256]{3,2,1,0:T(8,128)}, u32[]{:S(2)}, u32[]{:S(2)}) %all-to-all-start.2) | async-done | bytes 2097184 | tf_op jit(solution)/shard_map/all_to_all | solution.py:147
  264.1 5.2 %gather_fusion.1 = f32[1024,256]{1,0:T(8,128)S(1)} fusion(f32[2048,256]{1,0:T(8,128)} %bitcast.39, s32[1024]{0:T(1024)S(1)} %broadcast_clamp_fusion), kind=kCustom, calls=%fused_computation.1 | custom fusion | bytes 2101248 | tf_op jit(solution)/shard_map/jit(_take)/gather | solution.py:149
  269.3 1.3 reshape.112
  270.6 2.5 multiply_reduce_fusion
  273.1 1.7 add.183
  (77 shorter events, 1.1 us)
Async XLA Ops:
  6.5 115.8 %copy-start = (bf16[64,16,704]{2,1,0:T(8,128)(2,1)S(1)}, bf16[64,16,704]{2,1,0:T(8,128)(2,1)}, u32[]{:S(2)}) copy-start(bf16[64,16,704]{2,1,0:T(8,128)(2,1)} %param.25) | copy-start | bytes 4325380
  6.5 7.0 %copy-start.10 = (s32[256,4]{0,1:T(4,128)S(1)}, s32[256,4]{0,1:T(4,128)}, u32[]{:S(2)}) copy-start(s32[256,4]{0,1:T(4,128)} %param.26) | copy-start | bytes 12292
  6.5 34.6 %all-gather.3.cloned.1.call-start = ((), (), s32[]{:S(2)}) async-start(), calls=%async_computation.4 | async-start | bytes 2359296 | tf_op jit(solution)/shard_map/all_gather | solution.py:34
  11.5 194.0 %all-gather.5.cloned.1.call-start = ((), (), s32[]{:S(2)}) async-start(), calls=%async_computation.5 | async-start | bytes 9191424 | tf_op jit(solution)/shard_map/all_gather | solution.py:53
  41.2 1.2 slice-start
  110.2 3.2 %copy-start.2 = (bf16[16,2,64,1024]{3,2,1,0:T(8,128)(2,1)}, bf16[16,2,64,1024]{3,2,1,0:T(8,128)(2,1)S(1)}, u32[]{:S(2)}) copy-start(bf16[16,2,64,1024]{3,2,1,0:T(8,128)(2,1)S(1)} %all_to_all.28) | copy-start | bytes 12582916
  110.2 3.2 %copy-start.9 = (bf16[2,176,2048]{2,1,0:T(8,128)(2,1)S(1)}, bf16[2,176,2048]{2,1,0:T(8,128)(2,1)}, u32[]{:S(2)}) copy-start(bf16[2,176,2048]{2,1,0:T(8,128)(2,1)} %param.23) | copy-start | bytes 4325380
  113.4 47.2 %collective-permute-start = (bf16[16,2,64,1024]{3,2,0,1:T(8,128)(2,1)}, bf16[16,2,64,1024]{3,2,0,1:T(8,128)(2,1)}, u32[]{:S(2)}, u32[]{:S(2)}) collective-permute-start(bf16[16,2,64,1024]{3,2,0,1:T(8,128)(2,1)} %copy.56), channel_id=1, source_target_pairs={{0,16},{16,0},{32,48},{48,32},{64,80},{80,64},{96,112},{112,96},{1... | collective-permute-start | bytes 12582920 | tf_op jit(solution)/shard_map/ppermute | solution.py:101
  117.3 4.8 %copy-start.11 = (bf16[2048]{0:T(1024)(128)(2,1)S(1)}, bf16[2048]{0:T(1024)(128)(2,1)}, u32[]{:S(2)}) copy-start(bf16[2048]{0:T(1024)(128)(2,1)} %param.17) | copy-start | bytes 12292
  117.3 4.8 %copy-start.12 = (s32[1,16]{1,0:T(1,128)S(1)}, s32[1,16]{1,0:T(1,128)}, u32[]{:S(2)}) copy-start(s32[1,16]{1,0:T(1,128)} %param.27) | copy-start | bytes 196
  117.3 5.8 %copy-start.13 = (s32[1,16]{1,0:T(1,128)S(1)}, s32[1,16]{1,0:T(1,128)}, u32[]{:S(2)}) copy-start(s32[1,16]{1,0:T(1,128)} %param.28) | copy-start | bytes 196
  117.3 31.7 %all-to-all-start = ((bf16[2,176,2048]{1,0,2:T(2,128)(2,1)}), bf16[2,176,2048]{1,0,2:T(2,128)(2,1)}, u32[]{:S(2)}, u32[]{:S(2)}) async-start(bf16[2,176,2048]{1,0,2:T(2,128)(2,1)} %copy.54), calls=%async_computation | async-start | bytes 4194304 | tf_op jit(solution)/shard_map/all_to_all | solution.py:55
  121.8 151.4 %reduce-scatter.2.cloned.1.call-start = ((), (), s32[]{:S(2)}) async-start(), calls=%async_computation.6 | async-start | bytes 2359296 | tf_op jit(solution)/shard_map/reduce_scatter | solution.py:164
  155.3 3.8 %copy-start.3 = (bf16[16,2,64,1024]{3,2,1,0:T(8,128)(2,1)S(1)}, bf16[16,2,64,1024]{3,2,1,0:T(8,128)(2,1)}, u32[]{:S(2)}) copy-start(bf16[16,2,64,1024]{3,2,1,0:T(8,128)(2,1)} %copy-done.2) | copy-start | bytes 12582916
  155.3 4.1 %copy-start.15 = (bf16[2,2048,176]{1,2,0:T(8,128)(2,1)S(1)}, bf16[2,2048,176]{1,2,0:T(8,128)(2,1)}, u32[]{:S(2)}) copy-start(bf16[2,2048,176]{1,2,0:T(8,128)(2,1)} %param.22) | copy-start | bytes 4325380
  159.4 1.4 copy-start.14
  164.2 6.1 %copy-start.8 = (bf16[512,2048]{1,0:T(8,128)(2,1)S(1)}, bf16[512,2048]{1,0:T(8,128)(2,1)}, u32[]{:S(2)}) copy-start(bf16[512,2048]{1,0:T(8,128)(2,1)} %all-gather.3.cloned.1.call-done) | copy-start | bytes 6291460
  168.1 24.7 %collective-permute-start.4 = (bf16[16,2,64,176]{3,2,0,1:T(8,128)(2,1)S(1)}, bf16[16,2,64,176]{3,2,0,1:T(8,128)(2,1)S(1)}, u32[]{:S(2)}, u32[]{:S(2)}) collective-permute-start(bf16[16,2,64,176]{3,2,0,1:T(8,128)(2,1)S(1)} %fusion.5), channel_id=1, source_target_pairs={{0,96},{16,112},{32,0},{48,16},{64,32},{80,48},{96,64},{112,80},{1... | collective-permute-start | bytes 2162696 | tf_op jit(solution)/shard_map/ppermute | solution.py:117
  169.4 25.9 %collective-permute-start.2 = (bf16[16,2,64,176]{3,2,0,1:T(8,128)(2,1)S(1)}, bf16[16,2,64,176]{3,2,0,1:T(8,128)(2,1)}, u32[]{:S(2)}, u32[]{:S(2)}) collective-permute-start(bf16[16,2,64,176]{3,2,0,1:T(8,128)(2,1)S(1)} %fusion.5), channel_id=1, source_target_pairs={{0,32},{16,48},{32,64},{48,80},{64,96},{80,112},{96,0},{112,16},{1... | collective-permute-start | bytes 2162696 | tf_op jit(solution)/shard_map/ppermute | solution.py:117
  171.4 31.1 %collective-permute-start.1 = (bf16[16,2,64,176]{3,2,0,1:T(8,128)(2,1)S(1)}, bf16[16,2,64,176]{3,2,0,1:T(8,128)(2,1)S(1)}, u32[]{:S(2)}, u32[]{:S(2)}) collective-permute-start(bf16[16,2,64,176]{3,2,0,1:T(8,128)(2,1)S(1)} %fusion.5), channel_id=1, source_target_pairs={{0,16},{16,0},{32,48},{48,32},{64,80},{80,64},{96,112},{112,96},{1... | collective-permute-start | bytes 2162696 | tf_op jit(solution)/shard_map/ppermute | solution.py:120
  192.9 12.7 %collective-permute-start.8 = (bf16[8,2,64,176]{3,2,0,1:T(8,128)(2,1)S(1)}, bf16[8,2,64,176]{3,2,0,1:T(8,128)(2,1)S(1)}, u32[]{:S(2)}, u32[]{:S(2)}) collective-permute-start(bf16[8,2,64,176]{3,2,0,1:T(8,128)(2,1)S(1)} %slice.45), channel_id=1, source_target_pairs={{0,96},{16,112},{32,0},{48,16},{64,32},{80,48},{96,64},{112,80},{1... | collective-permute-start | bytes 1081352 | tf_op jit(solution)/shard_map/ppermute | solution.py:117
  197.2 21.6 %collective-permute-start.6 = (bf16[8,2,64,176]{3,2,0,1:T(8,128)(2,1)}, bf16[8,2,64,176]{3,2,0,1:T(8,128)(2,1)}, u32[]{:S(2)}, u32[]{:S(2)}) collective-permute-start(bf16[8,2,64,176]{3,2,0,1:T(8,128)(2,1)} %slice.44), channel_id=1, source_target_pairs={{0,32},{16,48},{32,64},{48,80},{64,96},{80,112},{96,0},{112,16},{1... | collective-permute-start | bytes 1081352 | tf_op jit(solution)/shard_map/ppermute | solution.py:117
  197.2 27.3 %collective-permute-start.5 = (bf16[16,2,64,176]{3,2,0,1:T(8,128)(2,1)S(1)}, bf16[16,2,64,176]{3,2,0,1:T(8,128)(2,1)}, u32[]{:S(2)}, u32[]{:S(2)}) collective-permute-start(bf16[16,2,64,176]{3,2,0,1:T(8,128)(2,1)S(1)} %collective-permute-done.4), channel_id=1, source_target_pairs={{0,16},{16,0},{32,48},{48,32},{64,80},{80,64},{96,112},{112,96},{1... | collective-permute-start | bytes 2162696 | tf_op jit(solution)/shard_map/ppermute | solution.py:120
  197.2 25.5 %collective-permute-start.3 = (bf16[16,2,64,176]{3,2,0,1:T(8,128)(2,1)}, bf16[16,2,64,176]{3,2,0,1:T(8,128)(2,1)}, u32[]{:S(2)}, u32[]{:S(2)}) collective-permute-start(bf16[16,2,64,176]{3,2,0,1:T(8,128)(2,1)} %collective-permute-done.2), channel_id=1, source_target_pairs={{0,16},{16,0},{32,48},{48,32},{64,80},{80,64},{96,112},{112,96},{1... | collective-permute-start | bytes 2162696 | tf_op jit(solution)/shard_map/ppermute | solution.py:120
  205.6 15.2 %collective-permute-start.9 = (bf16[8,2,64,176]{3,2,0,1:T(8,128)(2,1)S(1)}, bf16[8,2,64,176]{3,2,0,1:T(8,128)(2,1)}, u32[]{:S(2)}, u32[]{:S(2)}) collective-permute-start(bf16[8,2,64,176]{3,2,0,1:T(8,128)(2,1)S(1)} %collective-permute-done.8), channel_id=1, source_target_pairs={{0,16},{16,0},{32,48},{48,32},{64,80},{80,64},{96,112},{112,96},{1... | collective-permute-start | bytes 1081352 | tf_op jit(solution)/shard_map/ppermute | solution.py:120
  209.5 4.0 %copy-start.17 = (bf16[256,256]{1,0:T(8,128)(2,1)S(1)}, bf16[256,256]{1,0:T(8,128)(2,1)}, u32[]{:S(2)}) copy-start(bf16[256,256]{1,0:T(8,128)(2,1)} %fusion.14) | copy-start | bytes 393220
  218.9 3.5 %collective-permute-start.7 = (bf16[8,2,64,176]{3,2,0,1:T(8,128)(2,1)}, bf16[8,2,64,176]{3,2,0,1:T(8,128)(2,1)S(1)}, u32[]{:S(2)}, u32[]{:S(2)}) collective-permute-start(bf16[8,2,64,176]{3,2,0,1:T(8,128)(2,1)} %collective-permute-done.6), channel_id=1, source_target_pairs={{0,16},{16,0},{32,48},{48,32},{64,80},{80,64},{96,112},{112,96},{1... | collective-permute-start | bytes 1081352 | tf_op jit(solution)/shard_map/ppermute | solution.py:120
  220.8 3.7 %copy-start.6 = (f32[2,256,16,64]{1,3,2,0:T(8,128)S(1)}, f32[2,256,16,64]{1,3,2,0:T(8,128)}, u32[]{:S(2)}) copy-start(f32[2,256,16,64]{1,3,2,0:T(8,128)} %fusion.36) | copy-start | bytes 6291460
  220.8 3.7 %copy-start.7 = (f32[2,256,16,64]{1,3,2,0:T(8,128)S(1)}, f32[2,256,16,64]{1,3,2,0:T(8,128)}, u32[]{:S(2)}) copy-start(f32[2,256,16,64]{1,3,2,0:T(8,128)} %fusion.42) | copy-start | bytes 6291460
  222.3 2.2 copy-start.5
  222.7 2.3 copy-start.4
  228.7 5.1 %copy-start.16 = (bf16[2048,32]{0,1:T(8,128)(2,1)S(1)}, bf16[2048,32]{0,1:T(8,128)(2,1)}, u32[]{:S(2)}) copy-start(bf16[2048,32]{0,1:T(8,128)(2,1)} %param.16) | copy-start | bytes 393220
  228.7 35.5 %all-to-all-start.2 = ((f32[16,2,64,256]{3,2,1,0:T(8,128)}), f32[16,2,64,256]{3,2,1,0:T(8,128)}, u32[]{:S(2)}, u32[]{:S(2)}) async-start(f32[16,2,64,256]{3,2,1,0:T(8,128)} %copy.59), calls=%async_computation.2 | async-start | bytes 4194304 | tf_op jit(solution)/shard_map/all_to_all | solution.py:147
  264.1 10.7 %copy-start.1 = (bf16[64,16,704]{2,1,0:T(8,128)(2,1)S(1)}, bf16[64,16,704]{2,1,0:T(8,128)(2,1)}, u32[]{:S(2)}) copy-start(bf16[64,16,704]{2,1,0:T(8,128)(2,1)} %param.25) | copy-start | bytes 4325380
Sparse Core Ops, SparseCore 0:
  11.7 29.4 all-gather.2
  43.3 115.2 all-gather.4
  218.7 33.0 reduce-scatter.1

commit v4 on v3

--- a/solution.py
+++ b/solution.py
@@ -52,9 +52,6 @@
     )
     shared_full = lax.all_gather(shared_stack, "col", axis=1, tiled=True)
 
-    down_by_feature = lax.all_to_all(
-        routed_down_weight, "row", split_axis=2, concat_axis=1, tiled=True
-    )
 
     logits = jnp.dot(all_features, router, preferred_element_type=jnp.float32)
     onehot = routes[:, :, None] == jnp.arange(expert_count, dtype=jnp.int32)[None, None, :]
@@ -125,24 +122,33 @@
     from_above = shifted(hidden, -2)
     far_low = shifted(from_below[:group_half], 2)
     far_high = shifted(from_above[group_half:], -2)
-    far = (row_id + 4) % row_count
 
-    def down_of(block, source):
-        weight = lax.dynamic_slice_in_dim(down_by_feature, source * local_hidden, local_hidden, axis=1)
+    def down_slice(k):
+        return lax.dynamic_slice_in_dim(
+            routed_down_weight, ((row_id + k) % row_count) * local_width, local_width, axis=2
+        )
+
+    down_from = [down_slice(0)] + [shifted(down_slice(k), k) for k in range(1, row_count)]
+    odd = row_id % 2 == 1
+
+    def down_pick(k_even, k_odd):
+        return jnp.where(odd, down_from[k_odd], down_from[k_even])
+
+    def down_of(block, weight):
         return jnp.einsum("sexf,efd->sexd", block, weight, preferred_element_type=jnp.float32)
 
     whole_blocks = (
-        (hidden, row_id),
-        (from_below, (row_id - 2) % row_count),
-        (from_above, (row_id + 2) % row_count),
+        (hidden, down_from[0], down_pick(7, 1)),
+        (from_below, down_from[2], down_pick(1, 3)),
+        (from_above, down_from[6], down_pick(5, 7)),
     )
     expert_value = None
-    for block, source in whole_blocks:
-        for piece, piece_source in ((block, source), (partner(block), source ^ 1)):
-            term = down_of(piece, piece_source)
-            expert_value = term if expert_value is None else expert_value + term
-    low_part = down_of(far_low, far) + down_of(partner(far_low), far ^ 1)
-    high_part = down_of(far_high, far) + down_of(partner(far_high), far ^ 1)
+    for block, weight, partner_weight in whole_blocks:
+        term = down_of(block, weight) + down_of(partner(block), partner_weight)
+        expert_value = term if expert_value is None else expert_value + term
+    far_weight, far_partner_weight = down_from[4], down_pick(3, 5)
+    low_part = down_of(far_low, far_weight) + down_of(partner(far_low), far_partner_weight)
+    high_part = down_of(far_high, far_weight) + down_of(partner(far_high), far_partner_weight)
     expert_value = expert_value + jnp.concatenate([low_part, high_part], axis=0)
     returned = lax.all_to_all(expert_value, "col", split_axis=0, concat_axis=0, tiled=True)
     flat_rows = returned.reshape(expert_count * capacity, local_width)

time: 282 us -> 253 us (0.90)
  waiting for transfers between devices: 99.2 us -> 74.1 us
  local copies, waits for them, and re-layouts: 26.9 us -> 19.7 us
  starting transfers between devices: 15 us -> 20.5 us
  matrix products: 46.8 us -> 43.3 us
    all_to_all x1 -> x0, waiting for transfers between devices: 25.7 us -> none  [on_device(): lax.all_to_all(routed_down_weight, 'row', split_axis=2, concat_axis=1, ti...]
    ppermute x4 -> x11, starting transfers between devices: 4.55 us -> 14.8 us  [shifted(): lax.ppermute(x, 'row', [(i, (i + shift) % row_count) for i in range(row_c...]
    all_to_all x1 -> x0, local copies, waits for them, and re-layouts: 4.7 us -> none  [on_device(): lax.all_to_all(routed_down_weight, 'row', split_axis=2, concat_axis=1, ti...]
    all_to_all x1 -> x0, starting transfers between devices: 4.5 us -> none  [on_device(): lax.all_to_all(routed_down_weight, 'row', split_axis=2, concat_axis=1, ti...]
    dot_general x10, matrix products: 15.8 us -> 13 us  [down_of(): jnp.einsum('sexf,efd->sexd', block, weight, preferred_element_type=jnp.fl...]
    ppermute x4 -> x11, waiting for transfers between devices: 20.9 us -> 19.4 us  [shifted(): lax.ppermute(x, 'row', [(i, (i + shift) % row_count) for i in range(row_c...]
  transfers between devices with their start and end apart: 15 -> 21, of which waited for: 5 -> 8; matrix products, arithmetic and copies ran while one was open for 28% -> 26% of each run, Pallas kernels for 0% -> 0%
where the time goes in v4:
time: 253 us; the launch traced here: 252 us
  waiting for transfers between devices  74.1 us (29%)
  blocking collectives  66.5 us (26%)
  matrix products  43.3 us (17%)
  starting transfers between devices  20.5 us (8%)
  local copies, waits for them, and re-layouts  19.7 us (8%)
  other arithmetic  14.1 us (6%)
  between operations  13.7 us (5%)
    all_to_all x1, blocking collectives, on_device(): lax.all_to_all(outgoing, 'col', split_axis=0, concat_axis=0, tiled=True)  66.5 us
    all_to_all x1, waiting for transfers between devices, on_device(): lax.all_to_all(expert_value, 'col', split_axis=0, concat_axis=0, tiled=True)  28.8 us
    all_gather x1, waiting for transfers between devices, on_device(): lax.all_gather(jnp.concatenate([tokens, picked_input_factor.reshape(reduc...  23.9 us
    ppermute x11, waiting for transfers between devices, shifted(): lax.ppermute(x, 'row', [(i, (i + shift) % row_count) for i in range(row_c...  19.4 us
    ppermute x11, starting transfers between devices, shifted(): lax.ppermute(x, 'row', [(i, (i + shift) % row_count) for i in range(row_c...  14.8 us
    dot_general x10, matrix products, down_of(): jnp.einsum('sexf,efd->sexd', block, weight, preferred_element_type=jnp.fl...  13 us
    dot_general x2, matrix products, project(): jnp.einsum('sexd,edf->sexf', other_half, half_weights(w, 1 - half), prefe...  7.38 us
    gather x2, local copies, waits for them, and re-layouts, on_device(): routed_rows = jnp.take(flat_rows, row_index, axis=0)  6.45 us
  transfers between devices with their start and end apart: 21, of which 8 were waited for; matrix products, arithmetic and copies ran while one was open for 26% of the time, Pallas kernels for 0%

profile of v4, /device:TPU:0, one launch (start us, length us, event | category | flops | bytes accessed | tf_op | source)
XLA Modules:
  0.0 251.9 jit_solution(2499412015075722990)
XLA Ops:
  6.5 0.8 compare_and_fusion.1
  7.3 0.7 compare_select_fusion.1
  8.2 1.6 gather_fusion
  9.9 1.6 pad_maximum_fusion.1
  11.6 2.0 pad_maximum_fusion
  13.7 0.6 reduce-window.18
  14.3 0.2 slice_reduce_fusion
  14.7 2.6 %fusion = pred[2048,256]{1,0:T(8,128)(4,1)S(1)} fusion(s32[256,4]{0,1:T(4,128)S(1)} %get-tuple-element.6), kind=kLoop, calls=%fused_computation.4 | loop fusion | flops 3670016 | bytes 528384 | tf_op jit(solution)/shard_map/reduce_or | solution.py:93
  17.3 23.9 %all-gather.3.cloned.1.call-done = bf16[512,2048]{1,0:T(8,128)(2,1)} async-done(((bf16[512,256]{1,0:T(8,128)(2,1)}), bf16[512,2048]{1,0:T(8,128)(2,1)}) %all-gather.3.cloned.1.call-update) | async-done | bytes 2097168 | tf_op jit(solution)/shard_map/all_gather | solution.py:34
  41.2 1.2 slice-done
  42.4 1.3 convolution_convert_fusion
  43.7 66.5 %all_to_all.10 = bf16[16,2,64,1024]{3,2,1,0:T(8,128)(2,1)S(1)} all-to-all(bf16[16,2,64,1024]{3,2,1,0:T(8,128)(2,1)S(1)} %bitcast.146), channel_id=1, replica_groups=mesh['row'=8,'col'=16] {'col'}, dimensions={0} | all-to-all | bytes 8388608 | tf_op jit(solution)/shard_map/all_to_all | solution.py:97
  110.2 2.4 copy.50
  112.6 0.8 copy-done.2
  113.5 1.1 constant_dynamic-slice_fusion.5
  114.6 2.0 collective-permute-start.2
  116.9 0.6 gather_fusion.2
  117.7 0.9 bitcast_select_fusion
  118.5 1.6 fusion.68
  120.2 3.9 %fusion.21 = f32[2,176,16,64]{1,3,2,0:T(8,128)S(1)} fusion(bf16[2,2048,176]{1,2,0:T(8,128)(2,1)} %param.21, s32[]{:T(128)S(6)} %select_n.153, bf16[16,2,64,1024]{3,2,1,0:T(8,128)(2,1)} %copy-done.2), kind=kOutput, calls=%fused_computation.38 | convolution fusion | flops 738197504 | bytes 6356996 | tf_op jit(solution)/shard_map/sexd,edf->sexf/dot_general | solution.py:104
  124.1 0.3 copy-done.18
  124.4 1.3 fusion.17
  125.7 3.5 %fusion.19 = f32[2,176,16,64]{1,3,2,0:T(8,128)S(1)} fusion(bf16[16,2,64,1024]{3,2,0,1:T(8,128)(2,1)} %collective-permute-done, bf16[2,2048,176]{1,2,0:T(8,128)(2,1)S(1)} %copy-done.17, s32[]{:T(128)S(6)} %select_n.154), kind=kOutput, calls=%fused_computation.36 | convolution fusion | flops 738197504 | bytes 6356996 | tf_op jit(solution)/shard_map/sexd,edf->sexf/dot_general | solution.py:106
  129.2 3.9 %fusion.5 = bf16[16,2,64,176]{3,2,0,1:T(8,128)(2,1)S(1)} fusion(f32[2,176,16,64]{1,3,2,0:T(8,128)S(1)} %fusion.17, f32[2,176,16,64]{1,3,2,0:T(8,128)S(1)} %fusion.21, f32[2,176,16,64]{1,3,2,0:T(8,128)S(1)} %fusion.19, bf16[16,2,64,1024]{3,2,0,1:T(8,128)(2,1)} %collective-permute-done, bf16[2,2048,176]{1,2,0:T(8,128)(2,1)S(1)} %copy-done.18, s32[]{:T(128)S(6)} %select_n.154), kind=kOutput, calls=%fused_computation.15 | convolution fusion | flops 741081088 | bytes 11927556 | tf_op jit(solution)/shard_map/sexd,edf->sexf/dot_general | solution.py:106
  133.1 3.3 %collective-permute-start.9 = (bf16[16,2,64,176]{3,2,0,1:T(8,128)(2,1)S(1)}, bf16[16,2,64,176]{3,2,0,1:T(8,128)(2,1)S(1)}, u32[]{:S(2)}, u32[]{:S(2)}) collective-permute-start(bf16[16,2,64,176]{3,2,0,1:T(8,128)(2,1)S(1)} %fusion.5), channel_id=1, source_target_pairs={{0,96},{16,112},{32,0},{48,16},{64,32},{80,48},{96,64},{112,80},{1... | collective-permute-start | bytes 2162696 | tf_op jit(solution)/shard_map/ppermute | solution.py:114
  136.4 0.5 fusion.14
  137.0 1.8 fusion.44
  138.8 18.7 %collective-permute-done.9 = bf16[16,2,64,176]{3,2,0,1:T(8,128)(2,1)S(1)} collective-permute-done((bf16[16,2,64,176]{3,2,0,1:T(8,128)(2,1)S(1)}, bf16[16,2,64,176]{3,2,0,1:T(8,128)(2,1)S(1)}, u32[]{:S(2)}, u32[]{:S(2)}) %collective-permute-start.9) | collective-permute-done | bytes 720928 | tf_op jit(solution)/shard_map/ppermute | solution.py:114
  157.5 3.6 %collective-permute-start.8 = (bf16[2,176,256]{2,1,0:T(8,128)(2,1)S(1)}, bf16[2,176,256]{2,1,0:T(8,128)(2,1)S(1)}, u32[]{:S(2)}, u32[]{:S(2)}) collective-permute-start(bf16[2,176,256]{2,1,0:T(8,128)(2,1)S(1)} %copy-done.12), channel_id=1, source_target_pairs={{0,96},{16,112},{32,0},{48,16},{64,32},{80,48},{96,64},{112,80},{1... | collective-permute-start | bytes 540680 | tf_op jit(solution)/shard_map/ppermute | solution.py:114
  161.3 1.1 slice.44
  162.4 0.3 collective-permute-start.1
  162.7 3.1 %fusion.40 = f32[2,256,16,64]{1,3,2,0:T(8,128)} fusion(bf16[16,2,64,176]{3,2,0,1:T(8,128)(2,1)} %collective-permute-done.5, bf16[2,176,256]{2,1,0:T(8,128)(2,1)} %collective-permute-done.4), kind=kOutput, calls=%fused_computation.60 | convolution fusion | flops 184549376 | bytes 2998272 | tf_op jit(solution)/shard_map/sexf,efd->sexd/dot_general | solution.py:138
  165.7 0.4 collective-permute-done.8
  166.1 3.0 %collective-permute-start.12 = (bf16[2,176,256]{2,1,0:T(8,128)(2,1)}, bf16[2,176,256]{2,1,0:T(8,128)(2,1)S(1)}, u32[]{:S(2)}, u32[]{:S(2)}) collective-permute-start(bf16[2,176,256]{2,1,0:T(8,128)(2,1)} %get-tuple-element.12), channel_id=1, source_target_pairs={{0,64},{16,80},{32,96},{48,112},{64,0},{80,16},{96,32},{112,48},{1... | collective-permute-start | bytes 540680 | tf_op jit(solution)/shard_map/ppermute | solution.py:114
  169.1 1.7 fusion.36
  170.9 2.6 %collective-permute-start.15 = (bf16[8,2,64,176]{3,2,0,1:T(8,128)(2,1)S(1)}, bf16[8,2,64,176]{3,2,0,1:T(8,128)(2,1)S(1)}, u32[]{:S(2)}, u32[]{:S(2)}) collective-permute-start(bf16[8,2,64,176]{3,2,0,1:T(8,128)(2,1)S(1)} %slice.45), channel_id=1, source_target_pairs={{0,96},{16,112},{32,0},{48,16},{64,32},{80,48},{96,64},{112,80},{1... | collective-permute-start | bytes 1081352 | tf_op jit(solution)/shard_map/ppermute | solution.py:114
  173.4 2.7 %fusion.42 = f32[2,256,16,64]{1,3,2,0:T(8,128)} fusion(bf16[16,2,64,176]{3,2,0,1:T(8,128)(2,1)S(1)} %collective-permute-done.3, bf16[2,176,256]{2,1,0:T(8,128)(2,1)S(1)} %collective-permute-done.1, bf16[2,176,256]{2,1,0:T(8,128)(2,1)} %collective-permute-done.2, pred[]{:T(512)S(6)} %eq.72), kind=kOutput, calls=%fused_computation.62 | convolution fusion | flops 184639488 | bytes 3178497 | tf_op jit(solution)/shard_map/sexf,efd->sexd/dot_general | solution.py:138
  176.2 4.1 %fusion.2 = f32[256,704]{0,1:T(8,128)} fusion(bf16[3,2048,704]{1,2,0:T(8,128)(2,1)} %all-gather.5.cloned.1.call-done, bf16[512,2048]{1,0:T(8,128)(2,1)} %all-gather.3.cloned.1.call-done), kind=kOutput, calls=%fused_computation.9 | convolution fusion | flops 738197504 | bytes 4653056 | tf_op jit(solution)/shard_map/dot_general | solution.py:159
  180.3 3.6 %fusion.3 = f32[256,704]{0,1:T(8,128)} fusion(bf16[3,2048,704]{1,2,0:T(8,128)(2,1)} %all-gather.5.cloned.1.call-done, bf16[512,2048]{1,0:T(8,128)(2,1)S(1)} %copy-done.9), kind=kOutput, calls=%fused_computation.11 | convolution fusion | flops 738197504 | bytes 4653056 | tf_op jit(solution)/shard_map/dot_general | solution.py:158
  183.9 5.1 %fusion.4 = f32[256,2048]{1,0:T(8,128)} fusion(bf16[3,2048,704]{1,2,0:T(8,128)(2,1)} %all-gather.5.cloned.1.call-done, f32[256,704]{0,1:T(8,128)} %fusion.2, bf16[256,256]{1,0:T(8,128)(2,1)S(1)} %fusion.14, bf16[256,704]{1,0:T(8,128)(2,1)} %bitcast_select_fusion, f32[256]{0:T(256)S(1)} %add_divide_fusion, f32[256,704]{0,1:T(8,128)} %fusion.3), kind=kOutput, calls=%fused_computation.12 | convolution fusion | flops 832438272 | bytes 6947840 | tf_op jit(solution)/shard_map/dot_general | solution.py:163
  189.1 0.4 collective-permute-done.15
  189.6 0.3 fusion.48
  189.9 0.4 collective-permute-start.14
  190.3 1.3 fusion.50
  191.7 0.2 collective-permute-start.11
  191.9 0.8 collective-permute-done.16
  192.7 0.3 fusion.9
  193.0 0.4 collective-permute-done.14
  193.4 0.3 fusion.10
  193.8 0.5 fusion.38
  194.3 0.7 collective-permute-done.11
  194.9 0.2 copy-done.5
  195.2 0.6 copy-done.6
  195.8 0.7 copy-done.4
  196.6 0.9 maximum_add_fusion
  197.5 1.5 copy.53
  198.9 4.6 %all-to-all-start.1 = ((f32[16,2,64,256]{3,2,1,0:T(8,128)}), f32[16,2,64,256]{3,2,1,0:T(8,128)}, u32[]{:S(2)}, u32[]{:S(2)}) async-start(f32[16,2,64,256]{3,2,1,0:T(8,128)} %copy.53), calls=%async_computation.1 | async-start | bytes 4194304 | tf_op jit(solution)/shard_map/all_to_all | solution.py:153
  203.5 0.2 copy.49
  204.0 1.6 fusion.73
  205.9 28.8 %all-to-all-done.1 = f32[16,2,64,256]{3,2,1,0:T(8,128)} async-done(((f32[16,2,64,256]{3,2,1,0:T(8,128)}), f32[16,2,64,256]{3,2,1,0:T(8,128)}, u32[]{:S(2)}, u32[]{:S(2)}) %all-to-all-start.1) | async-done | bytes 2097184 | tf_op jit(solution)/shard_map/all_to_all | solution.py:153
  234.7 5.2 %gather_fusion.1 = f32[1024,256]{1,0:T(8,128)S(1)} fusion(f32[2048,256]{1,0:T(8,128)} %bitcast.35, s32[1024]{0:T(1024)S(1)} %broadcast_clamp_fusion), kind=kCustom, calls=%fused_computation.1 | custom fusion | bytes 2101248 | tf_op jit(solution)/shard_map/jit(_take)/gather | solution.py:155
  239.8 1.3 reshape.112
  241.1 2.5 %multiply_reduce_fusion = f32[256,256]{1,0:T(8,128)S(1)} fusion(f32[256,4,256]{2,1,0:T(4,128)} %reshape.112, f32[256,4]{1,0:T(8,128)S(1)} %copy.46, pred[256,4]{1,0:T(8,128)(4,1)S(1)} %copy.49), kind=kLoop, calls=%fused_computation.32 | loop fusion | flops 720896 | bytes 1315840 | tf_op jit(solution)/shard_map/reduce_sum | solution.py:156
  243.7 1.7 add.222
  (92 shorter events, 2.2 us)
Async XLA Ops:
  6.5 110.4 %copy-start = (bf16[64,16,704]{2,1,0:T(8,128)(2,1)S(1)}, bf16[64,16,704]{2,1,0:T(8,128)(2,1)}, u32[]{:S(2)}) copy-start(bf16[64,16,704]{2,1,0:T(8,128)(2,1)} %param.25) | copy-start | bytes 4325380
  6.5 7.1 %copy-start.13 = (s32[256,4]{0,1:T(4,128)S(1)}, s32[256,4]{0,1:T(4,128)}, u32[]{:S(2)}) copy-start(s32[256,4]{0,1:T(4,128)} %param.26) | copy-start | bytes 12292
  6.5 34.6 %all-gather.3.cloned.1.call-start = ((), (), s32[]{:S(2)}) async-start(), calls=%async_computation.3 | async-start | bytes 2359296 | tf_op jit(solution)/shard_map/all_gather | solution.py:34
  11.5 164.6 %all-gather.5.cloned.1.call-start = ((), (), s32[]{:S(2)}) async-start(), calls=%async_computation.4 | async-start | bytes 9191424 | tf_op jit(solution)/shard_map/all_gather | solution.py:53
  13.6 230.1 %reduce-scatter.2.cloned.1.call-start = ((), (), s32[]{:S(2)}) async-start(), calls=%async_computation.5 | async-start | bytes 2359296 | tf_op jit(solution)/shard_map/reduce_scatter | solution.py:170
  41.2 1.2 slice-start
  110.2 3.2 %copy-start.2 = (bf16[16,2,64,1024]{3,2,1,0:T(8,128)(2,1)}, bf16[16,2,64,1024]{3,2,1,0:T(8,128)(2,1)S(1)}, u32[]{:S(2)}) copy-start(bf16[16,2,64,1024]{3,2,1,0:T(8,128)(2,1)S(1)} %all_to_all.10) | copy-start | bytes 12582916
  110.2 3.4 %copy-start.10 = (bf16[2,176,2048]{2,1,0:T(8,128)(2,1)S(1)}, bf16[2,176,2048]{2,1,0:T(8,128)(2,1)}, u32[]{:S(2)}) copy-start(bf16[2,176,2048]{2,1,0:T(8,128)(2,1)} %param.23) | copy-start | bytes 4325380
  113.4 3.2 %copy-start.14 = (bf16[2048]{0:T(1024)(128)(2,1)S(1)}, bf16[2048]{0:T(1024)(128)(2,1)}, u32[]{:S(2)}) copy-start(bf16[2048]{0:T(1024)(128)(2,1)} %param.17) | copy-start | bytes 12292
  113.4 3.2 %copy-start.15 = (s32[1,16]{1,0:T(1,128)S(1)}, s32[1,16]{1,0:T(1,128)}, u32[]{:S(2)}) copy-start(s32[1,16]{1,0:T(1,128)} %param.27) | copy-start | bytes 196
  113.4 4.2 %copy-start.16 = (s32[1,16]{1,0:T(1,128)S(1)}, s32[1,16]{1,0:T(1,128)}, u32[]{:S(2)}) copy-start(s32[1,16]{1,0:T(1,128)} %param.28) | copy-start | bytes 196
  113.4 12.2 %collective-permute-start = (bf16[16,2,64,1024]{3,2,0,1:T(8,128)(2,1)}, bf16[16,2,64,1024]{3,2,0,1:T(8,128)(2,1)}, u32[]{:S(2)}, u32[]{:S(2)}) collective-permute-start(bf16[16,2,64,1024]{3,2,0,1:T(8,128)(2,1)} %copy.50), channel_id=1, source_target_pairs={{0,16},{16,0},{32,48},{48,32},{64,80},{80,64},{96,112},{112,96},{1... | collective-permute-start | bytes 12582920 | tf_op jit(solution)/shard_map/ppermute | solution.py:98
  114.6 56.2 %collective-permute-start.2 = (bf16[2,176,256]{2,1,0:T(8,128)(2,1)}, bf16[2,176,256]{2,1,0:T(8,128)(2,1)}, u32[]{:S(2)}, u32[]{:S(2)}) collective-permute-start(bf16[2,176,256]{2,1,0:T(8,128)(2,1)} %get-tuple-element.7), channel_id=1, source_target_pairs={{0,112},{16,0},{32,16},{48,32},{64,48},{80,64},{96,80},{112,96},{1... | collective-permute-start | bytes 540680 | tf_op jit(solution)/shard_map/ppermute | solution.py:114
  116.6 45.8 %collective-permute-start.4 = (bf16[2,176,256]{2,1,0:T(8,128)(2,1)}, bf16[2,176,256]{2,1,0:T(8,128)(2,1)}, u32[]{:S(2)}, u32[]{:S(2)}) collective-permute-start(bf16[2,176,256]{2,1,0:T(8,128)(2,1)} %get-tuple-element.10), channel_id=1, source_target_pairs={{0,32},{16,48},{32,64},{48,80},{64,96},{80,112},{96,0},{112,16},{1... | collective-permute-start | bytes 540680 | tf_op jit(solution)/shard_map/ppermute | solution.py:114
  120.2 3.9 %copy-start.3 = (bf16[16,2,64,1024]{3,2,1,0:T(8,128)(2,1)S(1)}, bf16[16,2,64,1024]{3,2,1,0:T(8,128)(2,1)}, u32[]{:S(2)}) copy-start(bf16[16,2,64,1024]{3,2,1,0:T(8,128)(2,1)} %copy-done.2) | copy-start | bytes 12582916
  120.2 4.2 %copy-start.18 = (bf16[2,2048,176]{1,2,0:T(8,128)(2,1)S(1)}, bf16[2,2048,176]{1,2,0:T(8,128)(2,1)}, u32[]{:S(2)}) copy-start(bf16[2,2048,176]{1,2,0:T(8,128)(2,1)} %param.22) | copy-start | bytes 4325380
  124.4 1.4 copy-start.17
  129.2 7.2 %copy-start.8 = (bf16[512,2048]{1,0:T(8,128)(2,1)S(1)}, bf16[512,2048]{1,0:T(8,128)(2,1)}, u32[]{:S(2)}) copy-start(bf16[512,2048]{1,0:T(8,128)(2,1)} %all-gather.3.cloned.1.call-done) | copy-start | bytes 6291460
  133.1 24.4 %collective-permute-start.9 = (bf16[16,2,64,176]{3,2,0,1:T(8,128)(2,1)S(1)}, bf16[16,2,64,176]{3,2,0,1:T(8,128)(2,1)S(1)}, u32[]{:S(2)}, u32[]{:S(2)}) collective-permute-start(bf16[16,2,64,176]{3,2,0,1:T(8,128)(2,1)S(1)} %fusion.5), channel_id=1, source_target_pairs={{0,96},{16,112},{32,0},{48,16},{64,32},{80,48},{96,64},{112,80},{1... | collective-permute-start | bytes 2162696 | tf_op jit(solution)/shard_map/ppermute | solution.py:114
  136.4 24.8 %collective-permute-start.5 = (bf16[16,2,64,176]{3,2,0,1:T(8,128)(2,1)S(1)}, bf16[16,2,64,176]{3,2,0,1:T(8,128)(2,1)}, u32[]{:S(2)}, u32[]{:S(2)}) collective-permute-start(bf16[16,2,64,176]{3,2,0,1:T(8,128)(2,1)S(1)} %fusion.5), channel_id=1, source_target_pairs={{0,32},{16,48},{32,64},{48,80},{64,96},{80,112},{96,0},{112,16},{1... | collective-permute-start | bytes 2162696 | tf_op jit(solution)/shard_map/ppermute | solution.py:114
  136.9 20.7 %copy-start.12 = (bf16[2,176,256]{2,1,0:T(8,128)(2,1)S(1)}, bf16[2,176,256]{2,1,0:T(8,128)(2,1)}, u32[]{:S(2)}) copy-start(bf16[2,176,256]{2,1,0:T(8,128)(2,1)} %get-tuple-element.8) | copy-start | bytes 540676
  136.9 25.5 %copy-start.11 = (bf16[2,176,256]{2,1,0:T(8,128)(2,1)S(1)}, bf16[2,176,256]{2,1,0:T(8,128)(2,1)}, u32[]{:S(2)}) copy-start(bf16[2,176,256]{2,1,0:T(8,128)(2,1)} %get-tuple-element.11) | copy-start | bytes 540676
  136.9 36.5 %collective-permute-start.3 = (bf16[16,2,64,176]{3,2,0,1:T(8,128)(2,1)S(1)}, bf16[16,2,64,176]{3,2,0,1:T(8,128)(2,1)S(1)}, u32[]{:S(2)}, u32[]{:S(2)}) collective-permute-start(bf16[16,2,64,176]{3,2,0,1:T(8,128)(2,1)S(1)} %fusion.5), channel_id=1, source_target_pairs={{0,16},{16,0},{32,48},{48,32},{64,80},{80,64},{96,112},{112,96},{1... | collective-permute-start | bytes 2162696 | tf_op jit(solution)/shard_map/ppermute | solution.py:117
  157.5 8.6 %collective-permute-start.8 = (bf16[2,176,256]{2,1,0:T(8,128)(2,1)S(1)}, bf16[2,176,256]{2,1,0:T(8,128)(2,1)S(1)}, u32[]{:S(2)}, u32[]{:S(2)}) collective-permute-start(bf16[2,176,256]{2,1,0:T(8,128)(2,1)S(1)} %copy-done.12), channel_id=1, source_target_pairs={{0,96},{16,112},{32,0},{48,16},{64,32},{80,48},{96,64},{112,80},{1... | collective-permute-start | bytes 540680 | tf_op jit(solution)/shard_map/ppermute | solution.py:114
  161.2 30.5 %collective-permute-start.6 = (bf16[2,176,256]{2,1,0:T(8,128)(2,1)}, bf16[2,176,256]{2,1,0:T(8,128)(2,1)S(1)}, u32[]{:S(2)}, u32[]{:S(2)}) collective-permute-start(bf16[2,176,256]{2,1,0:T(8,128)(2,1)} %get-tuple-element.9), channel_id=1, source_target_pairs={{0,48},{16,64},{32,80},{48,96},{64,112},{80,0},{96,16},{112,32},{1... | collective-permute-start | bytes 540680 | tf_op jit(solution)/shard_map/ppermute | solution.py:114
  162.4 8.5 %collective-permute-start.1 = (bf16[2,176,256]{2,1,0:T(8,128)(2,1)S(1)}, bf16[2,176,256]{2,1,0:T(8,128)(2,1)S(1)}, u32[]{:S(2)}, u32[]{:S(2)}) collective-permute-start(bf16[2,176,256]{2,1,0:T(8,128)(2,1)S(1)} %copy-done.11), channel_id=1, source_target_pairs={{0,16},{16,32},{32,48},{48,64},{64,80},{80,96},{96,112},{112,0},{1... | collective-permute-start | bytes 540680 | tf_op jit(solution)/shard_map/ppermute | solution.py:114
  166.1 22.9 %collective-permute-start.12 = (bf16[2,176,256]{2,1,0:T(8,128)(2,1)}, bf16[2,176,256]{2,1,0:T(8,128)(2,1)S(1)}, u32[]{:S(2)}, u32[]{:S(2)}) collective-permute-start(bf16[2,176,256]{2,1,0:T(8,128)(2,1)} %get-tuple-element.12), channel_id=1, source_target_pairs={{0,64},{16,80},{32,96},{48,112},{64,0},{80,16},{96,32},{112,48},{1... | collective-permute-start | bytes 540680 | tf_op jit(solution)/shard_map/ppermute | solution.py:114
  170.9 21.1 %collective-permute-start.10 = (bf16[2,176,256]{2,1,0:T(8,128)(2,1)}, bf16[2,176,256]{2,1,0:T(8,128)(2,1)S(1)}, u32[]{:S(2)}, u32[]{:S(2)}) collective-permute-start(bf16[2,176,256]{2,1,0:T(8,128)(2,1)} %get-tuple-element.13), channel_id=1, source_target_pairs={{0,80},{16,96},{32,112},{48,0},{64,16},{80,32},{96,48},{112,64},{1... | collective-permute-start | bytes 540680 | tf_op jit(solution)/shard_map/ppermute | solution.py:114
  170.9 18.6 %collective-permute-start.15 = (bf16[8,2,64,176]{3,2,0,1:T(8,128)(2,1)S(1)}, bf16[8,2,64,176]{3,2,0,1:T(8,128)(2,1)S(1)}, u32[]{:S(2)}, u32[]{:S(2)}) collective-permute-start(bf16[8,2,64,176]{3,2,0,1:T(8,128)(2,1)S(1)} %slice.45), channel_id=1, source_target_pairs={{0,96},{16,112},{32,0},{48,16},{64,32},{80,48},{96,64},{112,80},{1... | collective-permute-start | bytes 1081352 | tf_op jit(solution)/shard_map/ppermute | solution.py:114
  173.4 16.4 %collective-permute-start.13 = (bf16[8,2,64,176]{3,2,0,1:T(8,128)(2,1)S(1)}, bf16[8,2,64,176]{3,2,0,1:T(8,128)(2,1)}, u32[]{:S(2)}, u32[]{:S(2)}) collective-permute-start(bf16[8,2,64,176]{3,2,0,1:T(8,128)(2,1)S(1)} %slice.44), channel_id=1, source_target_pairs={{0,32},{16,48},{32,64},{48,80},{64,96},{80,112},{96,0},{112,16},{1... | collective-permute-start | bytes 1081352 | tf_op jit(solution)/shard_map/ppermute | solution.py:114
  176.2 4.1 %copy-start.9 = (bf16[512,2048]{1,0:T(8,128)(2,1)S(1)}, bf16[512,2048]{1,0:T(8,128)(2,1)}, u32[]{:S(2)}) copy-start(bf16[512,2048]{1,0:T(8,128)(2,1)} %all-gather.3.cloned.1.call-done) | copy-start | bytes 6291460
  189.0 4.8 %collective-permute-start.7 = (bf16[16,2,64,176]{3,2,0,1:T(8,128)(2,1)}, bf16[16,2,64,176]{3,2,0,1:T(8,128)(2,1)S(1)}, u32[]{:S(2)}, u32[]{:S(2)}) collective-permute-start(bf16[16,2,64,176]{3,2,0,1:T(8,128)(2,1)} %collective-permute-done.5), channel_id=1, source_target_pairs={{0,16},{16,0},{32,48},{48,32},{64,80},{80,64},{96,112},{112,96},{1... | collective-permute-start | bytes 2162696 | tf_op jit(solution)/shard_map/ppermute | solution.py:117
  189.4 3.3 %collective-permute-start.16 = (bf16[8,2,64,176]{3,2,0,1:T(8,128)(2,1)S(1)}, bf16[8,2,64,176]{3,2,0,1:T(8,128)(2,1)S(1)}, u32[]{:S(2)}, u32[]{:S(2)}) collective-permute-start(bf16[8,2,64,176]{3,2,0,1:T(8,128)(2,1)S(1)} %collective-permute-done.15), channel_id=1, source_target_pairs={{0,16},{16,0},{32,48},{48,32},{64,80},{80,64},{96,112},{112,96},{1... | collective-permute-start | bytes 1081352 | tf_op jit(solution)/shard_map/ppermute | solution.py:117
  189.9 3.6 %collective-permute-start.14 = (bf16[8,2,64,176]{3,2,0,1:T(8,128)(2,1)}, bf16[8,2,64,176]{3,2,0,1:T(8,128)(2,1)S(1)}, u32[]{:S(2)}, u32[]{:S(2)}) collective-permute-start(bf16[8,2,64,176]{3,2,0,1:T(8,128)(2,1)} %collective-permute-done.13), channel_id=1, source_target_pairs={{0,16},{16,0},{32,48},{48,32},{64,80},{80,64},{96,112},{112,96},{1... | collective-permute-start | bytes 1081352 | tf_op jit(solution)/shard_map/ppermute | solution.py:117
  191.7 3.3 %collective-permute-start.11 = (bf16[16,2,64,176]{3,2,0,1:T(8,128)(2,1)S(1)}, bf16[16,2,64,176]{3,2,0,1:T(8,128)(2,1)S(1)}, u32[]{:S(2)}, u32[]{:S(2)}) collective-permute-start(bf16[16,2,64,176]{3,2,0,1:T(8,128)(2,1)S(1)} %collective-permute-done.9), channel_id=1, source_target_pairs={{0,16},{16,0},{32,48},{48,32},{64,80},{80,64},{96,112},{112,96},{1... | collective-permute-start | bytes 2162696 | tf_op jit(solution)/shard_map/ppermute | solution.py:117
  192.7 2.3 copy-start.7
  193.4 1.7 copy-start.5
  193.4 2.4 copy-start.6
  193.8 2.8 %copy-start.4 = (f32[2,256,16,64]{1,3,2,0:T(8,128)S(1)}, f32[2,256,16,64]{1,3,2,0:T(8,128)}, u32[]{:S(2)}) copy-start(f32[2,256,16,64]{1,3,2,0:T(8,128)} %fusion.44) | copy-start | bytes 6291460
  198.9 5.1 %copy-start.19 = (bf16[2048,32]{0,1:T(8,128)(2,1)S(1)}, bf16[2048,32]{0,1:T(8,128)(2,1)}, u32[]{:S(2)}) copy-start(bf16[2048,32]{0,1:T(8,128)(2,1)} %param.16) | copy-start | bytes 393220
  198.9 35.7 %all-to-all-start.1 = ((f32[16,2,64,256]{3,2,1,0:T(8,128)}), f32[16,2,64,256]{3,2,1,0:T(8,128)}, u32[]{:S(2)}, u32[]{:S(2)}) async-start(f32[16,2,64,256]{3,2,1,0:T(8,128)} %copy.53), calls=%async_computation.1 | async-start | bytes 4194304 | tf_op jit(solution)/shard_map/all_to_all | solution.py:153
  234.6 10.7 %copy-start.1 = (bf16[64,16,704]{2,1,0:T(8,128)(2,1)S(1)}, bf16[64,16,704]{2,1,0:T(8,128)(2,1)}, u32[]{:S(2)}) copy-start(bf16[64,16,704]{2,1,0:T(8,128)(2,1)} %param.25) | copy-start | bytes 4325380
Sparse Core Ops, SparseCore 0:
  11.7 29.4 all-gather.2
  43.3 115.2 all-gather.4
  189.1 32.7 reduce-scatter.1

commit v5 on v4

--- a/solution.py
+++ b/solution.py
@@ -150,7 +150,9 @@
     low_part = down_of(far_low, far_weight) + down_of(partner(far_low), far_partner_weight)
     high_part = down_of(far_high, far_weight) + down_of(partner(far_high), far_partner_weight)
     expert_value = expert_value + jnp.concatenate([low_part, high_part], axis=0)
-    returned = lax.all_to_all(expert_value, "col", split_axis=0, concat_axis=0, tiled=True)
+    returned = lax.all_to_all(
+        expert_value.astype(jnp.bfloat16), "col", split_axis=0, concat_axis=0, tiled=True
+    ).astype(jnp.float32)
     flat_rows = returned.reshape(expert_count * capacity, local_width)
     routed_rows = jnp.take(flat_rows, row_index, axis=0)
     routed = jnp.sum(gate_weights[:, :, None] * routed_rows, axis=1)

time: 253 us -> 254 us (level)
    ppermute x11, waiting for transfers between devices: 19.4 us -> 33.3 us  [shifted(): lax.ppermute(x, 'row', [(i, (i + shift) % row_count) for i in range(row_c...]
    all_to_all x1, waiting for transfers between devices: 28.8 us -> 17.2 us  [on_device(): lax.all_to_all(expert_value.astype(jnp.bfloat16), 'col', split_axis=0, co...]
  transfers between devices with their start and end apart: 21 -> 21, of which waited for: 8 -> 7; matrix products, arithmetic and copies ran while one was open for 26% -> 26% of each run, Pallas kernels for 0% -> 0%
where the time goes in v5:
time: 254 us; the launch traced here: 253 us
  waiting for transfers between devices  76 us (30%)
  blocking collectives  66.5 us (26%)
  matrix products  42 us (17%)
  starting transfers between devices  19.6 us (8%)
  local copies, waits for them, and re-layouts  19.1 us (8%)
  other arithmetic  15.6 us (6%)
  between operations  13.7 us (5%)
    all_to_all x1, blocking collectives, on_device(): lax.all_to_all(outgoing, 'col', split_axis=0, concat_axis=0, tiled=True)  66.5 us
    ppermute x11, waiting for transfers between devices, shifted(): lax.ppermute(x, 'row', [(i, (i + shift) % row_count) for i in range(row_c...  33.3 us
    all_gather x1, waiting for transfers between devices, on_device(): lax.all_gather(jnp.concatenate([tokens, picked_input_factor.reshape(reduc...  23.9 us
    all_to_all x1, waiting for transfers between devices, on_device(): lax.all_to_all(expert_value.astype(jnp.bfloat16), 'col', split_axis=0, co...  17.2 us
    ppermute x11, starting transfers between devices, shifted(): lax.ppermute(x, 'row', [(i, (i + shift) % row_count) for i in range(row_c...  14.7 us
    dot_general x10, matrix products, down_of(): jnp.einsum('sexf,efd->sexd', block, weight, preferred_element_type=jnp.fl...  11.5 us
    dot_general x2, matrix products, project(): jnp.einsum('sexd,edf->sexf', other_half, half_weights(w, 1 - half), prefe...  7.4 us
    gather x2, local copies, waits for them, and re-layouts, on_device(): routed_rows = jnp.take(flat_rows, row_index, axis=0)  6.44 us
  transfers between devices with their start and end apart: 21, of which 7 were waited for; matrix products, arithmetic and copies ran while one was open for 26% of the time, Pallas kernels for 0%

profile of v5, /device:TPU:0, one launch (start us, length us, event | category | flops | bytes accessed | tf_op | source)
XLA Modules:
  0.0 252.6 jit_solution(14081246890508642907)
XLA Ops:
  6.5 0.8 compare_and_fusion.1
  7.3 0.7 compare_select_fusion.1
  8.2 1.6 gather_fusion
  9.9 1.6 pad_maximum_fusion.1
  11.6 2.0 pad_maximum_fusion
  13.7 0.6 reduce-window.18
  14.3 0.2 slice_reduce_fusion
  14.6 2.6 %fusion = pred[2048,256]{1,0:T(8,128)(4,1)S(1)} fusion(s32[256,4]{0,1:T(4,128)S(1)} %get-tuple-element.6), kind=kLoop, calls=%fused_computation.4 | loop fusion | flops 3670016 | bytes 528384 | tf_op jit(solution)/shard_map/reduce_or | solution.py:93
  17.3 23.9 %all-gather.3.cloned.1.call-done = bf16[512,2048]{1,0:T(8,128)(2,1)} async-done(((bf16[512,256]{1,0:T(8,128)(2,1)}), bf16[512,2048]{1,0:T(8,128)(2,1)}) %all-gather.3.cloned.1.call-update) | async-done | bytes 2097168 | tf_op jit(solution)/shard_map/all_gather | solution.py:34
  41.2 1.2 slice-done
  42.4 1.3 convolution_convert_fusion
  43.7 66.5 %all_to_all.10 = bf16[16,2,64,1024]{3,2,1,0:T(8,128)(2,1)S(1)} all-to-all(bf16[16,2,64,1024]{3,2,1,0:T(8,128)(2,1)S(1)} %bitcast.148), channel_id=1, replica_groups=mesh['row'=8,'col'=16] {'col'}, dimensions={0} | all-to-all | bytes 8388608 | tf_op jit(solution)/shard_map/all_to_all | solution.py:97
  110.2 2.4 copy.50
  112.6 0.8 copy-done.2
  113.6 1.1 constant_dynamic-slice_fusion.5
  114.6 2.0 collective-permute-start.2
  116.9 0.6 gather_fusion.2
  117.7 0.9 bitcast_select_fusion
  118.6 2.1 fusion.15
  120.7 3.6 %fusion.22 = f32[2,176,16,64]{1,3,2,0:T(8,128)S(1)} fusion(bf16[2,2048,176]{1,2,0:T(8,128)(2,1)S(1)} %copy-done.15, s32[]{:T(128)S(6)} %select_n.153, bf16[16,2,64,1024]{3,2,1,0:T(8,128)(2,1)} %copy-done.2), kind=kOutput, calls=%fused_computation.40 | convolution fusion | flops 738197504 | bytes 6356996 | tf_op jit(solution)/shard_map/sexd,edf->sexf/dot_general | solution.py:104
  124.3 0.2 copy-done.16
  124.6 1.3 fusion.18
  125.9 3.5 %fusion.20 = f32[2,176,16,64]{1,3,2,0:T(8,128)S(1)} fusion(bf16[16,2,64,1024]{3,2,0,1:T(8,128)(2,1)} %collective-permute-done, bf16[2,2048,176]{1,2,0:T(8,128)(2,1)S(1)} %copy-done.15, s32[]{:T(128)S(6)} %select_n.154), kind=kOutput, calls=%fused_computation.38 | convolution fusion | flops 738197504 | bytes 6356996 | tf_op jit(solution)/shard_map/sexd,edf->sexf/dot_general | solution.py:106
  129.3 3.9 %fusion.6 = bf16[16,2,64,176]{3,2,0,1:T(8,128)(2,1)S(1)} fusion(f32[2,176,16,64]{1,3,2,0:T(8,128)S(1)} %fusion.18, f32[2,176,16,64]{1,3,2,0:T(8,128)S(1)} %fusion.22, f32[2,176,16,64]{1,3,2,0:T(8,128)S(1)} %fusion.20, bf16[16,2,64,1024]{3,2,0,1:T(8,128)(2,1)} %collective-permute-done, bf16[2,2048,176]{1,2,0:T(8,128)(2,1)S(1)} %copy-done.16, s32[]{:T(128)S(6)} %select_n.154), kind=kOutput, calls=%fused_computation.16 | convolution fusion | flops 741081088 | bytes 11927556 | tf_op jit(solution)/shard_map/sexd,edf->sexf/dot_general | solution.py:106
  133.3 3.3 %collective-permute-start.9 = (bf16[16,2,64,176]{3,2,0,1:T(8,128)(2,1)S(1)}, bf16[16,2,64,176]{3,2,0,1:T(8,128)(2,1)S(1)}, u32[]{:S(2)}, u32[]{:S(2)}) collective-permute-start(bf16[16,2,64,176]{3,2,0,1:T(8,128)(2,1)S(1)} %fusion.6), channel_id=1, source_target_pairs={{0,96},{16,112},{32,0},{48,16},{64,32},{80,48},{96,64},{112,80},{1... | collective-permute-start | bytes 2162696 | tf_op jit(solution)/shard_map/ppermute | solution.py:114
  136.6 0.4 fusion.69
  137.0 1.8 fusion.45
  138.8 18.9 %collective-permute-done.9 = bf16[16,2,64,176]{3,2,0,1:T(8,128)(2,1)S(1)} collective-permute-done((bf16[16,2,64,176]{3,2,0,1:T(8,128)(2,1)S(1)}, bf16[16,2,64,176]{3,2,0,1:T(8,128)(2,1)S(1)}, u32[]{:S(2)}, u32[]{:S(2)}) %collective-permute-start.9) | collective-permute-done | bytes 720928 | tf_op jit(solution)/shard_map/ppermute | solution.py:114
  157.7 3.6 %collective-permute-start.8 = (bf16[2,176,256]{2,1,0:T(8,128)(2,1)}, bf16[2,176,256]{2,1,0:T(8,128)(2,1)}, u32[]{:S(2)}, u32[]{:S(2)}) collective-permute-start(bf16[2,176,256]{2,1,0:T(8,128)(2,1)} %get-tuple-element.8), channel_id=1, source_target_pairs={{0,96},{16,112},{32,0},{48,16},{64,32},{80,48},{96,64},{112,80},{1... | collective-permute-start | bytes 540680 | tf_op jit(solution)/shard_map/ppermute | solution.py:114
  161.4 1.1 slice.44
  162.5 0.3 collective-permute-start.1
  162.8 3.1 %fusion.41 = f32[2,256,16,64]{1,3,2,0:T(8,128)} fusion(bf16[16,2,64,176]{3,2,0,1:T(8,128)(2,1)} %collective-permute-done.5, bf16[2,176,256]{2,1,0:T(8,128)(2,1)} %collective-permute-done.4), kind=kOutput, calls=%fused_computation.62 | convolution fusion | flops 184549376 | bytes 2998272 | tf_op jit(solution)/shard_map/sexf,efd->sexd/dot_general | solution.py:138
  165.9 3.4 %collective-permute-start.12 = (bf16[2,176,256]{2,1,0:T(8,128)(2,1)}, bf16[2,176,256]{2,1,0:T(8,128)(2,1)S(1)}, u32[]{:S(2)}, u32[]{:S(2)}) collective-permute-start(bf16[2,176,256]{2,1,0:T(8,128)(2,1)} %get-tuple-element.12), channel_id=1, source_target_pairs={{0,64},{16,80},{32,96},{48,112},{64,0},{80,16},{96,32},{112,48},{1... | collective-permute-start | bytes 540680 | tf_op jit(solution)/shard_map/ppermute | solution.py:114
  169.2 0.7 collective-permute-done.1
  170.0 1.9 collective-permute-start.15
  171.8 2.7 %fusion.43 = f32[2,256,16,64]{1,3,2,0:T(8,128)} fusion(bf16[16,2,64,176]{3,2,0,1:T(8,128)(2,1)S(1)} %collective-permute-done.3, bf16[2,176,256]{2,1,0:T(8,128)(2,1)S(1)} %collective-permute-done.1, bf16[2,176,256]{2,1,0:T(8,128)(2,1)} %collective-permute-done.2, pred[]{:T(512)S(6)} %eq.72), kind=kOutput, calls=%fused_computation.64 | convolution fusion | flops 184639488 | bytes 3178497 | tf_op jit(solution)/shard_map/sexf,efd->sexd/dot_general | solution.py:138
  174.5 4.1 %fusion.2 = f32[256,704]{0,1:T(8,128)} fusion(bf16[3,2048,704]{1,2,0:T(8,128)(2,1)} %all-gather.5.cloned.1.call-done, bf16[512,2048]{1,0:T(8,128)(2,1)} %all-gather.3.cloned.1.call-done), kind=kOutput, calls=%fused_computation.9 | convolution fusion | flops 738197504 | bytes 4653056 | tf_op jit(solution)/shard_map/dot_general | solution.py:161
  178.6 3.7 %fusion.3 = f32[256,704]{0,1:T(8,128)} fusion(bf16[3,2048,704]{1,2,0:T(8,128)(2,1)} %all-gather.5.cloned.1.call-done, bf16[512,2048]{1,0:T(8,128)(2,1)S(1)} %copy-done.8), kind=kOutput, calls=%fused_computation.11 | convolution fusion | flops 738197504 | bytes 4653056 | tf_op jit(solution)/shard_map/dot_general | solution.py:160
  182.3 5.1 %fusion.4 = f32[256,2048]{1,0:T(8,128)} fusion(bf16[3,2048,704]{1,2,0:T(8,128)(2,1)} %all-gather.5.cloned.1.call-done, f32[256,704]{0,1:T(8,128)} %fusion.2, bf16[256,256]{1,0:T(8,128)(2,1)S(1)} %fusion.15, bf16[256,704]{1,0:T(8,128)(2,1)} %bitcast_select_fusion, f32[256]{0:T(256)S(1)} %add_divide_fusion, f32[256,704]{0,1:T(8,128)} %fusion.3), kind=kOutput, calls=%fused_computation.12 | convolution fusion | flops 832438272 | bytes 6947840 | tf_op jit(solution)/shard_map/dot_general | solution.py:165
  187.4 0.2 collective-permute-start.13
  187.7 1.3 fusion.37
  189.1 0.5 collective-permute-start.16
  189.6 0.3 fusion.49
  189.9 13.7 %collective-permute-done.13 = bf16[8,2,64,176]{3,2,0,1:T(8,128)(2,1)S(1)} collective-permute-done((bf16[8,2,64,176]{3,2,0,1:T(8,128)(2,1)S(1)}, bf16[8,2,64,176]{3,2,0,1:T(8,128)(2,1)S(1)}, u32[]{:S(2)}, u32[]{:S(2)}) %collective-permute-start.13) | collective-permute-done | bytes 360480 | tf_op jit(solution)/shard_map/ppermute | solution.py:114
  203.6 0.3 fusion.51
  203.9 0.6 collective-permute-start.11
  204.5 0.3 fusion.10
  204.8 0.7 collective-permute-done.14
  205.5 0.3 fusion.11
  205.9 0.5 fusion.39
  206.3 0.8 collective-permute-done.11
  207.2 0.6 copy-done.6
  207.8 0.7 copy-done.4
  208.5 0.9 fusion.5
  209.4 1.2 copy.53
  210.6 3.7 %all-to-all-start.1 = ((bf16[16,2,64,256]{3,2,1,0:T(8,128)(2,1)}), bf16[16,2,64,256]{3,2,1,0:T(8,128)(2,1)S(1)}, u32[]{:S(2)}, u32[]{:S(2)}) async-start(bf16[16,2,64,256]{3,2,1,0:T(8,128)(2,1)} %copy.53), calls=%async_computation.1 | async-start | bytes 2097152 | tf_op jit(solution)/shard_map/all_to_all | solution.py:153
  214.3 0.2 copy.49
  214.7 1.7 fusion.74
  216.6 17.2 %all-to-all-done.1 = bf16[16,2,64,256]{3,2,1,0:T(8,128)(2,1)S(1)} async-done(((bf16[16,2,64,256]{3,2,1,0:T(8,128)(2,1)}), bf16[16,2,64,256]{3,2,1,0:T(8,128)(2,1)S(1)}, u32[]{:S(2)}, u32[]{:S(2)}) %all-to-all-start.1) | async-done | bytes 1048608 | tf_op jit(solution)/shard_map/all_to_all | solution.py:153
  233.8 1.6 bitcast_convert_fusion
  235.4 5.2 %gather_fusion.1 = f32[1024,256]{1,0:T(8,128)S(1)} fusion(f32[2048,256]{1,0:T(8,128)} %bitcast_convert_fusion, s32[1024]{0:T(1024)S(1)} %broadcast_clamp_fusion), kind=kCustom, calls=%fused_computation.1 | custom fusion | bytes 2101248 | tf_op jit(solution)/shard_map/jit(_take)/gather | solution.py:157
  240.6 1.3 reshape.118
  241.8 2.5 multiply_reduce_fusion
  244.4 1.7 add.222
  (89 shorter events, 1.9 us)
Async XLA Ops:
  6.5 110.4 %copy-start = (bf16[64,16,704]{2,1,0:T(8,128)(2,1)S(1)}, bf16[64,16,704]{2,1,0:T(8,128)(2,1)}, u32[]{:S(2)}) copy-start(bf16[64,16,704]{2,1,0:T(8,128)(2,1)} %param.25) | copy-start | bytes 4325380
  6.5 7.1 %copy-start.11 = (s32[256,4]{0,1:T(4,128)S(1)}, s32[256,4]{0,1:T(4,128)}, u32[]{:S(2)}) copy-start(s32[256,4]{0,1:T(4,128)} %param.26) | copy-start | bytes 12292
  6.5 34.6 %all-gather.3.cloned.1.call-start = ((), (), s32[]{:S(2)}) async-start(), calls=%async_computation.3 | async-start | bytes 2359296 | tf_op jit(solution)/shard_map/all_gather | solution.py:34
  11.5 163.0 %all-gather.5.cloned.1.call-start = ((), (), s32[]{:S(2)}) async-start(), calls=%async_computation.4 | async-start | bytes 9191424 | tf_op jit(solution)/shard_map/all_gather | solution.py:53
  13.6 230.8 %reduce-scatter.2.cloned.1.call-start = ((), (), s32[]{:S(2)}) async-start(), calls=%async_computation.5 | async-start | bytes 2359296 | tf_op jit(solution)/shard_map/reduce_scatter | solution.py:172
  41.2 1.2 slice-start
  110.2 3.3 %copy-start.2 = (bf16[16,2,64,1024]{3,2,1,0:T(8,128)(2,1)}, bf16[16,2,64,1024]{3,2,1,0:T(8,128)(2,1)S(1)}, u32[]{:S(2)}) copy-start(bf16[16,2,64,1024]{3,2,1,0:T(8,128)(2,1)S(1)} %all_to_all.10) | copy-start | bytes 12582916
  110.2 3.4 %copy-start.9 = (bf16[2,176,2048]{2,1,0:T(8,128)(2,1)S(1)}, bf16[2,176,2048]{2,1,0:T(8,128)(2,1)}, u32[]{:S(2)}) copy-start(bf16[2,176,2048]{2,1,0:T(8,128)(2,1)} %param.23) | copy-start | bytes 4325380
  113.4 3.2 %copy-start.12 = (bf16[2048]{0:T(1024)(128)(2,1)S(1)}, bf16[2048]{0:T(1024)(128)(2,1)}, u32[]{:S(2)}) copy-start(bf16[2048]{0:T(1024)(128)(2,1)} %param.17) | copy-start | bytes 12292
  113.4 3.2 %copy-start.13 = (s32[1,16]{1,0:T(1,128)S(1)}, s32[1,16]{1,0:T(1,128)}, u32[]{:S(2)}) copy-start(s32[1,16]{1,0:T(1,128)} %param.27) | copy-start | bytes 196
  113.4 4.2 %copy-start.14 = (s32[1,16]{1,0:T(1,128)S(1)}, s32[1,16]{1,0:T(1,128)}, u32[]{:S(2)}) copy-start(s32[1,16]{1,0:T(1,128)} %param.28) | copy-start | bytes 196
  113.4 12.4 %collective-permute-start = (bf16[16,2,64,1024]{3,2,0,1:T(8,128)(2,1)}, bf16[16,2,64,1024]{3,2,0,1:T(8,128)(2,1)}, u32[]{:S(2)}, u32[]{:S(2)}) collective-permute-start(bf16[16,2,64,1024]{3,2,0,1:T(8,128)(2,1)} %copy.50), channel_id=1, source_target_pairs={{0,16},{16,0},{32,48},{48,32},{64,80},{80,64},{96,112},{112,96},{1... | collective-permute-start | bytes 12582920 | tf_op jit(solution)/shard_map/ppermute | solution.py:98
  114.6 51.2 %collective-permute-start.2 = (bf16[2,176,256]{2,1,0:T(8,128)(2,1)}, bf16[2,176,256]{2,1,0:T(8,128)(2,1)}, u32[]{:S(2)}, u32[]{:S(2)}) collective-permute-start(bf16[2,176,256]{2,1,0:T(8,128)(2,1)} %get-tuple-element.7), channel_id=1, source_target_pairs={{0,112},{16,0},{32,16},{48,32},{64,48},{80,64},{96,80},{112,96},{1... | collective-permute-start | bytes 540680 | tf_op jit(solution)/shard_map/ppermute | solution.py:114
  116.6 45.9 %collective-permute-start.4 = (bf16[2,176,256]{2,1,0:T(8,128)(2,1)}, bf16[2,176,256]{2,1,0:T(8,128)(2,1)}, u32[]{:S(2)}, u32[]{:S(2)}) collective-permute-start(bf16[2,176,256]{2,1,0:T(8,128)(2,1)} %get-tuple-element.10), channel_id=1, source_target_pairs={{0,32},{16,48},{32,64},{48,80},{64,96},{80,112},{96,0},{112,16},{1... | collective-permute-start | bytes 540680 | tf_op jit(solution)/shard_map/ppermute | solution.py:114
  117.5 3.2 %copy-start.15 = (bf16[2,2048,176]{1,2,0:T(8,128)(2,1)S(1)}, bf16[2,2048,176]{1,2,0:T(8,128)(2,1)}, u32[]{:S(2)}) copy-start(bf16[2,2048,176]{1,2,0:T(8,128)(2,1)} %param.21) | copy-start | bytes 4325380
  120.7 3.6 %copy-start.3 = (bf16[16,2,64,1024]{3,2,1,0:T(8,128)(2,1)S(1)}, bf16[16,2,64,1024]{3,2,1,0:T(8,128)(2,1)}, u32[]{:S(2)}) copy-start(bf16[16,2,64,1024]{3,2,1,0:T(8,128)(2,1)} %copy-done.2) | copy-start | bytes 12582916
  120.7 3.9 %copy-start.16 = (bf16[2,2048,176]{1,2,0:T(8,128)(2,1)S(1)}, bf16[2,2048,176]{1,2,0:T(8,128)(2,1)}, u32[]{:S(2)}) copy-start(bf16[2,2048,176]{1,2,0:T(8,128)(2,1)} %param.22) | copy-start | bytes 4325380
  129.3 7.2 %copy-start.7 = (bf16[512,2048]{1,0:T(8,128)(2,1)S(1)}, bf16[512,2048]{1,0:T(8,128)(2,1)}, u32[]{:S(2)}) copy-start(bf16[512,2048]{1,0:T(8,128)(2,1)} %all-gather.3.cloned.1.call-done) | copy-start | bytes 6291460
  133.3 24.4 %collective-permute-start.9 = (bf16[16,2,64,176]{3,2,0,1:T(8,128)(2,1)S(1)}, bf16[16,2,64,176]{3,2,0,1:T(8,128)(2,1)S(1)}, u32[]{:S(2)}, u32[]{:S(2)}) collective-permute-start(bf16[16,2,64,176]{3,2,0,1:T(8,128)(2,1)S(1)} %fusion.6), channel_id=1, source_target_pairs={{0,96},{16,112},{32,0},{48,16},{64,32},{80,48},{96,64},{112,80},{1... | collective-permute-start | bytes 2162696 | tf_op jit(solution)/shard_map/ppermute | solution.py:114
  136.6 24.8 %collective-permute-start.5 = (bf16[16,2,64,176]{3,2,0,1:T(8,128)(2,1)S(1)}, bf16[16,2,64,176]{3,2,0,1:T(8,128)(2,1)}, u32[]{:S(2)}, u32[]{:S(2)}) collective-permute-start(bf16[16,2,64,176]{3,2,0,1:T(8,128)(2,1)S(1)} %fusion.6), channel_id=1, source_target_pairs={{0,32},{16,48},{32,64},{48,80},{64,96},{80,112},{96,0},{112,16},{1... | collective-permute-start | bytes 2162696 | tf_op jit(solution)/shard_map/ppermute | solution.py:114
  136.9 33.0 %collective-permute-start.3 = (bf16[16,2,64,176]{3,2,0,1:T(8,128)(2,1)S(1)}, bf16[16,2,64,176]{3,2,0,1:T(8,128)(2,1)S(1)}, u32[]{:S(2)}, u32[]{:S(2)}) collective-permute-start(bf16[16,2,64,176]{3,2,0,1:T(8,128)(2,1)S(1)} %fusion.6), channel_id=1, source_target_pairs={{0,16},{16,0},{32,48},{48,32},{64,80},{80,64},{96,112},{112,96},{1... | collective-permute-start | bytes 2162696 | tf_op jit(solution)/shard_map/ppermute | solution.py:117
  137.0 25.5 %copy-start.10 = (bf16[2,176,256]{2,1,0:T(8,128)(2,1)S(1)}, bf16[2,176,256]{2,1,0:T(8,128)(2,1)}, u32[]{:S(2)}) copy-start(bf16[2,176,256]{2,1,0:T(8,128)(2,1)} %get-tuple-element.11) | copy-start | bytes 540676
  157.7 29.7 %collective-permute-start.8 = (bf16[2,176,256]{2,1,0:T(8,128)(2,1)}, bf16[2,176,256]{2,1,0:T(8,128)(2,1)}, u32[]{:S(2)}, u32[]{:S(2)}) collective-permute-start(bf16[2,176,256]{2,1,0:T(8,128)(2,1)} %get-tuple-element.8), channel_id=1, source_target_pairs={{0,96},{16,112},{32,0},{48,16},{64,32},{80,48},{96,64},{112,80},{1... | collective-permute-start | bytes 540680 | tf_op jit(solution)/shard_map/ppermute | solution.py:114
  161.3 42.6 %collective-permute-start.6 = (bf16[2,176,256]{2,1,0:T(8,128)(2,1)}, bf16[2,176,256]{2,1,0:T(8,128)(2,1)S(1)}, u32[]{:S(2)}, u32[]{:S(2)}) collective-permute-start(bf16[2,176,256]{2,1,0:T(8,128)(2,1)} %get-tuple-element.9), channel_id=1, source_target_pairs={{0,48},{16,64},{32,80},{48,96},{64,112},{80,0},{96,16},{112,32},{1... | collective-permute-start | bytes 540680 | tf_op jit(solution)/shard_map/ppermute | solution.py:114
  162.5 7.4 %collective-permute-start.1 = (bf16[2,176,256]{2,1,0:T(8,128)(2,1)S(1)}, bf16[2,176,256]{2,1,0:T(8,128)(2,1)S(1)}, u32[]{:S(2)}, u32[]{:S(2)}) collective-permute-start(bf16[2,176,256]{2,1,0:T(8,128)(2,1)S(1)} %copy-done.10), channel_id=1, source_target_pairs={{0,16},{16,32},{32,48},{48,64},{64,80},{80,96},{96,112},{112,0},{1... | collective-permute-start | bytes 540680 | tf_op jit(solution)/shard_map/ppermute | solution.py:114
  165.9 23.1 %collective-permute-start.12 = (bf16[2,176,256]{2,1,0:T(8,128)(2,1)}, bf16[2,176,256]{2,1,0:T(8,128)(2,1)S(1)}, u32[]{:S(2)}, u32[]{:S(2)}) collective-permute-start(bf16[2,176,256]{2,1,0:T(8,128)(2,1)} %get-tuple-element.12), channel_id=1, source_target_pairs={{0,64},{16,80},{32,96},{48,112},{64,0},{80,16},{96,32},{112,48},{1... | collective-permute-start | bytes 540680 | tf_op jit(solution)/shard_map/ppermute | solution.py:114
  170.0 34.5 %collective-permute-start.10 = (bf16[2,176,256]{2,1,0:T(8,128)(2,1)}, bf16[2,176,256]{2,1,0:T(8,128)(2,1)S(1)}, u32[]{:S(2)}, u32[]{:S(2)}) collective-permute-start(bf16[2,176,256]{2,1,0:T(8,128)(2,1)} %get-tuple-element.13), channel_id=1, source_target_pairs={{0,80},{16,96},{32,112},{48,0},{64,16},{80,32},{96,48},{112,64},{1... | collective-permute-start | bytes 540680 | tf_op jit(solution)/shard_map/ppermute | solution.py:114
  170.0 19.1 %collective-permute-start.15 = (bf16[8,2,64,176]{3,2,0,1:T(8,128)(2,1)S(1)}, bf16[8,2,64,176]{3,2,0,1:T(8,128)(2,1)S(1)}, u32[]{:S(2)}, u32[]{:S(2)}) collective-permute-start(bf16[8,2,64,176]{3,2,0,1:T(8,128)(2,1)S(1)} %slice.45), channel_id=1, source_target_pairs={{0,96},{16,112},{32,0},{48,16},{64,32},{80,48},{96,64},{112,80},{1... | collective-permute-start | bytes 1081352 | tf_op jit(solution)/shard_map/ppermute | solution.py:114
  174.5 4.1 %copy-start.8 = (bf16[512,2048]{1,0:T(8,128)(2,1)S(1)}, bf16[512,2048]{1,0:T(8,128)(2,1)}, u32[]{:S(2)}) copy-start(bf16[512,2048]{1,0:T(8,128)(2,1)} %all-gather.3.cloned.1.call-done) | copy-start | bytes 6291460
  187.4 16.2 %collective-permute-start.13 = (bf16[8,2,64,176]{3,2,0,1:T(8,128)(2,1)S(1)}, bf16[8,2,64,176]{3,2,0,1:T(8,128)(2,1)S(1)}, u32[]{:S(2)}, u32[]{:S(2)}) collective-permute-start(bf16[8,2,64,176]{3,2,0,1:T(8,128)(2,1)S(1)} %slice.44), channel_id=1, source_target_pairs={{0,32},{16,48},{32,64},{48,80},{64,96},{80,112},{96,0},{112,16},{1... | collective-permute-start | bytes 1081352 | tf_op jit(solution)/shard_map/ppermute | solution.py:114
  189.0 16.8 %collective-permute-start.7 = (bf16[16,2,64,176]{3,2,0,1:T(8,128)(2,1)}, bf16[16,2,64,176]{3,2,0,1:T(8,128)(2,1)S(1)}, u32[]{:S(2)}, u32[]{:S(2)}) collective-permute-start(bf16[16,2,64,176]{3,2,0,1:T(8,128)(2,1)} %collective-permute-done.5), channel_id=1, source_target_pairs={{0,16},{16,0},{32,48},{48,32},{64,80},{80,64},{96,112},{112,96},{1... | collective-permute-start | bytes 2162696 | tf_op jit(solution)/shard_map/ppermute | solution.py:117
  189.1 15.4 %collective-permute-start.16 = (bf16[8,2,64,176]{3,2,0,1:T(8,128)(2,1)S(1)}, bf16[8,2,64,176]{3,2,0,1:T(8,128)(2,1)S(1)}, u32[]{:S(2)}, u32[]{:S(2)}) collective-permute-start(bf16[8,2,64,176]{3,2,0,1:T(8,128)(2,1)S(1)} %collective-permute-done.15), channel_id=1, source_target_pairs={{0,16},{16,0},{32,48},{48,32},{64,80},{80,64},{96,112},{112,96},{1... | collective-permute-start | bytes 1081352 | tf_op jit(solution)/shard_map/ppermute | solution.py:117
  203.6 1.9 collective-permute-start.14
  203.9 3.2 %collective-permute-start.11 = (bf16[16,2,64,176]{3,2,0,1:T(8,128)(2,1)S(1)}, bf16[16,2,64,176]{3,2,0,1:T(8,128)(2,1)S(1)}, u32[]{:S(2)}, u32[]{:S(2)}) collective-permute-start(bf16[16,2,64,176]{3,2,0,1:T(8,128)(2,1)S(1)} %collective-permute-done.9), channel_id=1, source_target_pairs={{0,16},{16,0},{32,48},{48,32},{64,80},{80,64},{96,112},{112,96},{1... | collective-permute-start | bytes 2162696 | tf_op jit(solution)/shard_map/ppermute | solution.py:117
  205.5 1.6 copy-start.5
  205.5 2.3 copy-start.6
  205.8 2.7 %copy-start.4 = (f32[2,256,16,64]{1,3,2,0:T(8,128)S(1)}, f32[2,256,16,64]{1,3,2,0:T(8,128)}, u32[]{:S(2)}) copy-start(f32[2,256,16,64]{1,3,2,0:T(8,128)} %fusion.45) | copy-start | bytes 6291460
  209.4 5.3 %copy-start.17 = (bf16[2048,32]{0,1:T(8,128)(2,1)S(1)}, bf16[2048,32]{0,1:T(8,128)(2,1)}, u32[]{:S(2)}) copy-start(bf16[2048,32]{0,1:T(8,128)(2,1)} %param.16) | copy-start | bytes 393220
  210.6 23.2 %all-to-all-start.1 = ((bf16[16,2,64,256]{3,2,1,0:T(8,128)(2,1)}), bf16[16,2,64,256]{3,2,1,0:T(8,128)(2,1)S(1)}, u32[]{:S(2)}, u32[]{:S(2)}) async-start(bf16[16,2,64,256]{3,2,1,0:T(8,128)(2,1)} %copy.53), calls=%async_computation.1 | async-start | bytes 2097152 | tf_op jit(solution)/shard_map/all_to_all | solution.py:153
  235.4 10.7 %copy-start.1 = (bf16[64,16,704]{2,1,0:T(8,128)(2,1)S(1)}, bf16[64,16,704]{2,1,0:T(8,128)(2,1)}, u32[]{:S(2)}) copy-start(bf16[64,16,704]{2,1,0:T(8,128)(2,1)} %param.25) | copy-start | bytes 4325380
Sparse Core Ops, SparseCore 0:
  11.7 29.4 all-gather.2
  43.3 115.2 all-gather.4
  187.5 32.3 reduce-scatter.1

commit v6 on v4

--- a/solution.py
+++ b/solution.py
@@ -93,6 +93,19 @@
     selection = jnp.any(row_index[None, :, :] == slot_id[:, None, None], axis=2).astype(jnp.bfloat16)
     own_features = lax.dynamic_slice_in_dim(all_features, half * half_width, half_width, axis=1)
     chosen = jnp.dot(selection, own_features, preferred_element_type=jnp.float32).astype(jnp.bfloat16)
+    def shifted(x, shift):
+        return lax.ppermute(x, "row", [(i, (i + shift) % row_count) for i in range(row_count)])
+
+    def partner(x):
+        return lax.ppermute(x, "row", [(i, i ^ 1) for i in range(row_count)])
+
+    def down_slice(k):
+        return lax.dynamic_slice_in_dim(
+            routed_down_weight, ((row_id + k) % row_count) * local_width, local_width, axis=2
+        )
+
+    down_from = [down_slice(0)] + [shifted(down_slice(k), k) for k in range(1, row_count)]
+    chosen, down_from = lax.optimization_barrier((chosen, down_from))
     outgoing = chosen.reshape(col_count, local_experts, capacity, half_width)
     own_half = lax.all_to_all(outgoing, "col", split_axis=0, concat_axis=0, tiled=True)
     other_half = lax.ppermute(own_half, "row", [(i, i ^ 1) for i in range(row_count)])
@@ -110,12 +123,6 @@
     gate_part = project(routed_gate_weight)
     up_part = project(routed_up_weight)
     hidden = (jax.nn.silu(gate_part) * up_part).astype(jnp.bfloat16)
-    def shifted(x, shift):
-        return lax.ppermute(x, "row", [(i, (i + shift) % row_count) for i in range(row_count)])
-
-    def partner(x):
-        return lax.ppermute(x, "row", [(i, i ^ 1) for i in range(row_count)])
-
     local_hidden = hidden.shape[3]
     group_half = hidden.shape[0] // 2
     from_below = shifted(hidden, 2)
@@ -123,12 +130,6 @@
     far_low = shifted(from_below[:group_half], 2)
     far_high = shifted(from_above[group_half:], -2)
 
-    def down_slice(k):
-        return lax.dynamic_slice_in_dim(
-            routed_down_weight, ((row_id + k) % row_count) * local_width, local_width, axis=2
-        )
-
-    down_from = [down_slice(0)] + [shifted(down_slice(k), k) for k in range(1, row_count)]
     odd = row_id % 2 == 1
 
     def down_pick(k_even, k_odd):

time: 253 us -> 258 us (1.020)
  matrix products: 43.3 us -> 46.6 us
  blocking collectives: 66.5 us -> 63.7 us
  waiting for transfers between devices: 74.1 us -> 76.7 us
    ppermute x11, waiting for transfers between devices: 19.4 us -> 26.1 us  [shifted(): lax.ppermute(x, 'row', [(i, (i + shift) % row_count) for i in range(row_c...]
    dot_general x10, matrix products: 13 us -> 15.8 us  [down_of(): jnp.einsum('sexf,efd->sexd', block, weight, preferred_element_type=jnp.fl...]
    all_to_all x1, blocking collectives: 66.5 us -> 63.7 us  [on_device(): lax.all_to_all(outgoing, 'col', split_axis=0, concat_axis=0, tiled=True)]
  transfers between devices with their start and end apart: 21 -> 21, of which waited for: 8 -> 6; matrix products, arithmetic and copies ran while one was open for 26% -> 28% of each run, Pallas kernels for 0% -> 0%
where the time goes in v6:
time: 258 us; the launch traced here: 257 us
  waiting for transfers between devices  76.7 us (30%)
  blocking collectives  63.7 us (25%)
  matrix products  46.6 us (18%)
  starting transfers between devices  21.3 us (8%)
  local copies, waits for them, and re-layouts  20.7 us (8%)
  other arithmetic  14.1 us (5%)
  between operations  13.7 us (5%)
    all_to_all x1, blocking collectives, on_device(): lax.all_to_all(outgoing, 'col', split_axis=0, concat_axis=0, tiled=True)  63.7 us
    all_to_all x1, waiting for transfers between devices, on_device(): lax.all_to_all(expert_value, 'col', split_axis=0, concat_axis=0, tiled=True)  28.9 us
    ppermute x11, waiting for transfers between devices, shifted(): lax.ppermute(x, 'row', [(i, (i + shift) % row_count) for i in range(row_c...  26.1 us
    all_gather x1, waiting for transfers between devices, on_device(): lax.all_gather(jnp.concatenate([tokens, picked_input_factor.reshape(reduc...  21.5 us
    dot_general x10, matrix products, down_of(): jnp.einsum('sexf,efd->sexd', block, weight, preferred_element_type=jnp.fl...  15.8 us
    ppermute x11, starting transfers between devices, shifted(): lax.ppermute(x, 'row', [(i, (i + shift) % row_count) for i in range(row_c...  15.3 us
    dot_general x2, matrix products, project(): jnp.einsum('sexd,edf->sexf', other_half, half_weights(w, 1 - half), prefe...  7.39 us
    gather x2, local copies, waits for them, and re-layouts, on_device(): routed_rows = jnp.take(flat_rows, row_index, axis=0)  6.46 us
  transfers between devices with their start and end apart: 21, of which 6 were waited for; matrix products, arithmetic and copies ran while one was open for 28% of the time, Pallas kernels for 0%

profile of v6, /device:TPU:0, one launch (start us, length us, event | category | flops | bytes accessed | tf_op | source)
XLA Modules:
  0.0 256.7 jit_solution(11189603413065963285)
XLA Ops:
  6.5 0.8 compare_and_fusion.1
  7.4 0.7 compare_select_fusion.1
  8.2 1.6 gather_fusion
  9.9 1.6 pad_maximum_fusion.1
  11.7 2.0 pad_maximum_fusion
  13.8 1.2 constant_dynamic-slice_fusion
  15.1 3.6 %collective-permute-start.6 = (bf16[2,176,256]{2,1,0:T(8,128)(2,1)}, bf16[2,176,256]{2,1,0:T(8,128)(2,1)}, u32[]{:S(2)}, u32[]{:S(2)}) collective-permute-start(bf16[2,176,256]{2,1,0:T(8,128)(2,1)} %get-tuple-element.25), channel_id=1, source_target_pairs={{0,112},{16,0},{32,16},{48,32},{64,48},{80,64},{96,80},{112,96},{1... | collective-permute-start | bytes 540680 | tf_op jit(solution)/shard_map/ppermute | solution.py:97
  18.7 0.5 collective-permute-start.4
  19.2 1.2 collective-permute-start.2
  20.4 1.7 collective-permute-start.1
  22.2 0.6 reduce-window.18
  22.8 0.2 slice_reduce_fusion
  23.1 2.6 %fusion = pred[2048,256]{1,0:T(8,128)(4,1)S(1)} fusion(s32[256,4]{0,1:T(4,128)S(1)} %get-tuple-element.24), kind=kLoop, calls=%fused_computation.4 | loop fusion | flops 3670016 | bytes 528384 | tf_op jit(solution)/shard_map/reduce_or | solution.py:93
  25.8 21.5 %all-gather.3.cloned.1.call-done = bf16[512,2048]{1,0:T(8,128)(2,1)} async-done(((bf16[512,256]{1,0:T(8,128)(2,1)}), bf16[512,2048]{1,0:T(8,128)(2,1)}) %all-gather.3.cloned.1.call-update) | async-done | bytes 2097168 | tf_op jit(solution)/shard_map/all_gather | solution.py:34
  47.3 0.9 copy-done.16
  48.3 0.3 collective-permute-start
  48.5 1.3 collective-permute-start.5
  49.8 1.3 convolution_convert_fusion
  51.1 3.3 %collective-permute-done = bf16[2,176,256]{2,1,0:T(8,128)(2,1)S(1)} collective-permute-done((bf16[2,176,256]{2,1,0:T(8,128)(2,1)S(1)}, bf16[2,176,256]{2,1,0:T(8,128)(2,1)S(1)}, u32[]{:S(2)}, u32[]{:S(2)}) %collective-permute-start) | collective-permute-done | bytes 180256 | tf_op jit(solution)/shard_map/ppermute | solution.py:97
  54.4 1.3 collective-permute-done.5
  55.7 0.7 copy-done.13
  56.4 63.7 %all_to_all.10 = bf16[16,2,64,1024]{3,2,1,0:T(8,128)(2,1)S(1)} all-to-all(bf16[16,2,64,1024]{3,2,1,0:T(8,128)(2,1)S(1)} %bitcast.146), channel_id=1, replica_groups=mesh['row'=8,'col'=16] {'col'}, dimensions={0} | all-to-all | bytes 8388608 | tf_op jit(solution)/shard_map/all_to_all | solution.py:110
  120.1 2.7 %copy.50 = bf16[16,2,64,1024]{3,2,0,1:T(8,128)(2,1)} copy(bf16[16,2,64,1024]{3,2,1,0:T(8,128)(2,1)S(1)} %all_to_all.10) | data formatting | bytes 8388608 | tf_op jit(solution)/shard_map/all_to_all | solution.py:110
  122.7 0.5 copy-done.2
  123.5 0.6 gather_fusion.2
  124.3 0.9 bitcast_select_fusion
  125.2 1.6 fusion.66
  126.8 4.0 %fusion.21 = f32[2,176,16,64]{1,3,2,0:T(8,128)S(1)} fusion(bf16[2,2048,176]{1,2,0:T(8,128)(2,1)} %param.21, s32[]{:T(128)S(6)} %select_n.151, bf16[16,2,64,1024]{3,2,1,0:T(8,128)(2,1)} %copy-done.2), kind=kOutput, calls=%fused_computation.38 | convolution fusion | flops 738197504 | bytes 6356996 | tf_op jit(solution)/shard_map/sexd,edf->sexf/dot_general | solution.py:117
  130.9 0.3 copy-done.22
  131.2 1.3 fusion.17
  132.6 3.5 %fusion.19 = f32[2,176,16,64]{1,3,2,0:T(8,128)S(1)} fusion(bf16[16,2,64,1024]{3,2,0,1:T(8,128)(2,1)} %collective-permute-done.7, bf16[2,2048,176]{1,2,0:T(8,128)(2,1)S(1)} %copy-done.21, s32[]{:T(128)S(6)} %select_n.168), kind=kOutput, calls=%fused_computation.36 | convolution fusion | flops 738197504 | bytes 6356996 | tf_op jit(solution)/shard_map/sexd,edf->sexf/dot_general | solution.py:119
  136.0 3.9 %fusion.5 = bf16[16,2,64,176]{3,2,0,1:T(8,128)(2,1)S(1)} fusion(f32[2,176,16,64]{1,3,2,0:T(8,128)S(1)} %fusion.17, f32[2,176,16,64]{1,3,2,0:T(8,128)S(1)} %fusion.21, f32[2,176,16,64]{1,3,2,0:T(8,128)S(1)} %fusion.19, bf16[16,2,64,1024]{3,2,0,1:T(8,128)(2,1)} %collective-permute-done.7, bf16[2,2048,176]{1,2,0:T(8,128)(2,1)S(1)} %copy-done.22, s32[]{:T(128)S(6)} %select_n.168), kind=kOutput, calls=%fused_computation.15 | convolution fusion | flops 741081088 | bytes 11927556 | tf_op jit(solution)/shard_map/sexd,edf->sexf/dot_general | solution.py:119
  140.0 2.9 %collective-permute-start.11 = (bf16[16,2,64,176]{3,2,0,1:T(8,128)(2,1)S(1)}, bf16[16,2,64,176]{3,2,0,1:T(8,128)(2,1)S(1)}, u32[]{:S(2)}, u32[]{:S(2)}) collective-permute-start(bf16[16,2,64,176]{3,2,0,1:T(8,128)(2,1)S(1)} %fusion.5), channel_id=1, source_target_pairs={{0,96},{16,112},{32,0},{48,16},{64,32},{80,48},{96,64},{112,80},{1... | collective-permute-start | bytes 2162696 | tf_op jit(solution)/shard_map/ppermute | solution.py:97
  142.9 0.5 fusion.14
  143.4 0.2 collective-permute-start.8
  143.6 1.8 fusion.44
  145.4 20.5 %collective-permute-done.11 = bf16[16,2,64,176]{3,2,0,1:T(8,128)(2,1)S(1)} collective-permute-done((bf16[16,2,64,176]{3,2,0,1:T(8,128)(2,1)S(1)}, bf16[16,2,64,176]{3,2,0,1:T(8,128)(2,1)S(1)}, u32[]{:S(2)}, u32[]{:S(2)}) %collective-permute-start.11) | collective-permute-done | bytes 720928 | tf_op jit(solution)/shard_map/ppermute | solution.py:97
  165.9 3.8 %collective-permute-start.15 = (bf16[8,2,64,176]{3,2,0,1:T(8,128)(2,1)S(1)}, bf16[8,2,64,176]{3,2,0,1:T(8,128)(2,1)}, u32[]{:S(2)}, u32[]{:S(2)}) collective-permute-start(bf16[8,2,64,176]{3,2,0,1:T(8,128)(2,1)S(1)} %slice.45), channel_id=1, source_target_pairs={{0,96},{16,112},{32,0},{48,16},{64,32},{80,48},{96,64},{112,80},{1... | collective-permute-start | bytes 1081352 | tf_op jit(solution)/shard_map/ppermute | solution.py:97
  169.7 1.9 slice.44
  171.6 0.5 collective-permute-start.10
  172.1 3.1 %fusion.40 = f32[2,256,16,64]{1,3,2,0:T(8,128)} fusion(bf16[16,2,64,176]{3,2,0,1:T(8,128)(2,1)} %collective-permute-done.9, bf16[2,176,256]{2,1,0:T(8,128)(2,1)} %collective-permute-done.1), kind=kOutput, calls=%fused_computation.60 | convolution fusion | flops 184549376 | bytes 2998272 | tf_op jit(solution)/shard_map/sexf,efd->sexd/dot_general | solution.py:139
  175.2 1.8 fusion.36
  176.9 2.7 %fusion.42 = f32[2,256,16,64]{1,3,2,0:T(8,128)} fusion(bf16[16,2,64,176]{3,2,0,1:T(8,128)(2,1)S(1)} %collective-permute-done.8, bf16[2,176,256]{2,1,0:T(8,128)(2,1)S(1)} %copy-done.11, bf16[2,176,256]{2,1,0:T(8,128)(2,1)} %collective-permute-done.6, pred[]{:T(512)S(6)} %eq.72), kind=kOutput, calls=%fused_computation.62 | convolution fusion | flops 184639488 | bytes 3178497 | tf_op jit(solution)/shard_map/sexf,efd->sexd/dot_general | solution.py:139
  179.7 1.1 collective-permute-done.15
  180.7 4.0 %fusion.2 = f32[256,704]{0,1:T(8,128)} fusion(bf16[3,2048,704]{1,2,0:T(8,128)(2,1)} %all-gather.5.cloned.1.call-done, bf16[512,2048]{1,0:T(8,128)(2,1)} %all-gather.3.cloned.1.call-done), kind=kOutput, calls=%fused_computation.9 | convolution fusion | flops 738197504 | bytes 4653056 | tf_op jit(solution)/shard_map/dot_general | solution.py:160
  184.7 4.0 %fusion.3 = f32[256,704]{0,1:T(8,128)} fusion(bf16[3,2048,704]{1,2,0:T(8,128)(2,1)} %all-gather.5.cloned.1.call-done, bf16[512,2048]{1,0:T(8,128)(2,1)} %all-gather.3.cloned.1.call-done), kind=kOutput, calls=%fused_computation.11 | convolution fusion | flops 738197504 | bytes 4653056 | tf_op jit(solution)/shard_map/dot_general | solution.py:159
  188.7 5.1 %fusion.4 = f32[256,2048]{1,0:T(8,128)} fusion(bf16[3,2048,704]{1,2,0:T(8,128)(2,1)} %all-gather.5.cloned.1.call-done, f32[256,704]{0,1:T(8,128)} %fusion.2, bf16[256,256]{1,0:T(8,128)(2,1)S(1)} %fusion.14, bf16[256,704]{1,0:T(8,128)(2,1)} %bitcast_select_fusion, f32[256]{0:T(256)S(1)} %add_divide_fusion, f32[256,704]{0,1:T(8,128)} %fusion.3), kind=kOutput, calls=%fused_computation.12 | convolution fusion | flops 832438272 | bytes 6947840 | tf_op jit(solution)/shard_map/dot_general | solution.py:164
  193.8 1.4 fusion.48
  195.2 0.6 collective-permute-start.14
  195.8 1.4 fusion.50
  197.2 0.3 fusion.9
  197.6 0.3 fusion.10
  197.9 2.0 fusion.38
  200.0 0.5 copy-done.6
  200.5 0.7 copy-done.4
  201.2 1.0 maximum_add_fusion
  202.2 1.5 copy.53
  203.6 4.6 %all-to-all-start.1 = ((f32[16,2,64,256]{3,2,1,0:T(8,128)}), f32[16,2,64,256]{3,2,1,0:T(8,128)}, u32[]{:S(2)}, u32[]{:S(2)}) async-start(f32[16,2,64,256]{3,2,1,0:T(8,128)} %copy.53), calls=%async_computation.1 | async-start | bytes 4194304 | tf_op jit(solution)/shard_map/all_to_all | solution.py:154
  208.7 1.6 fusion.71
  210.6 28.9 %all-to-all-done.1 = f32[16,2,64,256]{3,2,1,0:T(8,128)} async-done(((f32[16,2,64,256]{3,2,1,0:T(8,128)}), f32[16,2,64,256]{3,2,1,0:T(8,128)}, u32[]{:S(2)}, u32[]{:S(2)}) %all-to-all-start.1) | async-done | bytes 2097184 | tf_op jit(solution)/shard_map/all_to_all | solution.py:154
  239.5 5.2 %gather_fusion.1 = f32[1024,256]{1,0:T(8,128)S(1)} fusion(f32[2048,256]{1,0:T(8,128)} %bitcast.35, s32[1024]{0:T(1024)S(1)} %broadcast_clamp_fusion), kind=kCustom, calls=%fused_computation.1 | custom fusion | bytes 2101248 | tf_op jit(solution)/shard_map/jit(_take)/gather | solution.py:156
  244.7 1.3 reshape.112
  245.9 2.5 multiply_reduce_fusion
  248.5 1.7 add.222
  (100 shorter events, 1.9 us)
Async XLA Ops:
  6.5 117.0 %copy-start = (bf16[64,16,704]{2,1,0:T(8,128)(2,1)S(1)}, bf16[64,16,704]{2,1,0:T(8,128)(2,1)}, u32[]{:S(2)}) copy-start(bf16[64,16,704]{2,1,0:T(8,128)(2,1)} %param.25) | copy-start | bytes 4325380
  6.5 7.3 %copy-start.9 = (bf16[2,176,2048]{2,1,0:T(8,128)(2,1)S(1)}, bf16[2,176,2048]{2,1,0:T(8,128)(2,1)}, u32[]{:S(2)}) copy-start(bf16[2,176,2048]{2,1,0:T(8,128)(2,1)} %param.23) | copy-start | bytes 4325380
  6.5 40.8 %all-gather.3.cloned.1.call-start = ((), (), s32[]{:S(2)}) async-start(), calls=%async_computation.3 | async-start | bytes 2359296 | tf_op jit(solution)/shard_map/all_gather | solution.py:34
  11.6 169.1 %all-gather.5.cloned.1.call-start = ((), (), s32[]{:S(2)}) async-start(), calls=%async_computation.4 | async-start | bytes 9191424 | tf_op jit(solution)/shard_map/all_gather | solution.py:53
  13.6 8.5 %copy-start.17 = (s32[256,4]{0,1:T(4,128)S(1)}, s32[256,4]{0,1:T(4,128)}, u32[]{:S(2)}) copy-start(s32[256,4]{0,1:T(4,128)} %param.26) | copy-start | bytes 12292
  13.7 234.8 %reduce-scatter.2.cloned.1.call-start = ((), (), s32[]{:S(2)}) async-start(), calls=%async_computation.5 | async-start | bytes 2359296 | tf_op jit(solution)/shard_map/reduce_scatter | solution.py:171
  15.1 32.3 %collective-permute-start.6 = (bf16[2,176,256]{2,1,0:T(8,128)(2,1)}, bf16[2,176,256]{2,1,0:T(8,128)(2,1)}, u32[]{:S(2)}, u32[]{:S(2)}) collective-permute-start(bf16[2,176,256]{2,1,0:T(8,128)(2,1)} %get-tuple-element.25), channel_id=1, source_target_pairs={{0,112},{16,0},{32,16},{48,32},{64,48},{80,64},{96,80},{112,96},{1... | collective-permute-start | bytes 540680 | tf_op jit(solution)/shard_map/ppermute | solution.py:97
  18.7 29.9 %collective-permute-start.4 = (bf16[2,176,256]{2,1,0:T(8,128)(2,1)}, bf16[2,176,256]{2,1,0:T(8,128)(2,1)S(1)}, u32[]{:S(2)}, u32[]{:S(2)}) collective-permute-start(bf16[2,176,256]{2,1,0:T(8,128)(2,1)} %get-tuple-element.26), channel_id=1, source_target_pairs={{0,80},{16,96},{32,112},{48,0},{64,16},{80,32},{96,48},{112,64},{1... | collective-permute-start | bytes 540680 | tf_op jit(solution)/shard_map/ppermute | solution.py:97
  19.2 31.9 %collective-permute-start.3 = (bf16[2,176,256]{2,1,0:T(8,128)(2,1)}, bf16[2,176,256]{2,1,0:T(8,128)(2,1)}, u32[]{:S(2)}, u32[]{:S(2)}) collective-permute-start(bf16[2,176,256]{2,1,0:T(8,128)(2,1)} %get-tuple-element.27), channel_id=1, source_target_pairs={{0,64},{16,80},{32,96},{48,112},{64,0},{80,16},{96,32},{112,48},{1... | collective-permute-start | bytes 540680 | tf_op jit(solution)/shard_map/ppermute | solution.py:97
  19.2 31.9 %collective-permute-start.2 = (bf16[2,176,256]{2,1,0:T(8,128)(2,1)}, bf16[2,176,256]{2,1,0:T(8,128)(2,1)S(1)}, u32[]{:S(2)}, u32[]{:S(2)}) collective-permute-start(bf16[2,176,256]{2,1,0:T(8,128)(2,1)} %get-tuple-element.28), channel_id=1, source_target_pairs={{0,48},{16,64},{32,80},{48,96},{64,112},{80,0},{96,16},{112,32},{1... | collective-permute-start | bytes 540680 | tf_op jit(solution)/shard_map/ppermute | solution.py:97
  20.4 30.7 %collective-permute-start.1 = (bf16[2,176,256]{2,1,0:T(8,128)(2,1)}, bf16[2,176,256]{2,1,0:T(8,128)(2,1)}, u32[]{:S(2)}, u32[]{:S(2)}) collective-permute-start(bf16[2,176,256]{2,1,0:T(8,128)(2,1)} %get-tuple-element.29), channel_id=1, source_target_pairs={{0,32},{16,48},{32,64},{48,80},{64,96},{80,112},{96,0},{112,16},{1... | collective-permute-start | bytes 540680 | tf_op jit(solution)/shard_map/ppermute | solution.py:97
  47.3 0.9 copy-start.16
  47.3 1.2 copy-start.15
  47.3 2.5 slice-start
  48.3 6.1 %collective-permute-start = (bf16[2,176,256]{2,1,0:T(8,128)(2,1)S(1)}, bf16[2,176,256]{2,1,0:T(8,128)(2,1)S(1)}, u32[]{:S(2)}, u32[]{:S(2)}) collective-permute-start(bf16[2,176,256]{2,1,0:T(8,128)(2,1)S(1)} %copy-done.16), channel_id=1, source_target_pairs={{0,16},{16,32},{32,48},{48,64},{64,80},{80,96},{96,112},{112,0},{1... | collective-permute-start | bytes 540680 | tf_op jit(solution)/shard_map/ppermute | solution.py:97
  48.5 7.2 %collective-permute-start.5 = (bf16[2,176,256]{2,1,0:T(8,128)(2,1)S(1)}, bf16[2,176,256]{2,1,0:T(8,128)(2,1)S(1)}, u32[]{:S(2)}, u32[]{:S(2)}) collective-permute-start(bf16[2,176,256]{2,1,0:T(8,128)(2,1)S(1)} %copy-done.15), channel_id=1, source_target_pairs={{0,96},{16,112},{32,0},{48,16},{64,32},{80,48},{96,64},{112,80},{1... | collective-permute-start | bytes 540680 | tf_op jit(solution)/shard_map/ppermute | solution.py:97
  54.4 1.3 copy-start.10
  55.7 0.7 copy-start.13
  120.0 3.2 %copy-start.2 = (bf16[16,2,64,1024]{3,2,1,0:T(8,128)(2,1)}, bf16[16,2,64,1024]{3,2,1,0:T(8,128)(2,1)S(1)}, u32[]{:S(2)}) copy-start(bf16[16,2,64,1024]{3,2,1,0:T(8,128)(2,1)S(1)} %all_to_all.10) | copy-start | bytes 12582916
  120.0 3.2 %copy-start.18 = (bf16[2048]{0:T(1024)(128)(2,1)S(1)}, bf16[2048]{0:T(1024)(128)(2,1)}, u32[]{:S(2)}) copy-start(bf16[2048]{0:T(1024)(128)(2,1)} %param.17) | copy-start | bytes 12292
  120.0 3.2 %copy-start.19 = (s32[1,16]{1,0:T(1,128)S(1)}, s32[1,16]{1,0:T(1,128)}, u32[]{:S(2)}) copy-start(s32[1,16]{1,0:T(1,128)} %param.27) | copy-start | bytes 196
  120.1 4.2 %copy-start.20 = (s32[1,16]{1,0:T(1,128)S(1)}, s32[1,16]{1,0:T(1,128)}, u32[]{:S(2)}) copy-start(s32[1,16]{1,0:T(1,128)} %param.28) | copy-start | bytes 196
  123.3 9.2 %collective-permute-start.7 = (bf16[16,2,64,1024]{3,2,0,1:T(8,128)(2,1)}, bf16[16,2,64,1024]{3,2,0,1:T(8,128)(2,1)}, u32[]{:S(2)}, u32[]{:S(2)}) collective-permute-start(bf16[16,2,64,1024]{3,2,0,1:T(8,128)(2,1)} %copy.50), channel_id=1, source_target_pairs={{0,16},{16,0},{32,48},{48,32},{64,80},{80,64},{96,112},{112,96},{1... | collective-permute-start | bytes 12582920 | tf_op jit(solution)/shard_map/ppermute | solution.py:111
  126.8 4.1 %copy-start.3 = (bf16[16,2,64,1024]{3,2,1,0:T(8,128)(2,1)S(1)}, bf16[16,2,64,1024]{3,2,1,0:T(8,128)(2,1)}, u32[]{:S(2)}) copy-start(bf16[16,2,64,1024]{3,2,1,0:T(8,128)(2,1)} %copy-done.2) | copy-start | bytes 12582916
  126.8 4.4 %copy-start.22 = (bf16[2,2048,176]{1,2,0:T(8,128)(2,1)S(1)}, bf16[2,2048,176]{1,2,0:T(8,128)(2,1)}, u32[]{:S(2)}) copy-start(bf16[2,2048,176]{1,2,0:T(8,128)(2,1)} %param.22) | copy-start | bytes 4325380
  131.2 1.4 copy-start.21
  136.0 6.8 %copy-start.8 = (bf16[512,2048]{1,0:T(8,128)(2,1)S(1)}, bf16[512,2048]{1,0:T(8,128)(2,1)}, u32[]{:S(2)}) copy-start(bf16[512,2048]{1,0:T(8,128)(2,1)} %all-gather.3.cloned.1.call-done) | copy-start | bytes 6291460
  140.0 3.6 %copy-start.12 = (bf16[2,176,256]{2,1,0:T(8,128)(2,1)S(1)}, bf16[2,176,256]{2,1,0:T(8,128)(2,1)}, u32[]{:S(2)}) copy-start(bf16[2,176,256]{2,1,0:T(8,128)(2,1)} %get-tuple-element.14) | copy-start | bytes 540676
  140.0 25.9 %collective-permute-start.11 = (bf16[16,2,64,176]{3,2,0,1:T(8,128)(2,1)S(1)}, bf16[16,2,64,176]{3,2,0,1:T(8,128)(2,1)S(1)}, u32[]{:S(2)}, u32[]{:S(2)}) collective-permute-start(bf16[16,2,64,176]{3,2,0,1:T(8,128)(2,1)S(1)} %fusion.5), channel_id=1, source_target_pairs={{0,96},{16,112},{32,0},{48,16},{64,32},{80,48},{96,64},{112,80},{1... | collective-permute-start | bytes 2162696 | tf_op jit(solution)/shard_map/ppermute | solution.py:97
  142.9 26.8 %collective-permute-start.9 = (bf16[16,2,64,176]{3,2,0,1:T(8,128)(2,1)S(1)}, bf16[16,2,64,176]{3,2,0,1:T(8,128)(2,1)}, u32[]{:S(2)}, u32[]{:S(2)}) collective-permute-start(bf16[16,2,64,176]{3,2,0,1:T(8,128)(2,1)S(1)} %fusion.5), channel_id=1, source_target_pairs={{0,32},{16,48},{32,64},{48,80},{64,96},{80,112},{96,0},{112,16},{1... | collective-permute-start | bytes 2162696 | tf_op jit(solution)/shard_map/ppermute | solution.py:97
  143.4 33.6 %collective-permute-start.8 = (bf16[16,2,64,176]{3,2,0,1:T(8,128)(2,1)S(1)}, bf16[16,2,64,176]{3,2,0,1:T(8,128)(2,1)S(1)}, u32[]{:S(2)}, u32[]{:S(2)}) collective-permute-start(bf16[16,2,64,176]{3,2,0,1:T(8,128)(2,1)S(1)} %fusion.5), channel_id=1, source_target_pairs={{0,16},{16,0},{32,48},{48,32},{64,80},{80,64},{96,112},{112,96},{1... | collective-permute-start | bytes 2162696 | tf_op jit(solution)/shard_map/ppermute | solution.py:100
  165.9 9.3 %copy-start.14 = (bf16[2,176,256]{2,1,0:T(8,128)(2,1)S(1)}, bf16[2,176,256]{2,1,0:T(8,128)(2,1)}, u32[]{:S(2)}) copy-start(bf16[2,176,256]{2,1,0:T(8,128)(2,1)} %copy-done.13) | copy-start | bytes 540676
  165.9 14.8 %collective-permute-start.15 = (bf16[8,2,64,176]{3,2,0,1:T(8,128)(2,1)S(1)}, bf16[8,2,64,176]{3,2,0,1:T(8,128)(2,1)}, u32[]{:S(2)}, u32[]{:S(2)}) collective-permute-start(bf16[8,2,64,176]{3,2,0,1:T(8,128)(2,1)S(1)} %slice.45), channel_id=1, source_target_pairs={{0,96},{16,112},{32,0},{48,16},{64,32},{80,48},{96,64},{112,80},{1... | collective-permute-start | bytes 1081352 | tf_op jit(solution)/shard_map/ppermute | solution.py:97
  171.6 23.6 %collective-permute-start.13 = (bf16[8,2,64,176]{3,2,0,1:T(8,128)(2,1)}, bf16[8,2,64,176]{3,2,0,1:T(8,128)(2,1)}, u32[]{:S(2)}, u32[]{:S(2)}) collective-permute-start(bf16[8,2,64,176]{3,2,0,1:T(8,128)(2,1)} %slice.44), channel_id=1, source_target_pairs={{0,32},{16,48},{32,64},{48,80},{64,96},{80,112},{96,0},{112,16},{1... | collective-permute-start | bytes 1081352 | tf_op jit(solution)/shard_map/ppermute | solution.py:97
  171.6 28.4 %collective-permute-start.12 = (bf16[16,2,64,176]{3,2,0,1:T(8,128)(2,1)S(1)}, bf16[16,2,64,176]{3,2,0,1:T(8,128)(2,1)S(1)}, u32[]{:S(2)}, u32[]{:S(2)}) collective-permute-start(bf16[16,2,64,176]{3,2,0,1:T(8,128)(2,1)S(1)} %collective-permute-done.11), channel_id=1, source_target_pairs={{0,16},{16,0},{32,48},{48,32},{64,80},{80,64},{96,112},{112,96},{1... | collective-permute-start | bytes 2162696 | tf_op jit(solution)/shard_map/ppermute | solution.py:100
  171.6 26.3 %collective-permute-start.10 = (bf16[16,2,64,176]{3,2,0,1:T(8,128)(2,1)}, bf16[16,2,64,176]{3,2,0,1:T(8,128)(2,1)}, u32[]{:S(2)}, u32[]{:S(2)}) collective-permute-start(bf16[16,2,64,176]{3,2,0,1:T(8,128)(2,1)} %collective-permute-done.9), channel_id=1, source_target_pairs={{0,16},{16,0},{32,48},{48,32},{64,80},{80,64},{96,112},{112,96},{1... | collective-permute-start | bytes 2162696 | tf_op jit(solution)/shard_map/ppermute | solution.py:100
  175.2 1.8 copy-start.11
  180.7 16.5 %collective-permute-start.16 = (bf16[8,2,64,176]{3,2,0,1:T(8,128)(2,1)}, bf16[8,2,64,176]{3,2,0,1:T(8,128)(2,1)S(1)}, u32[]{:S(2)}, u32[]{:S(2)}) collective-permute-start(bf16[8,2,64,176]{3,2,0,1:T(8,128)(2,1)} %collective-permute-done.15), channel_id=1, source_target_pairs={{0,16},{16,0},{32,48},{48,32},{64,80},{80,64},{96,112},{112,96},{1... | collective-permute-start | bytes 1081352 | tf_op jit(solution)/shard_map/ppermute | solution.py:100
  195.2 2.4 collective-permute-start.14
  197.2 2.7 %copy-start.7 = (f32[2,256,16,64]{1,3,2,0:T(8,128)S(1)}, f32[2,256,16,64]{1,3,2,0:T(8,128)}, u32[]{:S(2)}) copy-start(f32[2,256,16,64]{1,3,2,0:T(8,128)} %fusion.42) | copy-start | bytes 6291460
  197.6 2.4 copy-start.5
  197.6 2.9 %copy-start.6 = (f32[2,256,16,64]{1,3,2,0:T(8,128)S(1)}, f32[2,256,16,64]{1,3,2,0:T(8,128)}, u32[]{:S(2)}) copy-start(f32[2,256,16,64]{1,3,2,0:T(8,128)} %fusion.36) | copy-start | bytes 6291460
  197.9 3.2 %copy-start.4 = (f32[2,256,16,64]{1,3,2,0:T(8,128)S(1)}, f32[2,256,16,64]{1,3,2,0:T(8,128)}, u32[]{:S(2)}) copy-start(f32[2,256,16,64]{1,3,2,0:T(8,128)} %fusion.44) | copy-start | bytes 6291460
  203.6 5.1 %copy-start.23 = (bf16[2048,32]{0,1:T(8,128)(2,1)S(1)}, bf16[2048,32]{0,1:T(8,128)(2,1)}, u32[]{:S(2)}) copy-start(bf16[2048,32]{0,1:T(8,128)(2,1)} %param.16) | copy-start | bytes 393220
  203.6 35.9 %all-to-all-start.1 = ((f32[16,2,64,256]{3,2,1,0:T(8,128)}), f32[16,2,64,256]{3,2,1,0:T(8,128)}, u32[]{:S(2)}, u32[]{:S(2)}) async-start(f32[16,2,64,256]{3,2,1,0:T(8,128)} %copy.53), calls=%async_computation.1 | async-start | bytes 4194304 | tf_op jit(solution)/shard_map/all_to_all | solution.py:154
  239.5 10.7 %copy-start.1 = (bf16[64,16,704]{2,1,0:T(8,128)(2,1)S(1)}, bf16[64,16,704]{2,1,0:T(8,128)(2,1)}, u32[]{:S(2)}) copy-start(bf16[64,16,704]{2,1,0:T(8,128)(2,1)} %param.25) | copy-start | bytes 4325380
Sparse Core Ops, SparseCore 0:
  11.7 35.5 all-gather.2
  49.4 117.3 all-gather.4
  193.9 33.6 reduce-scatter.1

commit v7 on v4

--- a/solution.py
+++ b/solution.py
@@ -86,36 +86,42 @@
     )
     adapter_update = jnp.dot(low_masked, picked_output_factor, preferred_element_type=jnp.float32)
 
-    half_width = full_width // 2
-    half = row_id % 2
+    def shifted(x, shift):
+        return lax.ppermute(x, "row", [(i, (i + shift) % row_count) for i in range(row_count)])
+
+    def partner(x):
+        return lax.ppermute(x, "row", [(i, i ^ 1) for i in range(row_count)])
+
+    def row_blocks(x):
+        group_half = x.shape[0] // 2
+        from_below = shifted(x, 2)
+        from_above = shifted(x, -2)
+        far = jnp.concatenate(
+            [shifted(from_below[:group_half], 2), shifted(from_above[group_half:], -2)], axis=0
+        )
+        same = [x, from_below, from_above, far]
+        source = jnp.stack(
+            [row_id, (row_id - 2) % row_count, (row_id + 2) % row_count, (row_id + 4) % row_count]
+        ).astype(jnp.int32)
+        return same + [partner(block) for block in same], jnp.concatenate([source, source ^ 1])
+
     slot_count = expert_count * capacity
     slot_id = jnp.arange(slot_count, dtype=jnp.int32)
     selection = jnp.any(row_index[None, :, :] == slot_id[:, None, None], axis=2).astype(jnp.bfloat16)
-    own_features = lax.dynamic_slice_in_dim(all_features, half * half_width, half_width, axis=1)
-    chosen = jnp.dot(selection, own_features, preferred_element_type=jnp.float32).astype(jnp.bfloat16)
-    outgoing = chosen.reshape(col_count, local_experts, capacity, half_width)
-    own_half = lax.all_to_all(outgoing, "col", split_axis=0, concat_axis=0, tiled=True)
-    other_half = lax.ppermute(own_half, "row", [(i, i ^ 1) for i in range(row_count)])
-
-    def half_weights(w, which):
-        return lax.dynamic_slice_in_dim(w, which * half_width, half_width, axis=1)
+    chosen = jnp.dot(selection, tokens, preferred_element_type=jnp.float32).astype(jnp.bfloat16)
+    outgoing = chosen.reshape(col_count, local_experts, capacity, local_width)
+    own_block = lax.all_to_all(outgoing, "col", split_axis=0, concat_axis=0, tiled=True)
+    slot_blocks, slot_source = row_blocks(own_block)
+    slot_features = jnp.concatenate(slot_blocks, axis=3)
 
     def project(w):
-        return jnp.einsum(
-            "sexd,edf->sexf", own_half, half_weights(w, half), preferred_element_type=jnp.float32
-        ) + jnp.einsum(
-            "sexd,edf->sexf", other_half, half_weights(w, 1 - half), preferred_element_type=jnp.float32
-        )
+        blocks = w.reshape(w.shape[0], row_count, local_width, w.shape[2])
+        ordered = jnp.take(blocks, slot_source, axis=1).reshape(w.shape)
+        return jnp.einsum("sexd,edf->sexf", slot_features, ordered, preferred_element_type=jnp.float32)
 
     gate_part = project(routed_gate_weight)
     up_part = project(routed_up_weight)
     hidden = (jax.nn.silu(gate_part) * up_part).astype(jnp.bfloat16)
-    def shifted(x, shift):
-        return lax.ppermute(x, "row", [(i, (i + shift) % row_count) for i in range(row_count)])
-
-    def partner(x):
-        return lax.ppermute(x, "row", [(i, i ^ 1) for i in range(row_count)])
-
     local_hidden = hidden.shape[3]
     group_half = hidden.shape[0] // 2
     from_below = shifted(hidden, 2)

time: 253 us -> 244 us (0.964)
  blocking collectives: 66.5 us -> 23.8 us
  local copies, waits for them, and re-layouts: 19.7 us -> 49.1 us
  waiting for transfers between devices: 74.1 us -> 65.8 us
  starting transfers between devices: 20.5 us -> 26.9 us
  other arithmetic: 14.1 us -> 18.8 us
    all_to_all x1, blocking collectives: 66.5 us -> 23.8 us  [on_device(): lax.all_to_all(outgoing, 'col', split_axis=0, concat_axis=0, tiled=True)]
    all_gather x1, waiting for transfers between devices: 23.9 us -> 0.01 us  [on_device(): lax.all_gather(jnp.concatenate([tokens, picked_input_factor.reshape(reduc...]
    ppermute x11 -> x15, waiting for transfers between devices: 19.4 us -> 37.2 us  [shifted(): lax.ppermute(x, 'row', [(i, (i + shift) % row_count) for i in range(row_c...]
    unnamed x41 -> x54, local copies, waits for them, and re-layouts: 2.88 us -> 15.5 us
    reshape x0 -> x4, local copies, waits for them, and re-layouts: none -> 6.38 us  [the longest x2 4.1 us: project(): blocks = w.reshape(w.shape[0], row_count, local_width, w.shape[2])]
    ppermute x5 -> x9, starting transfers between devices: 0.99 us -> 4.81 us  [partner(): return lax.ppermute(x, 'row', [(i, i ^ 1) for i in range(row_count)])]
    gather x0 -> x2, local copies, waits for them, and re-layouts: none -> 3.73 us  [project(): ordered = jnp.take(blocks, slot_source, axis=1).reshape(w.shape)]
    dot_general x5 -> x3, matrix products: 13.8 us -> 10.1 us  [the longest x2 9.66 us: project(): jnp.einsum('sexd,edf->sexf', slot_features, ordered, preferred_element_ty...]
  transfers between devices with their start and end apart: 21 -> 28, of which waited for: 8 -> 8; matrix products, arithmetic and copies ran while one was open for 26% -> 43% of each run, Pallas kernels for 0% -> 0%
where the time goes in v7:
time: 244 us; the launch traced here: 243 us
  waiting for transfers between devices  65.8 us (27%)
  local copies, waits for them, and re-layouts  49.1 us (20%)
  matrix products  44.7 us (18%)
  starting transfers between devices  26.9 us (11%)
  blocking collectives  23.8 us (10%)
  other arithmetic  18.8 us (8%)
  between operations  13.6 us (6%)
    ppermute x15, waiting for transfers between devices, shifted(): lax.ppermute(x, 'row', [(i, (i + shift) % row_count) for i in range(row_c...  37.2 us
    all_to_all x1, waiting for transfers between devices, on_device(): lax.all_to_all(expert_value, 'col', split_axis=0, concat_axis=0, tiled=True)  28.5 us
    all_to_all x1, blocking collectives, on_device(): lax.all_to_all(outgoing, 'col', split_axis=0, concat_axis=0, tiled=True)  23.8 us
    ppermute x15, starting transfers between devices, shifted(): lax.ppermute(x, 'row', [(i, (i + shift) % row_count) for i in range(row_c...  17.4 us
    dot_general x10, matrix products, down_of(): jnp.einsum('sexf,efd->sexd', block, weight, preferred_element_type=jnp.fl...  15.8 us
    unnamed x54, local copies, waits for them, and re-layouts  15.5 us
    dot_general x2, matrix products, project(): jnp.einsum('sexd,edf->sexf', slot_features, ordered, preferred_element_ty...  9.66 us
    gather x2, local copies, waits for them, and re-layouts, on_device(): routed_rows = jnp.take(flat_rows, row_index, axis=0)  6.47 us
  transfers between devices with their start and end apart: 28, of which 8 were waited for; matrix products, arithmetic and copies ran while one was open for 43% of the time, Pallas kernels for 0%

profile of v7, /device:TPU:0, one launch (start us, length us, event | category | flops | bytes accessed | tf_op | source)
XLA Modules:
  0.0 242.7 jit_solution(5092560558791561620)
XLA Ops:
  8.2 1.6 gather_fusion
  9.9 1.6 pad_maximum_fusion.2
  11.6 2.0 pad_maximum_fusion.1
  15.2 2.6 %fusion = pred[2048,256]{1,0:T(8,128)(4,1)S(1)} fusion(s32[256,4]{0,1:T(4,128)S(1)} %get-tuple-element.7), kind=kLoop, calls=%fused_computation.6 | loop fusion | flops 3670016 | bytes 528384 | tf_op jit(solution)/shard_map/reduce_or | solution.py:110
  18.3 23.8 %all_to_all.10 = bf16[16,2,64,256]{3,2,1,0:T(8,128)(2,1)S(1)} all-to-all(bf16[16,2,64,256]{3,2,1,0:T(8,128)(2,1)S(1)} %bitcast.161), channel_id=1, replica_groups=mesh['row'=8,'col'=16] {'col'}, dimensions={0} | all-to-all | bytes 2097152 | tf_op jit(solution)/shard_map/all_to_all | solution.py:113
  42.1 1.7 fusion.61
  43.8 1.9 collective-permute-start
  45.7 2.1 collective-permute-start.1
  47.8 1.1 constant_dynamic-slice_fusion.5
  48.9 1.9 collective-permute-start.19
  50.8 1.5 copy.101
  52.4 2.6 %copy.102 = bf16[2,22,8,8,256]{4,3,1,2,0:T(8,128)(2,1)} copy(bf16[2,22,8,8,256]{4,3,2,1,0:T(8,128)(2,1)} %bitcast.160) | data formatting | bytes 2883584 | tf_op jit(solution)/shard_map/reshape | solution.py:118
  55.1 1.7 gather_fusion.4
  56.8 2.0 gather_fusion.3
  58.8 12.4 %collective-permute-done = bf16[16,2,64,256]{3,2,0,1:T(8,128)(2,1)} collective-permute-done((bf16[16,2,64,256]{3,2,0,1:T(8,128)(2,1)}, bf16[16,2,64,256]{3,2,0,1:T(8,128)(2,1)}, u32[]{:S(2)}, u32[]{:S(2)}) %collective-permute-start) | collective-permute-done | bytes 1048608 | tf_op jit(solution)/shard_map/ppermute | solution.py:90
  71.2 1.9 slice.56
  73.1 2.0 collective-permute-start.2
  75.1 1.9 slice.57
  77.0 1.8 collective-permute-start.3
  78.8 1.9 select_bitcast_fusion
  80.7 1.4 gather_fusion.2
  82.1 1.9 bitcast_select_fusion
  86.4 1.6 reshape.174
  89.7 1.1 pad_maximum_fusion
  91.4 2.4 constant_dynamic-update-slice_fusion.7
  93.8 2.3 constant_dynamic-update-slice_fusion.6
  96.1 0.9 constant_dynamic-update-slice_fusion.5
  97.1 2.0 constant_dynamic-update-slice_fusion.4
  99.0 1.4 collective-permute-start.15
  100.4 2.3 constant_dynamic-update-slice_fusion.3
  102.8 2.4 constant_dynamic-update-slice_fusion.2
  105.2 1.2 constant_dynamic-update-slice_fusion.1
  106.3 1.1 constant_dynamic-update-slice_fusion
  107.4 6.0 %fusion.10 = f32[2,176,16,64]{1,3,2,0:T(8,128)S(1)} fusion(bf16[16,2,64,2048]{3,2,0,1:T(8,128)(2,1)} %constant_dynamic-update-slice_fusion, bf16[2,2048,176,1]{1,2,0,3:T(8,128)(2,1)S(1)} %copy-done.10), kind=kOutput, calls=%fused_computation.26 | convolution fusion | flops 1476395008 | bytes 11272192 | tf_op jit(solution)/shard_map/sexd,edf->sexf/dot_general | solution.py:120
  113.7 3.6 %fusion.5 = bf16[16,2,64,176]{3,2,0,1:T(8,128)(2,1)} fusion(f32[2,176,16,64]{1,3,2,0:T(8,128)S(1)} %fusion.10, bf16[16,2,64,2048]{3,2,0,1:T(8,128)(2,1)S(1)} %copy-done.14, bf16[2,2048,176,1]{1,2,0,3:T(8,128)(2,1)S(1)} %reshape.175), kind=kOutput, calls=%fused_computation.17 | convolution fusion | flops 1478557696 | bytes 11993088 | tf_op jit(solution)/shard_map/sexd,edf->sexf/dot_general | solution.py:120
  117.3 2.0 collective-permute-start.16
  119.4 3.1 %fusion.42 = f32[2,256,16,64]{1,3,2,0:T(8,128)} fusion(bf16[16,2,64,176]{3,2,0,1:T(8,128)(2,1)} %fusion.5, bf16[2,176,2048]{2,1,0:T(8,128)(2,1)} %param.25, s32[]{:T(128)S(6)} %select_n.155), kind=kOutput, calls=%fused_computation.69 | convolution fusion | flops 184549376 | bytes 3325956 | tf_op jit(solution)/shard_map/sexf,efd->sexd/dot_general | solution.py:144
  122.5 1.6 fusion.24
  124.1 2.7 %fusion.17 = bf16[256,256]{1,0:T(8,128)(2,1)} fusion(bf16[512,2048]{1,0:T(8,128)(2,1)} %all-gather.3.cloned.1.call-done, s32[256]{0:T(256)S(1)} %and_select_fusion, s32[256]{0:T(256)S(1)} %select_reduce_fusion.2), kind=kOutput, calls=%fused_computation.39 | convolution fusion | flops 268632064 | bytes 2230272 | tf_op jit(solution)/shard_map/dot_general | solution.py:78
  126.8 15.6 %collective-permute-done.16 = bf16[16,2,64,176]{3,2,0,1:T(8,128)(2,1)S(1)} collective-permute-done((bf16[16,2,64,176]{3,2,0,1:T(8,128)(2,1)}, bf16[16,2,64,176]{3,2,0,1:T(8,128)(2,1)S(1)}, u32[]{:S(2)}, u32[]{:S(2)}) %collective-permute-start.16) | collective-permute-done | bytes 720928 | tf_op jit(solution)/shard_map/ppermute | solution.py:90
  143.8 1.5 collective-permute-done.12
  147.5 1.8 fusion.34
  149.3 4.3 %collective-permute-done.11 = bf16[2,176,256]{2,1,0:T(8,128)(2,1)S(1)} collective-permute-done((bf16[2,176,256]{2,1,0:T(8,128)(2,1)S(1)}, bf16[2,176,256]{2,1,0:T(8,128)(2,1)S(1)}, u32[]{:S(2)}, u32[]{:S(2)}) %collective-permute-start.11) | collective-permute-done | bytes 180256 | tf_op jit(solution)/shard_map/ppermute | solution.py:90
  153.6 1.7 fusion.38
  156.8 1.8 collective-permute-start.20
  158.9 3.0 %fusion.40 = f32[2,256,16,64]{1,3,2,0:T(8,128)} fusion(bf16[16,2,64,176]{3,2,0,1:T(8,128)(2,1)} %collective-permute-done.10, bf16[2,176,256]{2,1,0:T(8,128)(2,1)S(1)} %collective-permute-done.8, bf16[2,176,256]{2,1,0:T(8,128)(2,1)S(1)} %collective-permute-done.9, pred[]{:T(512)S(6)} %eq.74), kind=kOutput, calls=%fused_computation.67 | convolution fusion | flops 184639488 | bytes 3178497 | tf_op jit(solution)/shard_map/sexf,efd->sexd/dot_general | solution.py:144
  161.9 4.1 %fusion.2 = f32[256,704]{0,1:T(8,128)} fusion(bf16[3,2048,704]{1,2,0:T(8,128)(2,1)} %all-gather.5.cloned.1.call-done, bf16[512,2048]{1,0:T(8,128)(2,1)} %all-gather.3.cloned.1.call-done), kind=kOutput, calls=%fused_computation.10 | convolution fusion | flops 738197504 | bytes 4653056 | tf_op jit(solution)/shard_map/dot_general | solution.py:165
  166.0 3.7 %fusion.3 = f32[256,704]{0,1:T(8,128)} fusion(bf16[3,2048,704]{1,2,0:T(8,128)(2,1)} %all-gather.5.cloned.1.call-done, bf16[512,2048]{1,0:T(8,128)(2,1)S(1)} %copy-done.20), kind=kOutput, calls=%fused_computation.12 | convolution fusion | flops 738197504 | bytes 4653056 | tf_op jit(solution)/shard_map/dot_general | solution.py:164
  169.7 5.0 %fusion.4 = f32[256,2048]{1,0:T(8,128)} fusion(bf16[3,2048,704]{1,2,0:T(8,128)(2,1)} %all-gather.5.cloned.1.call-done, f32[256,704]{0,1:T(8,128)} %fusion.2, bf16[256,256]{1,0:T(8,128)(2,1)S(1)} %copy-done.22, bf16[256,704]{1,0:T(8,128)(2,1)} %bitcast_select_fusion, f32[256]{0:T(256)S(1)} %add_divide_fusion, f32[256,704]{0,1:T(8,128)} %fusion.3), kind=kOutput, calls=%fused_computation.13 | convolution fusion | flops 832438272 | bytes 6947840 | tf_op jit(solution)/shard_map/dot_general | solution.py:169
  175.3 2.3 collective-permute-start.18
  177.6 1.2 fusion.46
  178.9 1.4 fusion.48
  180.3 2.0 collective-permute-done.13
  183.3 1.8 fusion.36
  185.8 1.1 copy-done.4
  187.5 1.0 maximum_add_fusion
  188.5 1.5 copy.78
  190.0 4.6 %all-to-all-start.1 = ((f32[16,2,64,256]{3,2,1,0:T(8,128)}), f32[16,2,64,256]{3,2,1,0:T(8,128)}, u32[]{:S(2)}, u32[]{:S(2)}) async-start(f32[16,2,64,256]{3,2,1,0:T(8,128)} %copy.78), calls=%async_computation.1 | async-start | bytes 4194304 | tf_op jit(solution)/shard_map/all_to_all | solution.py:159
  195.1 1.7 fusion.29
  197.0 28.5 %all-to-all-done.1 = f32[16,2,64,256]{3,2,1,0:T(8,128)} async-done(((f32[16,2,64,256]{3,2,1,0:T(8,128)}), f32[16,2,64,256]{3,2,1,0:T(8,128)}, u32[]{:S(2)}, u32[]{:S(2)}) %all-to-all-start.1) | async-done | bytes 2097184 | tf_op jit(solution)/shard_map/all_to_all | solution.py:159
  225.4 5.2 %gather_fusion.1 = f32[1024,256]{1,0:T(8,128)S(1)} fusion(f32[2048,256]{1,0:T(8,128)} %bitcast.35, s32[1024]{0:T(1024)S(1)} %broadcast_clamp_fusion), kind=kCustom, calls=%fused_computation.3 | custom fusion | bytes 2101248 | tf_op jit(solution)/shard_map/jit(_take)/gather | solution.py:161
  230.6 1.3 reshape.149
  231.9 2.5 %multiply_reduce_fusion = f32[256,256]{1,0:T(8,128)S(1)} fusion(f32[256,4,256]{2,1,0:T(4,128)} %reshape.149, f32[256,4]{1,0:T(8,128)S(1)} %copy.66, pred[256,4]{1,0:T(8,128)(4,1)S(1)} %copy.69), kind=kLoop, calls=%fused_computation.42 | loop fusion | flops 720896 | bytes 1315840 | tf_op jit(solution)/shard_map/reduce_sum | solution.py:162
  234.5 1.7 add.206
  (133 shorter events, 17.7 us)
Async XLA Ops:
  6.5 74.2 %copy-start = (bf16[64,16,704]{2,1,0:T(8,128)(2,1)S(1)}, bf16[64,16,704]{2,1,0:T(8,128)(2,1)}, u32[]{:S(2)}) copy-start(bf16[64,16,704]{2,1,0:T(8,128)(2,1)} %param.27) | copy-start | bytes 4325380
  6.5 11.3 %copy-start.15 = (bf16[256,256]{1,0:T(8,128)(2,1)S(1)}, bf16[256,256]{1,0:T(8,128)(2,1)}, u32[]{:S(2)}) copy-start(bf16[256,256]{1,0:T(8,128)(2,1)} %param.17) | copy-start | bytes 393220
  6.5 7.1 %copy-start.16 = (s32[256,4]{0,1:T(4,128)S(1)}, s32[256,4]{0,1:T(4,128)}, u32[]{:S(2)}) copy-start(s32[256,4]{0,1:T(4,128)} %param.28) | copy-start | bytes 12292
  6.5 116.0 %all-gather.3.cloned.1.call-start = ((), (), s32[]{:S(2)}) async-start(), calls=%async_computation.3 | async-start | bytes 2359296 | tf_op jit(solution)/shard_map/all_gather | solution.py:34
  11.5 150.4 %all-gather.5.cloned.1.call-start = ((), (), s32[]{:S(2)}) async-start(), calls=%async_computation.4 | async-start | bytes 9191424 | tf_op jit(solution)/shard_map/all_gather | solution.py:53
  13.6 220.9 %reduce-scatter.2.cloned.1.call-start = ((), (), s32[]{:S(2)}) async-start(), calls=%async_computation.5 | async-start | bytes 2359296 | tf_op jit(solution)/shard_map/reduce_scatter | solution.py:176
  42.1 5.7 %copy-start.9 = (bf16[2,176,2048]{2,1,0:T(8,128)(2,1)S(1)}, bf16[2,176,2048]{2,1,0:T(8,128)(2,1)}, u32[]{:S(2)}) copy-start(bf16[2,176,2048]{2,1,0:T(8,128)(2,1)} %param.25) | copy-start | bytes 4325380
  43.8 27.5 %collective-permute-start = (bf16[16,2,64,256]{3,2,0,1:T(8,128)(2,1)}, bf16[16,2,64,256]{3,2,0,1:T(8,128)(2,1)}, u32[]{:S(2)}, u32[]{:S(2)}) collective-permute-start(bf16[16,2,64,256]{3,2,0,1:T(8,128)(2,1)} %get-tuple-element.15), channel_id=1, source_target_pairs={{0,32},{16,48},{32,64},{48,80},{64,96},{80,112},{96,0},{112,16},{1... | collective-permute-start | bytes 3145736 | tf_op jit(solution)/shard_map/ppermute | solution.py:90
  45.7 29.4 %collective-permute-start.1 = (bf16[16,2,64,256]{3,2,0,1:T(8,128)(2,1)}, bf16[16,2,64,256]{3,2,0,1:T(8,128)(2,1)}, u32[]{:S(2)}, u32[]{:S(2)}) collective-permute-start(bf16[16,2,64,256]{3,2,0,1:T(8,128)(2,1)} %get-tuple-element.15), channel_id=1, source_target_pairs={{0,96},{16,112},{32,0},{48,16},{64,32},{80,48},{96,64},{112,80},{1... | collective-permute-start | bytes 3145736 | tf_op jit(solution)/shard_map/ppermute | solution.py:90
  48.9 125.9 %collective-permute-start.19 = (bf16[2,176,256]{2,1,0:T(8,128)(2,1)}, bf16[2,176,256]{2,1,0:T(8,128)(2,1)}, u32[]{:S(2)}, u32[]{:S(2)}) collective-permute-start(bf16[2,176,256]{2,1,0:T(8,128)(2,1)} %get-tuple-element.13), channel_id=1, source_target_pairs={{0,64},{16,80},{32,96},{48,112},{64,0},{80,16},{96,32},{112,48},{1... | collective-permute-start | bytes 540680 | tf_op jit(solution)/shard_map/ppermute | solution.py:90
  58.8 20.0 %copy-start.2 = (bf16[8,2,256,176]{2,3,1,0:T(8,128)(2,1)S(1)}, bf16[8,2,256,176]{2,3,1,0:T(8,128)(2,1)}, u32[]{:S(2)}) copy-start(bf16[8,2,256,176]{2,3,1,0:T(8,128)(2,1)} %gather_fusion.4) | copy-start | bytes 4325380
  73.1 16.5 %collective-permute-start.2 = (bf16[8,2,64,256]{3,2,0,1:T(8,128)(2,1)}, bf16[8,2,64,256]{3,2,0,1:T(8,128)(2,1)S(1)}, u32[]{:S(2)}, u32[]{:S(2)}) collective-permute-start(bf16[8,2,64,256]{3,2,0,1:T(8,128)(2,1)} %slice.56), channel_id=1, source_target_pairs={{0,32},{16,48},{32,64},{48,80},{64,96},{80,112},{96,0},{112,16},{1... | collective-permute-start | bytes 1572872 | tf_op jit(solution)/shard_map/ppermute | solution.py:90
  77.0 12.7 %collective-permute-start.3 = (bf16[8,2,64,256]{3,2,0,1:T(8,128)(2,1)}, bf16[8,2,64,256]{3,2,0,1:T(8,128)(2,1)}, u32[]{:S(2)}, u32[]{:S(2)}) collective-permute-start(bf16[8,2,64,256]{3,2,0,1:T(8,128)(2,1)} %slice.57), channel_id=1, source_target_pairs={{0,96},{16,112},{32,0},{48,16},{64,32},{80,48},{96,64},{112,80},{1... | collective-permute-start | bytes 1572872 | tf_op jit(solution)/shard_map/ppermute | solution.py:90
  80.7 4.8 %copy-start.8 = (bf16[2,8,256,176]{2,3,0,1:T(8,128)(2,1)S(1)}, bf16[2,8,256,176]{2,3,0,1:T(8,128)(2,1)}, u32[]{:S(2)}) copy-start(bf16[2,8,256,176]{2,3,0,1:T(8,128)(2,1)} %get-tuple-element.18) | copy-start | bytes 4325380
  82.1 17.0 %collective-permute-start.4 = (bf16[16,2,64,256]{3,2,0,1:T(8,128)(2,1)}, bf16[16,2,64,256]{3,2,0,1:T(8,128)(2,1)}, u32[]{:S(2)}, u32[]{:S(2)}) collective-permute-start(bf16[16,2,64,256]{3,2,0,1:T(8,128)(2,1)} %get-tuple-element.15), channel_id=1, source_target_pairs={{0,16},{16,0},{32,48},{48,32},{64,80},{80,64},{96,112},{112,96},{1... | collective-permute-start | bytes 3145736 | tf_op jit(solution)/shard_map/ppermute | solution.py:93
  84.9 17.9 %collective-permute-start.5 = (bf16[16,2,64,256]{3,2,0,1:T(8,128)(2,1)}, bf16[16,2,64,256]{3,2,0,1:T(8,128)(2,1)}, u32[]{:S(2)}, u32[]{:S(2)}) collective-permute-start(bf16[16,2,64,256]{3,2,0,1:T(8,128)(2,1)} %collective-permute-done), channel_id=1, source_target_pairs={{0,16},{16,0},{32,48},{48,32},{64,80},{80,64},{96,112},{112,96},{1... | collective-permute-start | bytes 3145736 | tf_op jit(solution)/shard_map/ppermute | solution.py:93
  86.3 1.6 copy-start.7
  88.7 0.7 copy-start.17
  88.8 0.8 copy-start.19
  89.6 15.5 %collective-permute-start.6 = (bf16[16,2,64,256]{3,2,0,1:T(8,128)(2,1)}, bf16[16,2,64,256]{3,2,0,1:T(8,128)(2,1)S(1)}, u32[]{:S(2)}, u32[]{:S(2)}) collective-permute-start(bf16[16,2,64,256]{3,2,0,1:T(8,128)(2,1)} %collective-permute-done.1), channel_id=1, source_target_pairs={{0,16},{16,0},{32,48},{48,32},{64,80},{80,64},{96,112},{112,96},{1... | collective-permute-start | bytes 3145736 | tf_op jit(solution)/shard_map/ppermute | solution.py:93
  90.9 15.5 %collective-permute-start.7 = (bf16[16,2,64,256]{3,2,0,1:T(8,128)(2,1)S(1)}, bf16[16,2,64,256]{3,2,0,1:T(8,128)(2,1)S(1)}, u32[]{:S(2)}, u32[]{:S(2)}) collective-permute-start(bf16[16,2,64,256]{3,2,0,1:T(8,128)(2,1)S(1)} %pad_maximum_fusion), channel_id=1, source_target_pairs={{0,16},{16,0},{32,48},{48,32},{64,80},{80,64},{96,112},{112,96},{1... | collective-permute-start | bytes 3145736 | tf_op jit(solution)/shard_map/ppermute | solution.py:93
  99.0 47.8 %collective-permute-start.15 = (bf16[2,176,256]{2,1,0:T(8,128)(2,1)}, bf16[2,176,256]{2,1,0:T(8,128)(2,1)S(1)}, u32[]{:S(2)}, u32[]{:S(2)}) collective-permute-start(bf16[2,176,256]{2,1,0:T(8,128)(2,1)} %get-tuple-element.9), channel_id=1, source_target_pairs={{0,96},{16,112},{32,0},{48,16},{64,32},{80,48},{96,64},{112,80},{1... | collective-permute-start | bytes 540680 | tf_op jit(solution)/shard_map/ppermute | solution.py:90
  105.2 2.3 copy-start.10
  107.4 6.2 %copy-start.14 = (bf16[16,2,64,2048]{3,2,0,1:T(8,128)(2,1)S(1)}, bf16[16,2,64,2048]{3,2,0,1:T(8,128)(2,1)}, u32[]{:S(2)}) copy-start(bf16[16,2,64,2048]{3,2,0,1:T(8,128)(2,1)} %constant_dynamic-update-slice_fusion) | copy-start | bytes 25165828
  117.3 25.1 %collective-permute-start.16 = (bf16[16,2,64,176]{3,2,0,1:T(8,128)(2,1)}, bf16[16,2,64,176]{3,2,0,1:T(8,128)(2,1)S(1)}, u32[]{:S(2)}, u32[]{:S(2)}) collective-permute-start(bf16[16,2,64,176]{3,2,0,1:T(8,128)(2,1)} %fusion.5), channel_id=1, source_target_pairs={{0,96},{16,112},{32,0},{48,16},{64,32},{80,48},{96,64},{112,80},{1... | collective-permute-start | bytes 2162696 | tf_op jit(solution)/shard_map/ppermute | solution.py:90
  119.3 26.1 %collective-permute-start.12 = (bf16[16,2,64,176]{3,2,0,1:T(8,128)(2,1)}, bf16[16,2,64,176]{3,2,0,1:T(8,128)(2,1)S(1)}, u32[]{:S(2)}, u32[]{:S(2)}) collective-permute-start(bf16[16,2,64,176]{3,2,0,1:T(8,128)(2,1)} %fusion.5), channel_id=1, source_target_pairs={{0,32},{16,48},{32,64},{48,80},{64,96},{80,112},{96,0},{112,16},{1... | collective-permute-start | bytes 2162696 | tf_op jit(solution)/shard_map/ppermute | solution.py:90
  119.3 39.3 %collective-permute-start.10 = (bf16[16,2,64,176]{3,2,0,1:T(8,128)(2,1)}, bf16[16,2,64,176]{3,2,0,1:T(8,128)(2,1)}, u32[]{:S(2)}, u32[]{:S(2)}) collective-permute-start(bf16[16,2,64,176]{3,2,0,1:T(8,128)(2,1)} %fusion.5), channel_id=1, source_target_pairs={{0,16},{16,0},{32,48},{48,32},{64,80},{80,64},{96,112},{112,96},{1... | collective-permute-start | bytes 2162696 | tf_op jit(solution)/shard_map/ppermute | solution.py:93
  124.1 21.2 %copy-start.13 = (bf16[2,176,256]{2,1,0:T(8,128)(2,1)S(1)}, bf16[2,176,256]{2,1,0:T(8,128)(2,1)}, u32[]{:S(2)}) copy-start(bf16[2,176,256]{2,1,0:T(8,128)(2,1)} %get-tuple-element.11) | copy-start | bytes 540676
  124.1 22.7 %copy-start.12 = (bf16[2,176,256]{2,1,0:T(8,128)(2,1)S(1)}, bf16[2,176,256]{2,1,0:T(8,128)(2,1)}, u32[]{:S(2)}) copy-start(bf16[2,176,256]{2,1,0:T(8,128)(2,1)} %get-tuple-element.12) | copy-start | bytes 540676
  142.4 42.7 %collective-permute-start.17 = (bf16[2,176,256]{2,1,0:T(8,128)(2,1)}, bf16[2,176,256]{2,1,0:T(8,128)(2,1)S(1)}, u32[]{:S(2)}, u32[]{:S(2)}) collective-permute-start(bf16[2,176,256]{2,1,0:T(8,128)(2,1)} %get-tuple-element.14), channel_id=1, source_target_pairs={{0,80},{16,96},{32,112},{48,0},{64,16},{80,32},{96,48},{112,64},{1... | collective-permute-start | bytes 540680 | tf_op jit(solution)/shard_map/ppermute | solution.py:90
  145.3 8.3 %copy-start.11 = (bf16[2,176,256]{2,1,0:T(8,128)(2,1)S(1)}, bf16[2,176,256]{2,1,0:T(8,128)(2,1)}, u32[]{:S(2)}) copy-start(bf16[2,176,256]{2,1,0:T(8,128)(2,1)} %get-tuple-element.8) | copy-start | bytes 540676
  145.3 8.3 %collective-permute-start.11 = (bf16[2,176,256]{2,1,0:T(8,128)(2,1)S(1)}, bf16[2,176,256]{2,1,0:T(8,128)(2,1)S(1)}, u32[]{:S(2)}, u32[]{:S(2)}) collective-permute-start(bf16[2,176,256]{2,1,0:T(8,128)(2,1)S(1)} %copy-done.13), channel_id=1, source_target_pairs={{0,32},{16,48},{32,64},{48,80},{64,96},{80,112},{96,0},{112,16},{1... | collective-permute-start | bytes 540680 | tf_op jit(solution)/shard_map/ppermute | solution.py:90
  146.8 9.1 %collective-permute-start.8 = (bf16[2,176,256]{2,1,0:T(8,128)(2,1)S(1)}, bf16[2,176,256]{2,1,0:T(8,128)(2,1)S(1)}, u32[]{:S(2)}, u32[]{:S(2)}) collective-permute-start(bf16[2,176,256]{2,1,0:T(8,128)(2,1)S(1)} %copy-done.12), channel_id=1, source_target_pairs={{0,16},{16,32},{32,48},{48,64},{64,80},{80,96},{96,112},{112,0},{1... | collective-permute-start | bytes 540680 | tf_op jit(solution)/shard_map/ppermute | solution.py:90
  153.6 3.2 %collective-permute-start.9 = (bf16[2,176,256]{2,1,0:T(8,128)(2,1)S(1)}, bf16[2,176,256]{2,1,0:T(8,128)(2,1)S(1)}, u32[]{:S(2)}, u32[]{:S(2)}) collective-permute-start(bf16[2,176,256]{2,1,0:T(8,128)(2,1)S(1)} %copy-done.11), channel_id=1, source_target_pairs={{0,112},{16,0},{32,16},{48,32},{64,48},{80,64},{96,80},{112,96},{1... | collective-permute-start | bytes 540680 | tf_op jit(solution)/shard_map/ppermute | solution.py:90
  155.9 19.4 %collective-permute-start.22 = (bf16[8,2,64,176]{3,2,0,1:T(8,128)(2,1)}, bf16[8,2,64,176]{3,2,0,1:T(8,128)(2,1)S(1)}, u32[]{:S(2)}, u32[]{:S(2)}) collective-permute-start(bf16[8,2,64,176]{3,2,0,1:T(8,128)(2,1)} %slice.59), channel_id=1, source_target_pairs={{0,96},{16,112},{32,0},{48,16},{64,32},{80,48},{96,64},{112,80},{1... | collective-permute-start | bytes 1081352 | tf_op jit(solution)/shard_map/ppermute | solution.py:90
  156.8 22.0 %collective-permute-start.20 = (bf16[8,2,64,176]{3,2,0,1:T(8,128)(2,1)}, bf16[8,2,64,176]{3,2,0,1:T(8,128)(2,1)}, u32[]{:S(2)}, u32[]{:S(2)}) collective-permute-start(bf16[8,2,64,176]{3,2,0,1:T(8,128)(2,1)} %slice.58), channel_id=1, source_target_pairs={{0,32},{16,48},{32,64},{48,80},{64,96},{80,112},{96,0},{112,16},{1... | collective-permute-start | bytes 1081352 | tf_op jit(solution)/shard_map/ppermute | solution.py:90
  158.6 24.6 %collective-permute-start.14 = (bf16[16,2,64,176]{3,2,0,1:T(8,128)(2,1)S(1)}, bf16[16,2,64,176]{3,2,0,1:T(8,128)(2,1)}, u32[]{:S(2)}, u32[]{:S(2)}) collective-permute-start(bf16[16,2,64,176]{3,2,0,1:T(8,128)(2,1)S(1)} %collective-permute-done.12), channel_id=1, source_target_pairs={{0,16},{16,0},{32,48},{48,32},{64,80},{80,64},{96,112},{112,96},{1... | collective-permute-start | bytes 2162696 | tf_op jit(solution)/shard_map/ppermute | solution.py:93
  161.9 4.1 %copy-start.20 = (bf16[512,2048]{1,0:T(8,128)(2,1)S(1)}, bf16[512,2048]{1,0:T(8,128)(2,1)}, u32[]{:S(2)}) copy-start(bf16[512,2048]{1,0:T(8,128)(2,1)} %all-gather.3.cloned.1.call-done) | copy-start | bytes 6291460
  166.0 3.7 %copy-start.22 = (bf16[256,256]{1,0:T(8,128)(2,1)S(1)}, bf16[256,256]{1,0:T(8,128)(2,1)}, u32[]{:S(2)}) copy-start(bf16[256,256]{1,0:T(8,128)(2,1)} %fusion.17) | copy-start | bytes 393220
  174.8 7.6 %collective-permute-start.13 = (bf16[2,176,256]{2,1,0:T(8,128)(2,1)}, bf16[2,176,256]{2,1,0:T(8,128)(2,1)S(1)}, u32[]{:S(2)}, u32[]{:S(2)}) collective-permute-start(bf16[2,176,256]{2,1,0:T(8,128)(2,1)} %get-tuple-element.10), channel_id=1, source_target_pairs={{0,48},{16,64},{32,80},{48,96},{64,112},{80,0},{96,16},{112,32},{1... | collective-permute-start | bytes 540680 | tf_op jit(solution)/shard_map/ppermute | solution.py:90
  175.3 10.5 %collective-permute-start.18 = (bf16[16,2,64,176]{3,2,0,1:T(8,128)(2,1)S(1)}, bf16[16,2,64,176]{3,2,0,1:T(8,128)(2,1)S(1)}, u32[]{:S(2)}, u32[]{:S(2)}) collective-permute-start(bf16[16,2,64,176]{3,2,0,1:T(8,128)(2,1)S(1)} %collective-permute-done.16), channel_id=1, source_target_pairs={{0,16},{16,0},{32,48},{48,32},{64,80},{80,64},{96,112},{112,96},{1... | collective-permute-start | bytes 2162696 | tf_op jit(solution)/shard_map/ppermute | solution.py:93
  178.8 6.3 %collective-permute-start.23 = (bf16[8,2,64,176]{3,2,0,1:T(8,128)(2,1)S(1)}, bf16[8,2,64,176]{3,2,0,1:T(8,128)(2,1)S(1)}, u32[]{:S(2)}, u32[]{:S(2)}) collective-permute-start(bf16[8,2,64,176]{3,2,0,1:T(8,128)(2,1)S(1)} %collective-permute-done.22), channel_id=1, source_target_pairs={{0,16},{16,0},{32,48},{48,32},{64,80},{80,64},{96,112},{112,96},{1... | collective-permute-start | bytes 1081352 | tf_op jit(solution)/shard_map/ppermute | solution.py:93
  182.4 3.1 %collective-permute-start.21 = (bf16[8,2,64,176]{3,2,0,1:T(8,128)(2,1)}, bf16[8,2,64,176]{3,2,0,1:T(8,128)(2,1)S(1)}, u32[]{:S(2)}, u32[]{:S(2)}) collective-permute-start(bf16[8,2,64,176]{3,2,0,1:T(8,128)(2,1)} %collective-permute-done.20), channel_id=1, source_target_pairs={{0,16},{16,0},{32,48},{48,32},{64,80},{80,64},{96,112},{112,96},{1... | collective-permute-start | bytes 1081352 | tf_op jit(solution)/shard_map/ppermute | solution.py:93
  183.3 2.5 %copy-start.5 = (f32[2,256,16,64]{1,3,2,0:T(8,128)S(1)}, f32[2,256,16,64]{1,3,2,0:T(8,128)}, u32[]{:S(2)}) copy-start(f32[2,256,16,64]{1,3,2,0:T(8,128)} %fusion.38) | copy-start | bytes 6291460
  183.3 2.6 %copy-start.6 = (f32[2,256,16,64]{1,3,2,0:T(8,128)S(1)}, f32[2,256,16,64]{1,3,2,0:T(8,128)}, u32[]{:S(2)}) copy-start(f32[2,256,16,64]{1,3,2,0:T(8,128)} %fusion.40) | copy-start | bytes 6291460
  185.1 1.8 copy-start.4
  185.5 2.0 copy-start.3
  190.0 4.9 %copy-start.18 = (pred[256,4]{0,1:T(4,128)(4,1)S(1)}, pred[256,4]{0,1:T(4,128)(4,1)}, u32[]{:S(2)}) copy-start(pred[256,4]{0,1:T(4,128)(4,1)} %get-tuple-element.6) | copy-start | bytes 3076
  190.0 5.1 %copy-start.21 = (bf16[2048,32]{0,1:T(8,128)(2,1)S(1)}, bf16[2048,32]{0,1:T(8,128)(2,1)}, u32[]{:S(2)}) copy-start(bf16[2048,32]{0,1:T(8,128)(2,1)} %param.18) | copy-start | bytes 393220
  190.0 35.4 %all-to-all-start.1 = ((f32[16,2,64,256]{3,2,1,0:T(8,128)}), f32[16,2,64,256]{3,2,1,0:T(8,128)}, u32[]{:S(2)}, u32[]{:S(2)}) async-start(f32[16,2,64,256]{3,2,1,0:T(8,128)} %copy.78), calls=%async_computation.1 | async-start | bytes 4194304 | tf_op jit(solution)/shard_map/all_to_all | solution.py:159
  225.4 10.7 %copy-start.1 = (bf16[64,16,704]{2,1,0:T(8,128)(2,1)S(1)}, bf16[64,16,704]{2,1,0:T(8,128)(2,1)}, u32[]{:S(2)}) copy-start(bf16[64,16,704]{2,1,0:T(8,128)(2,1)} %param.27) | copy-start | bytes 4325380
Sparse Core Ops, SparseCore 0:
  11.7 29.4 all-gather.2
  43.3 79.1 all-gather.4
  174.9 32.5 reduce-scatter.1

commit v8 on v7

--- a/solution.py
+++ b/solution.py
@@ -126,6 +126,20 @@
     group_half = hidden.shape[0] // 2
     from_below = shifted(hidden, 2)
     from_above = shifted(hidden, -2)
+    shared_gate_value = jnp.dot(all_features, shared_full[0], preferred_element_type=jnp.float32)
+    shared_up_value = jnp.dot(all_features, shared_full[1], preferred_element_type=jnp.float32)
+    shared_hidden_units = (
+        jax.nn.silu(shared_gate_value) * (shared_up_value + ADAPTER_SCALE * adapter_update)
+    ).astype(jnp.bfloat16)
+    shared_part = lax.dot_general(
+        shared_hidden_units,
+        shared_full[2],
+        (((1,), (1,)), ((), ())),
+        preferred_element_type=jnp.float32,
+    )
+    shared_part = shared_part * share[:, None]
+    shared_part, from_below, from_above = lax.optimization_barrier((shared_part, from_below, from_above))
+    shared_sum = lax.psum_scatter(shared_part, "row", scatter_dimension=1, tiled=True)
     far_low = shifted(from_below[:group_half], 2)
     far_high = shifted(from_above[group_half:], -2)
 
@@ -161,19 +175,6 @@
     routed_rows = jnp.take(flat_rows, row_index, axis=0)
     routed = jnp.sum(gate_weights[:, :, None] * routed_rows, axis=1)
 
-    shared_gate_value = jnp.dot(all_features, shared_full[0], preferred_element_type=jnp.float32)
-    shared_up_value = jnp.dot(all_features, shared_full[1], preferred_element_type=jnp.float32)
-    shared_hidden_units = (
-        jax.nn.silu(shared_gate_value) * (shared_up_value + ADAPTER_SCALE * adapter_update)
-    ).astype(jnp.bfloat16)
-    shared_part = lax.dot_general(
-        shared_hidden_units,
-        shared_full[2],
-        (((1,), (1,)), ((), ())),
-        preferred_element_type=jnp.float32,
-    )
-    shared_part = shared_part * share[:, None]
-    shared_sum = lax.psum_scatter(shared_part, "row", scatter_dimension=1, tiled=True)
     return routed + shared_sum
 
 

time: 244 us -> 239 us (0.980)
  matrix products: 44.7 us -> 40 us
  starting transfers between devices: 26.9 us -> 23.7 us
  waiting for transfers between devices: 65.8 us -> 68.6 us
    ppermute x15, waiting for transfers between devices: 37.2 us -> 42.4 us  [shifted(): lax.ppermute(x, 'row', [(i, (i + shift) % row_count) for i in range(row_c...]
    dot_general x10, matrix products: 15.8 us -> 12 us  [down_of(): jnp.einsum('sexf,efd->sexd', block, weight, preferred_element_type=jnp.fl...]
    ppermute x9, starting transfers between devices: 4.81 us -> 2 us  [partner(): return lax.ppermute(x, 'row', [(i, i ^ 1) for i in range(row_count)])]
    reshape x2, local copies, waits for them, and re-layouts: 4.1 us -> 1.3 us  [project(): blocks = w.reshape(w.shape[0], row_count, local_width, w.shape[2])]
    unnamed x54 -> x60, local copies, waits for them, and re-layouts: 15.5 us -> 13.6 us
  transfers between devices with their start and end apart: 28 -> 28, of which waited for: 8 -> 7; matrix products, arithmetic and copies ran while one was open for 43% -> 42% of each run, Pallas kernels for 0% -> 0%
where the time goes in v8:
time: 239 us; the launch traced here: 237 us
  waiting for transfers between devices  68.6 us (29%)
  local copies, waits for them, and re-layouts  47.9 us (20%)
  matrix products  40 us (17%)
  blocking collectives  23.8 us (10%)
  starting transfers between devices  23.7 us (10%)
  other arithmetic  19.7 us (8%)
  between operations  13.7 us (6%)
    ppermute x15, waiting for transfers between devices, shifted(): lax.ppermute(x, 'row', [(i, (i + shift) % row_count) for i in range(row_c...  42.4 us
    all_to_all x1, waiting for transfers between devices, on_device(): lax.all_to_all(expert_value, 'col', split_axis=0, concat_axis=0, tiled=True)  26.1 us
    all_to_all x1, blocking collectives, on_device(): lax.all_to_all(outgoing, 'col', split_axis=0, concat_axis=0, tiled=True)  23.8 us
    ppermute x15, starting transfers between devices, shifted(): lax.ppermute(x, 'row', [(i, (i + shift) % row_count) for i in range(row_c...  17 us
    unnamed x60, local copies, waits for them, and re-layouts  13.6 us
    dot_general x10, matrix products, down_of(): jnp.einsum('sexf,efd->sexd', block, weight, preferred_element_type=jnp.fl...  12 us
    dot_general x2, matrix products, project(): jnp.einsum('sexd,edf->sexf', slot_features, ordered, preferred_element_ty...  9.55 us
    gather x2, local copies, waits for them, and re-layouts, on_device(): routed_rows = jnp.take(flat_rows, row_index, axis=0)  6.47 us
  transfers between devices with their start and end apart: 28, of which 7 were waited for; matrix products, arithmetic and copies ran while one was open for 42% of the time, Pallas kernels for 0%

profile of v8, /device:TPU:0, one launch (start us, length us, event | category | flops | bytes accessed | tf_op | source)
XLA Modules:
  0.0 237.5 jit_solution(16106380036565861581)
XLA Ops:
  6.6 0.8 compare_select_fusion.2
  8.4 1.6 gather_fusion
  10.1 1.6 pad_maximum_fusion.2
  11.8 2.0 pad_maximum_fusion.1
  15.4 2.6 %fusion = pred[2048,256]{1,0:T(8,128)(4,1)S(1)} fusion(s32[256,4]{0,1:T(4,128)S(1)} %get-tuple-element.13), kind=kLoop, calls=%fused_computation.6 | loop fusion | flops 3670016 | bytes 528384 | tf_op jit(solution)/shard_map/reduce_or | solution.py:110
  18.5 23.8 %all_to_all.10 = bf16[16,2,64,256]{3,2,1,0:T(8,128)(2,1)S(1)} all-to-all(bf16[16,2,64,256]{3,2,1,0:T(8,128)(2,1)S(1)} %bitcast.161), channel_id=1, replica_groups=mesh['row'=8,'col'=16] {'col'}, dimensions={0} | all-to-all | bytes 2097152 | tf_op jit(solution)/shard_map/all_to_all | solution.py:113
  42.3 1.6 fusion.61
  43.9 1.9 collective-permute-start
  45.9 2.1 collective-permute-start.1
  48.0 2.6 %constant_dynamic-slice_fusion.2 = (bf16[2,176,256]{2,1,0:T(8,128)(2,1)}, bf16[2,176,256]{2,1,0:T(8,128)(2,1)}, bf16[2,176,256]{2,1,0:T(8,128)(2,1)}, bf16[2,176...) fusion(bf16[2,176,2048]{2,1,0:T(8,128)(2,1)} %param.25, ...), kind=kLoop, calls=%fused_computation.124 | loop fusion | bytes 2523164 | tf_op jit(solution)/shard_map/dynamic_slice | solution.py:147
  50.6 1.2 copy.102
  51.9 3.2 %gather_fusion.3 = bf16[8,2,256,176]{2,3,1,0:T(8,128)(2,1)} fusion(bf16[2,8,256,176]{2,3,1,0:T(8,128)(2,1)} %bitcast.158, s32[1024]{0:T(1024)S(1)} %get-tuple-element.25), kind=kCustom, calls=%fused_computation.clone | custom fusion | bytes 2883616 | tf_op jit(solution)/shard_map/jit(_take)/gather | solution.py:119
  55.1 1.7 gather_fusion.4
  56.8 13.4 %collective-permute-done = bf16[16,2,64,256]{3,2,0,1:T(8,128)(2,1)} collective-permute-done((bf16[16,2,64,256]{3,2,0,1:T(8,128)(2,1)}, bf16[16,2,64,256]{3,2,0,1:T(8,128)(2,1)}, u32[]{:S(2)}, u32[]{:S(2)}) %collective-permute-start) | collective-permute-done | bytes 1048608 | tf_op jit(solution)/shard_map/ppermute | solution.py:90
  70.3 1.9 slice.56
  72.2 1.9 slice.57
  74.1 3.2 %collective-permute-start.3 = (bf16[8,2,64,256]{3,2,0,1:T(8,128)(2,1)}, bf16[8,2,64,256]{3,2,0,1:T(8,128)(2,1)}, u32[]{:S(2)}, u32[]{:S(2)}) collective-permute-start(bf16[8,2,64,256]{3,2,0,1:T(8,128)(2,1)} %slice.57), channel_id=1, source_target_pairs={{0,96},{16,112},{32,0},{48,16},{64,32},{80,48},{96,64},{112,80},{1... | collective-permute-start | bytes 1572872 | tf_op jit(solution)/shard_map/ppermute | solution.py:90
  77.3 2.9 %select_bitcast_fusion = (bf16[2,8,256,176]{2,3,0,1:T(8,128)(2,1)S(1)}, bf16[2,8,256,176]{2,3,0,1:T(8,128)(2,1)}) fusion(bf16[8,2,256,176]{2,3,1,0:T(8,128)(2,1)} %gather_fusion.4, pred[8]{0:T(512)(128)(4,1)S(1)} %compare_and_fusion.1, bf16[8,2,256,176]{2,3,1,0:T(8,128)(2,1)S(1)} %copy-done.2), kind=kLoop, calls=%fused_computation.28 | loop fusion | flops 1441792 | bytes 5767176 | tf_op jit(solution)/shard_map/jit(_take)/select_n | solution.py:119
  80.2 1.3 gather_fusion.1
  81.5 1.9 bitcast_select_fusion
  84.3 2.2 copy.71
  86.6 1.6 reshape.174
  88.1 0.8 copy.77
  89.9 1.1 pad_maximum_fusion
  91.1 0.7 collective-permute-start.7
  91.8 2.3 constant_dynamic-update-slice_fusion.7
  94.2 2.4 %constant_dynamic-update-slice_fusion.6 = bf16[16,2,64,2048]{3,2,0,1:T(8,128)(2,1)} fusion(bf16[16,2,64,2048]{3,2,0,1:T(8,128)(2,1)} %constant_dynamic-update-slice_fusion.7, bf16[16,2,64,256]{3,2,0,1:T(8,128)(2,1)} %collective-permute-done.1), kind=kLoop, calls=%fused_computation.102 | loop fusion | bytes 2097152
  96.5 0.9 constant_dynamic-update-slice_fusion.5
  97.4 1.9 constant_dynamic-update-slice_fusion.4
  99.4 2.4 constant_dynamic-update-slice_fusion.3
  101.7 2.3 constant_dynamic-update-slice_fusion.2
  104.1 1.1 constant_dynamic-update-slice_fusion.1
  105.2 1.1 constant_dynamic-update-slice_fusion
  106.3 5.9 %fusion.10 = f32[2,176,16,64]{1,3,2,0:T(8,128)S(1)} fusion(bf16[16,2,64,2048]{3,2,0,1:T(8,128)(2,1)} %constant_dynamic-update-slice_fusion, bf16[2,2048,176,1]{1,2,0,3:T(8,128)(2,1)S(1)} %copy-done.7), kind=kOutput, calls=%fused_computation.26 | convolution fusion | flops 1476395008 | bytes 11272192 | tf_op jit(solution)/shard_map/sexd,edf->sexf/dot_general | solution.py:120
  112.4 3.6 %fusion.5 = bf16[16,2,64,176]{3,2,0,1:T(8,128)(2,1)} fusion(f32[2,176,16,64]{1,3,2,0:T(8,128)S(1)} %fusion.10, bf16[16,2,64,2048]{3,2,0,1:T(8,128)(2,1)S(1)} %copy-done.14, bf16[2,2048,176,1]{1,2,0,3:T(8,128)(2,1)S(1)} %reshape.175), kind=kOutput, calls=%fused_computation.17 | convolution fusion | flops 1478557696 | bytes 11993088 | tf_op jit(solution)/shard_map/sexd,edf->sexf/dot_general | solution.py:120
  116.0 3.2 %collective-permute-start.13 = (bf16[16,2,64,176]{3,2,0,1:T(8,128)(2,1)}, bf16[16,2,64,176]{3,2,0,1:T(8,128)(2,1)S(1)}, u32[]{:S(2)}, u32[]{:S(2)}) collective-permute-start(bf16[16,2,64,176]{3,2,0,1:T(8,128)(2,1)} %fusion.5), channel_id=1, source_target_pairs={{0,96},{16,112},{32,0},{48,16},{64,32},{80,48},{96,64},{112,80},{1... | collective-permute-start | bytes 2162696 | tf_op jit(solution)/shard_map/ppermute | solution.py:90
  119.2 3.1 %fusion.42 = f32[2,256,16,64]{1,3,2,0:T(8,128)} fusion(bf16[16,2,64,176]{3,2,0,1:T(8,128)(2,1)} %fusion.5, bf16[2,176,2048]{2,1,0:T(8,128)(2,1)} %param.25, s32[]{:T(128)S(6)} %select_n.155), kind=kOutput, calls=%fused_computation.69 | convolution fusion | flops 184549376 | bytes 3325956 | tf_op jit(solution)/shard_map/sexf,efd->sexd/dot_general | solution.py:158
  122.3 1.6 fusion.24
  123.9 2.0 fusion.17
  126.0 4.1 %fusion.3 = f32[256,704]{0,1:T(8,128)} fusion(bf16[3,2048,704]{1,2,0:T(8,128)(2,1)} %all-gather.5.cloned.1.call-done, bf16[512,2048]{1,0:T(8,128)(2,1)} %all-gather.3.cloned.1.call-done), kind=kOutput, calls=%fused_computation.12 | convolution fusion | flops 738197504 | bytes 4653056 | tf_op jit(solution)/shard_map/dot_general | solution.py:129
  130.1 3.7 %fusion.2 = f32[256,704]{0,1:T(8,128)} fusion(bf16[3,2048,704]{1,2,0:T(8,128)(2,1)} %all-gather.5.cloned.1.call-done, bf16[512,2048]{1,0:T(8,128)(2,1)S(1)} %copy-done.24), kind=kOutput, calls=%fused_computation.10 | convolution fusion | flops 738197504 | bytes 4653056 | tf_op jit(solution)/shard_map/dot_general | solution.py:130
  133.8 5.0 %fusion.4 = f32[256,2048]{1,0:T(8,128)} fusion(bf16[3,2048,704]{1,2,0:T(8,128)(2,1)} %all-gather.5.cloned.1.call-done, f32[256,704]{0,1:T(8,128)} %fusion.2, bf16[256,256]{1,0:T(8,128)(2,1)S(1)} %fusion.17, bf16[256,704]{1,0:T(8,128)(2,1)S(1)} %copy-done.8, f32[256]{0:T(256)S(1)} %add_divide_fusion, f32[256,704]{0,1:T(8,128)} %fusion.3), kind=kOutput, calls=%fused_computation.13 | convolution fusion | flops 832438272 | bytes 6915072 | tf_op jit(solution)/shard_map/dot_general | solution.py:134
  138.8 4.3 %collective-permute-done.12 = bf16[16,2,64,176]{3,2,0,1:T(8,128)(2,1)S(1)} collective-permute-done((bf16[16,2,64,176]{3,2,0,1:T(8,128)(2,1)}, bf16[16,2,64,176]{3,2,0,1:T(8,128)(2,1)S(1)}, u32[]{:S(2)}, u32[]{:S(2)}) %collective-permute-start.12) | collective-permute-done | bytes 720928 | tf_op jit(solution)/shard_map/ppermute | solution.py:90
  143.0 2.8 %collective-permute-start.19 = (bf16[2,176,256]{2,1,0:T(8,128)(2,1)S(1)}, bf16[2,176,256]{2,1,0:T(8,128)(2,1)S(1)}, u32[]{:S(2)}, u32[]{:S(2)}) collective-permute-start(bf16[2,176,256]{2,1,0:T(8,128)(2,1)S(1)} %copy-done.12), channel_id=1, source_target_pairs={{0,64},{16,80},{32,96},{48,112},{64,0},{80,16},{96,32},{112,48},{1... | collective-permute-start | bytes 540680 | tf_op jit(solution)/shard_map/ppermute | solution.py:90
  145.8 0.8 slice.42
  146.7 1.0 collective-permute-start.11
  148.0 3.1 %fusion.40 = f32[2,256,16,64]{1,3,2,0:T(8,128)} fusion(bf16[16,2,64,176]{3,2,0,1:T(8,128)(2,1)} %collective-permute-done.10, bf16[2,176,256]{2,1,0:T(8,128)(2,1)S(1)} %collective-permute-done.8, bf16[2,176,256]{2,1,0:T(8,128)(2,1)} %collective-permute-done.9, pred[]{:T(512)S(6)} %eq.74), kind=kOutput, calls=%fused_computation.67 | convolution fusion | flops 184639488 | bytes 3178497 | tf_op jit(solution)/shard_map/sexf,efd->sexd/dot_general | solution.py:158
  151.1 0.8 slice.43
  152.0 5.1 %collective-permute-done.11 = bf16[2,176,256]{2,1,0:T(8,128)(2,1)S(1)} collective-permute-done((bf16[2,176,256]{2,1,0:T(8,128)(2,1)S(1)}, bf16[2,176,256]{2,1,0:T(8,128)(2,1)S(1)}, u32[]{:S(2)}, u32[]{:S(2)}) %collective-permute-start.11) | collective-permute-done | bytes 180256 | tf_op jit(solution)/shard_map/ppermute | solution.py:90
  157.1 2.3 collective-permute-start.22
  159.9 12.7 %collective-permute-done.20 = bf16[8,2,64,176]{3,2,0,1:T(8,128)(2,1)} collective-permute-done((bf16[8,2,64,176]{3,2,0,1:T(8,128)(2,1)}, bf16[8,2,64,176]{3,2,0,1:T(8,128)(2,1)}, u32[]{:S(2)}, u32[]{:S(2)}) %collective-permute-start.20) | collective-permute-done | bytes 360480 | tf_op jit(solution)/shard_map/ppermute | solution.py:90
  172.6 1.3 fusion.48
  173.9 3.3 %collective-permute-done.22 = bf16[8,2,64,176]{3,2,0,1:T(8,128)(2,1)S(1)} collective-permute-done((bf16[8,2,64,176]{3,2,0,1:T(8,128)(2,1)}, bf16[8,2,64,176]{3,2,0,1:T(8,128)(2,1)S(1)}, u32[]{:S(2)}, u32[]{:S(2)}) %collective-permute-start.22) | collective-permute-done | bytes 360480 | tf_op jit(solution)/shard_map/ppermute | solution.py:90
  178.2 1.7 fusion.33
  181.0 3.6 %collective-permute-done.16 = bf16[2,176,256]{2,1,0:T(8,128)(2,1)S(1)} collective-permute-done((bf16[2,176,256]{2,1,0:T(8,128)(2,1)S(1)}, bf16[2,176,256]{2,1,0:T(8,128)(2,1)S(1)}, u32[]{:S(2)}, u32[]{:S(2)}) %collective-permute-start.16) | collective-permute-done | bytes 180256 | tf_op jit(solution)/shard_map/ppermute | solution.py:90
  184.6 1.0 maximum_add_fusion
  185.7 1.5 copy.79
  187.2 4.6 %all-to-all-start.1 = ((f32[16,2,64,256]{3,2,1,0:T(8,128)}), f32[16,2,64,256]{3,2,1,0:T(8,128)}, u32[]{:S(2)}, u32[]{:S(2)}) async-start(f32[16,2,64,256]{3,2,1,0:T(8,128)} %copy.79), calls=%async_computation.1 | async-start | bytes 4194304 | tf_op jit(solution)/shard_map/all_to_all | solution.py:173
  192.3 1.6 fusion.29
  194.2 26.1 %all-to-all-done.1 = f32[16,2,64,256]{3,2,1,0:T(8,128)} async-done(((f32[16,2,64,256]{3,2,1,0:T(8,128)}), f32[16,2,64,256]{3,2,1,0:T(8,128)}, u32[]{:S(2)}, u32[]{:S(2)}) %all-to-all-start.1) | async-done | bytes 2097184 | tf_op jit(solution)/shard_map/all_to_all | solution.py:173
  220.2 5.2 %gather_fusion.2 = f32[1024,256]{1,0:T(8,128)S(1)} fusion(f32[2048,256]{1,0:T(8,128)} %bitcast.46, s32[1024]{0:T(1024)S(1)} %broadcast_clamp_fusion), kind=kCustom, calls=%fused_computation.4 | custom fusion | bytes 2101248 | tf_op jit(solution)/shard_map/jit(_take)/gather | solution.py:175
  225.4 1.3 reshape.157
  226.7 2.5 %multiply_reduce_fusion = f32[256,256]{1,0:T(8,128)S(1)} fusion(f32[256,4,256]{2,1,0:T(4,128)} %reshape.157, f32[256,4]{1,0:T(8,128)S(1)} %copy.66, pred[256,4]{1,0:T(8,128)(4,1)S(1)} %copy.69), kind=kLoop, calls=%fused_computation.42 | loop fusion | flops 720896 | bytes 1315840 | tf_op jit(solution)/shard_map/reduce_sum | solution.py:176
  229.2 1.7 add.206
  (138 shorter events, 8.9 us)
Async XLA Ops:
  6.5 73.7 %copy-start = (bf16[64,16,704]{2,1,0:T(8,128)(2,1)S(1)}, bf16[64,16,704]{2,1,0:T(8,128)(2,1)}, u32[]{:S(2)}) copy-start(bf16[64,16,704]{2,1,0:T(8,128)(2,1)} %param.27) | copy-start | bytes 4325380
  6.5 11.5 %copy-start.15 = (bf16[256,256]{1,0:T(8,128)(2,1)S(1)}, bf16[256,256]{1,0:T(8,128)(2,1)}, u32[]{:S(2)}) copy-start(bf16[256,256]{1,0:T(8,128)(2,1)} %param.17) | copy-start | bytes 393220
  6.5 7.3 %copy-start.16 = (s32[256,4]{0,1:T(4,128)S(1)}, s32[256,4]{0,1:T(4,128)}, u32[]{:S(2)}) copy-start(s32[256,4]{0,1:T(4,128)} %param.28) | copy-start | bytes 12292
  6.5 115.7 %all-gather.3.cloned.1.call-start = ((), (), s32[]{:S(2)}) async-start(), calls=%async_computation.3 | async-start | bytes 2359296 | tf_op jit(solution)/shard_map/all_gather | solution.py:34
  11.7 114.2 %all-gather.5.cloned.1.call-start = ((), (), s32[]{:S(2)}) async-start(), calls=%async_computation.4 | async-start | bytes 9191424 | tf_op jit(solution)/shard_map/all_gather | solution.py:53
  13.8 215.5 %reduce-scatter.2.cloned.1.call-start = ((), (), s32[]{:S(2)}) async-start(), calls=%async_computation.5 | async-start | bytes 2359296 | tf_op jit(solution)/shard_map/reduce_scatter | solution.py:142
  15.4 26.9 %copy-start.18 = (s32[256,4]{0,1:T(4,128)}, s32[256,4]{0,1:T(4,128)S(1)}, u32[]{:S(2)}) copy-start(s32[256,4]{0,1:T(4,128)S(1)} %get-tuple-element.13) | copy-start | bytes 12292
  43.9 6.6 %copy-start.5 = (bf16[2,2048,176]{1,2,0:T(8,128)(2,1)S(1)}, bf16[2,2048,176]{1,2,0:T(8,128)(2,1)}, u32[]{:S(2)}) copy-start(bf16[2,2048,176]{1,2,0:T(8,128)(2,1)} %param.23) | copy-start | bytes 4325380
  43.9 26.3 %collective-permute-start = (bf16[16,2,64,256]{3,2,0,1:T(8,128)(2,1)}, bf16[16,2,64,256]{3,2,0,1:T(8,128)(2,1)}, u32[]{:S(2)}, u32[]{:S(2)}) collective-permute-start(bf16[16,2,64,256]{3,2,0,1:T(8,128)(2,1)} %get-tuple-element.21), channel_id=1, source_target_pairs={{0,32},{16,48},{32,64},{48,80},{64,96},{80,112},{96,0},{112,16},{1... | collective-permute-start | bytes 3145736 | tf_op jit(solution)/shard_map/ppermute | solution.py:90
  45.9 26.3 %collective-permute-start.1 = (bf16[16,2,64,256]{3,2,0,1:T(8,128)(2,1)}, bf16[16,2,64,256]{3,2,0,1:T(8,128)(2,1)}, u32[]{:S(2)}, u32[]{:S(2)}) collective-permute-start(bf16[16,2,64,256]{3,2,0,1:T(8,128)(2,1)} %get-tuple-element.21), channel_id=1, source_target_pairs={{0,96},{16,112},{32,0},{48,16},{64,32},{80,48},{96,64},{112,80},{1... | collective-permute-start | bytes 3145736 | tf_op jit(solution)/shard_map/ppermute | solution.py:90
  48.0 3.8 %copy-start.6 = (bf16[2,2048,176]{1,2,0:T(8,128)(2,1)S(1)}, bf16[2,2048,176]{1,2,0:T(8,128)(2,1)}, u32[]{:S(2)}) copy-start(bf16[2,2048,176]{1,2,0:T(8,128)(2,1)} %param.24) | copy-start | bytes 4325380
  50.5 96.1 %collective-permute-start.9 = (bf16[2,176,256]{2,1,0:T(8,128)(2,1)}, bf16[2,176,256]{2,1,0:T(8,128)(2,1)}, u32[]{:S(2)}, u32[]{:S(2)}) collective-permute-start(bf16[2,176,256]{2,1,0:T(8,128)(2,1)} %get-tuple-element.17), channel_id=1, source_target_pairs={{0,112},{16,0},{32,16},{48,32},{64,48},{80,64},{96,80},{112,96},{1... | collective-permute-start | bytes 540680 | tf_op jit(solution)/shard_map/ppermute | solution.py:90
  56.8 20.5 %copy-start.2 = (bf16[8,2,256,176]{2,3,1,0:T(8,128)(2,1)S(1)}, bf16[8,2,256,176]{2,3,1,0:T(8,128)(2,1)}, u32[]{:S(2)}) copy-start(bf16[8,2,256,176]{2,3,1,0:T(8,128)(2,1)} %gather_fusion.3) | copy-start | bytes 4325380
  72.2 17.7 %collective-permute-start.2 = (bf16[8,2,64,256]{3,2,0,1:T(8,128)(2,1)}, bf16[8,2,64,256]{3,2,0,1:T(8,128)(2,1)S(1)}, u32[]{:S(2)}, u32[]{:S(2)}) collective-permute-start(bf16[8,2,64,256]{3,2,0,1:T(8,128)(2,1)} %slice.56), channel_id=1, source_target_pairs={{0,32},{16,48},{32,64},{48,80},{64,96},{80,112},{96,0},{112,16},{1... | collective-permute-start | bytes 1572872 | tf_op jit(solution)/shard_map/ppermute | solution.py:90
  74.1 9.3 %copy-start.22 = (s32[1,16]{1,0:T(1,128)S(1)}, s32[1,16]{1,0:T(1,128)}, u32[]{:S(2)}) copy-start(s32[1,16]{1,0:T(1,128)} %param.29) | copy-start | bytes 196
  74.1 15.8 %collective-permute-start.3 = (bf16[8,2,64,256]{3,2,0,1:T(8,128)(2,1)}, bf16[8,2,64,256]{3,2,0,1:T(8,128)(2,1)}, u32[]{:S(2)}, u32[]{:S(2)}) collective-permute-start(bf16[8,2,64,256]{3,2,0,1:T(8,128)(2,1)} %slice.57), channel_id=1, source_target_pairs={{0,96},{16,112},{32,0},{48,16},{64,32},{80,48},{96,64},{112,80},{1... | collective-permute-start | bytes 1572872 | tf_op jit(solution)/shard_map/ppermute | solution.py:90
  81.5 17.8 %collective-permute-start.4 = (bf16[16,2,64,256]{3,2,0,1:T(8,128)(2,1)}, bf16[16,2,64,256]{3,2,0,1:T(8,128)(2,1)}, u32[]{:S(2)}, u32[]{:S(2)}) collective-permute-start(bf16[16,2,64,256]{3,2,0,1:T(8,128)(2,1)} %get-tuple-element.21), channel_id=1, source_target_pairs={{0,16},{16,0},{32,48},{48,32},{64,80},{80,64},{96,112},{112,96},{1... | collective-permute-start | bytes 3145736 | tf_op jit(solution)/shard_map/ppermute | solution.py:93
  83.7 18.1 %collective-permute-start.5 = (bf16[16,2,64,256]{3,2,0,1:T(8,128)(2,1)}, bf16[16,2,64,256]{3,2,0,1:T(8,128)(2,1)}, u32[]{:S(2)}, u32[]{:S(2)}) collective-permute-start(bf16[16,2,64,256]{3,2,0,1:T(8,128)(2,1)} %collective-permute-done), channel_id=1, source_target_pairs={{0,16},{16,0},{32,48},{48,32},{64,80},{80,64},{96,112},{112,96},{1... | collective-permute-start | bytes 3145736 | tf_op jit(solution)/shard_map/ppermute | solution.py:93
  89.0 0.7 copy-start.20
  89.0 0.8 copy-start.23
  89.8 14.3 %collective-permute-start.6 = (bf16[16,2,64,256]{3,2,0,1:T(8,128)(2,1)}, bf16[16,2,64,256]{3,2,0,1:T(8,128)(2,1)S(1)}, u32[]{:S(2)}, u32[]{:S(2)}) collective-permute-start(bf16[16,2,64,256]{3,2,0,1:T(8,128)(2,1)} %collective-permute-done.1), channel_id=1, source_target_pairs={{0,16},{16,0},{32,48},{48,32},{64,80},{80,64},{96,112},{112,96},{1... | collective-permute-start | bytes 3145736 | tf_op jit(solution)/shard_map/ppermute | solution.py:93
  91.1 14.1 %collective-permute-start.7 = (bf16[16,2,64,256]{3,2,0,1:T(8,128)(2,1)S(1)}, bf16[16,2,64,256]{3,2,0,1:T(8,128)(2,1)S(1)}, u32[]{:S(2)}, u32[]{:S(2)}) collective-permute-start(bf16[16,2,64,256]{3,2,0,1:T(8,128)(2,1)S(1)} %pad_maximum_fusion), channel_id=1, source_target_pairs={{0,16},{16,0},{32,48},{48,32},{64,80},{80,64},{96,112},{112,96},{1... | collective-permute-start | bytes 3145736 | tf_op jit(solution)/shard_map/ppermute | solution.py:93
  99.3 48.3 %collective-permute-start.8 = (bf16[2,176,256]{2,1,0:T(8,128)(2,1)}, bf16[2,176,256]{2,1,0:T(8,128)(2,1)S(1)}, u32[]{:S(2)}, u32[]{:S(2)}) collective-permute-start(bf16[2,176,256]{2,1,0:T(8,128)(2,1)} %get-tuple-element.18), channel_id=1, source_target_pairs={{0,16},{16,32},{32,48},{48,64},{64,80},{80,96},{96,112},{112,0},{1... | collective-permute-start | bytes 540680 | tf_op jit(solution)/shard_map/ppermute | solution.py:90
  104.1 2.2 copy-start.7
  106.3 6.1 %copy-start.14 = (bf16[16,2,64,2048]{3,2,0,1:T(8,128)(2,1)S(1)}, bf16[16,2,64,2048]{3,2,0,1:T(8,128)(2,1)}, u32[]{:S(2)}) copy-start(bf16[16,2,64,2048]{3,2,0,1:T(8,128)(2,1)} %constant_dynamic-update-slice_fusion) | copy-start | bytes 25165828
  116.0 27.0 %collective-permute-start.12 = (bf16[16,2,64,176]{3,2,0,1:T(8,128)(2,1)}, bf16[16,2,64,176]{3,2,0,1:T(8,128)(2,1)S(1)}, u32[]{:S(2)}, u32[]{:S(2)}) collective-permute-start(bf16[16,2,64,176]{3,2,0,1:T(8,128)(2,1)} %fusion.5), channel_id=1, source_target_pairs={{0,32},{16,48},{32,64},{48,80},{64,96},{80,112},{96,0},{112,16},{1... | collective-permute-start | bytes 2162696 | tf_op jit(solution)/shard_map/ppermute | solution.py:90
  116.0 27.0 %collective-permute-start.13 = (bf16[16,2,64,176]{3,2,0,1:T(8,128)(2,1)}, bf16[16,2,64,176]{3,2,0,1:T(8,128)(2,1)S(1)}, u32[]{:S(2)}, u32[]{:S(2)}) collective-permute-start(bf16[16,2,64,176]{3,2,0,1:T(8,128)(2,1)} %fusion.5), channel_id=1, source_target_pairs={{0,96},{16,112},{32,0},{48,16},{64,32},{80,48},{96,64},{112,80},{1... | collective-permute-start | bytes 2162696 | tf_op jit(solution)/shard_map/ppermute | solution.py:90
  119.2 28.8 %collective-permute-start.10 = (bf16[16,2,64,176]{3,2,0,1:T(8,128)(2,1)}, bf16[16,2,64,176]{3,2,0,1:T(8,128)(2,1)}, u32[]{:S(2)}, u32[]{:S(2)}) collective-permute-start(bf16[16,2,64,176]{3,2,0,1:T(8,128)(2,1)} %fusion.5), channel_id=1, source_target_pairs={{0,16},{16,0},{32,48},{48,32},{64,80},{80,64},{96,112},{112,96},{1... | collective-permute-start | bytes 2162696 | tf_op jit(solution)/shard_map/ppermute | solution.py:93
  126.0 4.1 %copy-start.24 = (bf16[512,2048]{1,0:T(8,128)(2,1)S(1)}, bf16[512,2048]{1,0:T(8,128)(2,1)}, u32[]{:S(2)}) copy-start(bf16[512,2048]{1,0:T(8,128)(2,1)} %all-gather.3.cloned.1.call-done) | copy-start | bytes 6291460
  130.1 3.7 %copy-start.8 = (bf16[256,704]{1,0:T(8,128)(2,1)S(1)}, bf16[256,704]{1,0:T(8,128)(2,1)}, u32[]{:S(2)}) copy-start(bf16[256,704]{1,0:T(8,128)(2,1)} %bitcast_select_fusion) | copy-start | bytes 1081348
  133.8 9.2 %copy-start.11 = (bf16[2,176,256]{2,1,0:T(8,128)(2,1)S(1)}, bf16[2,176,256]{2,1,0:T(8,128)(2,1)}, u32[]{:S(2)}) copy-start(bf16[2,176,256]{2,1,0:T(8,128)(2,1)} %get-tuple-element.20) | copy-start | bytes 540676
  133.8 9.2 %copy-start.12 = (bf16[2,176,256]{2,1,0:T(8,128)(2,1)S(1)}, bf16[2,176,256]{2,1,0:T(8,128)(2,1)}, u32[]{:S(2)}) copy-start(bf16[2,176,256]{2,1,0:T(8,128)(2,1)} %get-tuple-element.19) | copy-start | bytes 540676
  133.8 12.9 %copy-start.13 = (bf16[2,176,256]{2,1,0:T(8,128)(2,1)S(1)}, bf16[2,176,256]{2,1,0:T(8,128)(2,1)}, u32[]{:S(2)}) copy-start(bf16[2,176,256]{2,1,0:T(8,128)(2,1)} %get-tuple-element.16) | copy-start | bytes 540676
  143.0 34.5 %collective-permute-start.17 = (bf16[2,176,256]{2,1,0:T(8,128)(2,1)S(1)}, bf16[2,176,256]{2,1,0:T(8,128)(2,1)S(1)}, u32[]{:S(2)}, u32[]{:S(2)}) collective-permute-start(bf16[2,176,256]{2,1,0:T(8,128)(2,1)S(1)} %copy-done.11), channel_id=1, source_target_pairs={{0,80},{16,96},{32,112},{48,0},{64,16},{80,32},{96,48},{112,64},{1... | collective-permute-start | bytes 540680 | tf_op jit(solution)/shard_map/ppermute | solution.py:90
  143.0 16.8 %collective-permute-start.19 = (bf16[2,176,256]{2,1,0:T(8,128)(2,1)S(1)}, bf16[2,176,256]{2,1,0:T(8,128)(2,1)S(1)}, u32[]{:S(2)}, u32[]{:S(2)}) collective-permute-start(bf16[2,176,256]{2,1,0:T(8,128)(2,1)S(1)} %copy-done.12), channel_id=1, source_target_pairs={{0,64},{16,80},{32,96},{48,112},{64,0},{80,16},{96,32},{112,48},{1... | collective-permute-start | bytes 540680 | tf_op jit(solution)/shard_map/ppermute | solution.py:90
  146.7 10.4 %collective-permute-start.11 = (bf16[2,176,256]{2,1,0:T(8,128)(2,1)S(1)}, bf16[2,176,256]{2,1,0:T(8,128)(2,1)S(1)}, u32[]{:S(2)}, u32[]{:S(2)}) collective-permute-start(bf16[2,176,256]{2,1,0:T(8,128)(2,1)S(1)} %copy-done.13), channel_id=1, source_target_pairs={{0,32},{16,48},{32,64},{48,80},{64,96},{80,112},{96,0},{112,16},{1... | collective-permute-start | bytes 540680 | tf_op jit(solution)/shard_map/ppermute | solution.py:90
  147.7 24.9 %collective-permute-start.20 = (bf16[8,2,64,176]{3,2,0,1:T(8,128)(2,1)}, bf16[8,2,64,176]{3,2,0,1:T(8,128)(2,1)}, u32[]{:S(2)}, u32[]{:S(2)}) collective-permute-start(bf16[8,2,64,176]{3,2,0,1:T(8,128)(2,1)} %slice.42), channel_id=1, source_target_pairs={{0,32},{16,48},{32,64},{48,80},{64,96},{80,112},{96,0},{112,16},{1... | collective-permute-start | bytes 1081352 | tf_op jit(solution)/shard_map/ppermute | solution.py:90
  151.1 26.6 %collective-permute-start.18 = (bf16[16,2,64,176]{3,2,0,1:T(8,128)(2,1)S(1)}, bf16[16,2,64,176]{3,2,0,1:T(8,128)(2,1)}, u32[]{:S(2)}, u32[]{:S(2)}) collective-permute-start(bf16[16,2,64,176]{3,2,0,1:T(8,128)(2,1)S(1)} %collective-permute-done.13), channel_id=1, source_target_pairs={{0,16},{16,0},{32,48},{48,32},{64,80},{80,64},{96,112},{112,96},{1... | collective-permute-start | bytes 2162696 | tf_op jit(solution)/shard_map/ppermute | solution.py:93
  151.9 7.9 %copy-start.10 = (bf16[2,176,256]{2,1,0:T(8,128)(2,1)S(1)}, bf16[2,176,256]{2,1,0:T(8,128)(2,1)}, u32[]{:S(2)}) copy-start(bf16[2,176,256]{2,1,0:T(8,128)(2,1)} %get-tuple-element.15) | copy-start | bytes 540676
  152.0 25.3 %copy-start.9 = (bf16[2,176,256]{2,1,0:T(8,128)(2,1)S(1)}, bf16[2,176,256]{2,1,0:T(8,128)(2,1)}, u32[]{:S(2)}) copy-start(bf16[2,176,256]{2,1,0:T(8,128)(2,1)} %get-tuple-element.14) | copy-start | bytes 540676
  157.1 20.2 %collective-permute-start.22 = (bf16[8,2,64,176]{3,2,0,1:T(8,128)(2,1)}, bf16[8,2,64,176]{3,2,0,1:T(8,128)(2,1)S(1)}, u32[]{:S(2)}, u32[]{:S(2)}) collective-permute-start(bf16[8,2,64,176]{3,2,0,1:T(8,128)(2,1)} %slice.43), channel_id=1, source_target_pairs={{0,96},{16,112},{32,0},{48,16},{64,32},{80,48},{96,64},{112,80},{1... | collective-permute-start | bytes 1081352 | tf_op jit(solution)/shard_map/ppermute | solution.py:90
  159.8 20.0 %collective-permute-start.14 = (bf16[2,176,256]{2,1,0:T(8,128)(2,1)S(1)}, bf16[2,176,256]{2,1,0:T(8,128)(2,1)S(1)}, u32[]{:S(2)}, u32[]{:S(2)}) collective-permute-start(bf16[2,176,256]{2,1,0:T(8,128)(2,1)S(1)} %copy-done.10), channel_id=1, source_target_pairs={{0,48},{16,64},{32,80},{48,96},{64,112},{80,0},{96,16},{112,32},{1... | collective-permute-start | bytes 540680 | tf_op jit(solution)/shard_map/ppermute | solution.py:90
  172.6 7.3 %collective-permute-start.15 = (bf16[16,2,64,176]{3,2,0,1:T(8,128)(2,1)S(1)}, bf16[16,2,64,176]{3,2,0,1:T(8,128)(2,1)S(1)}, u32[]{:S(2)}, u32[]{:S(2)}) collective-permute-start(bf16[16,2,64,176]{3,2,0,1:T(8,128)(2,1)S(1)} %collective-permute-done.12), channel_id=1, source_target_pairs={{0,16},{16,0},{32,48},{48,32},{64,80},{80,64},{96,112},{112,96},{1... | collective-permute-start | bytes 2162696 | tf_op jit(solution)/shard_map/ppermute | solution.py:93
  177.3 7.4 %collective-permute-start.16 = (bf16[2,176,256]{2,1,0:T(8,128)(2,1)S(1)}, bf16[2,176,256]{2,1,0:T(8,128)(2,1)S(1)}, u32[]{:S(2)}, u32[]{:S(2)}) collective-permute-start(bf16[2,176,256]{2,1,0:T(8,128)(2,1)S(1)} %copy-done.9), channel_id=1, source_target_pairs={{0,96},{16,112},{32,0},{48,16},{64,32},{80,48},{96,64},{112,80},{1... | collective-permute-start | bytes 540680 | tf_op jit(solution)/shard_map/ppermute | solution.py:90
  177.6 2.8 %collective-permute-start.21 = (bf16[8,2,64,176]{3,2,0,1:T(8,128)(2,1)}, bf16[8,2,64,176]{3,2,0,1:T(8,128)(2,1)S(1)}, u32[]{:S(2)}, u32[]{:S(2)}) collective-permute-start(bf16[8,2,64,176]{3,2,0,1:T(8,128)(2,1)} %collective-permute-done.20), channel_id=1, source_target_pairs={{0,16},{16,0},{32,48},{48,32},{64,80},{80,64},{96,112},{112,96},{1... | collective-permute-start | bytes 1081352 | tf_op jit(solution)/shard_map/ppermute | solution.py:93
  177.7 3.0 %collective-permute-start.23 = (bf16[8,2,64,176]{3,2,0,1:T(8,128)(2,1)S(1)}, bf16[8,2,64,176]{3,2,0,1:T(8,128)(2,1)S(1)}, u32[]{:S(2)}, u32[]{:S(2)}) collective-permute-start(bf16[8,2,64,176]{3,2,0,1:T(8,128)(2,1)S(1)} %collective-permute-done.22), channel_id=1, source_target_pairs={{0,16},{16,0},{32,48},{48,32},{64,80},{80,64},{96,112},{112,96},{1... | collective-permute-start | bytes 1081352 | tf_op jit(solution)/shard_map/ppermute | solution.py:93
  180.3 4.3 %copy-start.4 = (f32[2,256,16,64]{1,3,2,0:T(8,128)S(1)}, f32[2,256,16,64]{1,3,2,0:T(8,128)}, u32[]{:S(2)}) copy-start(f32[2,256,16,64]{1,3,2,0:T(8,128)} %fusion.40) | copy-start | bytes 6291460
  180.7 4.0 %copy-start.3 = (f32[2,256,16,64]{1,3,2,0:T(8,128)S(1)}, f32[2,256,16,64]{1,3,2,0:T(8,128)}, u32[]{:S(2)}) copy-start(f32[2,256,16,64]{1,3,2,0:T(8,128)} %fusion.42) | copy-start | bytes 6291460
  187.2 4.6 %copy-start.19 = (s32[256,4]{0,1:T(4,128)S(1)}, s32[256,4]{0,1:T(4,128)}, u32[]{:S(2)}) copy-start(s32[256,4]{0,1:T(4,128)} %copy-done.18) | copy-start | bytes 12292
  187.2 4.9 %copy-start.21 = (pred[256,4]{0,1:T(4,128)(4,1)S(1)}, pred[256,4]{0,1:T(4,128)(4,1)}, u32[]{:S(2)}) copy-start(pred[256,4]{0,1:T(4,128)(4,1)} %get-tuple-element.12) | copy-start | bytes 3076
  187.2 5.1 %copy-start.25 = (bf16[2048,32]{0,1:T(8,128)(2,1)S(1)}, bf16[2048,32]{0,1:T(8,128)(2,1)}, u32[]{:S(2)}) copy-start(bf16[2048,32]{0,1:T(8,128)(2,1)} %param.18) | copy-start | bytes 393220
  187.2 6.7 %copy-start.17 = (s32[256,4]{0,1:T(4,128)S(1)}, s32[256,4]{0,1:T(4,128)}, u32[]{:S(2)}) copy-start(s32[256,4]{0,1:T(4,128)} %param.28) | copy-start | bytes 12292
  187.2 33.0 %all-to-all-start.1 = ((f32[16,2,64,256]{3,2,1,0:T(8,128)}), f32[16,2,64,256]{3,2,1,0:T(8,128)}, u32[]{:S(2)}, u32[]{:S(2)}) async-start(f32[16,2,64,256]{3,2,1,0:T(8,128)} %copy.79), calls=%async_computation.1 | async-start | bytes 4194304 | tf_op jit(solution)/shard_map/all_to_all | solution.py:173
  220.2 10.7 %copy-start.1 = (bf16[64,16,704]{2,1,0:T(8,128)(2,1)S(1)}, bf16[64,16,704]{2,1,0:T(8,128)(2,1)}, u32[]{:S(2)}) copy-start(bf16[64,16,704]{2,1,0:T(8,128)(2,1)} %param.27) | copy-start | bytes 4325380
Sparse Core Ops, SparseCore 0:
  11.9 29.4 all-gather.2
  43.5 79.1 all-gather.4
  152.1 37.8 reduce-scatter.1

commit v9 on v8

--- a/solution.py
+++ b/solution.py
@@ -170,7 +170,9 @@
     low_part = down_of(far_low, far_weight) + down_of(partner(far_low), far_partner_weight)
     high_part = down_of(far_high, far_weight) + down_of(partner(far_high), far_partner_weight)
     expert_value = expert_value + jnp.concatenate([low_part, high_part], axis=0)
-    returned = lax.all_to_all(expert_value, "col", split_axis=0, concat_axis=0, tiled=True)
+    returned = lax.all_to_all(
+        expert_value.astype(jnp.bfloat16), "col", split_axis=0, concat_axis=0, tiled=True
+    ).astype(jnp.float32)
     flat_rows = returned.reshape(expert_count * capacity, local_width)
     routed_rows = jnp.take(flat_rows, row_index, axis=0)
     routed = jnp.sum(gate_weights[:, :, None] * routed_rows, axis=1)

time: 239 us -> 227 us (0.950)
  waiting for transfers between devices: 68.6 us -> 55.1 us
    all_to_all x1, waiting for transfers between devices: 26.1 us -> 13.3 us  [on_device(): lax.all_to_all(expert_value.astype(jnp.bfloat16), 'col', split_axis=0, co...]
  transfers between devices with their start and end apart: 28 -> 28, of which waited for: 7 -> 7; matrix products, arithmetic and copies ran while one was open for 42% -> 46% of each run, Pallas kernels for 0% -> 0%
where the time goes in v9:
time: 227 us; the launch traced here: 225 us
  waiting for transfers between devices  55.1 us (24%)
  local copies, waits for them, and re-layouts  47.6 us (21%)
  matrix products  40.9 us (18%)
  blocking collectives  23.8 us (10%)
  starting transfers between devices  22.9 us (10%)
  other arithmetic  21.3 us (9%)
  between operations  13.7 us (6%)
    ppermute x15, waiting for transfers between devices, shifted(): lax.ppermute(x, 'row', [(i, (i + shift) % row_count) for i in range(row_c...  41.7 us
    all_to_all x1, blocking collectives, on_device(): lax.all_to_all(outgoing, 'col', split_axis=0, concat_axis=0, tiled=True)  23.8 us
    ppermute x15, starting transfers between devices, shifted(): lax.ppermute(x, 'row', [(i, (i + shift) % row_count) for i in range(row_c...  17 us
    unnamed x60, local copies, waits for them, and re-layouts  13.6 us
    all_to_all x1, waiting for transfers between devices, on_device(): lax.all_to_all(expert_value.astype(jnp.bfloat16), 'col', split_axis=0, co...  13.3 us
    dot_general x10, matrix products, down_of(): jnp.einsum('sexf,efd->sexd', block, weight, preferred_element_type=jnp.fl...  12.9 us
    dot_general x2, matrix products, project(): jnp.einsum('sexd,edf->sexf', slot_features, ordered, preferred_element_ty...  9.55 us
    gather x2, local copies, waits for them, and re-layouts, on_device(): routed_rows = jnp.take(flat_rows, row_index, axis=0)  6.47 us
  transfers between devices with their start and end apart: 28, of which 7 were waited for; matrix products, arithmetic and copies ran while one was open for 46% of the time, Pallas kernels for 0%

profile of v9, /device:TPU:0, one launch (start us, length us, event | category | flops | bytes accessed | tf_op | source)
XLA Modules:
  0.0 225.3 jit_solution(14262621627624605134)
XLA Ops:
  8.4 1.6 gather_fusion
  10.1 1.6 pad_maximum_fusion.2
  11.8 2.0 pad_maximum_fusion.1
  15.4 2.6 %fusion = pred[2048,256]{1,0:T(8,128)(4,1)S(1)} fusion(s32[256,4]{0,1:T(4,128)S(1)} %get-tuple-element.13), kind=kLoop, calls=%fused_computation.6 | loop fusion | flops 3670016 | bytes 528384 | tf_op jit(solution)/shard_map/reduce_or | solution.py:110
  18.5 23.8 %all_to_all.10 = bf16[16,2,64,256]{3,2,1,0:T(8,128)(2,1)S(1)} all-to-all(bf16[16,2,64,256]{3,2,1,0:T(8,128)(2,1)S(1)} %bitcast.163), channel_id=1, replica_groups=mesh['row'=8,'col'=16] {'col'}, dimensions={0} | all-to-all | bytes 2097152 | tf_op jit(solution)/shard_map/all_to_all | solution.py:113
  42.3 1.6 fusion.62
  43.9 1.9 collective-permute-start
  45.9 2.1 collective-permute-start.1
  48.0 2.6 %constant_dynamic-slice_fusion.2 = (bf16[2,176,256]{2,1,0:T(8,128)(2,1)}, bf16[2,176,256]{2,1,0:T(8,128)(2,1)}, bf16[2,176,256]{2,1,0:T(8,128)(2,1)}, bf16[2,176...) fusion(bf16[2,176,2048]{2,1,0:T(8,128)(2,1)} %param.25, ...), kind=kLoop, calls=%fused_computation.126 | loop fusion | bytes 2523164 | tf_op jit(solution)/shard_map/dynamic_slice | solution.py:147
  50.6 1.2 copy.102
  51.9 3.2 %gather_fusion.3 = bf16[8,2,256,176]{2,3,1,0:T(8,128)(2,1)} fusion(bf16[2,8,256,176]{2,3,1,0:T(8,128)(2,1)} %bitcast.160, s32[1024]{0:T(1024)S(1)} %get-tuple-element.25), kind=kCustom, calls=%fused_computation.clone | custom fusion | bytes 2883616 | tf_op jit(solution)/shard_map/jit(_take)/gather | solution.py:119
  55.1 1.7 gather_fusion.4
  56.8 13.4 %collective-permute-done = bf16[16,2,64,256]{3,2,0,1:T(8,128)(2,1)} collective-permute-done((bf16[16,2,64,256]{3,2,0,1:T(8,128)(2,1)}, bf16[16,2,64,256]{3,2,0,1:T(8,128)(2,1)}, u32[]{:S(2)}, u32[]{:S(2)}) %collective-permute-start) | collective-permute-done | bytes 1048608 | tf_op jit(solution)/shard_map/ppermute | solution.py:90
  70.3 1.9 slice.56
  72.2 1.9 slice.57
  74.1 3.2 %collective-permute-start.3 = (bf16[8,2,64,256]{3,2,0,1:T(8,128)(2,1)}, bf16[8,2,64,256]{3,2,0,1:T(8,128)(2,1)}, u32[]{:S(2)}, u32[]{:S(2)}) collective-permute-start(bf16[8,2,64,256]{3,2,0,1:T(8,128)(2,1)} %slice.57), channel_id=1, source_target_pairs={{0,96},{16,112},{32,0},{48,16},{64,32},{80,48},{96,64},{112,80},{1... | collective-permute-start | bytes 1572872 | tf_op jit(solution)/shard_map/ppermute | solution.py:90
  77.3 2.9 %select_bitcast_fusion = (bf16[2,8,256,176]{2,3,0,1:T(8,128)(2,1)S(1)}, bf16[2,8,256,176]{2,3,0,1:T(8,128)(2,1)}) fusion(bf16[8,2,256,176]{2,3,1,0:T(8,128)(2,1)} %gather_fusion.4, pred[8]{0:T(512)(128)(4,1)S(1)} %compare_and_fusion.1, bf16[8,2,256,176]{2,3,1,0:T(8,128)(2,1)S(1)} %copy-done.2), kind=kLoop, calls=%fused_computation.29 | loop fusion | flops 1441792 | bytes 5767176 | tf_op jit(solution)/shard_map/jit(_take)/select_n | solution.py:119
  80.2 1.3 gather_fusion.1
  81.5 1.9 bitcast_select_fusion
  84.3 2.2 copy.71
  86.6 1.6 reshape.180
  88.1 0.8 copy.77
  89.9 1.1 pad_maximum_fusion
  91.8 2.3 %constant_dynamic-update-slice_fusion.7 = bf16[16,2,64,2048]{3,2,0,1:T(8,128)(2,1)} fusion(bf16[16,2,64,2048]{3,2,0,1:T(8,128)(2,1)} %get-tuple-element.22, bf16[16,2,64,256]{3,2,0,1:T(8,128)(2,1)} %collective-permute-done), kind=kLoop, calls=%fused_computation.105 | loop fusion | bytes 2097152
  94.2 2.4 %constant_dynamic-update-slice_fusion.6 = bf16[16,2,64,2048]{3,2,0,1:T(8,128)(2,1)} fusion(bf16[16,2,64,2048]{3,2,0,1:T(8,128)(2,1)} %constant_dynamic-update-slice_fusion.7, bf16[16,2,64,256]{3,2,0,1:T(8,128)(2,1)} %collective-permute-done.1), kind=kLoop, calls=%fused_computation.104 | loop fusion | bytes 2097152
  96.5 0.9 constant_dynamic-update-slice_fusion.5
  97.4 1.9 constant_dynamic-update-slice_fusion.4
  99.4 2.4 %constant_dynamic-update-slice_fusion.3 = bf16[16,2,64,2048]{3,2,0,1:T(8,128)(2,1)} fusion(bf16[16,2,64,2048]{3,2,0,1:T(8,128)(2,1)} %constant_dynamic-update-slice_fusion.4, bf16[16,2,64,256]{3,2,0,1:T(8,128)(2,1)} %collective-permute-done.4), kind=kLoop, calls=%fused_computation.101 | loop fusion | bytes 2097152
  101.7 2.3 %constant_dynamic-update-slice_fusion.2 = bf16[16,2,64,2048]{3,2,0,1:T(8,128)(2,1)} fusion(bf16[16,2,64,2048]{3,2,0,1:T(8,128)(2,1)} %constant_dynamic-update-slice_fusion.3, bf16[16,2,64,256]{3,2,0,1:T(8,128)(2,1)} %collective-permute-done.5), kind=kLoop, calls=%fused_computation.100 | loop fusion | bytes 2097152
  104.1 1.1 constant_dynamic-update-slice_fusion.1
  105.2 1.1 constant_dynamic-update-slice_fusion
  106.3 5.9 %fusion.11 = f32[2,176,16,64]{1,3,2,0:T(8,128)S(1)} fusion(bf16[16,2,64,2048]{3,2,0,1:T(8,128)(2,1)} %constant_dynamic-update-slice_fusion, bf16[2,2048,176,1]{1,2,0,3:T(8,128)(2,1)S(1)} %copy-done.7), kind=kOutput, calls=%fused_computation.27 | convolution fusion | flops 1476395008 | bytes 11272192 | tf_op jit(solution)/shard_map/sexd,edf->sexf/dot_general | solution.py:120
  112.4 3.6 %fusion.6 = bf16[16,2,64,176]{3,2,0,1:T(8,128)(2,1)} fusion(f32[2,176,16,64]{1,3,2,0:T(8,128)S(1)} %fusion.11, bf16[16,2,64,2048]{3,2,0,1:T(8,128)(2,1)S(1)} %copy-done.14, bf16[2,2048,176,1]{1,2,0,3:T(8,128)(2,1)S(1)} %reshape.181), kind=kOutput, calls=%fused_computation.18 | convolution fusion | flops 1478557696 | bytes 11993088 | tf_op jit(solution)/shard_map/sexd,edf->sexf/dot_general | solution.py:120
  116.0 3.2 %collective-permute-start.13 = (bf16[16,2,64,176]{3,2,0,1:T(8,128)(2,1)}, bf16[16,2,64,176]{3,2,0,1:T(8,128)(2,1)S(1)}, u32[]{:S(2)}, u32[]{:S(2)}) collective-permute-start(bf16[16,2,64,176]{3,2,0,1:T(8,128)(2,1)} %fusion.6), channel_id=1, source_target_pairs={{0,96},{16,112},{32,0},{48,16},{64,32},{80,48},{96,64},{112,80},{1... | collective-permute-start | bytes 2162696 | tf_op jit(solution)/shard_map/ppermute | solution.py:90
  119.2 3.1 %fusion.43 = f32[2,256,16,64]{1,3,2,0:T(8,128)} fusion(bf16[16,2,64,176]{3,2,0,1:T(8,128)(2,1)} %fusion.6, bf16[2,176,2048]{2,1,0:T(8,128)(2,1)} %param.25, s32[]{:T(128)S(6)} %select_n.155), kind=kOutput, calls=%fused_computation.71 | convolution fusion | flops 184549376 | bytes 3325956 | tf_op jit(solution)/shard_map/sexf,efd->sexd/dot_general | solution.py:158
  122.3 1.6 fusion.25
  123.9 2.0 fusion.18
  126.0 4.1 %fusion.3 = f32[256,704]{0,1:T(8,128)} fusion(bf16[3,2048,704]{1,2,0:T(8,128)(2,1)} %all-gather.5.cloned.1.call-done, bf16[512,2048]{1,0:T(8,128)(2,1)} %all-gather.3.cloned.1.call-done), kind=kOutput, calls=%fused_computation.12 | convolution fusion | flops 738197504 | bytes 4653056 | tf_op jit(solution)/shard_map/dot_general | solution.py:129
  130.1 3.7 %fusion.2 = f32[256,704]{0,1:T(8,128)} fusion(bf16[3,2048,704]{1,2,0:T(8,128)(2,1)} %all-gather.5.cloned.1.call-done, bf16[512,2048]{1,0:T(8,128)(2,1)S(1)} %copy-done.24), kind=kOutput, calls=%fused_computation.10 | convolution fusion | flops 738197504 | bytes 4653056 | tf_op jit(solution)/shard_map/dot_general | solution.py:130
  133.8 5.0 %fusion.4 = f32[256,2048]{1,0:T(8,128)} fusion(bf16[3,2048,704]{1,2,0:T(8,128)(2,1)} %all-gather.5.cloned.1.call-done, f32[256,704]{0,1:T(8,128)} %fusion.2, bf16[256,256]{1,0:T(8,128)(2,1)S(1)} %fusion.18, bf16[256,704]{1,0:T(8,128)(2,1)S(1)} %copy-done.8, f32[256]{0:T(256)S(1)} %add_divide_fusion, f32[256,704]{0,1:T(8,128)} %fusion.3), kind=kOutput, calls=%fused_computation.13 | convolution fusion | flops 832438272 | bytes 6915072 | tf_op jit(solution)/shard_map/dot_general | solution.py:134
  138.8 4.3 %collective-permute-done.12 = bf16[16,2,64,176]{3,2,0,1:T(8,128)(2,1)S(1)} collective-permute-done((bf16[16,2,64,176]{3,2,0,1:T(8,128)(2,1)}, bf16[16,2,64,176]{3,2,0,1:T(8,128)(2,1)S(1)}, u32[]{:S(2)}, u32[]{:S(2)}) %collective-permute-start.12) | collective-permute-done | bytes 720928 | tf_op jit(solution)/shard_map/ppermute | solution.py:90
  143.0 2.8 %collective-permute-start.19 = (bf16[2,176,256]{2,1,0:T(8,128)(2,1)S(1)}, bf16[2,176,256]{2,1,0:T(8,128)(2,1)S(1)}, u32[]{:S(2)}, u32[]{:S(2)}) collective-permute-start(bf16[2,176,256]{2,1,0:T(8,128)(2,1)S(1)} %copy-done.12), channel_id=1, source_target_pairs={{0,64},{16,80},{32,96},{48,112},{64,0},{80,16},{96,32},{112,48},{1... | collective-permute-start | bytes 540680 | tf_op jit(solution)/shard_map/ppermute | solution.py:90
  145.8 0.9 slice.42
  146.7 1.0 collective-permute-start.11
  148.0 3.1 %fusion.41 = f32[2,256,16,64]{1,3,2,0:T(8,128)} fusion(bf16[16,2,64,176]{3,2,0,1:T(8,128)(2,1)} %collective-permute-done.10, bf16[2,176,256]{2,1,0:T(8,128)(2,1)S(1)} %collective-permute-done.8, bf16[2,176,256]{2,1,0:T(8,128)(2,1)} %collective-permute-done.9, pred[]{:T(512)S(6)} %eq.74), kind=kOutput, calls=%fused_computation.69 | convolution fusion | flops 184639488 | bytes 3178497 | tf_op jit(solution)/shard_map/sexf,efd->sexd/dot_general | solution.py:158
  151.1 0.9 slice.43
  152.0 5.1 %collective-permute-done.11 = bf16[2,176,256]{2,1,0:T(8,128)(2,1)} collective-permute-done((bf16[2,176,256]{2,1,0:T(8,128)(2,1)S(1)}, bf16[2,176,256]{2,1,0:T(8,128)(2,1)}, u32[]{:S(2)}, u32[]{:S(2)}) %collective-permute-start.11) | collective-permute-done | bytes 180256 | tf_op jit(solution)/shard_map/ppermute | solution.py:90
  157.2 2.3 %collective-permute-start.22 = (bf16[8,2,64,176]{3,2,0,1:T(8,128)(2,1)}, bf16[8,2,64,176]{3,2,0,1:T(8,128)(2,1)S(1)}, u32[]{:S(2)}, u32[]{:S(2)}) collective-permute-start(bf16[8,2,64,176]{3,2,0,1:T(8,128)(2,1)} %slice.43), channel_id=1, source_target_pairs={{0,96},{16,112},{32,0},{48,16},{64,32},{80,48},{96,64},{112,80},{1... | collective-permute-start | bytes 1081352 | tf_op jit(solution)/shard_map/ppermute | solution.py:90
  159.5 1.3 fusion.39
  160.9 11.6 %collective-permute-done.20 = bf16[8,2,64,176]{3,2,0,1:T(8,128)(2,1)} collective-permute-done((bf16[8,2,64,176]{3,2,0,1:T(8,128)(2,1)}, bf16[8,2,64,176]{3,2,0,1:T(8,128)(2,1)}, u32[]{:S(2)}, u32[]{:S(2)}) %collective-permute-start.20) | collective-permute-done | bytes 360480 | tf_op jit(solution)/shard_map/ppermute | solution.py:90
  172.5 1.3 fusion.49
  173.9 3.5 %collective-permute-done.22 = bf16[8,2,64,176]{3,2,0,1:T(8,128)(2,1)S(1)} collective-permute-done((bf16[8,2,64,176]{3,2,0,1:T(8,128)(2,1)}, bf16[8,2,64,176]{3,2,0,1:T(8,128)(2,1)S(1)}, u32[]{:S(2)}, u32[]{:S(2)}) %collective-permute-start.22) | collective-permute-done | bytes 360480 | tf_op jit(solution)/shard_map/ppermute | solution.py:90
  178.3 1.7 fusion.34
  181.1 3.7 %collective-permute-done.16 = bf16[2,176,256]{2,1,0:T(8,128)(2,1)S(1)} collective-permute-done((bf16[2,176,256]{2,1,0:T(8,128)(2,1)S(1)}, bf16[2,176,256]{2,1,0:T(8,128)(2,1)S(1)}, u32[]{:S(2)}, u32[]{:S(2)}) %collective-permute-start.16) | collective-permute-done | bytes 180256 | tf_op jit(solution)/shard_map/ppermute | solution.py:90
  184.8 1.0 fusion.5
  185.9 1.1 copy.79
  187.0 3.8 %all-to-all-start.1 = ((bf16[16,2,64,256]{3,2,1,0:T(8,128)(2,1)}), bf16[16,2,64,256]{3,2,1,0:T(8,128)(2,1)S(1)}, u32[]{:S(2)}, u32[]{:S(2)}) async-start(bf16[16,2,64,256]{3,2,1,0:T(8,128)(2,1)} %copy.79), calls=%async_computation.1 | async-start | bytes 2097152 | tf_op jit(solution)/shard_map/all_to_all | solution.py:173
  191.3 1.6 fusion.30
  193.2 13.3 %all-to-all-done.1 = bf16[16,2,64,256]{3,2,1,0:T(8,128)(2,1)S(1)} async-done(((bf16[16,2,64,256]{3,2,1,0:T(8,128)(2,1)}), bf16[16,2,64,256]{3,2,1,0:T(8,128)(2,1)S(1)}, u32[]{:S(2)}, u32[]{:S(2)}) %all-to-all-start.1) | async-done | bytes 1048608 | tf_op jit(solution)/shard_map/all_to_all | solution.py:173
  206.5 1.6 bitcast_convert_fusion
  208.1 5.2 %gather_fusion.2 = f32[1024,256]{1,0:T(8,128)S(1)} fusion(f32[2048,256]{1,0:T(8,128)} %bitcast_convert_fusion, s32[1024]{0:T(1024)S(1)} %broadcast_clamp_fusion), kind=kCustom, calls=%fused_computation.4 | custom fusion | bytes 2101248 | tf_op jit(solution)/shard_map/jit(_take)/gather | solution.py:177
  213.2 1.3 reshape.163
  214.5 2.5 %multiply_reduce_fusion = f32[256,256]{1,0:T(8,128)S(1)} fusion(f32[256,4,256]{2,1,0:T(4,128)} %reshape.163, f32[256,4]{1,0:T(8,128)S(1)} %copy.66, pred[256,4]{1,0:T(8,128)(4,1)S(1)} %copy.69), kind=kLoop, calls=%fused_computation.44 | loop fusion | flops 720896 | bytes 1315840 | tf_op jit(solution)/shard_map/reduce_sum | solution.py:178
  217.1 1.7 add.206
  (139 shorter events, 10.0 us)
Async XLA Ops:
  6.5 73.7 %copy-start = (bf16[64,16,704]{2,1,0:T(8,128)(2,1)S(1)}, bf16[64,16,704]{2,1,0:T(8,128)(2,1)}, u32[]{:S(2)}) copy-start(bf16[64,16,704]{2,1,0:T(8,128)(2,1)} %param.27) | copy-start | bytes 4325380
  6.5 11.5 %copy-start.15 = (bf16[256,256]{1,0:T(8,128)(2,1)S(1)}, bf16[256,256]{1,0:T(8,128)(2,1)}, u32[]{:S(2)}) copy-start(bf16[256,256]{1,0:T(8,128)(2,1)} %param.17) | copy-start | bytes 393220
  6.5 7.3 %copy-start.16 = (s32[256,4]{0,1:T(4,128)S(1)}, s32[256,4]{0,1:T(4,128)}, u32[]{:S(2)}) copy-start(s32[256,4]{0,1:T(4,128)} %param.28) | copy-start | bytes 12292
  6.5 115.7 %all-gather.3.cloned.1.call-start = ((), (), s32[]{:S(2)}) async-start(), calls=%async_computation.3 | async-start | bytes 2359296 | tf_op jit(solution)/shard_map/all_gather | solution.py:34
  11.7 114.2 %all-gather.5.cloned.1.call-start = ((), (), s32[]{:S(2)}) async-start(), calls=%async_computation.4 | async-start | bytes 9191424 | tf_op jit(solution)/shard_map/all_gather | solution.py:53
  13.8 203.3 %reduce-scatter.2.cloned.1.call-start = ((), (), s32[]{:S(2)}) async-start(), calls=%async_computation.5 | async-start | bytes 2359296 | tf_op jit(solution)/shard_map/reduce_scatter | solution.py:142
  15.4 26.9 %copy-start.18 = (s32[256,4]{0,1:T(4,128)}, s32[256,4]{0,1:T(4,128)S(1)}, u32[]{:S(2)}) copy-start(s32[256,4]{0,1:T(4,128)S(1)} %get-tuple-element.13) | copy-start | bytes 12292
  43.9 6.6 %copy-start.5 = (bf16[2,2048,176]{1,2,0:T(8,128)(2,1)S(1)}, bf16[2,2048,176]{1,2,0:T(8,128)(2,1)}, u32[]{:S(2)}) copy-start(bf16[2,2048,176]{1,2,0:T(8,128)(2,1)} %param.23) | copy-start | bytes 4325380
  43.9 26.3 %collective-permute-start = (bf16[16,2,64,256]{3,2,0,1:T(8,128)(2,1)}, bf16[16,2,64,256]{3,2,0,1:T(8,128)(2,1)}, u32[]{:S(2)}, u32[]{:S(2)}) collective-permute-start(bf16[16,2,64,256]{3,2,0,1:T(8,128)(2,1)} %get-tuple-element.21), channel_id=1, source_target_pairs={{0,32},{16,48},{32,64},{48,80},{64,96},{80,112},{96,0},{112,16},{1... | collective-permute-start | bytes 3145736 | tf_op jit(solution)/shard_map/ppermute | solution.py:90
  45.9 26.3 %collective-permute-start.1 = (bf16[16,2,64,256]{3,2,0,1:T(8,128)(2,1)}, bf16[16,2,64,256]{3,2,0,1:T(8,128)(2,1)}, u32[]{:S(2)}, u32[]{:S(2)}) collective-permute-start(bf16[16,2,64,256]{3,2,0,1:T(8,128)(2,1)} %get-tuple-element.21), channel_id=1, source_target_pairs={{0,96},{16,112},{32,0},{48,16},{64,32},{80,48},{96,64},{112,80},{1... | collective-permute-start | bytes 3145736 | tf_op jit(solution)/shard_map/ppermute | solution.py:90
  48.0 3.8 %copy-start.6 = (bf16[2,2048,176]{1,2,0:T(8,128)(2,1)S(1)}, bf16[2,2048,176]{1,2,0:T(8,128)(2,1)}, u32[]{:S(2)}) copy-start(bf16[2,2048,176]{1,2,0:T(8,128)(2,1)} %param.24) | copy-start | bytes 4325380
  50.5 96.2 %collective-permute-start.9 = (bf16[2,176,256]{2,1,0:T(8,128)(2,1)}, bf16[2,176,256]{2,1,0:T(8,128)(2,1)}, u32[]{:S(2)}, u32[]{:S(2)}) collective-permute-start(bf16[2,176,256]{2,1,0:T(8,128)(2,1)} %get-tuple-element.17), channel_id=1, source_target_pairs={{0,112},{16,0},{32,16},{48,32},{64,48},{80,64},{96,80},{112,96},{1... | collective-permute-start | bytes 540680 | tf_op jit(solution)/shard_map/ppermute | solution.py:90
  56.8 20.5 %copy-start.2 = (bf16[8,2,256,176]{2,3,1,0:T(8,128)(2,1)S(1)}, bf16[8,2,256,176]{2,3,1,0:T(8,128)(2,1)}, u32[]{:S(2)}) copy-start(bf16[8,2,256,176]{2,3,1,0:T(8,128)(2,1)} %gather_fusion.3) | copy-start | bytes 4325380
  72.2 17.7 %collective-permute-start.2 = (bf16[8,2,64,256]{3,2,0,1:T(8,128)(2,1)}, bf16[8,2,64,256]{3,2,0,1:T(8,128)(2,1)S(1)}, u32[]{:S(2)}, u32[]{:S(2)}) collective-permute-start(bf16[8,2,64,256]{3,2,0,1:T(8,128)(2,1)} %slice.56), channel_id=1, source_target_pairs={{0,32},{16,48},{32,64},{48,80},{64,96},{80,112},{96,0},{112,16},{1... | collective-permute-start | bytes 1572872 | tf_op jit(solution)/shard_map/ppermute | solution.py:90
  74.1 9.3 %copy-start.22 = (s32[1,16]{1,0:T(1,128)S(1)}, s32[1,16]{1,0:T(1,128)}, u32[]{:S(2)}) copy-start(s32[1,16]{1,0:T(1,128)} %param.29) | copy-start | bytes 196
  74.1 15.8 %collective-permute-start.3 = (bf16[8,2,64,256]{3,2,0,1:T(8,128)(2,1)}, bf16[8,2,64,256]{3,2,0,1:T(8,128)(2,1)}, u32[]{:S(2)}, u32[]{:S(2)}) collective-permute-start(bf16[8,2,64,256]{3,2,0,1:T(8,128)(2,1)} %slice.57), channel_id=1, source_target_pairs={{0,96},{16,112},{32,0},{48,16},{64,32},{80,48},{96,64},{112,80},{1... | collective-permute-start | bytes 1572872 | tf_op jit(solution)/shard_map/ppermute | solution.py:90
  81.5 17.8 %collective-permute-start.4 = (bf16[16,2,64,256]{3,2,0,1:T(8,128)(2,1)}, bf16[16,2,64,256]{3,2,0,1:T(8,128)(2,1)}, u32[]{:S(2)}, u32[]{:S(2)}) collective-permute-start(bf16[16,2,64,256]{3,2,0,1:T(8,128)(2,1)} %get-tuple-element.21), channel_id=1, source_target_pairs={{0,16},{16,0},{32,48},{48,32},{64,80},{80,64},{96,112},{112,96},{1... | collective-permute-start | bytes 3145736 | tf_op jit(solution)/shard_map/ppermute | solution.py:93
  83.7 18.1 %collective-permute-start.5 = (bf16[16,2,64,256]{3,2,0,1:T(8,128)(2,1)}, bf16[16,2,64,256]{3,2,0,1:T(8,128)(2,1)}, u32[]{:S(2)}, u32[]{:S(2)}) collective-permute-start(bf16[16,2,64,256]{3,2,0,1:T(8,128)(2,1)} %collective-permute-done), channel_id=1, source_target_pairs={{0,16},{16,0},{32,48},{48,32},{64,80},{80,64},{96,112},{112,96},{1... | collective-permute-start | bytes 3145736 | tf_op jit(solution)/shard_map/ppermute | solution.py:93
  89.0 0.7 copy-start.20
  89.0 0.8 copy-start.23
  89.8 14.3 %collective-permute-start.6 = (bf16[16,2,64,256]{3,2,0,1:T(8,128)(2,1)}, bf16[16,2,64,256]{3,2,0,1:T(8,128)(2,1)S(1)}, u32[]{:S(2)}, u32[]{:S(2)}) collective-permute-start(bf16[16,2,64,256]{3,2,0,1:T(8,128)(2,1)} %collective-permute-done.1), channel_id=1, source_target_pairs={{0,16},{16,0},{32,48},{48,32},{64,80},{80,64},{96,112},{112,96},{1... | collective-permute-start | bytes 3145736 | tf_op jit(solution)/shard_map/ppermute | solution.py:93
  91.1 14.1 %collective-permute-start.7 = (bf16[16,2,64,256]{3,2,0,1:T(8,128)(2,1)S(1)}, bf16[16,2,64,256]{3,2,0,1:T(8,128)(2,1)S(1)}, u32[]{:S(2)}, u32[]{:S(2)}) collective-permute-start(bf16[16,2,64,256]{3,2,0,1:T(8,128)(2,1)S(1)} %pad_maximum_fusion), channel_id=1, source_target_pairs={{0,16},{16,0},{32,48},{48,32},{64,80},{80,64},{96,112},{112,96},{1... | collective-permute-start | bytes 3145736 | tf_op jit(solution)/shard_map/ppermute | solution.py:93
  99.3 48.4 %collective-permute-start.8 = (bf16[2,176,256]{2,1,0:T(8,128)(2,1)}, bf16[2,176,256]{2,1,0:T(8,128)(2,1)S(1)}, u32[]{:S(2)}, u32[]{:S(2)}) collective-permute-start(bf16[2,176,256]{2,1,0:T(8,128)(2,1)} %get-tuple-element.18), channel_id=1, source_target_pairs={{0,16},{16,32},{32,48},{48,64},{64,80},{80,96},{96,112},{112,0},{1... | collective-permute-start | bytes 540680 | tf_op jit(solution)/shard_map/ppermute | solution.py:90
  104.1 2.2 copy-start.7
  106.3 6.1 %copy-start.14 = (bf16[16,2,64,2048]{3,2,0,1:T(8,128)(2,1)S(1)}, bf16[16,2,64,2048]{3,2,0,1:T(8,128)(2,1)}, u32[]{:S(2)}) copy-start(bf16[16,2,64,2048]{3,2,0,1:T(8,128)(2,1)} %constant_dynamic-update-slice_fusion) | copy-start | bytes 25165828
  116.0 27.0 %collective-permute-start.12 = (bf16[16,2,64,176]{3,2,0,1:T(8,128)(2,1)}, bf16[16,2,64,176]{3,2,0,1:T(8,128)(2,1)S(1)}, u32[]{:S(2)}, u32[]{:S(2)}) collective-permute-start(bf16[16,2,64,176]{3,2,0,1:T(8,128)(2,1)} %fusion.6), channel_id=1, source_target_pairs={{0,32},{16,48},{32,64},{48,80},{64,96},{80,112},{96,0},{112,16},{1... | collective-permute-start | bytes 2162696 | tf_op jit(solution)/shard_map/ppermute | solution.py:90
  116.0 27.0 %collective-permute-start.13 = (bf16[16,2,64,176]{3,2,0,1:T(8,128)(2,1)}, bf16[16,2,64,176]{3,2,0,1:T(8,128)(2,1)S(1)}, u32[]{:S(2)}, u32[]{:S(2)}) collective-permute-start(bf16[16,2,64,176]{3,2,0,1:T(8,128)(2,1)} %fusion.6), channel_id=1, source_target_pairs={{0,96},{16,112},{32,0},{48,16},{64,32},{80,48},{96,64},{112,80},{1... | collective-permute-start | bytes 2162696 | tf_op jit(solution)/shard_map/ppermute | solution.py:90
  119.2 28.8 %collective-permute-start.10 = (bf16[16,2,64,176]{3,2,0,1:T(8,128)(2,1)}, bf16[16,2,64,176]{3,2,0,1:T(8,128)(2,1)}, u32[]{:S(2)}, u32[]{:S(2)}) collective-permute-start(bf16[16,2,64,176]{3,2,0,1:T(8,128)(2,1)} %fusion.6), channel_id=1, source_target_pairs={{0,16},{16,0},{32,48},{48,32},{64,80},{80,64},{96,112},{112,96},{1... | collective-permute-start | bytes 2162696 | tf_op jit(solution)/shard_map/ppermute | solution.py:93
  126.0 4.1 %copy-start.24 = (bf16[512,2048]{1,0:T(8,128)(2,1)S(1)}, bf16[512,2048]{1,0:T(8,128)(2,1)}, u32[]{:S(2)}) copy-start(bf16[512,2048]{1,0:T(8,128)(2,1)} %all-gather.3.cloned.1.call-done) | copy-start | bytes 6291460
  130.1 3.7 %copy-start.8 = (bf16[256,704]{1,0:T(8,128)(2,1)S(1)}, bf16[256,704]{1,0:T(8,128)(2,1)}, u32[]{:S(2)}) copy-start(bf16[256,704]{1,0:T(8,128)(2,1)} %bitcast_select_fusion) | copy-start | bytes 1081348
  133.8 9.2 %copy-start.11 = (bf16[2,176,256]{2,1,0:T(8,128)(2,1)S(1)}, bf16[2,176,256]{2,1,0:T(8,128)(2,1)}, u32[]{:S(2)}) copy-start(bf16[2,176,256]{2,1,0:T(8,128)(2,1)} %get-tuple-element.20) | copy-start | bytes 540676
  133.8 9.2 %copy-start.12 = (bf16[2,176,256]{2,1,0:T(8,128)(2,1)S(1)}, bf16[2,176,256]{2,1,0:T(8,128)(2,1)}, u32[]{:S(2)}) copy-start(bf16[2,176,256]{2,1,0:T(8,128)(2,1)} %get-tuple-element.19) | copy-start | bytes 540676
  133.8 12.9 %copy-start.13 = (bf16[2,176,256]{2,1,0:T(8,128)(2,1)S(1)}, bf16[2,176,256]{2,1,0:T(8,128)(2,1)}, u32[]{:S(2)}) copy-start(bf16[2,176,256]{2,1,0:T(8,128)(2,1)} %get-tuple-element.16) | copy-start | bytes 540676
  143.0 34.7 %collective-permute-start.17 = (bf16[2,176,256]{2,1,0:T(8,128)(2,1)S(1)}, bf16[2,176,256]{2,1,0:T(8,128)(2,1)S(1)}, u32[]{:S(2)}, u32[]{:S(2)}) collective-permute-start(bf16[2,176,256]{2,1,0:T(8,128)(2,1)S(1)} %copy-done.11), channel_id=1, source_target_pairs={{0,80},{16,96},{32,112},{48,0},{64,16},{80,32},{96,48},{112,64},{1... | collective-permute-start | bytes 540680 | tf_op jit(solution)/shard_map/ppermute | solution.py:90
  143.0 17.8 %collective-permute-start.19 = (bf16[2,176,256]{2,1,0:T(8,128)(2,1)S(1)}, bf16[2,176,256]{2,1,0:T(8,128)(2,1)S(1)}, u32[]{:S(2)}, u32[]{:S(2)}) collective-permute-start(bf16[2,176,256]{2,1,0:T(8,128)(2,1)S(1)} %copy-done.12), channel_id=1, source_target_pairs={{0,64},{16,80},{32,96},{48,112},{64,0},{80,16},{96,32},{112,48},{1... | collective-permute-start | bytes 540680 | tf_op jit(solution)/shard_map/ppermute | solution.py:90
  146.7 10.4 %collective-permute-start.11 = (bf16[2,176,256]{2,1,0:T(8,128)(2,1)S(1)}, bf16[2,176,256]{2,1,0:T(8,128)(2,1)}, u32[]{:S(2)}, u32[]{:S(2)}) collective-permute-start(bf16[2,176,256]{2,1,0:T(8,128)(2,1)S(1)} %copy-done.13), channel_id=1, source_target_pairs={{0,32},{16,48},{32,64},{48,80},{64,96},{80,112},{96,0},{112,16},{1... | collective-permute-start | bytes 540680 | tf_op jit(solution)/shard_map/ppermute | solution.py:90
  147.7 24.8 %collective-permute-start.20 = (bf16[8,2,64,176]{3,2,0,1:T(8,128)(2,1)}, bf16[8,2,64,176]{3,2,0,1:T(8,128)(2,1)}, u32[]{:S(2)}, u32[]{:S(2)}) collective-permute-start(bf16[8,2,64,176]{3,2,0,1:T(8,128)(2,1)} %slice.42), channel_id=1, source_target_pairs={{0,32},{16,48},{32,64},{48,80},{64,96},{80,112},{96,0},{112,16},{1... | collective-permute-start | bytes 1081352 | tf_op jit(solution)/shard_map/ppermute | solution.py:90
  151.1 26.7 %collective-permute-start.18 = (bf16[16,2,64,176]{3,2,0,1:T(8,128)(2,1)S(1)}, bf16[16,2,64,176]{3,2,0,1:T(8,128)(2,1)}, u32[]{:S(2)}, u32[]{:S(2)}) collective-permute-start(bf16[16,2,64,176]{3,2,0,1:T(8,128)(2,1)S(1)} %collective-permute-done.13), channel_id=1, source_target_pairs={{0,16},{16,0},{32,48},{48,32},{64,80},{80,64},{96,112},{112,96},{1... | collective-permute-start | bytes 2162696 | tf_op jit(solution)/shard_map/ppermute | solution.py:93
  152.0 8.8 %copy-start.10 = (bf16[2,176,256]{2,1,0:T(8,128)(2,1)S(1)}, bf16[2,176,256]{2,1,0:T(8,128)(2,1)}, u32[]{:S(2)}) copy-start(bf16[2,176,256]{2,1,0:T(8,128)(2,1)} %get-tuple-element.15) | copy-start | bytes 540676
  152.0 25.4 %copy-start.9 = (bf16[2,176,256]{2,1,0:T(8,128)(2,1)S(1)}, bf16[2,176,256]{2,1,0:T(8,128)(2,1)}, u32[]{:S(2)}) copy-start(bf16[2,176,256]{2,1,0:T(8,128)(2,1)} %get-tuple-element.14) | copy-start | bytes 540676
  157.2 20.2 %collective-permute-start.22 = (bf16[8,2,64,176]{3,2,0,1:T(8,128)(2,1)}, bf16[8,2,64,176]{3,2,0,1:T(8,128)(2,1)S(1)}, u32[]{:S(2)}, u32[]{:S(2)}) collective-permute-start(bf16[8,2,64,176]{3,2,0,1:T(8,128)(2,1)} %slice.43), channel_id=1, source_target_pairs={{0,96},{16,112},{32,0},{48,16},{64,32},{80,48},{96,64},{112,80},{1... | collective-permute-start | bytes 1081352 | tf_op jit(solution)/shard_map/ppermute | solution.py:90
  160.8 19.1 %collective-permute-start.14 = (bf16[2,176,256]{2,1,0:T(8,128)(2,1)S(1)}, bf16[2,176,256]{2,1,0:T(8,128)(2,1)S(1)}, u32[]{:S(2)}, u32[]{:S(2)}) collective-permute-start(bf16[2,176,256]{2,1,0:T(8,128)(2,1)S(1)} %copy-done.10), channel_id=1, source_target_pairs={{0,48},{16,64},{32,80},{48,96},{64,112},{80,0},{96,16},{112,32},{1... | collective-permute-start | bytes 540680 | tf_op jit(solution)/shard_map/ppermute | solution.py:90
  172.5 7.5 %collective-permute-start.15 = (bf16[16,2,64,176]{3,2,0,1:T(8,128)(2,1)S(1)}, bf16[16,2,64,176]{3,2,0,1:T(8,128)(2,1)S(1)}, u32[]{:S(2)}, u32[]{:S(2)}) collective-permute-start(bf16[16,2,64,176]{3,2,0,1:T(8,128)(2,1)S(1)} %collective-permute-done.12), channel_id=1, source_target_pairs={{0,16},{16,0},{32,48},{48,32},{64,80},{80,64},{96,112},{112,96},{1... | collective-permute-start | bytes 2162696 | tf_op jit(solution)/shard_map/ppermute | solution.py:93
  177.4 7.4 %collective-permute-start.16 = (bf16[2,176,256]{2,1,0:T(8,128)(2,1)S(1)}, bf16[2,176,256]{2,1,0:T(8,128)(2,1)S(1)}, u32[]{:S(2)}, u32[]{:S(2)}) collective-permute-start(bf16[2,176,256]{2,1,0:T(8,128)(2,1)S(1)} %copy-done.9), channel_id=1, source_target_pairs={{0,96},{16,112},{32,0},{48,16},{64,32},{80,48},{96,64},{112,80},{1... | collective-permute-start | bytes 540680 | tf_op jit(solution)/shard_map/ppermute | solution.py:90
  177.7 2.8 %collective-permute-start.21 = (bf16[8,2,64,176]{3,2,0,1:T(8,128)(2,1)}, bf16[8,2,64,176]{3,2,0,1:T(8,128)(2,1)S(1)}, u32[]{:S(2)}, u32[]{:S(2)}) collective-permute-start(bf16[8,2,64,176]{3,2,0,1:T(8,128)(2,1)} %collective-permute-done.20), channel_id=1, source_target_pairs={{0,16},{16,0},{32,48},{48,32},{64,80},{80,64},{96,112},{112,96},{1... | collective-permute-start | bytes 1081352 | tf_op jit(solution)/shard_map/ppermute | solution.py:93
  177.8 3.0 %collective-permute-start.23 = (bf16[8,2,64,176]{3,2,0,1:T(8,128)(2,1)S(1)}, bf16[8,2,64,176]{3,2,0,1:T(8,128)(2,1)S(1)}, u32[]{:S(2)}, u32[]{:S(2)}) collective-permute-start(bf16[8,2,64,176]{3,2,0,1:T(8,128)(2,1)S(1)} %collective-permute-done.22), channel_id=1, source_target_pairs={{0,16},{16,0},{32,48},{48,32},{64,80},{80,64},{96,112},{112,96},{1... | collective-permute-start | bytes 1081352 | tf_op jit(solution)/shard_map/ppermute | solution.py:93
  180.5 4.4 %copy-start.4 = (f32[2,256,16,64]{1,3,2,0:T(8,128)S(1)}, f32[2,256,16,64]{1,3,2,0:T(8,128)}, u32[]{:S(2)}) copy-start(f32[2,256,16,64]{1,3,2,0:T(8,128)} %fusion.41) | copy-start | bytes 6291460
  180.8 4.0 %copy-start.3 = (f32[2,256,16,64]{1,3,2,0:T(8,128)S(1)}, f32[2,256,16,64]{1,3,2,0:T(8,128)}, u32[]{:S(2)}) copy-start(f32[2,256,16,64]{1,3,2,0:T(8,128)} %fusion.43) | copy-start | bytes 6291460
  185.8 4.9 %copy-start.19 = (s32[256,4]{0,1:T(4,128)S(1)}, s32[256,4]{0,1:T(4,128)}, u32[]{:S(2)}) copy-start(s32[256,4]{0,1:T(4,128)} %copy-done.18) | copy-start | bytes 12292
  185.8 5.2 %copy-start.21 = (pred[256,4]{0,1:T(4,128)(4,1)S(1)}, pred[256,4]{0,1:T(4,128)(4,1)}, u32[]{:S(2)}) copy-start(pred[256,4]{0,1:T(4,128)(4,1)} %get-tuple-element.12) | copy-start | bytes 3076
  185.9 5.4 %copy-start.25 = (bf16[2048,32]{0,1:T(8,128)(2,1)S(1)}, bf16[2048,32]{0,1:T(8,128)(2,1)}, u32[]{:S(2)}) copy-start(bf16[2048,32]{0,1:T(8,128)(2,1)} %param.18) | copy-start | bytes 393220
  187.0 5.9 %copy-start.17 = (s32[256,4]{0,1:T(4,128)S(1)}, s32[256,4]{0,1:T(4,128)}, u32[]{:S(2)}) copy-start(s32[256,4]{0,1:T(4,128)} %param.28) | copy-start | bytes 12292
  187.0 19.5 %all-to-all-start.1 = ((bf16[16,2,64,256]{3,2,1,0:T(8,128)(2,1)}), bf16[16,2,64,256]{3,2,1,0:T(8,128)(2,1)S(1)}, u32[]{:S(2)}, u32[]{:S(2)}) async-start(bf16[16,2,64,256]{3,2,1,0:T(8,128)(2,1)} %copy.79), calls=%async_computation.1 | async-start | bytes 2097152 | tf_op jit(solution)/shard_map/all_to_all | solution.py:173
  208.1 10.7 %copy-start.1 = (bf16[64,16,704]{2,1,0:T(8,128)(2,1)S(1)}, bf16[64,16,704]{2,1,0:T(8,128)(2,1)}, u32[]{:S(2)}) copy-start(bf16[64,16,704]{2,1,0:T(8,128)(2,1)} %param.27) | copy-start | bytes 4325380
Sparse Core Ops, SparseCore 0:
  11.9 29.4 all-gather.2
  43.5 79.1 all-gather.4
  152.1 37.8 reduce-scatter.1

commit v10 on v9

--- a/solution.py
+++ b/solution.py
@@ -92,18 +92,22 @@
     def partner(x):
         return lax.ppermute(x, "row", [(i, i ^ 1) for i in range(row_count)])
 
-    def row_blocks(x):
+    def row_blocks(x, tie=None):
         group_half = x.shape[0] // 2
         from_below = shifted(x, 2)
         from_above = shifted(x, -2)
+        if tie is not None:
+            tie, from_below, from_above = lax.optimization_barrier((tie, from_below, from_above))
         far = jnp.concatenate(
             [shifted(from_below[:group_half], 2), shifted(from_above[group_half:], -2)], axis=0
         )
         same = [x, from_below, from_above, far]
+        swapped = partner(jnp.stack(same))
         source = jnp.stack(
             [row_id, (row_id - 2) % row_count, (row_id + 2) % row_count, (row_id + 4) % row_count]
         ).astype(jnp.int32)
-        return same + [partner(block) for block in same], jnp.concatenate([source, source ^ 1])
+        blocks = same + [swapped[j] for j in range(len(same))]
+        return blocks, jnp.concatenate([source, source ^ 1]), tie
 
     slot_count = expert_count * capacity
     slot_id = jnp.arange(slot_count, dtype=jnp.int32)
@@ -111,7 +115,7 @@
     chosen = jnp.dot(selection, tokens, preferred_element_type=jnp.float32).astype(jnp.bfloat16)
     outgoing = chosen.reshape(col_count, local_experts, capacity, local_width)
     own_block = lax.all_to_all(outgoing, "col", split_axis=0, concat_axis=0, tiled=True)
-    slot_blocks, slot_source = row_blocks(own_block)
+    slot_blocks, slot_source, _ = row_blocks(own_block)
     slot_features = jnp.concatenate(slot_blocks, axis=3)
 
     def project(w):
@@ -122,10 +126,6 @@
     gate_part = project(routed_gate_weight)
     up_part = project(routed_up_weight)
     hidden = (jax.nn.silu(gate_part) * up_part).astype(jnp.bfloat16)
-    local_hidden = hidden.shape[3]
-    group_half = hidden.shape[0] // 2
-    from_below = shifted(hidden, 2)
-    from_above = shifted(hidden, -2)
     shared_gate_value = jnp.dot(all_features, shared_full[0], preferred_element_type=jnp.float32)
     shared_up_value = jnp.dot(all_features, shared_full[1], preferred_element_type=jnp.float32)
     shared_hidden_units = (
@@ -138,11 +138,8 @@
         preferred_element_type=jnp.float32,
     )
     shared_part = shared_part * share[:, None]
-    shared_part, from_below, from_above = lax.optimization_barrier((shared_part, from_below, from_above))
+    hidden_blocks, _, shared_part = row_blocks(hidden, tie=shared_part)
     shared_sum = lax.psum_scatter(shared_part, "row", scatter_dimension=1, tiled=True)
-    far_low = shifted(from_below[:group_half], 2)
-    far_high = shifted(from_above[group_half:], -2)
-
     def down_slice(k):
         return lax.dynamic_slice_in_dim(
             routed_down_weight, ((row_id + k) % row_count) * local_width, local_width, axis=2
@@ -154,22 +151,16 @@
     def down_pick(k_even, k_odd):
         return jnp.where(odd, down_from[k_odd], down_from[k_even])
 
-    def down_of(block, weight):
-        return jnp.einsum("sexf,efd->sexd", block, weight, preferred_element_type=jnp.float32)
-
-    whole_blocks = (
-        (hidden, down_from[0], down_pick(7, 1)),
-        (from_below, down_from[2], down_pick(1, 3)),
-        (from_above, down_from[6], down_pick(5, 7)),
+    hidden_weights = [
+        down_from[0], down_from[2], down_from[6], down_from[4],
+        down_pick(7, 1), down_pick(1, 3), down_pick(5, 7), down_pick(3, 5),
+    ]
+    expert_value = jnp.einsum(
+        "sexf,efd->sexd",
+        jnp.concatenate(hidden_blocks, axis=3),
+        jnp.concatenate(hidden_weights, axis=1),
+        preferred_element_type=jnp.float32,
     )
-    expert_value = None
-    for block, weight, partner_weight in whole_blocks:
-        term = down_of(block, weight) + down_of(partner(block), partner_weight)
-        expert_value = term if expert_value is None else expert_value + term
-    far_weight, far_partner_weight = down_from[4], down_pick(3, 5)
-    low_part = down_of(far_low, far_weight) + down_of(partner(far_low), far_partner_weight)
-    high_part = down_of(far_high, far_weight) + down_of(partner(far_high), far_partner_weight)
-    expert_value = expert_value + jnp.concatenate([low_part, high_part], axis=0)
     returned = lax.all_to_all(
         expert_value.astype(jnp.bfloat16), "col", split_axis=0, concat_axis=0, tiled=True
     ).astype(jnp.float32)

time: 227 us -> 277 us (1.22)
  waiting for transfers between devices: 55.1 us -> 81.9 us
  local copies, waits for them, and re-layouts: 47.6 us -> 65.8 us
  other arithmetic: 21.3 us -> 33.2 us
  matrix products: 40.9 us -> 31.8 us
    ppermute x15, waiting for transfers between devices: 41.7 us -> 65.9 us  [shifted(): lax.ppermute(x, 'row', [(i, (i + shift) % row_count) for i in range(row_c...]
    concatenate x1 -> x3, local copies, waits for them, and re-layouts: 0.09 us -> 12.4 us  [the longest x1 12.3 us: on_device(): jnp.concatenate(hidden_blocks, axis=3)]
    dot_general x10 -> x1, matrix products: 12.9 us -> 4.9 us  [on_device(): jnp.einsum('sexf,efd->sexd', jnp.concatenate(hidden_blocks, axis=3), jnp....]
    another operation x5 -> x8, other arithmetic: 0.79 us -> 7.76 us  [the longest x3 6.38 us: row_blocks(): swapped = partner(jnp.stack(same))]
    ppermute x15, starting transfers between devices: 17 us -> 21.7 us  [shifted(): lax.ppermute(x, 'row', [(i, (i + shift) % row_count) for i in range(row_c...]
    squeeze x0 -> x1, local copies, waits for them, and re-layouts: none -> 4.45 us  [row_blocks(): blocks = same + [swapped[j] for j in range(len(same))]]
    unnamed x60 -> x62, local copies, waits for them, and re-layouts: 13.6 us -> 16.6 us
    reshape x2, local copies, waits for them, and re-layouts: 2.3 us -> 5.16 us  [project(): ordered = jnp.take(blocks, slot_source, axis=1).reshape(w.shape)]
  transfers between devices with their start and end apart: 28 -> 21, of which waited for: 7 -> 10; matrix products, arithmetic and copies ran while one was open for 46% -> 43% of each run, Pallas kernels for 0% -> 0%
where the time goes in v10:
time: 277 us; the launch traced here: 276 us
  waiting for transfers between devices  81.9 us (30%)
  local copies, waits for them, and re-layouts  65.8 us (24%)
  other arithmetic  33.2 us (12%)
  matrix products  31.8 us (11%)
  starting transfers between devices  25.5 us (9%)
  blocking collectives  23.8 us (9%)
  between operations  13.6 us (5%)
    ppermute x15, waiting for transfers between devices, shifted(): lax.ppermute(x, 'row', [(i, (i + shift) % row_count) for i in range(row_c...  65.9 us
    all_to_all x1, blocking collectives, on_device(): lax.all_to_all(outgoing, 'col', split_axis=0, concat_axis=0, tiled=True)  23.8 us
    ppermute x15, starting transfers between devices, shifted(): lax.ppermute(x, 'row', [(i, (i + shift) % row_count) for i in range(row_c...  21.7 us
    unnamed x62, local copies, waits for them, and re-layouts  16.6 us
    all_to_all x1, waiting for transfers between devices, on_device(): lax.all_to_all(expert_value.astype(jnp.bfloat16), 'col', split_axis=0, co...  15.9 us
    concatenate x1, local copies, waits for them, and re-layouts, on_device(): jnp.concatenate(hidden_blocks, axis=3)  12.3 us
    dot_general x2, matrix products, project(): jnp.einsum('sexd,edf->sexf', slot_features, ordered, preferred_element_ty...  9.57 us
    gather x2, local copies, waits for them, and re-layouts, on_device(): routed_rows = jnp.take(flat_rows, row_index, axis=0)  6.46 us
  transfers between devices with their start and end apart: 21, of which 10 were waited for; matrix products, arithmetic and copies ran while one was open for 43% of the time, Pallas kernels for 0%

profile of v10, /device:TPU:0, one launch (start us, length us, event | category | flops | bytes accessed | tf_op | source)
XLA Modules:
  0.0 275.7 jit_solution(13505211435513526517)
XLA Ops:
  8.8 1.6 gather_fusion
  10.5 1.6 pad_maximum_fusion.3
  12.2 2.0 pad_maximum_fusion.2
  15.9 2.6 fusion
  19.0 23.8 %all_to_all.10 = bf16[16,2,64,256]{3,2,1,0:T(8,128)(2,1)S(1)} all-to-all(bf16[16,2,64,256]{3,2,1,0:T(8,128)(2,1)S(1)} %bitcast.152), channel_id=1, replica_groups=mesh['row'=8,'col'=16] {'col'}, dimensions={0} | all-to-all | bytes 2097152 | tf_op jit(solution)/shard_map/all_to_all | solution.py:117
  42.8 1.3 copy_bitcast_fusion.3
  44.1 1.9 collective-permute-start.7
  46.0 2.1 collective-permute-start.8
  48.1 22.0 %collective-permute-done.7 = bf16[16,2,64,256]{3,2,0,1:T(8,128)(2,1)S(1)} collective-permute-done((bf16[16,2,64,256]{3,2,0,1:T(8,128)(2,1)S(1)}, bf16[16,2,64,256]{3,2,0,1:T(8,128)(2,1)S(1)}, u32[]{:S(2)}, u32[]{:S(2)}) %collective-permute-start.7) | collective-permute-done | bytes 1048608 | tf_op jit(solution)/shard_map/ppermute | solution.py:90
  70.3 3.3 %collective-permute-start.10 = (bf16[8,2,64,256]{3,2,0,1:T(8,128)(2,1)S(1)}, bf16[8,2,64,256]{3,2,0,1:T(8,128)(2,1)S(1)}, u32[]{:S(2)}, u32[]{:S(2)}) collective-permute-start(bf16[8,2,64,256]{3,2,0,1:T(8,128)(2,1)S(1)} %slice.89), channel_id=1, source_target_pairs={{0,96},{16,112},{32,0},{48,16},{64,32},{80,48},{96,64},{112,80},{1... | collective-permute-start | bytes 1572872 | tf_op jit(solution)/shard_map/ppermute | solution.py:90
  73.5 9.9 %collective-permute-done.9 = bf16[8,2,64,256]{3,2,0,1:T(8,128)(2,1)S(1)} collective-permute-done((bf16[8,2,64,256]{3,2,0,1:T(8,128)(2,1)S(1)}, bf16[8,2,64,256]{3,2,0,1:T(8,128)(2,1)S(1)}, u32[]{:S(2)}, u32[]{:S(2)}) %collective-permute-start.9) | collective-permute-done | bytes 524320 | tf_op jit(solution)/shard_map/ppermute | solution.py:90
  84.4 2.3 pad_maximum_fusion
  86.7 1.2 copy.95
  88.7 3.2 %gather_fusion.4 = bf16[8,2,256,176]{2,3,1,0:T(8,128)(2,1)} fusion(bf16[2,8,256,176]{2,3,1,0:T(8,128)(2,1)} %bitcast.144, s32[1024]{0:T(1024)S(1)} %get-tuple-element.31), kind=kCustom, calls=%fused_computation.1.clone | custom fusion | bytes 2883616 | tf_op jit(solution)/shard_map/jit(_take)/gather | solution.py:123
  91.9 1.7 gather_fusion.3
  94.3 3.3 %select_bitcast_fusion = (bf16[2,8,256,176]{2,3,0,1:T(8,128)(2,1)}, bf16[2,8,256,176]{2,3,0,1:T(8,128)(2,1)S(1)}) fusion(bf16[8,2,256,176]{2,3,1,0:T(8,128)(2,1)} %gather_fusion.4, pred[8]{0:T(512)(128)(4,1)S(1)} %compare_and_fusion.1, bf16[8,2,256,176]{2,3,1,0:T(8,128)(2,1)} %gather_fusion.3), kind=kLoop, calls=%fused_computation.31 | loop fusion | flops 1441792 | bytes 5767176 | tf_op jit(solution)/shard_map/jit(_take)/select_n | solution.py:123
  98.4 1.6 reshape.180
  99.9 3.3 %copy.77 = bf16[2,8,256,176]{2,1,3,0:T(8,128)(2,1)} copy(bf16[2,8,256,176]{2,3,0,1:T(8,128)(2,1)} %get-tuple-element.29) | data formatting | bytes 2883584 | tf_op jit(solution)/shard_map/jit(_take)/select_n | solution.py:123
  103.3 3.6 %reshape.181 = bf16[2,2048,176,1]{1,2,0,3:T(8,128)(2,1)} reshape(bf16[2,8,256,176]{2,1,3,0:T(8,128)(2,1)} %copy.77) | data formatting | bytes 2883584 | tf_op jit(solution)/shard_map/reshape | solution.py:123
  110.4 1.3 select_reduce_fusion.2
  111.8 1.4 bitcast_select_fusion
  113.2 1.1 constant_dynamic-update-slice_fusion.6
  114.3 1.2 constant_dynamic-update-slice_fusion.5
  116.4 0.9 constant_dynamic-update-slice_fusion.3
  117.3 1.6 fusion.30
  119.0 2.0 fusion.19
  121.0 2.4 fusion.24
  123.4 2.4 fusion.23
  125.8 2.5 fusion.22
  128.2 2.3 fusion.21
  130.6 5.9 %fusion.11 = f32[2,176,16,64]{1,3,2,0:T(8,128)S(1)} fusion(bf16[16,2,64,2048]{3,2,0,1:T(8,128)(2,1)} %fusion.21, bf16[2,2048,176,1]{1,2,0,3:T(8,128)(2,1)S(1)} %copy-done.11), kind=kOutput, calls=%fused_computation.29 | convolution fusion | flops 1476395008 | bytes 11272192 | tf_op jit(solution)/shard_map/sexd,edf->sexf/dot_general | solution.py:124
  136.8 3.7 %fusion.5 = bf16[16,2,64,176]{3,2,0,1:T(8,128)(2,1)} fusion(f32[2,176,16,64]{1,3,2,0:T(8,128)S(1)} %fusion.11, bf16[16,2,64,2048]{3,2,0,1:T(8,128)(2,1)S(1)} %copy-done.14, bf16[2,2048,176,1]{1,2,0,3:T(8,128)(2,1)S(1)} %copy-done.12), kind=kOutput, calls=%fused_computation.18 | convolution fusion | flops 1478557696 | bytes 11993088 | tf_op jit(solution)/shard_map/sexd,edf->sexf/dot_general | solution.py:124
  140.5 3.2 %collective-permute-start.13 = (bf16[16,2,64,176]{3,2,0,1:T(8,128)(2,1)}, bf16[16,2,64,176]{3,2,0,1:T(8,128)(2,1)S(1)}, u32[]{:S(2)}, u32[]{:S(2)}) collective-permute-start(bf16[16,2,64,176]{3,2,0,1:T(8,128)(2,1)} %fusion.5), channel_id=1, source_target_pairs={{0,96},{16,112},{32,0},{48,16},{64,32},{80,48},{96,64},{112,80},{1... | collective-permute-start | bytes 2162696 | tf_op jit(solution)/shard_map/ppermute | solution.py:90
  143.7 3.2 %fusion.2 = f32[256,704]{0,1:T(8,128)S(1)} fusion(bf16[3,2048,704]{1,2,0:T(8,128)(2,1)} %all-gather.5.cloned.1.call-done, bf16[512,2048]{1,0:T(8,128)(2,1)} %all-gather.3.cloned.1.call-done), kind=kOutput, calls=%fused_computation.12 | convolution fusion | flops 738197504 | bytes 4653056 | tf_op jit(solution)/shard_map/dot_general | solution.py:130
  147.0 3.7 %fusion.3 = f32[256,704]{0,1:T(8,128)} fusion(bf16[3,2048,704]{1,2,0:T(8,128)(2,1)} %all-gather.5.cloned.1.call-done, bf16[512,2048]{1,0:T(8,128)(2,1)S(1)} %copy-done.22), kind=kOutput, calls=%fused_computation.14 | convolution fusion | flops 738197504 | bytes 4653056 | tf_op jit(solution)/shard_map/dot_general | solution.py:129
  150.7 4.7 %fusion.4 = f32[256,2048]{1,0:T(8,128)} fusion(bf16[3,2048,704]{1,2,0:T(8,128)(2,1)} %all-gather.5.cloned.1.call-done, f32[256,704]{0,1:T(8,128)S(1)} %fusion.2, bf16[256,256]{1,0:T(8,128)(2,1)S(1)} %fusion.19, bf16[256,704]{1,0:T(8,128)(2,1)S(1)} %copy-done.13, f32[256]{0:T(256)S(1)} %add_divide_fusion, f32[256,704]{0,1:T(8,128)} %fusion.3), kind=kOutput, calls=%fused_computation.15 | convolution fusion | flops 832438272 | bytes 6915072 | tf_op jit(solution)/shard_map/dot_general | solution.py:134
  155.4 11.5 %collective-permute-done.12 = bf16[16,2,64,176]{3,2,0,1:T(8,128)(2,1)S(1)} collective-permute-done((bf16[16,2,64,176]{3,2,0,1:T(8,128)(2,1)}, bf16[16,2,64,176]{3,2,0,1:T(8,128)(2,1)S(1)}, u32[]{:S(2)}, u32[]{:S(2)}) %collective-permute-start.12) | collective-permute-done | bytes 720928 | tf_op jit(solution)/shard_map/ppermute | solution.py:90
  167.0 1.2 collective-permute-start.14
  168.3 2.1 collective-permute-start.15
  170.4 10.8 %collective-permute-done.14 = bf16[8,2,64,176]{3,2,0,1:T(8,128)(2,1)S(1)} collective-permute-done((bf16[8,2,64,176]{3,2,0,1:T(8,128)(2,1)S(1)}, bf16[8,2,64,176]{3,2,0,1:T(8,128)(2,1)S(1)}, u32[]{:S(2)}, u32[]{:S(2)}) %collective-permute-start.14) | collective-permute-done | bytes 360480 | tf_op jit(solution)/shard_map/ppermute | solution.py:90
  181.3 4.0 %pad_maximum_fusion.1 = bf16[4,16,2,64,176]{4,3,1,2,0:T(8,128)(2,1)} fusion(bf16[1,16,2,64,176]{4,3,1,2,0:T(8,128)(2,1)S(1)} %bitcast.147, bf16[1,16,2,64,176]{4,3,1,2,0:T(8,128)(2,1)S(1)} %bitcast.146, bf16[1,16,2,64,176]{4,3,1,2,0:T(8,128)(2,1)S(1)} %bitcast.145, bf16[1,16,2,64,176]{4,3,1,2,0:T(8,128)(2,1)} %bitcast.35), kind=kLoop, calls=%fused_computation.8 | loop fusion | flops 4325376 | bytes 5767168 | tf_op jit(solution)/shard_map/stack | solution.py:105
  185.3 2.4 constant_dynamic-slice_fusion
  187.6 1.1 collective-permute-start
  188.7 2.2 collective-permute-start.1
  190.9 1.5 collective-permute-start.2
  192.4 3.5 %collective-permute-done = bf16[2,176,256]{2,1,0:T(8,128)(2,1)S(1)} collective-permute-done((bf16[2,176,256]{2,1,0:T(8,128)(2,1)S(1)}, bf16[2,176,256]{2,1,0:T(8,128)(2,1)S(1)}, u32[]{:S(2)}, u32[]{:S(2)}) %collective-permute-start) | collective-permute-done | bytes 180256 | tf_op jit(solution)/shard_map/ppermute | solution.py:90
  195.9 1.0 collective-permute-start.4
  197.6 1.8 collective-permute-done.1
  200.1 1.3 collective-permute-done.2
  201.4 2.0 collective-permute-start.6
  204.8 1.8 collective-permute-done.5
  207.3 3.4 %collective-permute-done.6 = bf16[2,176,256]{2,1,0:T(8,128)(2,1)S(1)} collective-permute-done((bf16[2,176,256]{2,1,0:T(8,128)(2,1)S(1)}, bf16[2,176,256]{2,1,0:T(8,128)(2,1)S(1)}, u32[]{:S(2)}, u32[]{:S(2)}) %collective-permute-start.6) | collective-permute-done | bytes 180256 | tf_op jit(solution)/shard_map/ppermute | solution.py:90
  212.1 4.4 %slice_bitcast_fusion.8 = (bf16[16,2,64,176]{3,2,0,1:T(8,128)(2,1)}, bf16[16,2,64,176]{3,2,0,1:T(8,128)(2,1)}, bf16[16,2,64,176]{3,2,0,1:T(8,128)(2,1)}, bf16[16,2,64,176]{3,2,0,1:T(8,128)(2,1)}) fusion(bf16[4,16,2,64,176]{4,3,1,2,0:T(8,128)(2,1)} %collective-permute-done.16), kind=kLoop, calls=%fused_computation.40 | loop fusion | bytes 5767168 | tf_op jit(solution)/shard_map/squeeze | solution.py:109
  216.6 12.3 %concatenate.28 = bf16[16,2,64,1408]{3,2,0,1:T(8,128)(2,1)} concatenate(bf16[16,2,64,176]{3,2,0,1:T(8,128)(2,1)} %fusion.5, bf16[16,2,64,176]{3,2,0,1:T(8,128)(2,1)S(1)} %collective-permute-done.12, bf16[16,2,64,176]{3,2,0,1:T(8,128)(2,1)S(1)} %collective-permute-done.13, bf16[16,2,64,176]{3,2,0,1:T(8,128)(2,1)} %copy-done.2, bf16[16,2,64,176]{3,2,0,1:T(8,128)(2,1)} %get-tuple-element.17, ...), dimensions={3} | concatenate | bytes 11534336 | tf_op jit(solution)/shard_map/concatenate | solution.py:160
  228.9 4.9 %fusion.13 = bf16[16,2,64,256]{3,2,0,1:T(8,128)(2,1)S(1)} fusion(bf16[16,2,64,1408]{3,2,0,1:T(8,128)(2,1)} %concatenate.28, bf16[2,1408,256]{2,1,0:T(8,128)(2,1)} %select_dynamic-update-slice_fusion), kind=kOutput, calls=%fused_computation.33 | convolution fusion | flops 1476919296 | bytes 8257536 | tf_op jit(solution)/shard_map/sexf,efd->sexd/dot_general | solution.py:158
  233.8 1.1 copy.79
  234.9 3.7 %all-to-all-start.1 = ((bf16[16,2,64,256]{3,2,1,0:T(8,128)(2,1)}), bf16[16,2,64,256]{3,2,1,0:T(8,128)(2,1)S(1)}, u32[]{:S(2)}, u32[]{:S(2)}) async-start(bf16[16,2,64,256]{3,2,1,0:T(8,128)(2,1)} %copy.79), calls=%async_computation.1 | async-start | bytes 2097152 | tf_op jit(solution)/shard_map/all_to_all | solution.py:164
  239.1 1.6 fusion.35
  241.0 15.9 %all-to-all-done.1 = bf16[16,2,64,256]{3,2,1,0:T(8,128)(2,1)S(1)} async-done(((bf16[16,2,64,256]{3,2,1,0:T(8,128)(2,1)}), bf16[16,2,64,256]{3,2,1,0:T(8,128)(2,1)S(1)}, u32[]{:S(2)}, u32[]{:S(2)}) %all-to-all-start.1) | async-done | bytes 1048608 | tf_op jit(solution)/shard_map/all_to_all | solution.py:164
  256.9 1.6 bitcast_convert_fusion
  258.5 5.2 %gather_fusion.2 = f32[1024,256]{1,0:T(8,128)S(1)} fusion(f32[2048,256]{1,0:T(8,128)} %bitcast_convert_fusion, s32[1024]{0:T(1024)S(1)} %broadcast_clamp_fusion), kind=kCustom, calls=%fused_computation.4 | custom fusion | bytes 2101248 | tf_op jit(solution)/shard_map/jit(_take)/gather | solution.py:168
  263.6 1.3 reshape.163
  264.9 2.5 multiply_reduce_fusion
  267.5 1.7 add.158
  (127 shorter events, 18.4 us)
Async XLA Ops:
  6.5 101.2 %copy-start = (bf16[64,16,704]{2,1,0:T(8,128)(2,1)S(1)}, bf16[64,16,704]{2,1,0:T(8,128)(2,1)}, u32[]{:S(2)}) copy-start(bf16[64,16,704]{2,1,0:T(8,128)(2,1)} %param.27) | copy-start | bytes 4325380
  6.5 12.0 %copy-start.15 = (bf16[256,256]{1,0:T(8,128)(2,1)S(1)}, bf16[256,256]{1,0:T(8,128)(2,1)}, u32[]{:S(2)}) copy-start(bf16[256,256]{1,0:T(8,128)(2,1)} %param.17) | copy-start | bytes 393220
  6.5 7.7 %copy-start.16 = (s32[256,4]{0,1:T(4,128)S(1)}, s32[256,4]{0,1:T(4,128)}, u32[]{:S(2)}) copy-start(s32[256,4]{0,1:T(4,128)} %param.28) | copy-start | bytes 12292
  6.5 110.8 %all-gather.3.cloned.1.call-start = ((), (), s32[]{:S(2)}) async-start(), calls=%async_computation.3 | async-start | bytes 2359296 | tf_op jit(solution)/shard_map/all_gather | solution.py:34
  8.2 0.6 copy-start.21
  8.4 6.6 %copy-start.17 = (pred[256]{0:T(512)(128)(4,1)}, pred[256]{0:T(512)(128)(4,1)S(1)}, u32[]{:S(2)}) copy-start(pred[256]{0:T(512)(128)(4,1)S(1)} %broadcast_in_dim.105) | copy-start | bytes 772
  12.1 131.6 %all-gather.5.cloned.1.call-start = ((), (), s32[]{:S(2)}) async-start(), calls=%async_computation.4 | async-start | bytes 9191424 | tf_op jit(solution)/shard_map/all_gather | solution.py:53
  14.2 253.3 %reduce-scatter.2.cloned.1.call-start = ((), (), s32[]{:S(2)}) async-start(), calls=%async_computation.5 | async-start | bytes 2359296 | tf_op jit(solution)/shard_map/reduce_scatter | solution.py:142
  44.1 26.0 %collective-permute-start.7 = (bf16[16,2,64,256]{3,2,0,1:T(8,128)(2,1)S(1)}, bf16[16,2,64,256]{3,2,0,1:T(8,128)(2,1)S(1)}, u32[]{:S(2)}, u32[]{:S(2)}) collective-permute-start(bf16[16,2,64,256]{3,2,0,1:T(8,128)(2,1)S(1)} %get-tuple-element.28), channel_id=1, source_target_pairs={{0,32},{16,48},{32,64},{48,80},{64,96},{80,112},{96,0},{112,16},{1... | collective-permute-start | bytes 3145736 | tf_op jit(solution)/shard_map/ppermute | solution.py:90
  46.0 24.2 %collective-permute-start.8 = (bf16[16,2,64,256]{3,2,0,1:T(8,128)(2,1)S(1)}, bf16[16,2,64,256]{3,2,0,1:T(8,128)(2,1)S(1)}, u32[]{:S(2)}, u32[]{:S(2)}) collective-permute-start(bf16[16,2,64,256]{3,2,0,1:T(8,128)(2,1)S(1)} %get-tuple-element.28), channel_id=1, source_target_pairs={{0,96},{16,112},{32,0},{48,16},{64,32},{80,48},{96,64},{112,80},{1... | collective-permute-start | bytes 3145736 | tf_op jit(solution)/shard_map/ppermute | solution.py:90
  70.1 14.3 %copy-start.3 = (bf16[16,2,64,256]{3,2,0,1:T(8,128)(2,1)}, bf16[16,2,64,256]{3,2,0,1:T(8,128)(2,1)S(1)}, u32[]{:S(2)}) copy-start(bf16[16,2,64,256]{3,2,0,1:T(8,128)(2,1)S(1)} %collective-permute-done.7) | copy-start | bytes 3145732
  70.1 13.3 %collective-permute-start.9 = (bf16[8,2,64,256]{3,2,0,1:T(8,128)(2,1)S(1)}, bf16[8,2,64,256]{3,2,0,1:T(8,128)(2,1)S(1)}, u32[]{:S(2)}, u32[]{:S(2)}) collective-permute-start(bf16[8,2,64,256]{3,2,0,1:T(8,128)(2,1)S(1)} %slice.88), channel_id=1, source_target_pairs={{0,32},{16,48},{32,64},{48,80},{64,96},{80,112},{96,0},{112,16},{1... | collective-permute-start | bytes 1572872 | tf_op jit(solution)/shard_map/ppermute | solution.py:90
  70.2 16.5 %copy-start.5 = (bf16[16,2,64,256]{3,2,0,1:T(8,128)(2,1)}, bf16[16,2,64,256]{3,2,0,1:T(8,128)(2,1)S(1)}, u32[]{:S(2)}) copy-start(bf16[16,2,64,256]{3,2,0,1:T(8,128)(2,1)S(1)} %collective-permute-done.8) | copy-start | bytes 3145732
  70.3 13.1 %collective-permute-start.10 = (bf16[8,2,64,256]{3,2,0,1:T(8,128)(2,1)S(1)}, bf16[8,2,64,256]{3,2,0,1:T(8,128)(2,1)S(1)}, u32[]{:S(2)}, u32[]{:S(2)}) collective-permute-start(bf16[8,2,64,256]{3,2,0,1:T(8,128)(2,1)S(1)} %slice.89), channel_id=1, source_target_pairs={{0,96},{16,112},{32,0},{48,16},{64,32},{80,48},{96,64},{112,80},{1... | collective-permute-start | bytes 1572872 | tf_op jit(solution)/shard_map/ppermute | solution.py:90
  83.4 0.8 copy-start.7
  84.3 2.4 copy-start.9
  86.7 1.9 copy-start.10
  86.7 34.3 %collective-permute-start.11 = (bf16[4,16,2,64,256]{4,3,1,2,0:T(8,128)(2,1)}, bf16[4,16,2,64,256]{4,3,1,2,0:T(8,128)(2,1)}, u32[]{:S(2)}, u32[]{:S(2)}) collective-permute-start(bf16[4,16,2,64,256]{4,3,1,2,0:T(8,128)(2,1)} %pad_maximum_fusion), channel_id=1, source_target_pairs={{0,16},{16,0},{32,48},{48,32},{64,80},{80,64},{96,112},{112,96},{1... | collective-permute-start | bytes 12582920 | tf_op jit(solution)/shard_map/ppermute | solution.py:93
  103.3 3.6 %copy-start.20 = (s32[1,16]{1,0:T(1,128)S(1)}, s32[1,16]{1,0:T(1,128)}, u32[]{:S(2)}) copy-start(s32[1,16]{1,0:T(1,128)} %param.29) | copy-start | bytes 196
  103.3 9.9 %copy-start.4 = (bf16[16,2,64,256]{3,2,0,1:T(8,128)(2,1)S(1)}, bf16[16,2,64,256]{3,2,0,1:T(8,128)(2,1)}, u32[]{:S(2)}) copy-start(bf16[16,2,64,256]{3,2,0,1:T(8,128)(2,1)} %copy-done.3) | copy-start | bytes 3145732
  108.3 6.0 %copy-start.6 = (bf16[16,2,64,256]{3,2,0,1:T(8,128)(2,1)S(1)}, bf16[16,2,64,256]{3,2,0,1:T(8,128)(2,1)}, u32[]{:S(2)}) copy-start(bf16[16,2,64,256]{3,2,0,1:T(8,128)(2,1)} %copy-done.5) | copy-start | bytes 3145732
  114.3 2.1 copy-start.8
  115.5 3.4 %copy-start.19 = (s32[256]{0:T(256)S(1)}, s32[256]{0:T(256)}, u32[]{:S(2)}) copy-start(s32[256]{0:T(256)} %select_reduce_fusion.2) | copy-start | bytes 3076
  115.5 3.5 %copy-start.24 = (s32[256]{0:T(256)S(1)}, s32[256]{0:T(256)}, u32[]{:S(2)}) copy-start(s32[256]{0:T(256)} %and_select_fusion) | copy-start | bytes 3076
  125.8 4.8 %copy-start.11 = (bf16[2,2048,176,1]{1,2,0,3:T(8,128)(2,1)S(1)}, bf16[2,2048,176,1]{1,2,0,3:T(8,128)(2,1)}, u32[]{:S(2)}) copy-start(bf16[2,2048,176,1]{1,2,0,3:T(8,128)(2,1)} %reshape.180) | copy-start | bytes 4325380
  130.6 5.9 %copy-start.12 = (bf16[2,2048,176,1]{1,2,0,3:T(8,128)(2,1)S(1)}, bf16[2,2048,176,1]{1,2,0,3:T(8,128)(2,1)}, u32[]{:S(2)}) copy-start(bf16[2,2048,176,1]{1,2,0,3:T(8,128)(2,1)} %reshape.181) | copy-start | bytes 4325380
  130.6 6.2 %copy-start.14 = (bf16[16,2,64,2048]{3,2,0,1:T(8,128)(2,1)S(1)}, bf16[16,2,64,2048]{3,2,0,1:T(8,128)(2,1)}, u32[]{:S(2)}) copy-start(bf16[16,2,64,2048]{3,2,0,1:T(8,128)(2,1)} %fusion.21) | copy-start | bytes 25165828
  140.5 26.5 %collective-permute-start.12 = (bf16[16,2,64,176]{3,2,0,1:T(8,128)(2,1)}, bf16[16,2,64,176]{3,2,0,1:T(8,128)(2,1)S(1)}, u32[]{:S(2)}, u32[]{:S(2)}) collective-permute-start(bf16[16,2,64,176]{3,2,0,1:T(8,128)(2,1)} %fusion.5), channel_id=1, source_target_pairs={{0,32},{16,48},{32,64},{48,80},{64,96},{80,112},{96,0},{112,16},{1... | collective-permute-start | bytes 2162696 | tf_op jit(solution)/shard_map/ppermute | solution.py:90
  140.5 26.5 %collective-permute-start.13 = (bf16[16,2,64,176]{3,2,0,1:T(8,128)(2,1)}, bf16[16,2,64,176]{3,2,0,1:T(8,128)(2,1)S(1)}, u32[]{:S(2)}, u32[]{:S(2)}) collective-permute-start(bf16[16,2,64,176]{3,2,0,1:T(8,128)(2,1)} %fusion.5), channel_id=1, source_target_pairs={{0,96},{16,112},{32,0},{48,16},{64,32},{80,48},{96,64},{112,80},{1... | collective-permute-start | bytes 2162696 | tf_op jit(solution)/shard_map/ppermute | solution.py:90
  143.7 3.2 %copy-start.22 = (bf16[512,2048]{1,0:T(8,128)(2,1)S(1)}, bf16[512,2048]{1,0:T(8,128)(2,1)}, u32[]{:S(2)}) copy-start(bf16[512,2048]{1,0:T(8,128)(2,1)} %all-gather.3.cloned.1.call-done) | copy-start | bytes 6291460
  147.0 3.7 %copy-start.13 = (bf16[256,704]{1,0:T(8,128)(2,1)S(1)}, bf16[256,704]{1,0:T(8,128)(2,1)}, u32[]{:S(2)}) copy-start(bf16[256,704]{1,0:T(8,128)(2,1)} %bitcast_select_fusion) | copy-start | bytes 1081348
  167.0 14.2 %collective-permute-start.14 = (bf16[8,2,64,176]{3,2,0,1:T(8,128)(2,1)S(1)}, bf16[8,2,64,176]{3,2,0,1:T(8,128)(2,1)S(1)}, u32[]{:S(2)}, u32[]{:S(2)}) collective-permute-start(bf16[8,2,64,176]{3,2,0,1:T(8,128)(2,1)S(1)} %slice.70), channel_id=1, source_target_pairs={{0,32},{16,48},{32,64},{48,80},{64,96},{80,112},{96,0},{112,16},{1... | collective-permute-start | bytes 1081352 | tf_op jit(solution)/shard_map/ppermute | solution.py:90
  168.3 13.0 %collective-permute-start.15 = (bf16[8,2,64,176]{3,2,0,1:T(8,128)(2,1)S(1)}, bf16[8,2,64,176]{3,2,0,1:T(8,128)(2,1)S(1)}, u32[]{:S(2)}, u32[]{:S(2)}) collective-permute-start(bf16[8,2,64,176]{3,2,0,1:T(8,128)(2,1)S(1)} %slice.71), channel_id=1, source_target_pairs={{0,96},{16,112},{32,0},{48,16},{64,32},{80,48},{96,64},{112,80},{1... | collective-permute-start | bytes 1081352 | tf_op jit(solution)/shard_map/ppermute | solution.py:90
  181.3 4.0 %copy-start.2 = (bf16[16,2,64,176]{3,2,0,1:T(8,128)(2,1)}, bf16[16,2,64,176]{3,2,0,1:T(8,128)(2,1)S(1)}, u32[]{:S(2)}) copy-start(bf16[16,2,64,176]{3,2,0,1:T(8,128)(2,1)S(1)} %constant_dynamic-update-slice_fusion.8) | copy-start | bytes 2162692
  185.3 26.9 %collective-permute-start.16 = (bf16[4,16,2,64,176]{4,3,1,2,0:T(8,128)(2,1)}, bf16[4,16,2,64,176]{4,3,1,2,0:T(8,128)(2,1)}, u32[]{:S(2)}, u32[]{:S(2)}) collective-permute-start(bf16[4,16,2,64,176]{4,3,1,2,0:T(8,128)(2,1)} %pad_maximum_fusion.1), channel_id=1, source_target_pairs={{0,16},{16,0},{32,48},{48,32},{64,80},{80,64},{96,112},{112,96},{1... | collective-permute-start | bytes 8650760 | tf_op jit(solution)/shard_map/ppermute | solution.py:93
  187.6 8.2 %collective-permute-start = (bf16[2,176,256]{2,1,0:T(8,128)(2,1)S(1)}, bf16[2,176,256]{2,1,0:T(8,128)(2,1)S(1)}, u32[]{:S(2)}, u32[]{:S(2)}) collective-permute-start(bf16[2,176,256]{2,1,0:T(8,128)(2,1)S(1)} %get-tuple-element.23), channel_id=1, source_target_pairs={{0,32},{16,48},{32,64},{48,80},{64,96},{80,112},{96,0},{112,16},{1... | collective-permute-start | bytes 540680 | tf_op jit(solution)/shard_map/ppermute | solution.py:90
  188.7 10.7 %collective-permute-start.1 = (bf16[2,176,256]{2,1,0:T(8,128)(2,1)}, bf16[2,176,256]{2,1,0:T(8,128)(2,1)S(1)}, u32[]{:S(2)}, u32[]{:S(2)}) collective-permute-start(bf16[2,176,256]{2,1,0:T(8,128)(2,1)} %get-tuple-element.22), channel_id=1, source_target_pairs={{0,96},{16,112},{32,0},{48,16},{64,32},{80,48},{96,64},{112,80},{1... | collective-permute-start | bytes 540680 | tf_op jit(solution)/shard_map/ppermute | solution.py:90
  190.9 10.5 %collective-permute-start.2 = (bf16[2,176,256]{2,1,0:T(8,128)(2,1)}, bf16[2,176,256]{2,1,0:T(8,128)(2,1)S(1)}, u32[]{:S(2)}, u32[]{:S(2)}) collective-permute-start(bf16[2,176,256]{2,1,0:T(8,128)(2,1)} %get-tuple-element.21), channel_id=1, source_target_pairs={{0,64},{16,80},{32,96},{48,112},{64,0},{80,16},{96,32},{112,48},{1... | collective-permute-start | bytes 540680 | tf_op jit(solution)/shard_map/ppermute | solution.py:90
  192.4 11.7 %collective-permute-start.3 = (bf16[2,176,256]{2,1,0:T(8,128)(2,1)}, bf16[2,176,256]{2,1,0:T(8,128)(2,1)S(1)}, u32[]{:S(2)}, u32[]{:S(2)}) collective-permute-start(bf16[2,176,256]{2,1,0:T(8,128)(2,1)} %get-tuple-element.20), channel_id=1, source_target_pairs={{0,16},{16,32},{32,48},{48,64},{64,80},{80,96},{96,112},{112,0},{1... | collective-permute-start | bytes 540680 | tf_op jit(solution)/shard_map/ppermute | solution.py:90
  195.9 8.2 %collective-permute-start.4 = (bf16[2,176,256]{2,1,0:T(8,128)(2,1)}, bf16[2,176,256]{2,1,0:T(8,128)(2,1)S(1)}, u32[]{:S(2)}, u32[]{:S(2)}) collective-permute-start(bf16[2,176,256]{2,1,0:T(8,128)(2,1)} %get-tuple-element.19), channel_id=1, source_target_pairs={{0,112},{16,0},{32,16},{48,32},{64,48},{80,64},{96,80},{112,96},{1... | collective-permute-start | bytes 540680 | tf_op jit(solution)/shard_map/ppermute | solution.py:90
  199.4 7.2 %collective-permute-start.5 = (bf16[2,176,256]{2,1,0:T(8,128)(2,1)S(1)}, bf16[2,176,256]{2,1,0:T(8,128)(2,1)S(1)}, u32[]{:S(2)}, u32[]{:S(2)}) collective-permute-start(bf16[2,176,256]{2,1,0:T(8,128)(2,1)S(1)} %get-tuple-element.25), channel_id=1, source_target_pairs={{0,48},{16,64},{32,80},{48,96},{64,112},{80,0},{96,16},{112,32},{1... | collective-permute-start | bytes 540680 | tf_op jit(solution)/shard_map/ppermute | solution.py:90
  201.4 9.2 %collective-permute-start.6 = (bf16[2,176,256]{2,1,0:T(8,128)(2,1)S(1)}, bf16[2,176,256]{2,1,0:T(8,128)(2,1)S(1)}, u32[]{:S(2)}, u32[]{:S(2)}) collective-permute-start(bf16[2,176,256]{2,1,0:T(8,128)(2,1)S(1)} %get-tuple-element.18), channel_id=1, source_target_pairs={{0,80},{16,96},{32,112},{48,0},{64,16},{80,32},{96,48},{112,64},{1... | collective-permute-start | bytes 540680 | tf_op jit(solution)/shard_map/ppermute | solution.py:90
  233.8 5.1 %copy-start.18 = (pred[256,4]{0,1:T(4,128)(4,1)S(1)}, pred[256,4]{0,1:T(4,128)(4,1)}, u32[]{:S(2)}) copy-start(pred[256,4]{0,1:T(4,128)(4,1)} %get-tuple-element.12) | copy-start | bytes 3076
  233.8 5.3 %copy-start.23 = (bf16[2048,32]{0,1:T(8,128)(2,1)S(1)}, bf16[2048,32]{0,1:T(8,128)(2,1)}, u32[]{:S(2)}) copy-start(bf16[2048,32]{0,1:T(8,128)(2,1)} %param.18) | copy-start | bytes 393220
  234.9 22.0 %all-to-all-start.1 = ((bf16[16,2,64,256]{3,2,1,0:T(8,128)(2,1)}), bf16[16,2,64,256]{3,2,1,0:T(8,128)(2,1)S(1)}, u32[]{:S(2)}, u32[]{:S(2)}) async-start(bf16[16,2,64,256]{3,2,1,0:T(8,128)(2,1)} %copy.79), calls=%async_computation.1 | async-start | bytes 2097152 | tf_op jit(solution)/shard_map/all_to_all | solution.py:164
  258.4 10.7 %copy-start.1 = (bf16[64,16,704]{2,1,0:T(8,128)(2,1)S(1)}, bf16[64,16,704]{2,1,0:T(8,128)(2,1)}, u32[]{:S(2)}) copy-start(bf16[64,16,704]{2,1,0:T(8,128)(2,1)} %param.27) | copy-start | bytes 4325380
Sparse Core Ops, SparseCore 0:
  12.3 29.4 all-gather.2
  43.9 79.1 all-gather.4
  200.2 33.3 reduce-scatter.1

commit v11 on v9

--- a/solution.py
+++ b/solution.py
@@ -119,8 +119,9 @@
         ordered = jnp.take(blocks, slot_source, axis=1).reshape(w.shape)
         return jnp.einsum("sexd,edf->sexf", slot_features, ordered, preferred_element_type=jnp.float32)
 
-    gate_part = project(routed_gate_weight)
-    up_part = project(routed_up_weight)
+    gate_up = project(jnp.concatenate([routed_gate_weight, routed_up_weight], axis=2))
+    gate_part = gate_up[..., : routed_gate_weight.shape[2]]
+    up_part = gate_up[..., routed_gate_weight.shape[2] :]
     hidden = (jax.nn.silu(gate_part) * up_part).astype(jnp.bfloat16)
     local_hidden = hidden.shape[3]
     group_half = hidden.shape[0] // 2
@@ -172,10 +173,14 @@
     expert_value = expert_value + jnp.concatenate([low_part, high_part], axis=0)
     returned = lax.all_to_all(
         expert_value.astype(jnp.bfloat16), "col", split_axis=0, concat_axis=0, tiled=True
-    ).astype(jnp.float32)
+    )
     flat_rows = returned.reshape(expert_count * capacity, local_width)
-    routed_rows = jnp.take(flat_rows, row_index, axis=0)
-    routed = jnp.sum(gate_weights[:, :, None] * routed_rows, axis=1)
+    routed = None
+    for k in range(route_count):
+        pick = (row_index[:, k][:, None] == slot_id[None, :]).astype(jnp.bfloat16)
+        row = jnp.dot(pick, flat_rows, preferred_element_type=jnp.float32)
+        term = gate_weights[:, k][:, None] * row
+        routed = term if routed is None else routed + term
 
     return routed + shared_sum
 

time: 227 us -> 212 us (0.934)
  local copies, waits for them, and re-layouts: 47.6 us -> 34 us
  other arithmetic: 21.3 us -> 17.2 us
    gather x2 -> x0, local copies, waits for them, and re-layouts: 6.47 us -> none  [on_device(): routed_rows = jnp.take(flat_rows, row_index, axis=0)]
    all_gather x1, waiting for transfers between devices: 0.02 us -> 5.59 us  [on_device(): shared_full = lax.all_gather(shared_stack, 'col', axis=1, tiled=True)]
    ppermute x15, waiting for transfers between devices: 41.7 us -> 36.4 us  [shifted(): lax.ppermute(x, 'row', [(i, (i + shift) % row_count) for i in range(row_c...]
    concatenate x0 -> x2, other arithmetic: none -> 3.81 us  [the longest x1 3.73 us: on_device(): jnp.concatenate([routed_gate_weight, routed_up_weight], axis=2)]
    select_n x3 -> x0, local copies, waits for them, and re-layouts: 3.16 us -> none  [the longest x2 3.02 us: project(): ordered = jnp.take(blocks, slot_source, axis=1).reshape(w.shape)]
    select_n x2 -> x1, other arithmetic: 2.86 us -> 0.01 us  [project(): ordered = jnp.take(blocks, slot_source, axis=1).reshape(w.shape)]
    dot_general x2 -> x1, matrix products: 9.55 us -> 6.94 us  [project(): jnp.einsum('sexd,edf->sexf', slot_features, ordered, preferred_element_ty...]
    reduce_sum x1 -> x0, other arithmetic: 2.53 us -> none  [on_device(): routed = jnp.sum(gate_weights[:, :, None] * routed_rows, axis=1)]
  transfers between devices with their start and end apart: 28 -> 28, of which waited for: 7 -> 9; matrix products, arithmetic and copies ran while one was open for 46% -> 41% of each run, Pallas kernels for 0% -> 0%
where the time goes in v11:
time: 212 us; the launch traced here: 211 us
  waiting for transfers between devices  56.2 us (27%)
  matrix products  41.3 us (19%)
  local copies, waits for them, and re-layouts  34 us (16%)
  starting transfers between devices  24.7 us (12%)
  blocking collectives  23.8 us (11%)
  other arithmetic  17.2 us (8%)
  between operations  13.7 us (6%)
    ppermute x15, waiting for transfers between devices, shifted(): lax.ppermute(x, 'row', [(i, (i + shift) % row_count) for i in range(row_c...  36.4 us
    all_to_all x1, blocking collectives, on_device(): lax.all_to_all(outgoing, 'col', split_axis=0, concat_axis=0, tiled=True)  23.8 us
    ppermute x15, starting transfers between devices, shifted(): lax.ppermute(x, 'row', [(i, (i + shift) % row_count) for i in range(row_c...  18 us
    all_to_all x1, waiting for transfers between devices, on_device(): lax.all_to_all(expert_value.astype(jnp.bfloat16), 'col', split_axis=0, co...  14 us
    dot_general x10, matrix products, down_of(): jnp.einsum('sexf,efd->sexd', block, weight, preferred_element_type=jnp.fl...  13.8 us
    unnamed x36, local copies, waits for them, and re-layouts  12.4 us
    dot_general x1, matrix products, project(): jnp.einsum('sexd,edf->sexf', slot_features, ordered, preferred_element_ty...  6.94 us
    all_gather x1, waiting for transfers between devices, on_device(): shared_full = lax.all_gather(shared_stack, 'col', axis=1, tiled=True)  5.59 us
  transfers between devices with their start and end apart: 28, of which 9 were waited for; matrix products, arithmetic and copies ran while one was open for 41% of the time, Pallas kernels for 0%

profile of v11, /device:TPU:0, one launch (start us, length us, event | category | flops | bytes accessed | tf_op | source)
XLA Modules:
  0.0 210.9 jit_solution(18235514354314308818)
XLA Ops:
  6.6 0.8 compare_select_fusion.2
  7.4 0.7 compare_and_fusion.1
  8.4 1.6 gather_fusion
  10.1 1.6 pad_maximum_fusion.3
  11.8 2.0 pad_maximum_fusion.2
  14.8 2.6 %fusion = pred[2048,256]{1,0:T(8,128)(4,1)S(1)} fusion(s32[256,4]{0,1:T(4,128)S(1)} %multiply_add_fusion), kind=kLoop, calls=%fused_computation.4 | loop fusion | flops 3670016 | bytes 528384 | tf_op jit(solution)/shard_map/reduce_or | solution.py:110
  17.9 23.8 %all_to_all.10 = bf16[16,2,64,256]{3,2,1,0:T(8,128)(2,1)S(1)} all-to-all(bf16[16,2,64,256]{3,2,1,0:T(8,128)(2,1)S(1)} %bitcast.157), channel_id=1, replica_groups=mesh['row'=8,'col'=16] {'col'}, dimensions={0} | all-to-all | bytes 2097152 | tf_op jit(solution)/shard_map/all_to_all | solution.py:113
  41.7 1.6 fusion.81
  43.4 1.9 collective-permute-start
  45.3 2.1 %collective-permute-start.1 = (bf16[16,2,64,256]{3,2,0,1:T(8,128)(2,1)}, bf16[16,2,64,256]{3,2,0,1:T(8,128)(2,1)S(1)}, u32[]{:S(2)}, u32[]{:S(2)}) collective-permute-start(bf16[16,2,64,256]{3,2,0,1:T(8,128)(2,1)} %get-tuple-element.18), channel_id=1, source_target_pairs={{0,96},{16,112},{32,0},{48,16},{64,32},{80,48},{96,64},{112,80},{1... | collective-permute-start | bytes 3145736 | tf_op jit(solution)/shard_map/ppermute | solution.py:90
  47.4 2.4 %constant_dynamic-slice_fusion.2 = (bf16[2,176,256]{2,1,0:T(8,128)(2,1)}, bf16[2,176,256]{2,1,0:T(8,128)(2,1)}, bf16[2,176,256]{2,1,0:T(8,128)(2,1)}, bf16[2,176...) fusion(bf16[2,176,2048]{2,1,0:T(8,128)(2,1)} %param.23, ...), kind=kLoop, calls=%fused_computation.135 | loop fusion | bytes 2523164 | tf_op jit(solution)/shard_map/dynamic_slice | solution.py:148
  50.4 0.9 bitcast_select_fusion
  51.3 3.7 %pad_maximum_fusion = bf16[2,2048,352]{1,2,0:T(8,128)(2,1)} fusion(bf16[2,2048,176]{1,2,0:T(8,128)(2,1)} %param.22, bf16[2,2048,176]{1,2,0:T(8,128)(2,1)} %param.21), kind=kLoop, calls=%fused_computation.12 | loop fusion | flops 5767168 | bytes 5767168 | tf_op jit(solution)/shard_map/concatenate | solution.py:122
  55.1 14.6 %collective-permute-done = bf16[16,2,64,256]{3,2,0,1:T(8,128)(2,1)} collective-permute-done((bf16[16,2,64,256]{3,2,0,1:T(8,128)(2,1)}, bf16[16,2,64,256]{3,2,0,1:T(8,128)(2,1)}, u32[]{:S(2)}, u32[]{:S(2)}) %collective-permute-start) | collective-permute-done | bytes 1048608 | tf_op jit(solution)/shard_map/ppermute | solution.py:90
  69.7 1.9 slice.94
  71.6 0.9 slice.95
  72.5 3.2 %collective-permute-start.3 = (bf16[8,2,64,256]{3,2,0,1:T(8,128)(2,1)}, bf16[8,2,64,256]{3,2,0,1:T(8,128)(2,1)}, u32[]{:S(2)}, u32[]{:S(2)}) collective-permute-start(bf16[8,2,64,256]{3,2,0,1:T(8,128)(2,1)} %slice.95), channel_id=1, source_target_pairs={{0,96},{16,112},{32,0},{48,16},{64,32},{80,48},{96,64},{112,80},{1... | collective-permute-start | bytes 1572872 | tf_op jit(solution)/shard_map/ppermute | solution.py:90
  76.8 2.1 copy.83
  78.9 2.3 %gather_fusion.1 = bf16[8,2,256,352]{2,3,1,0:T(8,128)(2,1)} fusion(bf16[2,8,256,352]{2,3,1,0:T(8,128)(2,1)S(1)} %bitcast.149, s32[1024]{0:T(1024)S(1)} %get-tuple-element.28), kind=kCustom, calls=%fused_computation.1 | custom fusion | bytes 5767200 | tf_op jit(solution)/shard_map/jit(_take)/gather | solution.py:119
  81.2 2.3 %copy.77 = bf16[8,2,44,8,256]{4,3,0,2,1:T(8,128)(2,1)S(1)} copy(bf16[8,2,44,8,256]{4,3,2,1,0:T(8,128)(2,1)} %bitcast.150) | data formatting | bytes 5767168 | tf_op jit(solution)/shard_map/jit(_take)/gather | solution.py:119
  83.8 1.1 collective-permute-done.2
  85.2 1.1 pad_maximum_fusion.1
  86.7 2.4 %constant_dynamic-update-slice_fusion.7 = bf16[16,2,64,2048]{3,2,0,1:T(8,128)(2,1)} fusion(bf16[16,2,64,2048]{3,2,0,1:T(8,128)(2,1)} %get-tuple-element.19, bf16[16,2,64,256]{3,2,0,1:T(8,128)(2,1)} %collective-permute-done), kind=kLoop, calls=%fused_computation.116 | loop fusion | bytes 2097152
  89.1 1.2 constant_dynamic-update-slice_fusion.6
  90.2 0.9 constant_dynamic-update-slice_fusion.5
  91.1 2.0 constant_dynamic-update-slice_fusion.4
  93.4 2.4 %constant_dynamic-update-slice_fusion.3 = bf16[16,2,64,2048]{3,2,0,1:T(8,128)(2,1)} fusion(bf16[16,2,64,2048]{3,2,0,1:T(8,128)(2,1)} %constant_dynamic-update-slice_fusion.4, bf16[16,2,64,256]{3,2,0,1:T(8,128)(2,1)} %collective-permute-done.4), kind=kLoop, calls=%fused_computation.112 | loop fusion | bytes 2097152
  95.8 2.4 %constant_dynamic-update-slice_fusion.2 = bf16[16,2,64,2048]{3,2,0,1:T(8,128)(2,1)} fusion(bf16[16,2,64,2048]{3,2,0,1:T(8,128)(2,1)} %constant_dynamic-update-slice_fusion.3, bf16[16,2,64,256]{3,2,0,1:T(8,128)(2,1)} %collective-permute-done.5), kind=kLoop, calls=%fused_computation.111 | loop fusion | bytes 2097152
  98.2 1.1 constant_dynamic-update-slice_fusion.1
  99.3 1.1 constant_dynamic-update-slice_fusion
  100.4 6.9 %fusion.15 = f32[16,2,64,352]{3,2,0,1:T(8,128)S(1)} fusion(bf16[16,2,64,2048]{3,2,0,1:T(8,128)(2,1)} %constant_dynamic-update-slice_fusion, bf16[2,2048,352]{1,2,0:T(8,128)(2,1)S(1)} %bitcast.152, pred[2048]{0:T(1024)(128)(4,1)S(1)} %broadcast_in_dim.110), kind=kOutput, calls=%fused_computation.31 | convolution fusion | flops 2954231808 | bytes 14157824 | tf_op jit(solution)/shard_map/sexd,edf->sexf/dot_general | solution.py:120
  107.3 0.6 fusion.9
  108.0 0.7 collective-permute-start.12
  108.7 3.3 %collective-permute-start.13 = (bf16[16,2,64,176]{3,2,0,1:T(8,128)(2,1)S(1)}, bf16[16,2,64,176]{3,2,0,1:T(8,128)(2,1)}, u32[]{:S(2)}, u32[]{:S(2)}) collective-permute-start(bf16[16,2,64,176]{3,2,0,1:T(8,128)(2,1)S(1)} %fusion.9), channel_id=1, source_target_pairs={{0,96},{16,112},{32,0},{48,16},{64,32},{80,48},{96,64},{112,80},{1... | collective-permute-start | bytes 2162696 | tf_op jit(solution)/shard_map/ppermute | solution.py:90
  112.0 1.4 fusion.60
  113.4 1.6 fusion.42
  115.0 2.1 fusion.31
  117.1 5.6 %all-gather.5.cloned.1.call-done = bf16[3,2048,704]{1,2,0:T(8,128)(2,1)} async-done(((bf16[3,128,704]{1,2,0:T(8,128)(2,1)}), bf16[3,2048,704]{1,2,0:T(8,128)(2,1)}) %all-gather.5.cloned.1.call-update) | async-done | bytes 8650768 | tf_op jit(solution)/shard_map/all_gather | solution.py:53
  122.7 4.1 %fusion.3 = f32[256,704]{0,1:T(8,128)} fusion(bf16[3,2048,704]{1,2,0:T(8,128)(2,1)} %all-gather.5.cloned.1.call-done, bf16[512,2048]{1,0:T(8,128)(2,1)} %all-gather.3.cloned.1.call-done), kind=kOutput, calls=%fused_computation.11 | convolution fusion | flops 738197504 | bytes 4653056 | tf_op jit(solution)/shard_map/dot_general | solution.py:130
  126.8 3.6 %fusion.2 = f32[256,704]{0,1:T(8,128)} fusion(bf16[3,2048,704]{1,2,0:T(8,128)(2,1)} %all-gather.5.cloned.1.call-done, bf16[512,2048]{1,0:T(8,128)(2,1)S(1)} %copy-done.12), kind=kOutput, calls=%fused_computation.9 | convolution fusion | flops 738197504 | bytes 4653056 | tf_op jit(solution)/shard_map/dot_general | solution.py:131
  130.4 5.1 %fusion.8 = f32[256,2048]{1,0:T(8,128)} fusion(bf16[3,2048,704]{1,2,0:T(8,128)(2,1)} %all-gather.5.cloned.1.call-done, f32[256,704]{0,1:T(8,128)} %fusion.2, bf16[256,256]{1,0:T(8,128)(2,1)S(1)} %fusion.31, bf16[256,704]{1,0:T(8,128)(2,1)} %bitcast_select_fusion, f32[256]{0:T(256)S(1)} %add_divide_fusion, f32[256,704]{0,1:T(8,128)} %fusion.3), kind=kOutput, calls=%fused_computation.17 | convolution fusion | flops 832438272 | bytes 6947840 | tf_op jit(solution)/shard_map/dot_general | solution.py:135
  135.5 1.2 collective-permute-start.17
  136.7 2.0 collective-permute-start.19
  138.7 1.9 slice.76
  140.6 0.7 collective-permute-start.11
  141.3 0.8 collective-permute-start.20
  142.1 3.1 %fusion.58 = f32[2,256,16,64]{1,3,2,0:T(8,128)} fusion(bf16[16,2,64,176]{3,2,0,1:T(8,128)(2,1)} %collective-permute-done.10, bf16[2,176,256]{2,1,0:T(8,128)(2,1)S(1)} %collective-permute-done.8, bf16[2,176,256]{2,1,0:T(8,128)(2,1)} %collective-permute-done.9, pred[]{:T(512)S(6)} %eq.138), kind=kOutput, calls=%fused_computation.80 | convolution fusion | flops 184639488 | bytes 3178497 | tf_op jit(solution)/shard_map/sexf,efd->sexd/dot_general | solution.py:159
  145.2 0.9 collective-permute-start.18
  146.1 1.1 slice.77
  147.3 3.0 %collective-permute-done.11 = bf16[2,176,256]{2,1,0:T(8,128)(2,1)} collective-permute-done((bf16[2,176,256]{2,1,0:T(8,128)(2,1)}, bf16[2,176,256]{2,1,0:T(8,128)(2,1)}, u32[]{:S(2)}, u32[]{:S(2)}) %collective-permute-start.11) | collective-permute-done | bytes 180256 | tf_op jit(solution)/shard_map/ppermute | solution.py:90
  150.2 1.8 fusion.56
  152.0 1.4 collective-permute-start.14
  153.4 9.6 %collective-permute-done.20 = bf16[8,2,64,176]{3,2,0,1:T(8,128)(2,1)} collective-permute-done((bf16[8,2,64,176]{3,2,0,1:T(8,128)(2,1)}, bf16[8,2,64,176]{3,2,0,1:T(8,128)(2,1)}, u32[]{:S(2)}, u32[]{:S(2)}) %collective-permute-start.20) | collective-permute-done | bytes 360480 | tf_op jit(solution)/shard_map/ppermute | solution.py:90
  163.1 1.4 fusion.66
  164.5 4.5 %collective-permute-done.22 = bf16[8,2,64,176]{3,2,0,1:T(8,128)(2,1)S(1)} collective-permute-done((bf16[8,2,64,176]{3,2,0,1:T(8,128)(2,1)S(1)}, bf16[8,2,64,176]{3,2,0,1:T(8,128)(2,1)S(1)}, u32[]{:S(2)}, u32[]{:S(2)}) %collective-permute-start.22) | collective-permute-done | bytes 360480 | tf_op jit(solution)/shard_map/ppermute | solution.py:90
  169.4 1.2 fusion.64
  171.4 1.7 fusion.51
  174.2 3.3 %collective-permute-done.16 = bf16[2,176,256]{2,1,0:T(8,128)(2,1)S(1)} collective-permute-done((bf16[2,176,256]{2,1,0:T(8,128)(2,1)S(1)}, bf16[2,176,256]{2,1,0:T(8,128)(2,1)S(1)}, u32[]{:S(2)}, u32[]{:S(2)}) %collective-permute-start.16) | collective-permute-done | bytes 180256 | tf_op jit(solution)/shard_map/ppermute | solution.py:90
  177.5 2.2 %fusion.10 = bf16[16,2,64,256]{3,2,0,1:T(8,128)(2,1)S(1)} fusion(f32[8,2,64,256]{3,2,0,1:T(8,128)S(1)} %fusion.19, f32[8,2,64,256]{3,2,0,1:T(8,128)S(1)} %fusion.20, f32[2,256,16,64]{1,3,2,0:T(8,128)S(1)} %fusion.51, f32[2,256,16,64]{1,3,2,0:T(8,128)S(1)} %fusion.56, f32[2,256,16,64]{1,3,2,0:T(8,128)S(1)} %fusion.54, f32[2,256,16,64]{1,3,2,0:T(8,128)S(1)} %fusion.60, ...), kind=kOutput, calls=%fused_computation.22 | convolution fusion | flops 188743680 | bytes 14532608 | tf_op jit(solution)/shard_map/sexf,efd->sexd/dot_general | solution.py:159
  179.7 1.1 copy.64
  180.8 4.0 %all-to-all-start.1 = ((bf16[16,2,64,256]{3,2,1,0:T(8,128)(2,1)}), bf16[16,2,64,256]{3,2,1,0:T(8,128)(2,1)S(1)}, u32[]{:S(2)}, u32[]{:S(2)}) async-start(bf16[16,2,64,256]{3,2,1,0:T(8,128)(2,1)} %copy.64), calls=%async_computation.1 | async-start | bytes 2097152 | tf_op jit(solution)/shard_map/all_to_all | solution.py:174
  184.9 1.6 fusion.47
  186.6 14.0 %all-to-all-done.1 = bf16[16,2,64,256]{3,2,1,0:T(8,128)(2,1)S(1)} async-done(((bf16[16,2,64,256]{3,2,1,0:T(8,128)(2,1)}), bf16[16,2,64,256]{3,2,1,0:T(8,128)(2,1)S(1)}, u32[]{:S(2)}, u32[]{:S(2)}) %all-to-all-start.1) | async-done | bytes 1048608 | tf_op jit(solution)/shard_map/all_to_all | solution.py:174
  202.7 1.7 add.222
  (110 shorter events, 9.1 us)
Async XLA Ops:
  6.5 43.3 %copy-start = (bf16[64,16,704]{2,1,0:T(8,128)(2,1)S(1)}, bf16[64,16,704]{2,1,0:T(8,128)(2,1)}, u32[]{:S(2)}) copy-start(bf16[64,16,704]{2,1,0:T(8,128)(2,1)} %param.25) | copy-start | bytes 4325380
  6.5 11.0 %copy-start.7 = (bf16[256,256]{1,0:T(8,128)(2,1)S(1)}, bf16[256,256]{1,0:T(8,128)(2,1)}, u32[]{:S(2)}) copy-start(bf16[256,256]{1,0:T(8,128)(2,1)} %param.15) | copy-start | bytes 393220
  6.5 7.3 %copy-start.8 = (s32[256,4]{0,1:T(4,128)S(1)}, s32[256,4]{0,1:T(4,128)}, u32[]{:S(2)}) copy-start(s32[256,4]{0,1:T(4,128)} %param.26) | copy-start | bytes 12292
  6.5 106.8 %all-gather.3.cloned.1.call-start = ((), (), s32[]{:S(2)}) async-start(), calls=%async_computation.3 | async-start | bytes 2359296 | tf_op jit(solution)/shard_map/all_gather | solution.py:34
  11.8 110.9 %all-gather.5.cloned.1.call-start = ((), (), s32[]{:S(2)}) async-start(), calls=%async_computation.4 | async-start | bytes 9191424 | tf_op jit(solution)/shard_map/all_gather | solution.py:53
  13.8 188.9 %reduce-scatter.2.cloned.1.call-start = ((), (), s32[]{:S(2)}) async-start(), calls=%async_computation.5 | async-start | bytes 2359296 | tf_op jit(solution)/shard_map/reduce_scatter | solution.py:143
  43.4 26.3 %collective-permute-start = (bf16[16,2,64,256]{3,2,0,1:T(8,128)(2,1)}, bf16[16,2,64,256]{3,2,0,1:T(8,128)(2,1)}, u32[]{:S(2)}, u32[]{:S(2)}) collective-permute-start(bf16[16,2,64,256]{3,2,0,1:T(8,128)(2,1)} %get-tuple-element.18), channel_id=1, source_target_pairs={{0,32},{16,48},{32,64},{48,80},{64,96},{80,112},{96,0},{112,16},{1... | collective-permute-start | bytes 3145736 | tf_op jit(solution)/shard_map/ppermute | solution.py:90
  45.3 26.3 %collective-permute-start.1 = (bf16[16,2,64,256]{3,2,0,1:T(8,128)(2,1)}, bf16[16,2,64,256]{3,2,0,1:T(8,128)(2,1)S(1)}, u32[]{:S(2)}, u32[]{:S(2)}) collective-permute-start(bf16[16,2,64,256]{3,2,0,1:T(8,128)(2,1)} %get-tuple-element.18), channel_id=1, source_target_pairs={{0,96},{16,112},{32,0},{48,16},{64,32},{80,48},{96,64},{112,80},{1... | collective-permute-start | bytes 3145736 | tf_op jit(solution)/shard_map/ppermute | solution.py:90
  49.9 90.8 %collective-permute-start.9 = (bf16[2,176,256]{2,1,0:T(8,128)(2,1)}, bf16[2,176,256]{2,1,0:T(8,128)(2,1)}, u32[]{:S(2)}, u32[]{:S(2)}) collective-permute-start(bf16[2,176,256]{2,1,0:T(8,128)(2,1)} %get-tuple-element.14), channel_id=1, source_target_pairs={{0,112},{16,0},{32,16},{48,32},{64,48},{80,64},{96,80},{112,96},{1... | collective-permute-start | bytes 540680 | tf_op jit(solution)/shard_map/ppermute | solution.py:90
  55.1 20.9 %copy-start.10 = (s32[1,16]{1,0:T(1,128)S(1)}, s32[1,16]{1,0:T(1,128)}, u32[]{:S(2)}) copy-start(s32[1,16]{1,0:T(1,128)} %param.27) | copy-start | bytes 196
  71.6 13.3 %collective-permute-start.2 = (bf16[8,2,64,256]{3,2,0,1:T(8,128)(2,1)}, bf16[8,2,64,256]{3,2,0,1:T(8,128)(2,1)S(1)}, u32[]{:S(2)}, u32[]{:S(2)}) collective-permute-start(bf16[8,2,64,256]{3,2,0,1:T(8,128)(2,1)} %slice.94), channel_id=1, source_target_pairs={{0,32},{16,48},{32,64},{48,80},{64,96},{80,112},{96,0},{112,16},{1... | collective-permute-start | bytes 1572872 | tf_op jit(solution)/shard_map/ppermute | solution.py:90
  71.6 5.2 %copy-start.3 = (bf16[16,2,64,256]{3,2,0,1:T(8,128)(2,1)}, bf16[16,2,64,256]{3,2,0,1:T(8,128)(2,1)S(1)}, u32[]{:S(2)}) copy-start(bf16[16,2,64,256]{3,2,0,1:T(8,128)(2,1)S(1)} %collective-permute-done.1) | copy-start | bytes 3145732
  72.5 12.7 %collective-permute-start.3 = (bf16[8,2,64,256]{3,2,0,1:T(8,128)(2,1)}, bf16[8,2,64,256]{3,2,0,1:T(8,128)(2,1)}, u32[]{:S(2)}, u32[]{:S(2)}) collective-permute-start(bf16[8,2,64,256]{3,2,0,1:T(8,128)(2,1)} %slice.95), channel_id=1, source_target_pairs={{0,96},{16,112},{32,0},{48,16},{64,32},{80,48},{96,64},{112,80},{1... | collective-permute-start | bytes 1572872 | tf_op jit(solution)/shard_map/ppermute | solution.py:90
  75.9 17.2 %collective-permute-start.4 = (bf16[16,2,64,256]{3,2,0,1:T(8,128)(2,1)}, bf16[16,2,64,256]{3,2,0,1:T(8,128)(2,1)}, u32[]{:S(2)}, u32[]{:S(2)}) collective-permute-start(bf16[16,2,64,256]{3,2,0,1:T(8,128)(2,1)} %get-tuple-element.18), channel_id=1, source_target_pairs={{0,16},{16,0},{32,48},{48,32},{64,80},{80,64},{96,112},{112,96},{1... | collective-permute-start | bytes 3145736 | tf_op jit(solution)/shard_map/ppermute | solution.py:93
  76.2 19.6 %collective-permute-start.5 = (bf16[16,2,64,256]{3,2,0,1:T(8,128)(2,1)}, bf16[16,2,64,256]{3,2,0,1:T(8,128)(2,1)}, u32[]{:S(2)}, u32[]{:S(2)}) collective-permute-start(bf16[16,2,64,256]{3,2,0,1:T(8,128)(2,1)} %collective-permute-done), channel_id=1, source_target_pairs={{0,16},{16,0},{32,48},{48,32},{64,80},{80,64},{96,112},{112,96},{1... | collective-permute-start | bytes 3145736 | tf_op jit(solution)/shard_map/ppermute | solution.py:93
  81.2 2.5 %copy-start.9 = (bf16[2048]{0:T(1024)(128)(2,1)S(1)}, bf16[2048]{0:T(1024)(128)(2,1)}, u32[]{:S(2)}) copy-start(bf16[2048]{0:T(1024)(128)(2,1)} %param.17) | copy-start | bytes 12292
  81.2 2.5 %copy-start.11 = (s32[1,16]{1,0:T(1,128)S(1)}, s32[1,16]{1,0:T(1,128)}, u32[]{:S(2)}) copy-start(s32[1,16]{1,0:T(1,128)} %param.28) | copy-start | bytes 196
  83.8 5.2 %copy-start.4 = (bf16[16,2,64,256]{3,2,0,1:T(8,128)(2,1)S(1)}, bf16[16,2,64,256]{3,2,0,1:T(8,128)(2,1)}, u32[]{:S(2)}) copy-start(bf16[16,2,64,256]{3,2,0,1:T(8,128)(2,1)} %copy-done.3) | copy-start | bytes 3145732
  84.9 13.2 %collective-permute-start.6 = (bf16[16,2,64,256]{3,2,0,1:T(8,128)(2,1)}, bf16[16,2,64,256]{3,2,0,1:T(8,128)(2,1)S(1)}, u32[]{:S(2)}, u32[]{:S(2)}) collective-permute-start(bf16[16,2,64,256]{3,2,0,1:T(8,128)(2,1)} %copy-done.3), channel_id=1, source_target_pairs={{0,16},{16,0},{32,48},{48,32},{64,80},{80,64},{96,112},{112,96},{1... | collective-permute-start | bytes 3145736 | tf_op jit(solution)/shard_map/ppermute | solution.py:93
  86.3 13.0 %collective-permute-start.7 = (bf16[16,2,64,256]{3,2,0,1:T(8,128)(2,1)S(1)}, bf16[16,2,64,256]{3,2,0,1:T(8,128)(2,1)S(1)}, u32[]{:S(2)}, u32[]{:S(2)}) collective-permute-start(bf16[16,2,64,256]{3,2,0,1:T(8,128)(2,1)S(1)} %pad_maximum_fusion.1), channel_id=1, source_target_pairs={{0,16},{16,0},{32,48},{48,32},{64,80},{80,64},{96,112},{112,96},{1... | collective-permute-start | bytes 3145736 | tf_op jit(solution)/shard_map/ppermute | solution.py:93
  93.1 48.2 %collective-permute-start.8 = (bf16[2,176,256]{2,1,0:T(8,128)(2,1)}, bf16[2,176,256]{2,1,0:T(8,128)(2,1)S(1)}, u32[]{:S(2)}, u32[]{:S(2)}) collective-permute-start(bf16[2,176,256]{2,1,0:T(8,128)(2,1)} %get-tuple-element.15), channel_id=1, source_target_pairs={{0,16},{16,32},{32,48},{48,64},{64,80},{80,96},{96,112},{112,0},{1... | collective-permute-start | bytes 540680 | tf_op jit(solution)/shard_map/ppermute | solution.py:90
  108.0 27.5 %collective-permute-start.12 = (bf16[16,2,64,176]{3,2,0,1:T(8,128)(2,1)S(1)}, bf16[16,2,64,176]{3,2,0,1:T(8,128)(2,1)}, u32[]{:S(2)}, u32[]{:S(2)}) collective-permute-start(bf16[16,2,64,176]{3,2,0,1:T(8,128)(2,1)S(1)} %fusion.9), channel_id=1, source_target_pairs={{0,32},{16,48},{32,64},{48,80},{64,96},{80,112},{96,0},{112,16},{1... | collective-permute-start | bytes 2162696 | tf_op jit(solution)/shard_map/ppermute | solution.py:90
  108.7 28.0 %collective-permute-start.13 = (bf16[16,2,64,176]{3,2,0,1:T(8,128)(2,1)S(1)}, bf16[16,2,64,176]{3,2,0,1:T(8,128)(2,1)}, u32[]{:S(2)}, u32[]{:S(2)}) collective-permute-start(bf16[16,2,64,176]{3,2,0,1:T(8,128)(2,1)S(1)} %fusion.9), channel_id=1, source_target_pairs={{0,96},{16,112},{32,0},{48,16},{64,32},{80,48},{96,64},{112,80},{1... | collective-permute-start | bytes 2162696 | tf_op jit(solution)/shard_map/ppermute | solution.py:90
  112.0 30.1 %collective-permute-start.10 = (bf16[16,2,64,176]{3,2,0,1:T(8,128)(2,1)S(1)}, bf16[16,2,64,176]{3,2,0,1:T(8,128)(2,1)}, u32[]{:S(2)}, u32[]{:S(2)}) collective-permute-start(bf16[16,2,64,176]{3,2,0,1:T(8,128)(2,1)S(1)} %fusion.9), channel_id=1, source_target_pairs={{0,16},{16,0},{32,48},{48,32},{64,80},{80,64},{96,112},{112,96},{1... | collective-permute-start | bytes 2162696 | tf_op jit(solution)/shard_map/ppermute | solution.py:93
  122.7 4.1 %copy-start.12 = (bf16[512,2048]{1,0:T(8,128)(2,1)S(1)}, bf16[512,2048]{1,0:T(8,128)(2,1)}, u32[]{:S(2)}) copy-start(bf16[512,2048]{1,0:T(8,128)(2,1)} %all-gather.3.cloned.1.call-done) | copy-start | bytes 6291460
  135.5 35.1 %collective-permute-start.17 = (bf16[2,176,256]{2,1,0:T(8,128)(2,1)}, bf16[2,176,256]{2,1,0:T(8,128)(2,1)S(1)}, u32[]{:S(2)}, u32[]{:S(2)}) collective-permute-start(bf16[2,176,256]{2,1,0:T(8,128)(2,1)} %get-tuple-element.17), channel_id=1, source_target_pairs={{0,80},{16,96},{32,112},{48,0},{64,16},{80,32},{96,48},{112,64},{1... | collective-permute-start | bytes 540680 | tf_op jit(solution)/shard_map/ppermute | solution.py:90
  136.7 15.3 %collective-permute-start.19 = (bf16[2,176,256]{2,1,0:T(8,128)(2,1)}, bf16[2,176,256]{2,1,0:T(8,128)(2,1)}, u32[]{:S(2)}, u32[]{:S(2)}) collective-permute-start(bf16[2,176,256]{2,1,0:T(8,128)(2,1)} %get-tuple-element.16), channel_id=1, source_target_pairs={{0,64},{16,80},{32,96},{48,112},{64,0},{80,16},{96,32},{112,48},{1... | collective-permute-start | bytes 540680 | tf_op jit(solution)/shard_map/ppermute | solution.py:90
  140.6 9.6 %collective-permute-start.11 = (bf16[2,176,256]{2,1,0:T(8,128)(2,1)}, bf16[2,176,256]{2,1,0:T(8,128)(2,1)}, u32[]{:S(2)}, u32[]{:S(2)}) collective-permute-start(bf16[2,176,256]{2,1,0:T(8,128)(2,1)} %get-tuple-element.13), channel_id=1, source_target_pairs={{0,32},{16,48},{32,64},{48,80},{64,96},{80,112},{96,0},{112,16},{1... | collective-permute-start | bytes 540680 | tf_op jit(solution)/shard_map/ppermute | solution.py:90
  141.3 21.8 %collective-permute-start.20 = (bf16[8,2,64,176]{3,2,0,1:T(8,128)(2,1)}, bf16[8,2,64,176]{3,2,0,1:T(8,128)(2,1)}, u32[]{:S(2)}, u32[]{:S(2)}) collective-permute-start(bf16[8,2,64,176]{3,2,0,1:T(8,128)(2,1)} %slice.76), channel_id=1, source_target_pairs={{0,32},{16,48},{32,64},{48,80},{64,96},{80,112},{96,0},{112,16},{1... | collective-permute-start | bytes 1081352 | tf_op jit(solution)/shard_map/ppermute | solution.py:90
  145.2 25.8 %collective-permute-start.18 = (bf16[16,2,64,176]{3,2,0,1:T(8,128)(2,1)}, bf16[16,2,64,176]{3,2,0,1:T(8,128)(2,1)}, u32[]{:S(2)}, u32[]{:S(2)}) collective-permute-start(bf16[16,2,64,176]{3,2,0,1:T(8,128)(2,1)} %collective-permute-done.13), channel_id=1, source_target_pairs={{0,16},{16,0},{32,48},{48,32},{64,80},{80,64},{96,112},{112,96},{1... | collective-permute-start | bytes 2162696 | tf_op jit(solution)/shard_map/ppermute | solution.py:93
  147.2 4.8 %copy-start.6 = (bf16[2,176,256]{2,1,0:T(8,128)(2,1)S(1)}, bf16[2,176,256]{2,1,0:T(8,128)(2,1)}, u32[]{:S(2)}) copy-start(bf16[2,176,256]{2,1,0:T(8,128)(2,1)} %get-tuple-element.12) | copy-start | bytes 540676
  147.2 21.7 %copy-start.5 = (bf16[2,176,256]{2,1,0:T(8,128)(2,1)S(1)}, bf16[2,176,256]{2,1,0:T(8,128)(2,1)}, u32[]{:S(2)}) copy-start(bf16[2,176,256]{2,1,0:T(8,128)(2,1)} %get-tuple-element.11) | copy-start | bytes 540676
  150.2 18.8 %collective-permute-start.22 = (bf16[8,2,64,176]{3,2,0,1:T(8,128)(2,1)S(1)}, bf16[8,2,64,176]{3,2,0,1:T(8,128)(2,1)S(1)}, u32[]{:S(2)}, u32[]{:S(2)}) collective-permute-start(bf16[8,2,64,176]{3,2,0,1:T(8,128)(2,1)S(1)} %slice.77), channel_id=1, source_target_pairs={{0,96},{16,112},{32,0},{48,16},{64,32},{80,48},{96,64},{112,80},{1... | collective-permute-start | bytes 1081352 | tf_op jit(solution)/shard_map/ppermute | solution.py:90
  152.0 21.1 %collective-permute-start.14 = (bf16[2,176,256]{2,1,0:T(8,128)(2,1)S(1)}, bf16[2,176,256]{2,1,0:T(8,128)(2,1)S(1)}, u32[]{:S(2)}, u32[]{:S(2)}) collective-permute-start(bf16[2,176,256]{2,1,0:T(8,128)(2,1)S(1)} %copy-done.6), channel_id=1, source_target_pairs={{0,48},{16,64},{32,80},{48,96},{64,112},{80,0},{96,16},{112,32},{1... | collective-permute-start | bytes 540680 | tf_op jit(solution)/shard_map/ppermute | solution.py:90
  163.1 10.0 %collective-permute-start.15 = (bf16[16,2,64,176]{3,2,0,1:T(8,128)(2,1)}, bf16[16,2,64,176]{3,2,0,1:T(8,128)(2,1)S(1)}, u32[]{:S(2)}, u32[]{:S(2)}) collective-permute-start(bf16[16,2,64,176]{3,2,0,1:T(8,128)(2,1)} %collective-permute-done.12), channel_id=1, source_target_pairs={{0,16},{16,0},{32,48},{48,32},{64,80},{80,64},{96,112},{112,96},{1... | collective-permute-start | bytes 2162696 | tf_op jit(solution)/shard_map/ppermute | solution.py:93
  169.0 8.5 %collective-permute-start.16 = (bf16[2,176,256]{2,1,0:T(8,128)(2,1)S(1)}, bf16[2,176,256]{2,1,0:T(8,128)(2,1)S(1)}, u32[]{:S(2)}, u32[]{:S(2)}) collective-permute-start(bf16[2,176,256]{2,1,0:T(8,128)(2,1)S(1)} %copy-done.5), channel_id=1, source_target_pairs={{0,96},{16,112},{32,0},{48,16},{64,32},{80,48},{96,64},{112,80},{1... | collective-permute-start | bytes 540680 | tf_op jit(solution)/shard_map/ppermute | solution.py:90
  170.6 3.0 %collective-permute-start.21 = (bf16[8,2,64,176]{3,2,0,1:T(8,128)(2,1)}, bf16[8,2,64,176]{3,2,0,1:T(8,128)(2,1)S(1)}, u32[]{:S(2)}, u32[]{:S(2)}) collective-permute-start(bf16[8,2,64,176]{3,2,0,1:T(8,128)(2,1)} %collective-permute-done.20), channel_id=1, source_target_pairs={{0,16},{16,0},{32,48},{48,32},{64,80},{80,64},{96,112},{112,96},{1... | collective-permute-start | bytes 1081352 | tf_op jit(solution)/shard_map/ppermute | solution.py:93
  171.1 2.8 %collective-permute-start.23 = (bf16[8,2,64,176]{3,2,0,1:T(8,128)(2,1)S(1)}, bf16[8,2,64,176]{3,2,0,1:T(8,128)(2,1)S(1)}, u32[]{:S(2)}, u32[]{:S(2)}) collective-permute-start(bf16[8,2,64,176]{3,2,0,1:T(8,128)(2,1)S(1)} %collective-permute-done.22), channel_id=1, source_target_pairs={{0,16},{16,0},{32,48},{48,32},{64,80},{80,64},{96,112},{112,96},{1... | collective-permute-start | bytes 1081352 | tf_op jit(solution)/shard_map/ppermute | solution.py:93
  173.9 3.6 %copy-start.2 = (f32[2,256,16,64]{1,3,2,0:T(8,128)S(1)}, f32[2,256,16,64]{1,3,2,0:T(8,128)}, u32[]{:S(2)}) copy-start(f32[2,256,16,64]{1,3,2,0:T(8,128)} %fusion.58) | copy-start | bytes 6291460
  179.7 5.1 %copy-start.13 = (bf16[2048,32]{0,1:T(8,128)(2,1)S(1)}, bf16[2048,32]{0,1:T(8,128)(2,1)}, u32[]{:S(2)}) copy-start(bf16[2048,32]{0,1:T(8,128)(2,1)} %param.16) | copy-start | bytes 393220
  180.8 19.8 %all-to-all-start.1 = ((bf16[16,2,64,256]{3,2,1,0:T(8,128)(2,1)}), bf16[16,2,64,256]{3,2,1,0:T(8,128)(2,1)S(1)}, u32[]{:S(2)}, u32[]{:S(2)}) async-start(bf16[16,2,64,256]{3,2,1,0:T(8,128)(2,1)} %copy.64), calls=%async_computation.1 | async-start | bytes 2097152 | tf_op jit(solution)/shard_map/all_to_all | solution.py:174
  201.6 2.7 %copy-start.1 = (bf16[64,16,704]{2,1,0:T(8,128)(2,1)S(1)}, bf16[64,16,704]{2,1,0:T(8,128)(2,1)}, u32[]{:S(2)}) copy-start(bf16[64,16,704]{2,1,0:T(8,128)(2,1)} %param.25) | copy-start | bytes 4325380
Sparse Core Ops, SparseCore 0:
  11.9 29.4 all-gather.2
  43.5 79.1 all-gather.4
  147.4 37.7 reduce-scatter.1

commit v12 on v11

--- a/solution.py
+++ b/solution.py
@@ -112,12 +112,18 @@
     outgoing = chosen.reshape(col_count, local_experts, capacity, local_width)
     own_block = lax.all_to_all(outgoing, "col", split_axis=0, concat_axis=0, tiled=True)
     slot_blocks, slot_source = row_blocks(own_block)
-    slot_features = jnp.concatenate(slot_blocks, axis=3)
+    arrival_groups = ((0, 4, 1, 2), (5, 6, 3, 7))
 
     def project(w):
         blocks = w.reshape(w.shape[0], row_count, local_width, w.shape[2])
-        ordered = jnp.take(blocks, slot_source, axis=1).reshape(w.shape)
-        return jnp.einsum("sexd,edf->sexf", slot_features, ordered, preferred_element_type=jnp.float32)
+        total = None
+        for group in arrival_groups:
+            features = jnp.concatenate([slot_blocks[j] for j in group], axis=3)
+            order = jnp.stack([slot_source[j] for j in group])
+            ordered = jnp.take(blocks, order, axis=1).reshape(w.shape[0], -1, w.shape[2])
+            term = jnp.einsum("sexd,edf->sexf", features, ordered, preferred_element_type=jnp.float32)
+            total = term if total is None else total + term
+        return total
 
     gate_up = project(jnp.concatenate([routed_gate_weight, routed_up_weight], axis=2))
     gate_part = gate_up[..., : routed_gate_weight.shape[2]]

time: 212 us -> 216 us (1.019)
  blocking collectives: 23.8 us -> 0 us
  waiting for transfers between devices: 56.2 us -> 69.4 us
  starting transfers between devices: 24.7 us -> 34.1 us
  other arithmetic: 17.2 us -> 20.6 us
  local copies, waits for them, and re-layouts: 34 us -> 36.9 us
    all_to_all x1 -> x0, blocking collectives: 23.8 us -> none  [on_device(): lax.all_to_all(outgoing, 'col', split_axis=0, concat_axis=0, tiled=True)]
    all_gather x1, waiting for transfers between devices: 5.59 us -> 17.8 us  [on_device(): shared_full = lax.all_gather(shared_stack, 'col', axis=1, tiled=True)]
    ppermute x15, waiting for transfers between devices: 36.4 us -> 26.9 us  [shifted(): lax.ppermute(x, 'row', [(i, (i + shift) % row_count) for i in range(row_c...]
    unnamed x36 -> x42, local copies, waits for them, and re-layouts: 12.4 us -> 2.96 us
    all_to_all x0 -> x1, waiting for transfers between devices: none -> 8.14 us  [on_device(): lax.all_to_all(outgoing, 'col', split_axis=0, concat_axis=0, tiled=True)]
    all_to_all x0 -> x1, starting transfers between devices: none -> 7.14 us  [on_device(): lax.all_to_all(outgoing, 'col', split_axis=0, concat_axis=0, tiled=True)]
    reshape x0 -> x2, local copies, waits for them, and re-layouts: none -> 5.9 us  [project(): jnp.take(blocks, order, axis=1).reshape(w.shape[0], -1, w.shape[2])]
    select_n x1 -> x2, other arithmetic: 0.01 us -> 3.99 us  [project(): jnp.take(blocks, order, axis=1).reshape(w.shape[0], -1, w.shape[2])]
  transfers between devices with their start and end apart: 28 -> 29, of which waited for: 9 -> 8; matrix products, arithmetic and copies ran while one was open for 41% -> 42% of each run, Pallas kernels for 0% -> 0%
where the time goes in v12:
time: 216 us; the launch traced here: 215 us
  waiting for transfers between devices  69.4 us (32%)
  matrix products  40.4 us (19%)
  local copies, waits for them, and re-layouts  36.9 us (17%)
  starting transfers between devices  34.1 us (16%)
  other arithmetic  20.6 us (10%)
  between operations  13.8 us (6%)
    ppermute x15, waiting for transfers between devices, shifted(): lax.ppermute(x, 'row', [(i, (i + shift) % row_count) for i in range(row_c...  26.9 us
    ppermute x15, starting transfers between devices, shifted(): lax.ppermute(x, 'row', [(i, (i + shift) % row_count) for i in range(row_c...  19.7 us
    all_gather x1, waiting for transfers between devices, on_device(): shared_full = lax.all_gather(shared_stack, 'col', axis=1, tiled=True)  17.8 us
    all_to_all x1, waiting for transfers between devices, on_device(): lax.all_to_all(expert_value.astype(jnp.bfloat16), 'col', split_axis=0, co...  16.4 us
    dot_general x10, matrix products, down_of(): jnp.einsum('sexf,efd->sexd', block, weight, preferred_element_type=jnp.fl...  12.4 us
    all_to_all x1, waiting for transfers between devices, on_device(): lax.all_to_all(outgoing, 'col', split_axis=0, concat_axis=0, tiled=True)  8.14 us
    all_to_all x1, starting transfers between devices, on_device(): lax.all_to_all(outgoing, 'col', split_axis=0, concat_axis=0, tiled=True)  7.14 us
    dot_general x2, matrix products, project(): jnp.einsum('sexd,edf->sexf', features, ordered, preferred_element_type=jn...  6.66 us
  transfers between devices with their start and end apart: 29, of which 8 were waited for; matrix products, arithmetic and copies ran while one was open for 42% of the time, Pallas kernels for 0%

profile of v12, /device:TPU:0, one launch (start us, length us, event | category | flops | bytes accessed | tf_op | source)
XLA Modules:
  0.0 215.1 jit_solution(10709020652952614220)
XLA Ops:
  6.5 0.8 compare_and_fusion.2
  7.3 0.7 compare_select_fusion.2
  8.2 1.6 gather_fusion
  9.9 1.6 pad_maximum_fusion.2
  11.6 2.0 pad_maximum_fusion.1
  14.6 2.6 %fusion = pred[2048,256]{1,0:T(8,128)(4,1)S(1)} fusion(s32[256,4]{0,1:T(4,128)S(1)} %multiply_add_fusion), kind=kLoop, calls=%fused_computation.5 | loop fusion | flops 3670016 | bytes 528384 | tf_op jit(solution)/shard_map/reduce_or | solution.py:110
  17.2 1.4 convolution_convert_fusion
  18.7 7.1 %all-to-all-start = ((bf16[16,2,64,256]{3,2,1,0:T(8,128)(2,1)}), bf16[16,2,64,256]{3,2,1,0:T(8,128)(2,1)S(1)}, u32[]{:S(2)}, u32[]{:S(2)}) async-start(bf16[16,2,64,256]{3,2,1,0:T(8,128)(2,1)} %bitcast.147), calls=%async_computation | async-start | bytes 2097152 | tf_op jit(solution)/shard_map/all_to_all | solution.py:113
  26.0 2.5 %constant_dynamic-slice_fusion.2 = (bf16[2,176,256]{2,1,0:T(8,128)(2,1)}, bf16[2,176,256]{2,1,0:T(8,128)(2,1)}, bf16[2,176,256]{2,1,0:T(8,128)(2,1)}, bf16[2,176...) fusion(bf16[2,176,2048]{2,1,0:T(8,128)(2,1)} %param.25, ...), kind=kLoop, calls=%fused_computation.144 | loop fusion | bytes 2523164 | tf_op jit(solution)/shard_map/dynamic_slice | solution.py:154
  28.5 3.2 %collective-permute-start.9 = (bf16[2,176,256]{2,1,0:T(8,128)(2,1)}, bf16[2,176,256]{2,1,0:T(8,128)(2,1)}, u32[]{:S(2)}, u32[]{:S(2)}) collective-permute-start(bf16[2,176,256]{2,1,0:T(8,128)(2,1)} %get-tuple-element.19), channel_id=1, source_target_pairs={{0,112},{16,0},{32,16},{48,32},{64,48},{80,64},{96,80},{112,96},{1... | collective-permute-start | bytes 540680 | tf_op jit(solution)/shard_map/ppermute | solution.py:90
  31.7 3.8 %pad_maximum_fusion = bf16[2,2048,352]{1,2,0:T(8,128)(2,1)} fusion(bf16[2,2048,176]{1,2,0:T(8,128)(2,1)} %param.24, bf16[2,2048,176]{1,2,0:T(8,128)(2,1)} %param.23), kind=kLoop, calls=%fused_computation.30 | loop fusion | flops 5767168 | bytes 5767168 | tf_op jit(solution)/shard_map/concatenate | solution.py:128
  35.4 8.1 %all-to-all-done = bf16[16,2,64,256]{3,2,1,0:T(8,128)(2,1)S(1)} async-done(((bf16[16,2,64,256]{3,2,1,0:T(8,128)(2,1)}), bf16[16,2,64,256]{3,2,1,0:T(8,128)(2,1)S(1)}, u32[]{:S(2)}, u32[]{:S(2)}) %all-to-all-start) | async-done | bytes 1048608 | tf_op jit(solution)/shard_map/all_to_all | solution.py:113
  43.6 1.1 copy.66
  44.7 1.9 collective-permute-start.1
  46.7 2.1 collective-permute-start.2
  48.8 0.6 fusion.95
  49.8 3.7 %copy.90 = bf16[2,44,8,8,256]{4,3,1,2,0:T(8,128)(2,1)} copy(bf16[2,44,8,8,256]{4,3,2,1,0:T(8,128)(2,1)} %bitcast.146) | data formatting | bytes 5767168 | tf_op jit(solution)/shard_map/reshape | solution.py:118
  53.5 1.3 compare_and_fusion
  54.8 2.7 %gather_fusion.3 = bf16[4,2,256,352]{2,3,1,0:T(8,128)(2,1)S(1)} fusion(bf16[2,8,256,352]{2,3,1,0:T(8,128)(2,1)} %bitcast.144, s32[1024]{0:T(1024)S(1)} %pad_clamp_fusion), kind=kCustom, calls=%fused_computation.1.clone | custom fusion | bytes 2883600 | tf_op jit(solution)/shard_map/jit(_take)/gather | solution.py:123
  57.5 3.6 %gather_fusion.2 = bf16[4,2,256,352]{2,3,1,0:T(8,128)(2,1)} fusion(bf16[2,8,256,352]{2,3,1,0:T(8,128)(2,1)} %bitcast.145, s32[1024]{0:T(1024)S(1)} %pad_clamp_fusion.1), kind=kCustom, calls=%fused_computation.clone | custom fusion | bytes 2883600 | tf_op jit(solution)/shard_map/jit(_take)/gather | solution.py:123
  61.0 2.7 %select_bitcast_fusion.1 = bf16[2,4,256,352]{2,3,0,1:T(8,128)(2,1)} fusion(bf16[4,2,256,352]{2,3,1,0:T(8,128)(2,1)} %gather_fusion.2, pred[4]{0:T(512)(128)(4,1)S(1)} %get-tuple-element.33), kind=kLoop, calls=%fused_computation.48 | loop fusion | flops 720896 | bytes 2883588 | tf_op jit(solution)/shard_map/jit(_take)/select_n | solution.py:123
  63.7 1.3 select_bitcast_fusion
  65.0 4.8 %collective-permute-done.1 = bf16[16,2,64,256]{3,2,0,1:T(8,128)(2,1)} collective-permute-done((bf16[16,2,64,256]{3,2,0,1:T(8,128)(2,1)}, bf16[16,2,64,256]{3,2,0,1:T(8,128)(2,1)}, u32[]{:S(2)}, u32[]{:S(2)}) %collective-permute-start.1) | collective-permute-done | bytes 1048608 | tf_op jit(solution)/shard_map/ppermute | solution.py:90
  69.8 1.9 slice.110
  71.8 1.9 slice.111
  73.8 3.2 %collective-permute-start.6 = (bf16[8,2,64,256]{3,2,0,1:T(8,128)(2,1)}, bf16[8,2,64,256]{3,2,0,1:T(8,128)(2,1)}, u32[]{:S(2)}, u32[]{:S(2)}) collective-permute-start(bf16[8,2,64,256]{3,2,0,1:T(8,128)(2,1)} %slice.111), channel_id=1, source_target_pairs={{0,96},{16,112},{32,0},{48,16},{64,32},{80,48},{96,64},{112,80},{1... | collective-permute-start | bytes 1572872 | tf_op jit(solution)/shard_map/ppermute | solution.py:90
  77.6 2.2 %copy.68 = bf16[2,4,256,352]{2,1,3,0:T(4,128)(2,1)} copy(bf16[2,4,256,352]{2,3,0,1:T(8,128)(2,1)S(1)} %copy-done.5) | data formatting | bytes 2883584 | tf_op jit(solution)/shard_map/jit(_take)/select_n | solution.py:123
  79.8 4.0 %reshape.138 = bf16[2,1024,352,1]{1,2,0,3:T(8,128)(2,1)} reshape(bf16[2,4,256,352]{2,1,3,0:T(4,128)(2,1)} %copy.68) | data formatting | bytes 2883584 | tf_op jit(solution)/shard_map/reshape | solution.py:123
  83.8 1.1 copy.62
  84.9 1.9 reshape.137
  87.2 1.2 constant_dynamic-update-slice_fusion.1
  89.0 1.1 constant_dynamic-update-slice_fusion
  90.4 4.1 %fusion.1 = f32[2,352,16,64]{1,3,2,0:T(8,128)S(1)} fusion(bf16[16,2,64,256]{3,2,0,1:T(8,128)(2,1)} %collective-permute-done.2, bf16[16,2,64,256]{3,2,0,1:T(8,128)(2,1)} %collective-permute-done.1, bf16[16,2,64,256]{3,2,0,1:T(8,128)(2,1)} %collective-permute-done, bf16[2,1024,352,1]{1,2,0,3:T(8,128)(2,1)S(1)} %copy-done.9, ...), kind=kOutput, calls=%fused_computation.6 | convolution fusion | flops 1493172224 | bytes 8519680 | tf_op jit(solution)/shard_map/sexd,edf->sexf/dot_general | solution.py:124
  94.5 2.6 %add_bitcast_fusion = f32[16,2,64,352]{3,2,0,1:T(8,128)S(1)} fusion(f32[2,352,16,64]{1,3,2,0:T(8,128)S(1)} %fusion.1, bf16[16,2,64,256]{3,2,0,1:T(8,128)(2,1)S(1)} %collective-permute-done.7, bf16[16,2,64,256]{3,2,0,1:T(8,128)(2,1)S(1)} %constant_dynamic-update-slice_fusion, bf16[16,2,64,256]{3,2,0,1:T(8,128)(2,1)S(1)} %collective-permute-done.4, ...), kind=kOutput, calls=%fused_computation.22 | convolution fusion | flops 1493893120 | bytes 11403264 | tf_op jit(solution)/shard_map/sexd,edf->sexf/dot_general | solution.py:124
  97.1 0.6 fusion.21
  97.7 0.6 collective-permute-start.13
  98.3 1.5 collective-permute-start.12
  99.8 2.7 %fusion.72 = f32[2,256,16,64]{1,3,2,0:T(8,128)} fusion(bf16[16,2,64,176]{3,2,0,1:T(8,128)(2,1)S(1)} %fusion.21, bf16[2,176,2048]{2,1,0:T(8,128)(2,1)} %param.25, s32[]{:T(128)S(6)} %select_n.145), kind=kOutput, calls=%fused_computation.97 | convolution fusion | flops 184549376 | bytes 2998276 | tf_op jit(solution)/shard_map/sexf,efd->sexd/dot_general | solution.py:165
  102.5 1.6 fusion.54
  104.1 2.0 fusion.43
  106.1 17.8 %all-gather.5.cloned.1.call-done = bf16[3,2048,704]{1,2,0:T(8,128)(2,1)} async-done(((bf16[3,128,704]{1,2,0:T(8,128)(2,1)}), bf16[3,2048,704]{1,2,0:T(8,128)(2,1)}) %all-gather.5.cloned.1.call-update) | async-done | bytes 8650768 | tf_op jit(solution)/shard_map/all_gather | solution.py:53
  123.9 4.1 %fusion.18 = f32[256,704]{0,1:T(8,128)} fusion(bf16[3,2048,704]{1,2,0:T(8,128)(2,1)} %all-gather.5.cloned.1.call-done, bf16[512,2048]{1,0:T(8,128)(2,1)} %all-gather.3.cloned.1.call-done), kind=kOutput, calls=%fused_computation.27 | convolution fusion | flops 738197504 | bytes 4653056 | tf_op jit(solution)/shard_map/dot_general | solution.py:137
  128.0 3.6 %fusion.19 = f32[256,704]{0,1:T(8,128)} fusion(bf16[3,2048,704]{1,2,0:T(8,128)(2,1)} %all-gather.5.cloned.1.call-done, bf16[512,2048]{1,0:T(8,128)(2,1)S(1)} %copy-done.18), kind=kOutput, calls=%fused_computation.29 | convolution fusion | flops 738197504 | bytes 4653056 | tf_op jit(solution)/shard_map/dot_general | solution.py:136
  131.7 5.0 %fusion.20 = f32[256,2048]{1,0:T(8,128)} fusion(bf16[3,2048,704]{1,2,0:T(8,128)(2,1)} %all-gather.5.cloned.1.call-done, f32[256,704]{0,1:T(8,128)} %fusion.18, bf16[256,256]{1,0:T(8,128)(2,1)S(1)} %fusion.43, bf16[256,704]{1,0:T(8,128)(2,1)S(1)} %bitcast_select_fusion, f32[256]{0:T(256)S(1)} %add_divide_fusion, f32[256,704]{0,1:T(8,128)} %fusion.19), kind=kOutput, calls=%fused_computation.31 | convolution fusion | flops 832438272 | bytes 6915072 | tf_op jit(solution)/shard_map/dot_general | solution.py:141
  136.6 2.9 %collective-permute-start.16 = (bf16[2,176,256]{2,1,0:T(8,128)(2,1)S(1)}, bf16[2,176,256]{2,1,0:T(8,128)(2,1)}, u32[]{:S(2)}, u32[]{:S(2)}) collective-permute-start(bf16[2,176,256]{2,1,0:T(8,128)(2,1)S(1)} %copy-done.10), channel_id=1, source_target_pairs={{0,96},{16,112},{32,0},{48,16},{64,32},{80,48},{96,64},{112,80},{1... | collective-permute-start | bytes 540680 | tf_op jit(solution)/shard_map/ppermute | solution.py:90
  139.6 1.9 slice.90
  141.5 2.2 %collective-permute-start.19 = (bf16[2,176,256]{2,1,0:T(8,128)(2,1)}, bf16[2,176,256]{2,1,0:T(8,128)(2,1)S(1)}, u32[]{:S(2)}, u32[]{:S(2)}) collective-permute-start(bf16[2,176,256]{2,1,0:T(8,128)(2,1)} %get-tuple-element.21), channel_id=1, source_target_pairs={{0,64},{16,80},{32,96},{48,112},{64,0},{80,16},{96,32},{112,48},{1... | collective-permute-start | bytes 540680 | tf_op jit(solution)/shard_map/ppermute | solution.py:90
  143.7 1.9 collective-permute-start.20
  145.6 3.1 %fusion.70 = f32[2,256,16,64]{1,3,2,0:T(8,128)} fusion(bf16[16,2,64,176]{3,2,0,1:T(8,128)(2,1)} %collective-permute-done.10, bf16[2,176,256]{2,1,0:T(8,128)(2,1)} %collective-permute-done.8, bf16[2,176,256]{2,1,0:T(8,128)(2,1)} %collective-permute-done.9, pred[]{:T(512)S(6)} %eq.138), kind=kOutput, calls=%fused_computation.95 | convolution fusion | flops 184639488 | bytes 3178497 | tf_op jit(solution)/shard_map/sexf,efd->sexd/dot_general | solution.py:165
  148.8 2.8 %collective-permute-done.11 = bf16[2,176,256]{2,1,0:T(8,128)(2,1)S(1)} collective-permute-done((bf16[2,176,256]{2,1,0:T(8,128)(2,1)}, bf16[2,176,256]{2,1,0:T(8,128)(2,1)S(1)}, u32[]{:S(2)}, u32[]{:S(2)}) %collective-permute-start.11) | collective-permute-done | bytes 180256 | tf_op jit(solution)/shard_map/ppermute | solution.py:90
  151.6 1.6 fusion.68
  153.4 12.0 %collective-permute-done.20 = bf16[8,2,64,176]{3,2,0,1:T(8,128)(2,1)S(1)} collective-permute-done((bf16[8,2,64,176]{3,2,0,1:T(8,128)(2,1)}, bf16[8,2,64,176]{3,2,0,1:T(8,128)(2,1)S(1)}, u32[]{:S(2)}, u32[]{:S(2)}) %collective-permute-start.20) | collective-permute-done | bytes 360480 | tf_op jit(solution)/shard_map/ppermute | solution.py:90
  165.7 3.9 %collective-permute-done.22 = bf16[8,2,64,176]{3,2,0,1:T(8,128)(2,1)S(1)} collective-permute-done((bf16[8,2,64,176]{3,2,0,1:T(8,128)(2,1)S(1)}, bf16[8,2,64,176]{3,2,0,1:T(8,128)(2,1)S(1)}, u32[]{:S(2)}, u32[]{:S(2)}) %collective-permute-start.22) | collective-permute-done | bytes 360480 | tf_op jit(solution)/shard_map/ppermute | solution.py:90
  169.8 2.0 collective-permute-start.23
  172.0 1.4 fusion.66
  173.4 3.4 %collective-permute-done.17 = bf16[2,176,256]{2,1,0:T(8,128)(2,1)S(1)} collective-permute-done((bf16[2,176,256]{2,1,0:T(8,128)(2,1)S(1)}, bf16[2,176,256]{2,1,0:T(8,128)(2,1)S(1)}, u32[]{:S(2)}, u32[]{:S(2)}) %collective-permute-start.17) | collective-permute-done | bytes 180256 | tf_op jit(solution)/shard_map/ppermute | solution.py:90
  178.0 0.9 copy-done.3
  178.9 0.7 copy-done.2
  179.6 1.9 fusion.22
  181.6 1.1 copy.70
  182.7 4.1 %all-to-all-start.1 = ((bf16[16,2,64,256]{3,2,1,0:T(8,128)(2,1)}), bf16[16,2,64,256]{3,2,1,0:T(8,128)(2,1)S(1)}, u32[]{:S(2)}, u32[]{:S(2)}) async-start(bf16[16,2,64,256]{3,2,1,0:T(8,128)(2,1)} %copy.70), calls=%async_computation.1 | async-start | bytes 2097152 | tf_op jit(solution)/shard_map/all_to_all | solution.py:180
  186.8 1.6 fusion.59
  188.5 16.4 %all-to-all-done.1 = bf16[16,2,64,256]{3,2,1,0:T(8,128)(2,1)S(1)} async-done(((bf16[16,2,64,256]{3,2,1,0:T(8,128)(2,1)}), bf16[16,2,64,256]{3,2,1,0:T(8,128)(2,1)S(1)}, u32[]{:S(2)}, u32[]{:S(2)}) %all-to-all-start.1) | async-done | bytes 1048608 | tf_op jit(solution)/shard_map/all_to_all | solution.py:180
  206.9 1.7 add.216
  (121 shorter events, 7.7 us)
Async XLA Ops:
  6.5 70.5 %copy-start = (bf16[64,16,704]{2,1,0:T(8,128)(2,1)S(1)}, bf16[64,16,704]{2,1,0:T(8,128)(2,1)}, u32[]{:S(2)}) copy-start(bf16[64,16,704]{2,1,0:T(8,128)(2,1)} %param.27) | copy-start | bytes 4325380
  6.5 10.7 %copy-start.13 = (bf16[256,256]{1,0:T(8,128)(2,1)S(1)}, bf16[256,256]{1,0:T(8,128)(2,1)}, u32[]{:S(2)}) copy-start(bf16[256,256]{1,0:T(8,128)(2,1)} %param.17) | copy-start | bytes 393220
  6.5 7.1 %copy-start.14 = (s32[256,4]{0,1:T(4,128)S(1)}, s32[256,4]{0,1:T(4,128)}, u32[]{:S(2)}) copy-start(s32[256,4]{0,1:T(4,128)} %param.28) | copy-start | bytes 12292
  6.5 95.9 %all-gather.3.cloned.1.call-start = ((), (), s32[]{:S(2)}) async-start(), calls=%async_computation.3 | async-start | bytes 2359296 | tf_op jit(solution)/shard_map/all_gather | solution.py:34
  11.5 112.4 %all-gather.5.cloned.1.call-start = ((), (), s32[]{:S(2)}) async-start(), calls=%async_computation.4 | async-start | bytes 9191424 | tf_op jit(solution)/shard_map/all_gather | solution.py:53
  18.7 24.9 %all-to-all-start = ((bf16[16,2,64,256]{3,2,1,0:T(8,128)(2,1)}), bf16[16,2,64,256]{3,2,1,0:T(8,128)(2,1)S(1)}, u32[]{:S(2)}, u32[]{:S(2)}) async-start(bf16[16,2,64,256]{3,2,1,0:T(8,128)(2,1)} %bitcast.147), calls=%async_computation | async-start | bytes 2097152 | tf_op jit(solution)/shard_map/all_to_all | solution.py:113
  25.8 181.1 %reduce-scatter.2.cloned.1.call-start = ((), (), s32[]{:S(2)}) async-start(), calls=%async_computation.5 | async-start | bytes 2359296 | tf_op jit(solution)/shard_map/reduce_scatter | solution.py:149
  28.5 113.0 %collective-permute-start.9 = (bf16[2,176,256]{2,1,0:T(8,128)(2,1)}, bf16[2,176,256]{2,1,0:T(8,128)(2,1)}, u32[]{:S(2)}, u32[]{:S(2)}) collective-permute-start(bf16[2,176,256]{2,1,0:T(8,128)(2,1)} %get-tuple-element.19), channel_id=1, source_target_pairs={{0,112},{16,0},{32,16},{48,32},{64,48},{80,64},{96,80},{112,96},{1... | collective-permute-start | bytes 540680 | tf_op jit(solution)/shard_map/ppermute | solution.py:90
  31.6 112.0 %collective-permute-start.8 = (bf16[2,176,256]{2,1,0:T(8,128)(2,1)}, bf16[2,176,256]{2,1,0:T(8,128)(2,1)}, u32[]{:S(2)}, u32[]{:S(2)}) collective-permute-start(bf16[2,176,256]{2,1,0:T(8,128)(2,1)} %get-tuple-element.20), channel_id=1, source_target_pairs={{0,16},{16,32},{32,48},{48,64},{64,80},{80,96},{96,112},{112,0},{1... | collective-permute-start | bytes 540680 | tf_op jit(solution)/shard_map/ppermute | solution.py:90
  35.4 14.1 %copy-start.16 = (s32[1,16]{1,0:T(1,128)S(1)}, s32[1,16]{1,0:T(1,128)}, u32[]{:S(2)}) copy-start(s32[1,16]{1,0:T(1,128)} %param.29) | copy-start | bytes 196
  43.6 9.9 %copy-start.6 = (bf16[16,2,64,256]{3,2,1,0:T(8,128)(2,1)}, bf16[16,2,64,256]{3,2,1,0:T(8,128)(2,1)S(1)}, u32[]{:S(2)}) copy-start(bf16[16,2,64,256]{3,2,1,0:T(8,128)(2,1)S(1)} %all-to-all-done) | copy-start | bytes 3145732
  44.7 25.1 %collective-permute-start.1 = (bf16[16,2,64,256]{3,2,0,1:T(8,128)(2,1)}, bf16[16,2,64,256]{3,2,0,1:T(8,128)(2,1)}, u32[]{:S(2)}, u32[]{:S(2)}) collective-permute-start(bf16[16,2,64,256]{3,2,0,1:T(8,128)(2,1)} %copy.66), channel_id=1, source_target_pairs={{0,32},{16,48},{32,64},{48,80},{64,96},{80,112},{96,0},{112,16},{1... | collective-permute-start | bytes 3145736 | tf_op jit(solution)/shard_map/ppermute | solution.py:90
  46.7 25.2 %collective-permute-start.2 = (bf16[16,2,64,256]{3,2,0,1:T(8,128)(2,1)}, bf16[16,2,64,256]{3,2,0,1:T(8,128)(2,1)}, u32[]{:S(2)}, u32[]{:S(2)}) collective-permute-start(bf16[16,2,64,256]{3,2,0,1:T(8,128)(2,1)} %copy.66), channel_id=1, source_target_pairs={{0,96},{16,112},{32,0},{48,16},{64,32},{80,48},{96,64},{112,80},{1... | collective-permute-start | bytes 3145736 | tf_op jit(solution)/shard_map/ppermute | solution.py:90
  63.7 26.4 %collective-permute-start = (bf16[16,2,64,256]{3,2,0,1:T(8,128)(2,1)}, bf16[16,2,64,256]{3,2,0,1:T(8,128)(2,1)}, u32[]{:S(2)}, u32[]{:S(2)}) collective-permute-start(bf16[16,2,64,256]{3,2,0,1:T(8,128)(2,1)} %copy.66), channel_id=1, source_target_pairs={{0,16},{16,0},{32,48},{48,32},{64,80},{80,64},{96,112},{112,96},{1... | collective-permute-start | bytes 3145736 | tf_op jit(solution)/shard_map/ppermute | solution.py:93
  63.7 13.3 %copy-start.15 = (bf16[2048]{0:T(1024)(128)(2,1)S(1)}, bf16[2048]{0:T(1024)(128)(2,1)}, u32[]{:S(2)}) copy-start(bf16[2048]{0:T(1024)(128)(2,1)} %param.19) | copy-start | bytes 12292
  65.0 12.6 %copy-start.5 = (bf16[2,4,256,352]{2,3,0,1:T(8,128)(2,1)S(1)}, bf16[2,4,256,352]{2,3,0,1:T(8,128)(2,1)}, u32[]{:S(2)}) copy-start(bf16[2,4,256,352]{2,3,0,1:T(8,128)(2,1)} %select_bitcast_fusion) | copy-start | bytes 4325380
  71.8 15.3 %collective-permute-start.5 = (bf16[8,2,64,256]{3,2,0,1:T(8,128)(2,1)}, bf16[8,2,64,256]{3,2,0,1:T(8,128)(2,1)}, u32[]{:S(2)}, u32[]{:S(2)}) collective-permute-start(bf16[8,2,64,256]{3,2,0,1:T(8,128)(2,1)} %slice.110), channel_id=1, source_target_pairs={{0,32},{16,48},{32,64},{48,80},{64,96},{80,112},{96,0},{112,16},{1... | collective-permute-start | bytes 1572872 | tf_op jit(solution)/shard_map/ppermute | solution.py:90
  73.8 14.7 %collective-permute-start.6 = (bf16[8,2,64,256]{3,2,0,1:T(8,128)(2,1)}, bf16[8,2,64,256]{3,2,0,1:T(8,128)(2,1)}, u32[]{:S(2)}, u32[]{:S(2)}) collective-permute-start(bf16[8,2,64,256]{3,2,0,1:T(8,128)(2,1)} %slice.111), channel_id=1, source_target_pairs={{0,96},{16,112},{32,0},{48,16},{64,32},{80,48},{96,64},{112,80},{1... | collective-permute-start | bytes 1572872 | tf_op jit(solution)/shard_map/ppermute | solution.py:90
  79.8 4.0 %copy-start.4 = (bf16[2,4,256,352]{2,3,0,1:T(8,128)(2,1)S(1)}, bf16[2,4,256,352]{2,3,0,1:T(8,128)(2,1)}, u32[]{:S(2)}) copy-start(bf16[2,4,256,352]{2,3,0,1:T(8,128)(2,1)} %select_bitcast_fusion.1) | copy-start | bytes 4325380
  84.9 1.9 copy-start.17
  86.9 3.5 %copy-start.7 = (bf16[16,2,64,256]{3,2,1,0:T(8,128)(2,1)S(1)}, bf16[16,2,64,256]{3,2,1,0:T(8,128)(2,1)}, u32[]{:S(2)}) copy-start(bf16[16,2,64,256]{3,2,1,0:T(8,128)(2,1)} %copy-done.6) | copy-start | bytes 3145732
  86.9 3.5 %copy-start.9 = (bf16[2,1024,352,1]{1,2,0,3:T(8,128)(2,1)S(1)}, bf16[2,1024,352,1]{1,2,0,3:T(8,128)(2,1)}, u32[]{:S(2)}) copy-start(bf16[2,1024,352,1]{1,2,0,3:T(8,128)(2,1)} %reshape.137) | copy-start | bytes 4325380
  87.1 7.4 %collective-permute-start.3 = (bf16[16,2,64,256]{3,2,0,1:T(8,128)(2,1)}, bf16[16,2,64,256]{3,2,0,1:T(8,128)(2,1)S(1)}, u32[]{:S(2)}, u32[]{:S(2)}) collective-permute-start(bf16[16,2,64,256]{3,2,0,1:T(8,128)(2,1)} %collective-permute-done.1), channel_id=1, source_target_pairs={{0,16},{16,0},{32,48},{48,32},{64,80},{80,64},{96,112},{112,96},{1... | collective-permute-start | bytes 3145736 | tf_op jit(solution)/shard_map/ppermute | solution.py:93
  88.4 6.0 %collective-permute-start.4 = (bf16[16,2,64,256]{3,2,0,1:T(8,128)(2,1)}, bf16[16,2,64,256]{3,2,0,1:T(8,128)(2,1)S(1)}, u32[]{:S(2)}, u32[]{:S(2)}) collective-permute-start(bf16[16,2,64,256]{3,2,0,1:T(8,128)(2,1)} %collective-permute-done.2), channel_id=1, source_target_pairs={{0,16},{16,0},{32,48},{48,32},{64,80},{80,64},{96,112},{112,96},{1... | collective-permute-start | bytes 3145736 | tf_op jit(solution)/shard_map/ppermute | solution.py:93
  90.1 4.4 %copy-start.8 = (bf16[2,1024,352,1]{1,2,0,3:T(8,128)(2,1)S(1)}, bf16[2,1024,352,1]{1,2,0,3:T(8,128)(2,1)}, u32[]{:S(2)}) copy-start(bf16[2,1024,352,1]{1,2,0,3:T(8,128)(2,1)} %reshape.138) | copy-start | bytes 4325380
  90.1 4.3 %collective-permute-start.7 = (bf16[16,2,64,256]{3,2,0,1:T(8,128)(2,1)S(1)}, bf16[16,2,64,256]{3,2,0,1:T(8,128)(2,1)S(1)}, u32[]{:S(2)}, u32[]{:S(2)}) collective-permute-start(bf16[16,2,64,256]{3,2,0,1:T(8,128)(2,1)S(1)} %constant_dynamic-update-slice_fusion), channel_id=1, source_target_pairs={{0,16},{16,0},{32,48},{48,32},{64,80},{80,64},{96,112},{112,96},{1... | collective-permute-start | bytes 3145736 | tf_op jit(solution)/shard_map/ppermute | solution.py:93
  97.7 38.9 %collective-permute-start.13 = (bf16[16,2,64,176]{3,2,0,1:T(8,128)(2,1)S(1)}, bf16[16,2,64,176]{3,2,0,1:T(8,128)(2,1)S(1)}, u32[]{:S(2)}, u32[]{:S(2)}) collective-permute-start(bf16[16,2,64,176]{3,2,0,1:T(8,128)(2,1)S(1)} %fusion.21), channel_id=1, source_target_pairs={{0,96},{16,112},{32,0},{48,16},{64,32},{80,48},{96,64},{112,80},{1... | collective-permute-start | bytes 2162696 | tf_op jit(solution)/shard_map/ppermute | solution.py:90
  98.3 41.2 %collective-permute-start.12 = (bf16[16,2,64,176]{3,2,0,1:T(8,128)(2,1)S(1)}, bf16[16,2,64,176]{3,2,0,1:T(8,128)(2,1)}, u32[]{:S(2)}, u32[]{:S(2)}) collective-permute-start(bf16[16,2,64,176]{3,2,0,1:T(8,128)(2,1)S(1)} %fusion.21), channel_id=1, source_target_pairs={{0,32},{16,48},{32,64},{48,80},{64,96},{80,112},{96,0},{112,16},{1... | collective-permute-start | bytes 2162696 | tf_op jit(solution)/shard_map/ppermute | solution.py:90
  99.8 45.7 %collective-permute-start.10 = (bf16[16,2,64,176]{3,2,0,1:T(8,128)(2,1)S(1)}, bf16[16,2,64,176]{3,2,0,1:T(8,128)(2,1)}, u32[]{:S(2)}, u32[]{:S(2)}) collective-permute-start(bf16[16,2,64,176]{3,2,0,1:T(8,128)(2,1)S(1)} %fusion.21), channel_id=1, source_target_pairs={{0,16},{16,0},{32,48},{48,32},{64,80},{80,64},{96,112},{112,96},{1... | collective-permute-start | bytes 2162696 | tf_op jit(solution)/shard_map/ppermute | solution.py:93
  123.9 4.1 %copy-start.18 = (bf16[512,2048]{1,0:T(8,128)(2,1)S(1)}, bf16[512,2048]{1,0:T(8,128)(2,1)}, u32[]{:S(2)}) copy-start(bf16[512,2048]{1,0:T(8,128)(2,1)} %all-gather.3.cloned.1.call-done) | copy-start | bytes 6291460
  131.7 5.0 %copy-start.10 = (bf16[2,176,256]{2,1,0:T(8,128)(2,1)S(1)}, bf16[2,176,256]{2,1,0:T(8,128)(2,1)}, u32[]{:S(2)}) copy-start(bf16[2,176,256]{2,1,0:T(8,128)(2,1)} %get-tuple-element.16) | copy-start | bytes 540676
  136.6 41.3 %collective-permute-start.16 = (bf16[2,176,256]{2,1,0:T(8,128)(2,1)S(1)}, bf16[2,176,256]{2,1,0:T(8,128)(2,1)}, u32[]{:S(2)}, u32[]{:S(2)}) collective-permute-start(bf16[2,176,256]{2,1,0:T(8,128)(2,1)S(1)} %copy-done.10), channel_id=1, source_target_pairs={{0,96},{16,112},{32,0},{48,16},{64,32},{80,48},{96,64},{112,80},{1... | collective-permute-start | bytes 540680 | tf_op jit(solution)/shard_map/ppermute | solution.py:90
  139.6 12.0 %collective-permute-start.11 = (bf16[2,176,256]{2,1,0:T(8,128)(2,1)}, bf16[2,176,256]{2,1,0:T(8,128)(2,1)S(1)}, u32[]{:S(2)}, u32[]{:S(2)}) collective-permute-start(bf16[2,176,256]{2,1,0:T(8,128)(2,1)} %get-tuple-element.18), channel_id=1, source_target_pairs={{0,32},{16,48},{32,64},{48,80},{64,96},{80,112},{96,0},{112,16},{1... | collective-permute-start | bytes 540680 | tf_op jit(solution)/shard_map/ppermute | solution.py:90
  141.5 11.8 %collective-permute-start.19 = (bf16[2,176,256]{2,1,0:T(8,128)(2,1)}, bf16[2,176,256]{2,1,0:T(8,128)(2,1)S(1)}, u32[]{:S(2)}, u32[]{:S(2)}) collective-permute-start(bf16[2,176,256]{2,1,0:T(8,128)(2,1)} %get-tuple-element.21), channel_id=1, source_target_pairs={{0,64},{16,80},{32,96},{48,112},{64,0},{80,16},{96,32},{112,48},{1... | collective-permute-start | bytes 540680 | tf_op jit(solution)/shard_map/ppermute | solution.py:90
  143.7 21.7 %collective-permute-start.20 = (bf16[8,2,64,176]{3,2,0,1:T(8,128)(2,1)}, bf16[8,2,64,176]{3,2,0,1:T(8,128)(2,1)S(1)}, u32[]{:S(2)}, u32[]{:S(2)}) collective-permute-start(bf16[8,2,64,176]{3,2,0,1:T(8,128)(2,1)} %slice.90), channel_id=1, source_target_pairs={{0,32},{16,48},{32,64},{48,80},{64,96},{80,112},{96,0},{112,16},{1... | collective-permute-start | bytes 1081352 | tf_op jit(solution)/shard_map/ppermute | solution.py:90
  148.7 23.2 %collective-permute-start.15 = (bf16[16,2,64,176]{3,2,0,1:T(8,128)(2,1)}, bf16[16,2,64,176]{3,2,0,1:T(8,128)(2,1)S(1)}, u32[]{:S(2)}, u32[]{:S(2)}) collective-permute-start(bf16[16,2,64,176]{3,2,0,1:T(8,128)(2,1)} %collective-permute-done.12), channel_id=1, source_target_pairs={{0,16},{16,0},{32,48},{48,32},{64,80},{80,64},{96,112},{112,96},{1... | collective-permute-start | bytes 2162696 | tf_op jit(solution)/shard_map/ppermute | solution.py:93
  148.7 4.6 %copy-start.12 = (bf16[2,176,256]{2,1,0:T(8,128)(2,1)S(1)}, bf16[2,176,256]{2,1,0:T(8,128)(2,1)}, u32[]{:S(2)}) copy-start(bf16[2,176,256]{2,1,0:T(8,128)(2,1)} %get-tuple-element.17) | copy-start | bytes 540676
  148.8 20.8 %copy-start.11 = (bf16[2,176,256]{2,1,0:T(8,128)(2,1)S(1)}, bf16[2,176,256]{2,1,0:T(8,128)(2,1)}, u32[]{:S(2)}) copy-start(bf16[2,176,256]{2,1,0:T(8,128)(2,1)} %get-tuple-element.22) | copy-start | bytes 540676
  151.6 17.9 %collective-permute-start.22 = (bf16[8,2,64,176]{3,2,0,1:T(8,128)(2,1)S(1)}, bf16[8,2,64,176]{3,2,0,1:T(8,128)(2,1)S(1)}, u32[]{:S(2)}, u32[]{:S(2)}) collective-permute-start(bf16[8,2,64,176]{3,2,0,1:T(8,128)(2,1)S(1)} %slice.91), channel_id=1, source_target_pairs={{0,96},{16,112},{32,0},{48,16},{64,32},{80,48},{96,64},{112,80},{1... | collective-permute-start | bytes 1081352 | tf_op jit(solution)/shard_map/ppermute | solution.py:90
  153.3 16.6 %collective-permute-start.14 = (bf16[2,176,256]{2,1,0:T(8,128)(2,1)S(1)}, bf16[2,176,256]{2,1,0:T(8,128)(2,1)S(1)}, u32[]{:S(2)}, u32[]{:S(2)}) collective-permute-start(bf16[2,176,256]{2,1,0:T(8,128)(2,1)S(1)} %copy-done.12), channel_id=1, source_target_pairs={{0,48},{16,64},{32,80},{48,96},{64,112},{80,0},{96,16},{112,32},{1... | collective-permute-start | bytes 540680 | tf_op jit(solution)/shard_map/ppermute | solution.py:90
  165.4 11.4 %collective-permute-start.18 = (bf16[16,2,64,176]{3,2,0,1:T(8,128)(2,1)S(1)}, bf16[16,2,64,176]{3,2,0,1:T(8,128)(2,1)S(1)}, u32[]{:S(2)}, u32[]{:S(2)}) collective-permute-start(bf16[16,2,64,176]{3,2,0,1:T(8,128)(2,1)S(1)} %collective-permute-done.13), channel_id=1, source_target_pairs={{0,16},{16,0},{32,48},{48,32},{64,80},{80,64},{96,112},{112,96},{1... | collective-permute-start | bytes 2162696 | tf_op jit(solution)/shard_map/ppermute | solution.py:93
  169.5 7.3 %collective-permute-start.17 = (bf16[2,176,256]{2,1,0:T(8,128)(2,1)S(1)}, bf16[2,176,256]{2,1,0:T(8,128)(2,1)S(1)}, u32[]{:S(2)}, u32[]{:S(2)}) collective-permute-start(bf16[2,176,256]{2,1,0:T(8,128)(2,1)S(1)} %copy-done.11), channel_id=1, source_target_pairs={{0,80},{16,96},{32,112},{48,0},{64,16},{80,32},{96,48},{112,64},{1... | collective-permute-start | bytes 540680 | tf_op jit(solution)/shard_map/ppermute | solution.py:90
  169.8 7.8 %collective-permute-start.23 = (bf16[8,2,64,176]{3,2,0,1:T(8,128)(2,1)S(1)}, bf16[8,2,64,176]{3,2,0,1:T(8,128)(2,1)S(1)}, u32[]{:S(2)}, u32[]{:S(2)}) collective-permute-start(bf16[8,2,64,176]{3,2,0,1:T(8,128)(2,1)S(1)} %collective-permute-done.22), channel_id=1, source_target_pairs={{0,16},{16,0},{32,48},{48,32},{64,80},{80,64},{96,112},{112,96},{1... | collective-permute-start | bytes 1081352 | tf_op jit(solution)/shard_map/ppermute | solution.py:93
  171.9 5.4 %collective-permute-start.21 = (bf16[8,2,64,176]{3,2,0,1:T(8,128)(2,1)S(1)}, bf16[8,2,64,176]{3,2,0,1:T(8,128)(2,1)S(1)}, u32[]{:S(2)}, u32[]{:S(2)}) collective-permute-start(bf16[8,2,64,176]{3,2,0,1:T(8,128)(2,1)S(1)} %collective-permute-done.20), channel_id=1, source_target_pairs={{0,16},{16,0},{32,48},{48,32},{64,80},{80,64},{96,112},{112,96},{1... | collective-permute-start | bytes 1081352 | tf_op jit(solution)/shard_map/ppermute | solution.py:93
  177.3 1.6 copy-start.3
  177.6 2.0 copy-start.2
  181.5 5.2 %copy-start.19 = (bf16[2048,32]{0,1:T(8,128)(2,1)S(1)}, bf16[2048,32]{0,1:T(8,128)(2,1)}, u32[]{:S(2)}) copy-start(bf16[2048,32]{0,1:T(8,128)(2,1)} %param.18) | copy-start | bytes 393220
  182.7 22.2 %all-to-all-start.1 = ((bf16[16,2,64,256]{3,2,1,0:T(8,128)(2,1)}), bf16[16,2,64,256]{3,2,1,0:T(8,128)(2,1)S(1)}, u32[]{:S(2)}, u32[]{:S(2)}) async-start(bf16[16,2,64,256]{3,2,1,0:T(8,128)(2,1)} %copy.70), calls=%async_computation.1 | async-start | bytes 2097152 | tf_op jit(solution)/shard_map/all_to_all | solution.py:180
  205.9 2.7 %copy-start.1 = (bf16[64,16,704]{2,1,0:T(8,128)(2,1)S(1)}, bf16[64,16,704]{2,1,0:T(8,128)(2,1)}, u32[]{:S(2)}) copy-start(bf16[64,16,704]{2,1,0:T(8,128)(2,1)} %param.27) | copy-start | bytes 4325380
Sparse Core Ops, SparseCore 0:
  11.7 31.6 all-gather.2
  45.5 78.3 all-gather.4
  148.8 37.2 reduce-scatter.1

commit v13 on v12

--- a/solution.py
+++ b/solution.py
@@ -145,10 +145,10 @@
         preferred_element_type=jnp.float32,
     )
     shared_part = shared_part * share[:, None]
-    shared_part, from_below, from_above = lax.optimization_barrier((shared_part, from_below, from_above))
-    shared_sum = lax.psum_scatter(shared_part, "row", scatter_dimension=1, tiled=True)
     far_low = shifted(from_below[:group_half], 2)
     far_high = shifted(from_above[group_half:], -2)
+    shared_part, far_low, far_high = lax.optimization_barrier((shared_part, far_low, far_high))
+    shared_sum = lax.psum_scatter(shared_part, "row", scatter_dimension=1, tiled=True)
 
     def down_slice(k):
         return lax.dynamic_slice_in_dim(

time: 216 us -> 204 us (0.944)
  waiting for transfers between devices: 69.4 us -> 53.8 us
  matrix products: 40.4 us -> 44.1 us
    all_gather x1, waiting for transfers between devices: 17.8 us -> 0.01 us  [on_device(): shared_full = lax.all_gather(shared_stack, 'col', axis=1, tiled=True)]
    dot_general x10, matrix products: 12.4 us -> 17 us  [down_of(): jnp.einsum('sexf,efd->sexd', block, weight, preferred_element_type=jnp.fl...]
    ppermute x15, waiting for transfers between devices: 26.9 us -> 29.7 us  [shifted(): lax.ppermute(x, 'row', [(i, (i + shift) % row_count) for i in range(row_c...]
  transfers between devices with their start and end apart: 29 -> 29, of which waited for: 8 -> 6; matrix products, arithmetic and copies ran while one was open for 42% -> 46% of each run, Pallas kernels for 0% -> 0%
where the time goes in v13:
time: 204 us; the launch traced here: 203 us
  waiting for transfers between devices  53.8 us (26%)
  matrix products  44.1 us (22%)
  local copies, waits for them, and re-layouts  35.7 us (18%)
  starting transfers between devices  34 us (17%)
  other arithmetic  21.2 us (10%)
  between operations  13.8 us (7%)
    ppermute x15, waiting for transfers between devices, shifted(): lax.ppermute(x, 'row', [(i, (i + shift) % row_count) for i in range(row_c...  29.7 us
    ppermute x15, starting transfers between devices, shifted(): lax.ppermute(x, 'row', [(i, (i + shift) % row_count) for i in range(row_c...  20.7 us
    dot_general x10, matrix products, down_of(): jnp.einsum('sexf,efd->sexd', block, weight, preferred_element_type=jnp.fl...  17 us
    all_to_all x1, waiting for transfers between devices, on_device(): lax.all_to_all(expert_value.astype(jnp.bfloat16), 'col', split_axis=0, co...  15.8 us
    all_to_all x1, waiting for transfers between devices, on_device(): lax.all_to_all(outgoing, 'col', split_axis=0, concat_axis=0, tiled=True)  8.18 us
    all_to_all x1, starting transfers between devices, on_device(): lax.all_to_all(outgoing, 'col', split_axis=0, concat_axis=0, tiled=True)  7.15 us
    dot_general x2, matrix products, project(): jnp.einsum('sexd,edf->sexf', features, ordered, preferred_element_type=jn...  6.63 us
    gather x2, local copies, waits for them, and re-layouts, project(): jnp.take(blocks, order, axis=1).reshape(w.shape[0], -1, w.shape[2])  6.27 us
  transfers between devices with their start and end apart: 29, of which 6 were waited for; matrix products, arithmetic and copies ran while one was open for 46% of the time, Pallas kernels for 0%

profile of v13, /device:TPU:0, one launch (start us, length us, event | category | flops | bytes accessed | tf_op | source)
XLA Modules:
  0.0 202.5 jit_solution(1894644447374990762)
XLA Ops:
  6.5 0.8 compare_and_fusion.2
  7.3 0.7 compare_select_fusion.2
  8.2 1.6 gather_fusion
  9.9 1.6 pad_maximum_fusion.2
  11.6 2.0 pad_maximum_fusion.1
  13.6 0.6 reduce-window.18
  14.6 2.6 %fusion = pred[2048,256]{1,0:T(8,128)(4,1)S(1)} fusion(s32[256,4]{0,1:T(4,128)S(1)} %multiply_add_fusion), kind=kLoop, calls=%fused_computation.5 | loop fusion | flops 3670016 | bytes 528384 | tf_op jit(solution)/shard_map/reduce_or | solution.py:110
  17.2 1.4 convolution_convert_fusion
  18.7 7.1 %all-to-all-start = ((bf16[16,2,64,256]{3,2,1,0:T(8,128)(2,1)}), bf16[16,2,64,256]{3,2,1,0:T(8,128)(2,1)S(1)}, u32[]{:S(2)}, u32[]{:S(2)}) async-start(bf16[16,2,64,256]{3,2,1,0:T(8,128)(2,1)} %bitcast.147), calls=%async_computation | async-start | bytes 2097152 | tf_op jit(solution)/shard_map/all_to_all | solution.py:113
  26.0 2.4 %constant_dynamic-slice_fusion.5 = (bf16[2,176,256]{2,1,0:T(8,128)(2,1)}, bf16[2,176,256]{2,1,0:T(8,128)(2,1)}, bf16[2,176,256]{2,1,0:T(8,128)(2,1)}, bf16[2,176...) fusion(bf16[2,176,2048]{2,1,0:T(8,128)(2,1)} %param.25, ...), kind=kLoop, calls=%fused_computation.147 | loop fusion | bytes 2523164 | tf_op jit(solution)/shard_map/dynamic_slice | solution.py:154
  28.4 3.2 %collective-permute-start.9 = (bf16[2,176,256]{2,1,0:T(8,128)(2,1)}, bf16[2,176,256]{2,1,0:T(8,128)(2,1)}, u32[]{:S(2)}, u32[]{:S(2)}) collective-permute-start(bf16[2,176,256]{2,1,0:T(8,128)(2,1)} %get-tuple-element.16), channel_id=1, source_target_pairs={{0,112},{16,0},{32,16},{48,32},{64,48},{80,64},{96,80},{112,96},{1... | collective-permute-start | bytes 540680 | tf_op jit(solution)/shard_map/ppermute | solution.py:90
  31.6 3.8 %pad_maximum_fusion = bf16[2,2048,352]{1,2,0:T(8,128)(2,1)} fusion(bf16[2,2048,176]{1,2,0:T(8,128)(2,1)} %param.24, bf16[2,2048,176]{1,2,0:T(8,128)(2,1)} %param.23), kind=kLoop, calls=%fused_computation.30 | loop fusion | flops 5767168 | bytes 5767168 | tf_op jit(solution)/shard_map/concatenate | solution.py:128
  35.4 8.2 %all-to-all-done = bf16[16,2,64,256]{3,2,1,0:T(8,128)(2,1)S(1)} async-done(((bf16[16,2,64,256]{3,2,1,0:T(8,128)(2,1)}), bf16[16,2,64,256]{3,2,1,0:T(8,128)(2,1)S(1)}, u32[]{:S(2)}, u32[]{:S(2)}) %all-to-all-start) | async-done | bytes 1048608 | tf_op jit(solution)/shard_map/all_to_all | solution.py:113
  43.6 1.1 copy.66
  44.7 1.9 collective-permute-start.1
  46.7 2.1 %collective-permute-start.2 = (bf16[16,2,64,256]{3,2,0,1:T(8,128)(2,1)}, bf16[16,2,64,256]{3,2,0,1:T(8,128)(2,1)}, u32[]{:S(2)}, u32[]{:S(2)}) collective-permute-start(bf16[16,2,64,256]{3,2,0,1:T(8,128)(2,1)} %copy.66), channel_id=1, source_target_pairs={{0,96},{16,112},{32,0},{48,16},{64,32},{80,48},{96,64},{112,80},{1... | collective-permute-start | bytes 3145736 | tf_op jit(solution)/shard_map/ppermute | solution.py:90
  48.8 0.6 fusion.95
  49.7 3.7 %copy.90 = bf16[2,44,8,8,256]{4,3,1,2,0:T(8,128)(2,1)} copy(bf16[2,44,8,8,256]{4,3,2,1,0:T(8,128)(2,1)} %bitcast.146) | data formatting | bytes 5767168 | tf_op jit(solution)/shard_map/reshape | solution.py:118
  53.4 1.3 compare_and_fusion
  54.7 2.6 %gather_fusion.3 = bf16[4,2,256,352]{2,3,1,0:T(8,128)(2,1)S(1)} fusion(bf16[2,8,256,352]{2,3,1,0:T(8,128)(2,1)} %bitcast.144, s32[1024]{0:T(1024)S(1)} %pad_clamp_fusion), kind=kCustom, calls=%fused_computation.1.clone | custom fusion | bytes 2883600 | tf_op jit(solution)/shard_map/jit(_take)/gather | solution.py:123
  57.3 3.7 %gather_fusion.2 = bf16[4,2,256,352]{2,3,1,0:T(8,128)(2,1)} fusion(bf16[2,8,256,352]{2,3,1,0:T(8,128)(2,1)} %bitcast.145, s32[1024]{0:T(1024)S(1)} %pad_clamp_fusion.1), kind=kCustom, calls=%fused_computation.clone | custom fusion | bytes 2883600 | tf_op jit(solution)/shard_map/jit(_take)/gather | solution.py:123
  61.0 2.7 %select_bitcast_fusion.1 = bf16[2,4,256,352]{2,3,0,1:T(8,128)(2,1)} fusion(bf16[4,2,256,352]{2,3,1,0:T(8,128)(2,1)} %gather_fusion.2, pred[4]{0:T(512)(128)(4,1)S(1)} %get-tuple-element.33), kind=kLoop, calls=%fused_computation.48 | loop fusion | flops 720896 | bytes 2883588 | tf_op jit(solution)/shard_map/jit(_take)/select_n | solution.py:123
  63.7 1.3 select_bitcast_fusion
  65.0 4.8 %collective-permute-done.1 = bf16[16,2,64,256]{3,2,0,1:T(8,128)(2,1)} collective-permute-done((bf16[16,2,64,256]{3,2,0,1:T(8,128)(2,1)}, bf16[16,2,64,256]{3,2,0,1:T(8,128)(2,1)}, u32[]{:S(2)}, u32[]{:S(2)}) %collective-permute-start.1) | collective-permute-done | bytes 1048608 | tf_op jit(solution)/shard_map/ppermute | solution.py:90
  69.8 1.9 slice.110
  71.8 1.9 slice.111
  73.7 3.2 %collective-permute-start.6 = (bf16[8,2,64,256]{3,2,0,1:T(8,128)(2,1)}, bf16[8,2,64,256]{3,2,0,1:T(8,128)(2,1)}, u32[]{:S(2)}, u32[]{:S(2)}) collective-permute-start(bf16[8,2,64,256]{3,2,0,1:T(8,128)(2,1)} %slice.111), channel_id=1, source_target_pairs={{0,96},{16,112},{32,0},{48,16},{64,32},{80,48},{96,64},{112,80},{1... | collective-permute-start | bytes 1572872 | tf_op jit(solution)/shard_map/ppermute | solution.py:90
  77.6 2.3 %copy.68 = bf16[2,4,256,352]{2,1,3,0:T(4,128)(2,1)} copy(bf16[2,4,256,352]{2,3,0,1:T(8,128)(2,1)S(1)} %copy-done.7) | data formatting | bytes 2883584 | tf_op jit(solution)/shard_map/jit(_take)/select_n | solution.py:123
  79.8 4.0 %reshape.138 = bf16[2,1024,352,1]{1,2,0,3:T(8,128)(2,1)} reshape(bf16[2,4,256,352]{2,1,3,0:T(4,128)(2,1)} %copy.68) | data formatting | bytes 2883584 | tf_op jit(solution)/shard_map/reshape | solution.py:123
  83.8 1.1 copy.62
  85.0 1.9 reshape.137
  87.0 0.9 bitcast_select_fusion
  87.8 1.1 constant_dynamic-update-slice_fusion.1
  88.9 0.6 collective-permute-start.4
  89.5 1.1 constant_dynamic-update-slice_fusion
  90.7 4.0 %fusion.1 = f32[2,352,16,64]{1,3,2,0:T(8,128)S(1)} fusion(bf16[16,2,64,256]{3,2,0,1:T(8,128)(2,1)} %collective-permute-done.2, bf16[16,2,64,256]{3,2,0,1:T(8,128)(2,1)} %collective-permute-done.1, bf16[16,2,64,256]{3,2,0,1:T(8,128)(2,1)} %collective-permute-done, bf16[2,1024,352,1]{1,2,0,3:T(8,128)(2,1)S(1)} %copy-done.11, ...), kind=kOutput, calls=%fused_computation.6 | convolution fusion | flops 1493172224 | bytes 8519680 | tf_op jit(solution)/shard_map/sexd,edf->sexf/dot_general | solution.py:124
  94.8 2.6 %add_bitcast_fusion = f32[16,2,64,352]{3,2,0,1:T(8,128)S(1)} fusion(f32[2,352,16,64]{1,3,2,0:T(8,128)S(1)} %fusion.1, bf16[16,2,64,256]{3,2,0,1:T(8,128)(2,1)S(1)} %collective-permute-done.7, bf16[16,2,64,256]{3,2,0,1:T(8,128)(2,1)S(1)} %constant_dynamic-update-slice_fusion, bf16[16,2,64,256]{3,2,0,1:T(8,128)(2,1)S(1)} %collective-permute-done.4, ...), kind=kOutput, calls=%fused_computation.22 | convolution fusion | flops 1493893120 | bytes 11403264 | tf_op jit(solution)/shard_map/sexd,edf->sexf/dot_general | solution.py:124
  97.4 0.6 fusion.21
  98.0 0.6 collective-permute-start.16
  98.7 1.5 collective-permute-start.12
  100.1 2.7 %fusion.72 = f32[2,256,16,64]{1,3,2,0:T(8,128)} fusion(bf16[16,2,64,176]{3,2,0,1:T(8,128)(2,1)S(1)} %fusion.21, bf16[2,176,2048]{2,1,0:T(8,128)(2,1)} %param.25, s32[]{:T(128)S(6)} %select_n.145), kind=kOutput, calls=%fused_computation.97 | convolution fusion | flops 184549376 | bytes 2998276 | tf_op jit(solution)/shard_map/sexf,efd->sexd/dot_general | solution.py:165
  102.8 2.2 %fusion.43 = bf16[256,256]{1,0:T(8,128)(2,1)S(1)} fusion(bf16[512,2048]{1,0:T(8,128)(2,1)} %all-gather.3.cloned.1.call-done, s32[256]{0:T(256)S(1)} %and_select_fusion, s32[256]{0:T(256)S(1)} %select_reduce_fusion.2), kind=kOutput, calls=%fused_computation.65 | convolution fusion | flops 268632064 | bytes 2230272 | tf_op jit(solution)/shard_map/dot_general | solution.py:78
  105.5 18.1 %collective-permute-done.16 = bf16[16,2,64,176]{3,2,0,1:T(8,128)(2,1)S(1)} collective-permute-done((bf16[16,2,64,176]{3,2,0,1:T(8,128)(2,1)S(1)}, bf16[16,2,64,176]{3,2,0,1:T(8,128)(2,1)S(1)}, u32[]{:S(2)}, u32[]{:S(2)}) %collective-permute-start.16) | collective-permute-done | bytes 720928 | tf_op jit(solution)/shard_map/ppermute | solution.py:90
  123.5 1.8 collective-permute-start.15
  125.5 1.9 slice.118
  127.7 3.1 %fusion.68 = f32[2,256,16,64]{1,3,2,0:T(8,128)} fusion(bf16[16,2,64,176]{3,2,0,1:T(8,128)(2,1)} %collective-permute-done.12, bf16[2,176,256]{2,1,0:T(8,128)(2,1)} %collective-permute-done.11), kind=kOutput, calls=%fused_computation.93 | convolution fusion | flops 184549376 | bytes 2998272 | tf_op jit(solution)/shard_map/sexf,efd->sexd/dot_general | solution.py:165
  130.8 2.6 %collective-permute-start.21 = (bf16[8,2,64,176]{3,2,0,1:T(8,128)(2,1)S(1)}, bf16[8,2,64,176]{3,2,0,1:T(8,128)(2,1)}, u32[]{:S(2)}, u32[]{:S(2)}) collective-permute-start(bf16[8,2,64,176]{3,2,0,1:T(8,128)(2,1)S(1)} %slice.119), channel_id=1, source_target_pairs={{0,96},{16,112},{32,0},{48,16},{64,32},{80,48},{96,64},{112,80},{1... | collective-permute-start | bytes 1081352 | tf_op jit(solution)/shard_map/ppermute | solution.py:90
  133.5 1.7 collective-permute-done.8
  135.2 3.2 %fusion.70 = f32[2,256,16,64]{1,3,2,0:T(8,128)} fusion(bf16[16,2,64,176]{3,2,0,1:T(8,128)(2,1)} %collective-permute-done.10, bf16[2,176,256]{2,1,0:T(8,128)(2,1)S(1)} %collective-permute-done.8, bf16[2,176,256]{2,1,0:T(8,128)(2,1)} %collective-permute-done.9, pred[]{:T(512)S(6)} %eq.138), kind=kOutput, calls=%fused_computation.95 | convolution fusion | flops 184639488 | bytes 3178497 | tf_op jit(solution)/shard_map/sexf,efd->sexd/dot_general | solution.py:165
  138.4 4.1 %fusion.18 = f32[256,704]{0,1:T(8,128)} fusion(bf16[3,2048,704]{1,2,0:T(8,128)(2,1)} %all-gather.5.cloned.1.call-done, bf16[512,2048]{1,0:T(8,128)(2,1)} %all-gather.3.cloned.1.call-done), kind=kOutput, calls=%fused_computation.27 | convolution fusion | flops 738197504 | bytes 4653056 | tf_op jit(solution)/shard_map/dot_general | solution.py:137
  142.5 3.7 %fusion.19 = f32[256,704]{0,1:T(8,128)} fusion(bf16[3,2048,704]{1,2,0:T(8,128)(2,1)} %all-gather.5.cloned.1.call-done, bf16[512,2048]{1,0:T(8,128)(2,1)S(1)} %copy-done.20), kind=kOutput, calls=%fused_computation.29 | convolution fusion | flops 738197504 | bytes 4653056 | tf_op jit(solution)/shard_map/dot_general | solution.py:136
  146.2 5.1 %fusion.20 = f32[256,2048]{1,0:T(8,128)} fusion(bf16[3,2048,704]{1,2,0:T(8,128)(2,1)} %all-gather.5.cloned.1.call-done, f32[256,704]{0,1:T(8,128)} %fusion.18, bf16[256,256]{1,0:T(8,128)(2,1)S(1)} %fusion.43, bf16[256,704]{1,0:T(8,128)(2,1)} %bitcast_select_fusion, f32[256]{0:T(256)S(1)} %add_divide_fusion, f32[256,704]{0,1:T(8,128)} %fusion.19), kind=kOutput, calls=%fused_computation.31 | convolution fusion | flops 832438272 | bytes 6947840 | tf_op jit(solution)/shard_map/dot_general | solution.py:141
  151.2 0.9 collective-permute-start.19
  152.2 2.3 %collective-permute-start.17 = (bf16[2,176,256]{2,1,0:T(8,128)(2,1)}, bf16[2,176,256]{2,1,0:T(8,128)(2,1)S(1)}, u32[]{:S(2)}, u32[]{:S(2)}) collective-permute-start(bf16[2,176,256]{2,1,0:T(8,128)(2,1)} %get-tuple-element.22), channel_id=1, source_target_pairs={{0,80},{16,96},{32,112},{48,0},{64,16},{80,32},{96,48},{112,64},{1... | collective-permute-start | bytes 540680 | tf_op jit(solution)/shard_map/ppermute | solution.py:90
  154.9 2.7 %fusion.64 = f32[2,256,16,64]{1,3,2,0:T(8,128)} fusion(bf16[16,2,64,176]{3,2,0,1:T(8,128)(2,1)S(1)} %collective-permute-done.16, bf16[2,176,256]{2,1,0:T(8,128)(2,1)} %collective-permute-done.15), kind=kOutput, calls=%fused_computation.89 | convolution fusion | flops 184549376 | bytes 2998272 | tf_op jit(solution)/shard_map/sexf,efd->sexd/dot_general | solution.py:165
  158.6 5.1 %collective-permute-done.17 = bf16[2,176,256]{2,1,0:T(8,128)(2,1)S(1)} collective-permute-done((bf16[2,176,256]{2,1,0:T(8,128)(2,1)}, bf16[2,176,256]{2,1,0:T(8,128)(2,1)S(1)}, u32[]{:S(2)}, u32[]{:S(2)}) %collective-permute-start.17) | collective-permute-done | bytes 180256 | tf_op jit(solution)/shard_map/ppermute | solution.py:90
  164.4 1.9 fusion.32
  166.3 1.5 fusion.31
  168.2 1.0 fusion.22
  169.2 1.1 copy.70
  170.3 4.4 %all-to-all-start.1 = ((bf16[16,2,64,256]{3,2,1,0:T(8,128)(2,1)}), bf16[16,2,64,256]{3,2,1,0:T(8,128)(2,1)S(1)}, u32[]{:S(2)}, u32[]{:S(2)}) async-start(bf16[16,2,64,256]{3,2,1,0:T(8,128)(2,1)} %copy.70), calls=%async_computation.1 | async-start | bytes 2097152 | tf_op jit(solution)/shard_map/all_to_all | solution.py:180
  174.7 1.6 fusion.59
  176.5 15.8 %all-to-all-done.1 = bf16[16,2,64,256]{3,2,1,0:T(8,128)(2,1)S(1)} async-done(((bf16[16,2,64,256]{3,2,1,0:T(8,128)(2,1)}), bf16[16,2,64,256]{3,2,1,0:T(8,128)(2,1)S(1)}, u32[]{:S(2)}, u32[]{:S(2)}) %all-to-all-start.1) | async-done | bytes 1048608 | tf_op jit(solution)/shard_map/all_to_all | solution.py:180
  194.3 1.7 add.216
  (125 shorter events, 7.6 us)
Async XLA Ops:
  6.5 70.4 %copy-start = (bf16[64,16,704]{2,1,0:T(8,128)(2,1)S(1)}, bf16[64,16,704]{2,1,0:T(8,128)(2,1)}, u32[]{:S(2)}) copy-start(bf16[64,16,704]{2,1,0:T(8,128)(2,1)} %param.27) | copy-start | bytes 4325380
  6.5 10.7 %copy-start.14 = (bf16[256,256]{1,0:T(8,128)(2,1)S(1)}, bf16[256,256]{1,0:T(8,128)(2,1)}, u32[]{:S(2)}) copy-start(bf16[256,256]{1,0:T(8,128)(2,1)} %param.17) | copy-start | bytes 393220
  6.5 7.0 %copy-start.15 = (s32[256,4]{0,1:T(4,128)S(1)}, s32[256,4]{0,1:T(4,128)}, u32[]{:S(2)}) copy-start(s32[256,4]{0,1:T(4,128)} %param.28) | copy-start | bytes 12292
  6.5 96.2 %all-gather.3.cloned.1.call-start = ((), (), s32[]{:S(2)}) async-start(), calls=%async_computation.3 | async-start | bytes 2359296 | tf_op jit(solution)/shard_map/all_gather | solution.py:34
  11.5 126.8 %all-gather.5.cloned.1.call-start = ((), (), s32[]{:S(2)}) async-start(), calls=%async_computation.4 | async-start | bytes 9191424 | tf_op jit(solution)/shard_map/all_gather | solution.py:53
  18.7 24.9 %all-to-all-start = ((bf16[16,2,64,256]{3,2,1,0:T(8,128)(2,1)}), bf16[16,2,64,256]{3,2,1,0:T(8,128)(2,1)S(1)}, u32[]{:S(2)}, u32[]{:S(2)}) async-start(bf16[16,2,64,256]{3,2,1,0:T(8,128)(2,1)} %bitcast.147), calls=%async_computation | async-start | bytes 2097152 | tf_op jit(solution)/shard_map/all_to_all | solution.py:113
  25.8 168.5 %reduce-scatter.2.cloned.1.call-start = ((), (), s32[]{:S(2)}) async-start(), calls=%async_computation.5 | async-start | bytes 2359296 | tf_op jit(solution)/shard_map/reduce_scatter | solution.py:151
  28.4 102.4 %collective-permute-start.9 = (bf16[2,176,256]{2,1,0:T(8,128)(2,1)}, bf16[2,176,256]{2,1,0:T(8,128)(2,1)}, u32[]{:S(2)}, u32[]{:S(2)}) collective-permute-start(bf16[2,176,256]{2,1,0:T(8,128)(2,1)} %get-tuple-element.16), channel_id=1, source_target_pairs={{0,112},{16,0},{32,16},{48,32},{64,48},{80,64},{96,80},{112,96},{1... | collective-permute-start | bytes 540680 | tf_op jit(solution)/shard_map/ppermute | solution.py:90
  31.6 95.7 %collective-permute-start.11 = (bf16[2,176,256]{2,1,0:T(8,128)(2,1)}, bf16[2,176,256]{2,1,0:T(8,128)(2,1)}, u32[]{:S(2)}, u32[]{:S(2)}) collective-permute-start(bf16[2,176,256]{2,1,0:T(8,128)(2,1)} %get-tuple-element.19), channel_id=1, source_target_pairs={{0,32},{16,48},{32,64},{48,80},{64,96},{80,112},{96,0},{112,16},{1... | collective-permute-start | bytes 540680 | tf_op jit(solution)/shard_map/ppermute | solution.py:90
  35.4 14.1 %copy-start.17 = (s32[1,16]{1,0:T(1,128)S(1)}, s32[1,16]{1,0:T(1,128)}, u32[]{:S(2)}) copy-start(s32[1,16]{1,0:T(1,128)} %param.29) | copy-start | bytes 196
  43.6 9.8 %copy-start.8 = (bf16[16,2,64,256]{3,2,1,0:T(8,128)(2,1)}, bf16[16,2,64,256]{3,2,1,0:T(8,128)(2,1)S(1)}, u32[]{:S(2)}) copy-start(bf16[16,2,64,256]{3,2,1,0:T(8,128)(2,1)S(1)} %all-to-all-done) | copy-start | bytes 3145732
  44.7 25.1 %collective-permute-start.1 = (bf16[16,2,64,256]{3,2,0,1:T(8,128)(2,1)}, bf16[16,2,64,256]{3,2,0,1:T(8,128)(2,1)}, u32[]{:S(2)}, u32[]{:S(2)}) collective-permute-start(bf16[16,2,64,256]{3,2,0,1:T(8,128)(2,1)} %copy.66), channel_id=1, source_target_pairs={{0,32},{16,48},{32,64},{48,80},{64,96},{80,112},{96,0},{112,16},{1... | collective-permute-start | bytes 3145736 | tf_op jit(solution)/shard_map/ppermute | solution.py:90
  46.7 25.1 %collective-permute-start.2 = (bf16[16,2,64,256]{3,2,0,1:T(8,128)(2,1)}, bf16[16,2,64,256]{3,2,0,1:T(8,128)(2,1)}, u32[]{:S(2)}, u32[]{:S(2)}) collective-permute-start(bf16[16,2,64,256]{3,2,0,1:T(8,128)(2,1)} %copy.66), channel_id=1, source_target_pairs={{0,96},{16,112},{32,0},{48,16},{64,32},{80,48},{96,64},{112,80},{1... | collective-permute-start | bytes 3145736 | tf_op jit(solution)/shard_map/ppermute | solution.py:90
  63.7 26.9 %collective-permute-start = (bf16[16,2,64,256]{3,2,0,1:T(8,128)(2,1)}, bf16[16,2,64,256]{3,2,0,1:T(8,128)(2,1)}, u32[]{:S(2)}, u32[]{:S(2)}) collective-permute-start(bf16[16,2,64,256]{3,2,0,1:T(8,128)(2,1)} %copy.66), channel_id=1, source_target_pairs={{0,16},{16,0},{32,48},{48,32},{64,80},{80,64},{96,112},{112,96},{1... | collective-permute-start | bytes 3145736 | tf_op jit(solution)/shard_map/ppermute | solution.py:93
  63.7 13.3 %copy-start.16 = (bf16[2048]{0:T(1024)(128)(2,1)S(1)}, bf16[2048]{0:T(1024)(128)(2,1)}, u32[]{:S(2)}) copy-start(bf16[2048]{0:T(1024)(128)(2,1)} %param.19) | copy-start | bytes 12292
  65.0 12.6 %copy-start.7 = (bf16[2,4,256,352]{2,3,0,1:T(8,128)(2,1)S(1)}, bf16[2,4,256,352]{2,3,0,1:T(8,128)(2,1)}, u32[]{:S(2)}) copy-start(bf16[2,4,256,352]{2,3,0,1:T(8,128)(2,1)} %select_bitcast_fusion) | copy-start | bytes 4325380
  71.7 16.1 %collective-permute-start.5 = (bf16[8,2,64,256]{3,2,0,1:T(8,128)(2,1)}, bf16[8,2,64,256]{3,2,0,1:T(8,128)(2,1)}, u32[]{:S(2)}, u32[]{:S(2)}) collective-permute-start(bf16[8,2,64,256]{3,2,0,1:T(8,128)(2,1)} %slice.110), channel_id=1, source_target_pairs={{0,32},{16,48},{32,64},{48,80},{64,96},{80,112},{96,0},{112,16},{1... | collective-permute-start | bytes 1572872 | tf_op jit(solution)/shard_map/ppermute | solution.py:90
  73.7 15.2 %collective-permute-start.6 = (bf16[8,2,64,256]{3,2,0,1:T(8,128)(2,1)}, bf16[8,2,64,256]{3,2,0,1:T(8,128)(2,1)}, u32[]{:S(2)}, u32[]{:S(2)}) collective-permute-start(bf16[8,2,64,256]{3,2,0,1:T(8,128)(2,1)} %slice.111), channel_id=1, source_target_pairs={{0,96},{16,112},{32,0},{48,16},{64,32},{80,48},{96,64},{112,80},{1... | collective-permute-start | bytes 1572872 | tf_op jit(solution)/shard_map/ppermute | solution.py:90
  79.8 4.0 %copy-start.6 = (bf16[2,4,256,352]{2,3,0,1:T(8,128)(2,1)S(1)}, bf16[2,4,256,352]{2,3,0,1:T(8,128)(2,1)}, u32[]{:S(2)}) copy-start(bf16[2,4,256,352]{2,3,0,1:T(8,128)(2,1)} %select_bitcast_fusion.1) | copy-start | bytes 4325380
  85.0 1.9 copy-start.18
  86.9 3.8 %copy-start.9 = (bf16[16,2,64,256]{3,2,1,0:T(8,128)(2,1)S(1)}, bf16[16,2,64,256]{3,2,1,0:T(8,128)(2,1)}, u32[]{:S(2)}) copy-start(bf16[16,2,64,256]{3,2,1,0:T(8,128)(2,1)} %copy-done.8) | copy-start | bytes 3145732
  86.9 3.8 %copy-start.11 = (bf16[2,1024,352,1]{1,2,0,3:T(8,128)(2,1)S(1)}, bf16[2,1024,352,1]{1,2,0,3:T(8,128)(2,1)}, u32[]{:S(2)}) copy-start(bf16[2,1024,352,1]{1,2,0,3:T(8,128)(2,1)} %reshape.137) | copy-start | bytes 4325380
  87.8 6.9 %collective-permute-start.3 = (bf16[16,2,64,256]{3,2,0,1:T(8,128)(2,1)}, bf16[16,2,64,256]{3,2,0,1:T(8,128)(2,1)S(1)}, u32[]{:S(2)}, u32[]{:S(2)}) collective-permute-start(bf16[16,2,64,256]{3,2,0,1:T(8,128)(2,1)} %collective-permute-done.1), channel_id=1, source_target_pairs={{0,16},{16,0},{32,48},{48,32},{64,80},{80,64},{96,112},{112,96},{1... | collective-permute-start | bytes 3145736 | tf_op jit(solution)/shard_map/ppermute | solution.py:93
  88.9 5.8 %collective-permute-start.4 = (bf16[16,2,64,256]{3,2,0,1:T(8,128)(2,1)}, bf16[16,2,64,256]{3,2,0,1:T(8,128)(2,1)S(1)}, u32[]{:S(2)}, u32[]{:S(2)}) collective-permute-start(bf16[16,2,64,256]{3,2,0,1:T(8,128)(2,1)} %collective-permute-done.2), channel_id=1, source_target_pairs={{0,16},{16,0},{32,48},{48,32},{64,80},{80,64},{96,112},{112,96},{1... | collective-permute-start | bytes 3145736 | tf_op jit(solution)/shard_map/ppermute | solution.py:93
  90.6 4.2 %copy-start.10 = (bf16[2,1024,352,1]{1,2,0,3:T(8,128)(2,1)S(1)}, bf16[2,1024,352,1]{1,2,0,3:T(8,128)(2,1)}, u32[]{:S(2)}) copy-start(bf16[2,1024,352,1]{1,2,0,3:T(8,128)(2,1)} %reshape.138) | copy-start | bytes 4325380
  90.6 4.2 %collective-permute-start.7 = (bf16[16,2,64,256]{3,2,0,1:T(8,128)(2,1)S(1)}, bf16[16,2,64,256]{3,2,0,1:T(8,128)(2,1)S(1)}, u32[]{:S(2)}, u32[]{:S(2)}) collective-permute-start(bf16[16,2,64,256]{3,2,0,1:T(8,128)(2,1)S(1)} %constant_dynamic-update-slice_fusion), channel_id=1, source_target_pairs={{0,16},{16,0},{32,48},{48,32},{64,80},{80,64},{96,112},{112,96},{1... | collective-permute-start | bytes 3145736 | tf_op jit(solution)/shard_map/ppermute | solution.py:93
  98.0 25.5 %collective-permute-start.16 = (bf16[16,2,64,176]{3,2,0,1:T(8,128)(2,1)S(1)}, bf16[16,2,64,176]{3,2,0,1:T(8,128)(2,1)S(1)}, u32[]{:S(2)}, u32[]{:S(2)}) collective-permute-start(bf16[16,2,64,176]{3,2,0,1:T(8,128)(2,1)S(1)} %fusion.21), channel_id=1, source_target_pairs={{0,96},{16,112},{32,0},{48,16},{64,32},{80,48},{96,64},{112,80},{1... | collective-permute-start | bytes 2162696 | tf_op jit(solution)/shard_map/ppermute | solution.py:90
  98.7 26.7 %collective-permute-start.12 = (bf16[16,2,64,176]{3,2,0,1:T(8,128)(2,1)S(1)}, bf16[16,2,64,176]{3,2,0,1:T(8,128)(2,1)}, u32[]{:S(2)}, u32[]{:S(2)}) collective-permute-start(bf16[16,2,64,176]{3,2,0,1:T(8,128)(2,1)S(1)} %fusion.21), channel_id=1, source_target_pairs={{0,32},{16,48},{32,64},{48,80},{64,96},{80,112},{96,0},{112,16},{1... | collective-permute-start | bytes 2162696 | tf_op jit(solution)/shard_map/ppermute | solution.py:90
  100.1 35.1 %collective-permute-start.10 = (bf16[16,2,64,176]{3,2,0,1:T(8,128)(2,1)S(1)}, bf16[16,2,64,176]{3,2,0,1:T(8,128)(2,1)}, u32[]{:S(2)}, u32[]{:S(2)}) collective-permute-start(bf16[16,2,64,176]{3,2,0,1:T(8,128)(2,1)S(1)} %fusion.21), channel_id=1, source_target_pairs={{0,16},{16,0},{32,48},{48,32},{64,80},{80,64},{96,112},{112,96},{1... | collective-permute-start | bytes 2162696 | tf_op jit(solution)/shard_map/ppermute | solution.py:93
  102.8 20.8 %copy-start.12 = (bf16[2,176,256]{2,1,0:T(8,128)(2,1)S(1)}, bf16[2,176,256]{2,1,0:T(8,128)(2,1)}, u32[]{:S(2)}) copy-start(bf16[2,176,256]{2,1,0:T(8,128)(2,1)} %get-tuple-element.17) | copy-start | bytes 540676
  102.8 2.3 %copy-start.19 = (bf16[512,2048]{1,0:T(8,128)(2,1)S(1)}, bf16[512,2048]{1,0:T(8,128)(2,1)}, u32[]{:S(2)}) copy-start(bf16[512,2048]{1,0:T(8,128)(2,1)} %all-gather.3.cloned.1.call-done) | copy-start | bytes 6291460
  105.1 22.3 %copy-start.13 = (bf16[2,176,256]{2,1,0:T(8,128)(2,1)S(1)}, bf16[2,176,256]{2,1,0:T(8,128)(2,1)}, u32[]{:S(2)}) copy-start(bf16[2,176,256]{2,1,0:T(8,128)(2,1)} %get-tuple-element.20) | copy-start | bytes 540676
  123.5 30.9 %collective-permute-start.15 = (bf16[2,176,256]{2,1,0:T(8,128)(2,1)S(1)}, bf16[2,176,256]{2,1,0:T(8,128)(2,1)}, u32[]{:S(2)}, u32[]{:S(2)}) collective-permute-start(bf16[2,176,256]{2,1,0:T(8,128)(2,1)S(1)} %copy-done.12), channel_id=1, source_target_pairs={{0,96},{16,112},{32,0},{48,16},{64,32},{80,48},{96,64},{112,80},{1... | collective-permute-start | bytes 540680 | tf_op jit(solution)/shard_map/ppermute | solution.py:90
  125.4 32.2 %collective-permute-start.13 = (bf16[2,176,256]{2,1,0:T(8,128)(2,1)}, bf16[2,176,256]{2,1,0:T(8,128)(2,1)S(1)}, u32[]{:S(2)}, u32[]{:S(2)}) collective-permute-start(bf16[2,176,256]{2,1,0:T(8,128)(2,1)} %get-tuple-element.18), channel_id=1, source_target_pairs={{0,48},{16,64},{32,80},{48,96},{64,112},{80,0},{96,16},{112,32},{1... | collective-permute-start | bytes 540680 | tf_op jit(solution)/shard_map/ppermute | solution.py:90
  127.4 7.8 %collective-permute-start.8 = (bf16[2,176,256]{2,1,0:T(8,128)(2,1)S(1)}, bf16[2,176,256]{2,1,0:T(8,128)(2,1)S(1)}, u32[]{:S(2)}, u32[]{:S(2)}) collective-permute-start(bf16[2,176,256]{2,1,0:T(8,128)(2,1)S(1)} %copy-done.13), channel_id=1, source_target_pairs={{0,16},{16,32},{32,48},{48,64},{64,80},{80,96},{96,112},{112,0},{1... | collective-permute-start | bytes 540680 | tf_op jit(solution)/shard_map/ppermute | solution.py:90
  130.8 20.4 %collective-permute-start.21 = (bf16[8,2,64,176]{3,2,0,1:T(8,128)(2,1)S(1)}, bf16[8,2,64,176]{3,2,0,1:T(8,128)(2,1)}, u32[]{:S(2)}, u32[]{:S(2)}) collective-permute-start(bf16[8,2,64,176]{3,2,0,1:T(8,128)(2,1)S(1)} %slice.119), channel_id=1, source_target_pairs={{0,96},{16,112},{32,0},{48,16},{64,32},{80,48},{96,64},{112,80},{1... | collective-permute-start | bytes 1081352 | tf_op jit(solution)/shard_map/ppermute | solution.py:90
  135.2 17.0 %collective-permute-start.20 = (bf16[8,2,64,176]{3,2,0,1:T(8,128)(2,1)}, bf16[8,2,64,176]{3,2,0,1:T(8,128)(2,1)}, u32[]{:S(2)}, u32[]{:S(2)}) collective-permute-start(bf16[8,2,64,176]{3,2,0,1:T(8,128)(2,1)} %slice.118), channel_id=1, source_target_pairs={{0,32},{16,48},{32,64},{48,80},{64,96},{80,112},{96,0},{112,16},{1... | collective-permute-start | bytes 1081352 | tf_op jit(solution)/shard_map/ppermute | solution.py:90
  135.2 22.6 %collective-permute-start.14 = (bf16[16,2,64,176]{3,2,0,1:T(8,128)(2,1)}, bf16[16,2,64,176]{3,2,0,1:T(8,128)(2,1)S(1)}, u32[]{:S(2)}, u32[]{:S(2)}) collective-permute-start(bf16[16,2,64,176]{3,2,0,1:T(8,128)(2,1)} %collective-permute-done.12), channel_id=1, source_target_pairs={{0,16},{16,0},{32,48},{48,32},{64,80},{80,64},{96,112},{112,96},{1... | collective-permute-start | bytes 2162696 | tf_op jit(solution)/shard_map/ppermute | solution.py:93
  138.4 4.1 %copy-start.20 = (bf16[512,2048]{1,0:T(8,128)(2,1)S(1)}, bf16[512,2048]{1,0:T(8,128)(2,1)}, u32[]{:S(2)}) copy-start(bf16[512,2048]{1,0:T(8,128)(2,1)} %all-gather.3.cloned.1.call-done) | copy-start | bytes 6291460
  151.2 13.1 %collective-permute-start.19 = (bf16[2,176,256]{2,1,0:T(8,128)(2,1)}, bf16[2,176,256]{2,1,0:T(8,128)(2,1)S(1)}, u32[]{:S(2)}, u32[]{:S(2)}) collective-permute-start(bf16[2,176,256]{2,1,0:T(8,128)(2,1)} %get-tuple-element.21), channel_id=1, source_target_pairs={{0,64},{16,80},{32,96},{48,112},{64,0},{80,16},{96,32},{112,48},{1... | collective-permute-start | bytes 540680 | tf_op jit(solution)/shard_map/ppermute | solution.py:90
  152.2 11.5 %collective-permute-start.17 = (bf16[2,176,256]{2,1,0:T(8,128)(2,1)}, bf16[2,176,256]{2,1,0:T(8,128)(2,1)S(1)}, u32[]{:S(2)}, u32[]{:S(2)}) collective-permute-start(bf16[2,176,256]{2,1,0:T(8,128)(2,1)} %get-tuple-element.22), channel_id=1, source_target_pairs={{0,80},{16,96},{32,112},{48,0},{64,16},{80,32},{96,48},{112,64},{1... | collective-permute-start | bytes 540680 | tf_op jit(solution)/shard_map/ppermute | solution.py:90
  154.5 9.2 %collective-permute-start.22 = (bf16[8,2,64,176]{3,2,0,1:T(8,128)(2,1)}, bf16[8,2,64,176]{3,2,0,1:T(8,128)(2,1)S(1)}, u32[]{:S(2)}, u32[]{:S(2)}) collective-permute-start(bf16[8,2,64,176]{3,2,0,1:T(8,128)(2,1)} %collective-permute-done.20), channel_id=1, source_target_pairs={{0,16},{16,0},{32,48},{48,32},{64,80},{80,64},{96,112},{112,96},{1... | collective-permute-start | bytes 1081352 | tf_op jit(solution)/shard_map/ppermute | solution.py:93
  157.6 10.2 %collective-permute-start.18 = (bf16[16,2,64,176]{3,2,0,1:T(8,128)(2,1)S(1)}, bf16[16,2,64,176]{3,2,0,1:T(8,128)(2,1)S(1)}, u32[]{:S(2)}, u32[]{:S(2)}) collective-permute-start(bf16[16,2,64,176]{3,2,0,1:T(8,128)(2,1)S(1)} %collective-permute-done.16), channel_id=1, source_target_pairs={{0,16},{16,0},{32,48},{48,32},{64,80},{80,64},{96,112},{112,96},{1... | collective-permute-start | bytes 2162696 | tf_op jit(solution)/shard_map/ppermute | solution.py:93
  157.8 6.2 %collective-permute-start.23 = (bf16[8,2,64,176]{3,2,0,1:T(8,128)(2,1)}, bf16[8,2,64,176]{3,2,0,1:T(8,128)(2,1)S(1)}, u32[]{:S(2)}, u32[]{:S(2)}) collective-permute-start(bf16[8,2,64,176]{3,2,0,1:T(8,128)(2,1)} %collective-permute-done.21), channel_id=1, source_target_pairs={{0,16},{16,0},{32,48},{48,32},{64,80},{80,64},{96,112},{112,96},{1... | collective-permute-start | bytes 1081352 | tf_op jit(solution)/shard_map/ppermute | solution.py:93
  163.7 4.1 %copy-start.5 = (f32[2,256,16,64]{1,3,2,0:T(8,128)S(1)}, f32[2,256,16,64]{1,3,2,0:T(8,128)}, u32[]{:S(2)}) copy-start(f32[2,256,16,64]{1,3,2,0:T(8,128)} %fusion.64) | copy-start | bytes 6291460
  164.0 3.7 %copy-start.4 = (f32[2,256,16,64]{1,3,2,0:T(8,128)S(1)}, f32[2,256,16,64]{1,3,2,0:T(8,128)}, u32[]{:S(2)}) copy-start(f32[2,256,16,64]{1,3,2,0:T(8,128)} %fusion.70) | copy-start | bytes 6291460
  164.4 3.4 %copy-start.3 = (f32[2,256,16,64]{1,3,2,0:T(8,128)S(1)}, f32[2,256,16,64]{1,3,2,0:T(8,128)}, u32[]{:S(2)}) copy-start(f32[2,256,16,64]{1,3,2,0:T(8,128)} %fusion.68) | copy-start | bytes 6291460
  166.2 1.9 copy-start.2
  169.2 5.6 %copy-start.21 = (bf16[2048,32]{0,1:T(8,128)(2,1)S(1)}, bf16[2048,32]{0,1:T(8,128)(2,1)}, u32[]{:S(2)}) copy-start(bf16[2048,32]{0,1:T(8,128)(2,1)} %param.18) | copy-start | bytes 393220
  170.3 22.0 %all-to-all-start.1 = ((bf16[16,2,64,256]{3,2,1,0:T(8,128)(2,1)}), bf16[16,2,64,256]{3,2,1,0:T(8,128)(2,1)S(1)}, u32[]{:S(2)}, u32[]{:S(2)}) async-start(bf16[16,2,64,256]{3,2,1,0:T(8,128)(2,1)} %copy.70), calls=%async_computation.1 | async-start | bytes 2097152 | tf_op jit(solution)/shard_map/all_to_all | solution.py:180
  193.3 2.7 %copy-start.1 = (bf16[64,16,704]{2,1,0:T(8,128)(2,1)S(1)}, bf16[64,16,704]{2,1,0:T(8,128)(2,1)}, u32[]{:S(2)}) copy-start(bf16[64,16,704]{2,1,0:T(8,128)(2,1)} %param.27) | copy-start | bytes 4325380
Sparse Core Ops, SparseCore 0:
  11.7 32.8 all-gather.2
  46.6 78.5 all-gather.4
  157.7 32.9 reduce-scatter.1

commit v14 on v13

--- a/solution.py
+++ b/solution.py
@@ -133,8 +133,10 @@
     group_half = hidden.shape[0] // 2
     from_below = shifted(hidden, 2)
     from_above = shifted(hidden, -2)
-    shared_gate_value = jnp.dot(all_features, shared_full[0], preferred_element_type=jnp.float32)
-    shared_up_value = jnp.dot(all_features, shared_full[1], preferred_element_type=jnp.float32)
+    shared_gate_up = jnp.einsum(
+        "tf,kfh->kth", all_features, shared_full[:2], preferred_element_type=jnp.float32
+    )
+    shared_gate_value, shared_up_value = shared_gate_up[0], shared_gate_up[1]
     shared_hidden_units = (
         jax.nn.silu(shared_gate_value) * (shared_up_value + ADAPTER_SCALE * adapter_update)
     ).astype(jnp.bfloat16)

time: 204 us -> 202 us (level)
    dot_general x2 -> x1, matrix products: 7.81 us -> 5.82 us  [on_device(): jnp.einsum('tf,kfh->kth', all_features, shared_full[:2], preferred_elemen...]
where the time goes in v14:
time: 202 us; the launch traced here: 200 us
  waiting for transfers between devices  53.3 us (26%)
  matrix products  42.1 us (21%)
  local copies, waits for them, and re-layouts  35.7 us (18%)
  starting transfers between devices  33.8 us (17%)
  other arithmetic  21.3 us (11%)
  between operations  13.8 us (7%)
    ppermute x15, waiting for transfers between devices, shifted(): lax.ppermute(x, 'row', [(i, (i + shift) % row_count) for i in range(row_c...  29.8 us
    ppermute x15, starting transfers between devices, shifted(): lax.ppermute(x, 'row', [(i, (i + shift) % row_count) for i in range(row_c...  20.7 us
    dot_general x10, matrix products, down_of(): jnp.einsum('sexf,efd->sexd', block, weight, preferred_element_type=jnp.fl...  17 us
    all_to_all x1, waiting for transfers between devices, on_device(): lax.all_to_all(expert_value.astype(jnp.bfloat16), 'col', split_axis=0, co...  15.2 us
    all_to_all x1, waiting for transfers between devices, on_device(): lax.all_to_all(outgoing, 'col', split_axis=0, concat_axis=0, tiled=True)  8.18 us
    all_to_all x1, starting transfers between devices, on_device(): lax.all_to_all(outgoing, 'col', split_axis=0, concat_axis=0, tiled=True)  7.15 us
    dot_general x2, matrix products, project(): jnp.einsum('sexd,edf->sexf', features, ordered, preferred_element_type=jn...  6.62 us
    gather x2, local copies, waits for them, and re-layouts, project(): jnp.take(blocks, order, axis=1).reshape(w.shape[0], -1, w.shape[2])  6.28 us
  transfers between devices with their start and end apart: 29, of which 6 were waited for; matrix products, arithmetic and copies ran while one was open for 46% of the time, Pallas kernels for 0%

profile of v14, /device:TPU:0, one launch (start us, length us, event | category | flops | bytes accessed | tf_op | source)
XLA Modules:
  0.0 200.0 jit_solution(12609534288750831204)
XLA Ops:
  6.5 0.8 compare_and_fusion.2
  7.3 0.7 compare_select_fusion.2
  8.2 1.6 gather_fusion
  9.9 1.6 pad_maximum_fusion.2
  11.6 1.9 pad_maximum_fusion.1
  13.6 0.6 reduce-window.18
  14.6 2.6 %fusion = pred[2048,256]{1,0:T(8,128)(4,1)S(1)} fusion(s32[256,4]{0,1:T(4,128)S(1)} %multiply_add_fusion), kind=kLoop, calls=%fused_computation.5 | loop fusion | flops 3670016 | bytes 528384 | tf_op jit(solution)/shard_map/reduce_or | solution.py:110
  17.2 1.4 convolution_convert_fusion
  18.7 7.1 %all-to-all-start = ((bf16[16,2,64,256]{3,2,1,0:T(8,128)(2,1)}), bf16[16,2,64,256]{3,2,1,0:T(8,128)(2,1)S(1)}, u32[]{:S(2)}, u32[]{:S(2)}) async-start(bf16[16,2,64,256]{3,2,1,0:T(8,128)(2,1)} %bitcast.157), calls=%async_computation | async-start | bytes 2097152 | tf_op jit(solution)/shard_map/all_to_all | solution.py:113
  26.0 2.4 %constant_dynamic-slice_fusion.5 = (bf16[2,176,256]{2,1,0:T(8,128)(2,1)}, bf16[2,176,256]{2,1,0:T(8,128)(2,1)}, bf16[2,176,256]{2,1,0:T(8,128)(2,1)}, bf16[2,176...) fusion(bf16[2,176,2048]{2,1,0:T(8,128)(2,1)} %param.25, ...), kind=kLoop, calls=%fused_computation.146 | loop fusion | bytes 2523164 | tf_op jit(solution)/shard_map/dynamic_slice | solution.py:156
  28.4 3.2 %collective-permute-start.9 = (bf16[2,176,256]{2,1,0:T(8,128)(2,1)}, bf16[2,176,256]{2,1,0:T(8,128)(2,1)}, u32[]{:S(2)}, u32[]{:S(2)}) collective-permute-start(bf16[2,176,256]{2,1,0:T(8,128)(2,1)} %get-tuple-element.16), channel_id=1, source_target_pairs={{0,112},{16,0},{32,16},{48,32},{64,48},{80,64},{96,80},{112,96},{1... | collective-permute-start | bytes 540680 | tf_op jit(solution)/shard_map/ppermute | solution.py:90
  31.6 3.8 %pad_maximum_fusion = bf16[2,2048,352]{1,2,0:T(8,128)(2,1)} fusion(bf16[2,2048,176]{1,2,0:T(8,128)(2,1)} %param.24, bf16[2,2048,176]{1,2,0:T(8,128)(2,1)} %param.23), kind=kLoop, calls=%fused_computation.26 | loop fusion | flops 5767168 | bytes 5767168 | tf_op jit(solution)/shard_map/concatenate | solution.py:128
  35.4 8.2 %all-to-all-done = bf16[16,2,64,256]{3,2,1,0:T(8,128)(2,1)S(1)} async-done(((bf16[16,2,64,256]{3,2,1,0:T(8,128)(2,1)}), bf16[16,2,64,256]{3,2,1,0:T(8,128)(2,1)S(1)}, u32[]{:S(2)}, u32[]{:S(2)}) %all-to-all-start) | async-done | bytes 1048608 | tf_op jit(solution)/shard_map/all_to_all | solution.py:113
  43.6 1.1 copy.66
  44.7 1.9 collective-permute-start.1
  46.7 2.1 %collective-permute-start.2 = (bf16[16,2,64,256]{3,2,0,1:T(8,128)(2,1)}, bf16[16,2,64,256]{3,2,0,1:T(8,128)(2,1)}, u32[]{:S(2)}, u32[]{:S(2)}) collective-permute-start(bf16[16,2,64,256]{3,2,0,1:T(8,128)(2,1)} %copy.66), channel_id=1, source_target_pairs={{0,96},{16,112},{32,0},{48,16},{64,32},{80,48},{96,64},{112,80},{1... | collective-permute-start | bytes 3145736 | tf_op jit(solution)/shard_map/ppermute | solution.py:90
  48.8 0.6 fusion.93
  49.7 3.7 %copy.90 = bf16[2,44,8,8,256]{4,3,1,2,0:T(8,128)(2,1)} copy(bf16[2,44,8,8,256]{4,3,2,1,0:T(8,128)(2,1)} %bitcast.156) | data formatting | bytes 5767168 | tf_op jit(solution)/shard_map/reshape | solution.py:118
  53.4 1.3 compare_and_fusion
  54.8 2.6 %gather_fusion.3 = bf16[4,2,256,352]{2,3,1,0:T(8,128)(2,1)S(1)} fusion(bf16[2,8,256,352]{2,3,1,0:T(8,128)(2,1)} %bitcast.154, s32[1024]{0:T(1024)S(1)} %pad_clamp_fusion), kind=kCustom, calls=%fused_computation.1.clone | custom fusion | bytes 2883600 | tf_op jit(solution)/shard_map/jit(_take)/gather | solution.py:123
  57.4 3.7 %gather_fusion.2 = bf16[4,2,256,352]{2,3,1,0:T(8,128)(2,1)} fusion(bf16[2,8,256,352]{2,3,1,0:T(8,128)(2,1)} %bitcast.155, s32[1024]{0:T(1024)S(1)} %pad_clamp_fusion.1), kind=kCustom, calls=%fused_computation.clone | custom fusion | bytes 2883600 | tf_op jit(solution)/shard_map/jit(_take)/gather | solution.py:123
  61.1 2.7 %select_bitcast_fusion.1 = bf16[2,4,256,352]{2,3,0,1:T(8,128)(2,1)} fusion(bf16[4,2,256,352]{2,3,1,0:T(8,128)(2,1)} %gather_fusion.2, pred[4]{0:T(512)(128)(4,1)S(1)} %get-tuple-element.33), kind=kLoop, calls=%fused_computation.45 | loop fusion | flops 720896 | bytes 2883588 | tf_op jit(solution)/shard_map/jit(_take)/select_n | solution.py:123
  63.8 1.3 select_bitcast_fusion
  65.1 4.7 %collective-permute-done.1 = bf16[16,2,64,256]{3,2,0,1:T(8,128)(2,1)} collective-permute-done((bf16[16,2,64,256]{3,2,0,1:T(8,128)(2,1)}, bf16[16,2,64,256]{3,2,0,1:T(8,128)(2,1)}, u32[]{:S(2)}, u32[]{:S(2)}) %collective-permute-start.1) | collective-permute-done | bytes 1048608 | tf_op jit(solution)/shard_map/ppermute | solution.py:90
  69.8 1.9 slice.114
  71.8 1.9 slice.115
  73.7 3.2 %collective-permute-start.6 = (bf16[8,2,64,256]{3,2,0,1:T(8,128)(2,1)}, bf16[8,2,64,256]{3,2,0,1:T(8,128)(2,1)}, u32[]{:S(2)}, u32[]{:S(2)}) collective-permute-start(bf16[8,2,64,256]{3,2,0,1:T(8,128)(2,1)} %slice.115), channel_id=1, source_target_pairs={{0,96},{16,112},{32,0},{48,16},{64,32},{80,48},{96,64},{112,80},{1... | collective-permute-start | bytes 1572872 | tf_op jit(solution)/shard_map/ppermute | solution.py:90
  77.0 0.6 gather_fusion.1
  77.5 2.3 %copy.68 = bf16[2,4,256,352]{2,1,3,0:T(4,128)(2,1)} copy(bf16[2,4,256,352]{2,3,0,1:T(8,128)(2,1)S(1)} %copy-done.7) | data formatting | bytes 2883584 | tf_op jit(solution)/shard_map/jit(_take)/select_n | solution.py:123
  79.8 4.0 %reshape.138 = bf16[2,1024,352,1]{1,2,0,3:T(8,128)(2,1)} reshape(bf16[2,4,256,352]{2,1,3,0:T(4,128)(2,1)} %copy.68) | data formatting | bytes 2883584 | tf_op jit(solution)/shard_map/reshape | solution.py:123
  83.8 1.1 copy.62
  84.9 1.9 reshape.137
  86.9 0.8 bitcast_select_fusion
  87.8 1.1 constant_dynamic-update-slice_fusion.1
  88.9 0.6 collective-permute-start.4
  89.5 1.1 constant_dynamic-update-slice_fusion
  90.7 4.0 %fusion.1 = f32[2,352,16,64]{1,3,2,0:T(8,128)S(1)} fusion(bf16[16,2,64,256]{3,2,0,1:T(8,128)(2,1)} %collective-permute-done.2, bf16[16,2,64,256]{3,2,0,1:T(8,128)(2,1)} %collective-permute-done.1, bf16[16,2,64,256]{3,2,0,1:T(8,128)(2,1)} %collective-permute-done, bf16[2,1024,352,1]{1,2,0,3:T(8,128)(2,1)S(1)} %copy-done.11, ...), kind=kOutput, calls=%fused_computation.6 | convolution fusion | flops 1493172224 | bytes 8519680 | tf_op jit(solution)/shard_map/sexd,edf->sexf/dot_general | solution.py:124
  94.7 2.6 %add_bitcast_fusion = f32[16,2,64,352]{3,2,0,1:T(8,128)S(1)} fusion(f32[2,352,16,64]{1,3,2,0:T(8,128)S(1)} %fusion.1, bf16[16,2,64,256]{3,2,0,1:T(8,128)(2,1)S(1)} %collective-permute-done.7, bf16[16,2,64,256]{3,2,0,1:T(8,128)(2,1)S(1)} %constant_dynamic-update-slice_fusion, bf16[16,2,64,256]{3,2,0,1:T(8,128)(2,1)S(1)} %collective-permute-done.4, ...), kind=kOutput, calls=%fused_computation.22 | convolution fusion | flops 1493893120 | bytes 11403264 | tf_op jit(solution)/shard_map/sexd,edf->sexf/dot_general | solution.py:124
  97.4 0.6 fusion.19
  98.0 0.7 collective-permute-start.16
  98.6 1.4 collective-permute-start.12
  100.1 2.7 %fusion.70 = f32[2,256,16,64]{1,3,2,0:T(8,128)} fusion(bf16[16,2,64,176]{3,2,0,1:T(8,128)(2,1)S(1)} %fusion.19, bf16[2,176,2048]{2,1,0:T(8,128)(2,1)} %param.25, s32[]{:T(128)S(6)} %select_n.145), kind=kOutput, calls=%fused_computation.96 | convolution fusion | flops 184549376 | bytes 2998276 | tf_op jit(solution)/shard_map/sexf,efd->sexd/dot_general | solution.py:167
  102.7 2.2 %fusion.41 = bf16[256,256]{1,0:T(8,128)(2,1)S(1)} fusion(bf16[512,2048]{1,0:T(8,128)(2,1)} %all-gather.3.cloned.1.call-done, s32[256]{0:T(256)S(1)} %and_select_fusion, s32[256]{0:T(256)S(1)} %select_reduce_fusion.2), kind=kOutput, calls=%fused_computation.62 | convolution fusion | flops 268632064 | bytes 2230272 | tf_op jit(solution)/shard_map/dot_general | solution.py:78
  105.4 18.1 %collective-permute-done.16 = bf16[16,2,64,176]{3,2,0,1:T(8,128)(2,1)S(1)} collective-permute-done((bf16[16,2,64,176]{3,2,0,1:T(8,128)(2,1)S(1)}, bf16[16,2,64,176]{3,2,0,1:T(8,128)(2,1)S(1)}, u32[]{:S(2)}, u32[]{:S(2)}) %collective-permute-start.16) | collective-permute-done | bytes 720928 | tf_op jit(solution)/shard_map/ppermute | solution.py:90
  123.5 1.8 collective-permute-start.15
  125.4 1.9 slice.122
  127.7 3.1 %fusion.66 = f32[2,256,16,64]{1,3,2,0:T(8,128)} fusion(bf16[16,2,64,176]{3,2,0,1:T(8,128)(2,1)} %collective-permute-done.12, bf16[2,176,256]{2,1,0:T(8,128)(2,1)} %collective-permute-done.11), kind=kOutput, calls=%fused_computation.92 | convolution fusion | flops 184549376 | bytes 2998272 | tf_op jit(solution)/shard_map/sexf,efd->sexd/dot_general | solution.py:167
  130.8 2.6 %collective-permute-start.21 = (bf16[8,2,64,176]{3,2,0,1:T(8,128)(2,1)S(1)}, bf16[8,2,64,176]{3,2,0,1:T(8,128)(2,1)}, u32[]{:S(2)}, u32[]{:S(2)}) collective-permute-start(bf16[8,2,64,176]{3,2,0,1:T(8,128)(2,1)S(1)} %slice.123), channel_id=1, source_target_pairs={{0,96},{16,112},{32,0},{48,16},{64,32},{80,48},{96,64},{112,80},{1... | collective-permute-start | bytes 1081352 | tf_op jit(solution)/shard_map/ppermute | solution.py:90
  133.4 1.7 collective-permute-done.8
  135.2 3.2 %fusion.68 = f32[2,256,16,64]{1,3,2,0:T(8,128)} fusion(bf16[16,2,64,176]{3,2,0,1:T(8,128)(2,1)} %collective-permute-done.10, bf16[2,176,256]{2,1,0:T(8,128)(2,1)S(1)} %collective-permute-done.8, bf16[2,176,256]{2,1,0:T(8,128)(2,1)} %collective-permute-done.9, pred[]{:T(512)S(6)} %eq.138), kind=kOutput, calls=%fused_computation.94 | convolution fusion | flops 184639488 | bytes 3178497 | tf_op jit(solution)/shard_map/sexf,efd->sexd/dot_general | solution.py:167
  138.3 5.8 %convolution_bitcast_fusion = f32[2,256,704]{1,2,0:T(8,128)} fusion(bf16[3,2048,704]{1,2,0:T(8,128)(2,1)} %all-gather.5.cloned.1.call-done, bf16[512,2048]{1,0:T(8,128)(2,1)} %all-gather.3.cloned.1.call-done), kind=kOutput, calls=%fused_computation.41 | convolution fusion | flops 1476395008 | bytes 11141120 | tf_op jit(solution)/shard_map/tf,kfh->kth/dot_general | solution.py:136
  144.1 5.1 %fusion.18 = f32[256,2048]{1,0:T(8,128)} fusion(bf16[3,2048,704]{1,2,0:T(8,128)(2,1)} %all-gather.5.cloned.1.call-done, bf16[256,256]{1,0:T(8,128)(2,1)S(1)} %fusion.41, bf16[256,704]{1,0:T(8,128)(2,1)} %bitcast_select_fusion, f32[256]{0:T(256)S(1)} %add_divide_fusion, f32[2,256,704]{1,2,0:T(8,128)} %convolution_bitcast_fusion), kind=kOutput, calls=%fused_computation.27 | convolution fusion | flops 832438272 | bytes 6947840 | tf_op jit(solution)/shard_map/dot_general | solution.py:143
  149.2 0.9 collective-permute-start.19
  150.1 2.3 %collective-permute-start.17 = (bf16[2,176,256]{2,1,0:T(8,128)(2,1)}, bf16[2,176,256]{2,1,0:T(8,128)(2,1)S(1)}, u32[]{:S(2)}, u32[]{:S(2)}) collective-permute-start(bf16[2,176,256]{2,1,0:T(8,128)(2,1)} %get-tuple-element.22), channel_id=1, source_target_pairs={{0,80},{16,96},{32,112},{48,0},{64,16},{80,32},{96,48},{112,64},{1... | collective-permute-start | bytes 540680 | tf_op jit(solution)/shard_map/ppermute | solution.py:90
  152.6 2.7 %fusion.62 = f32[2,256,16,64]{1,3,2,0:T(8,128)} fusion(bf16[16,2,64,176]{3,2,0,1:T(8,128)(2,1)S(1)} %collective-permute-done.16, bf16[2,176,256]{2,1,0:T(8,128)(2,1)} %collective-permute-done.15), kind=kOutput, calls=%fused_computation.88 | convolution fusion | flops 184549376 | bytes 2998272 | tf_op jit(solution)/shard_map/sexf,efd->sexd/dot_general | solution.py:167
  156.4 5.3 %collective-permute-done.17 = bf16[2,176,256]{2,1,0:T(8,128)(2,1)S(1)} collective-permute-done((bf16[2,176,256]{2,1,0:T(8,128)(2,1)}, bf16[2,176,256]{2,1,0:T(8,128)(2,1)S(1)}, u32[]{:S(2)}, u32[]{:S(2)}) %collective-permute-start.17) | collective-permute-done | bytes 180256 | tf_op jit(solution)/shard_map/ppermute | solution.py:90
  162.4 1.8 fusion.30
  164.2 1.5 fusion.29
  166.1 1.0 fusion.20
  167.2 1.1 copy.70
  168.2 4.5 %all-to-all-start.1 = ((bf16[16,2,64,256]{3,2,1,0:T(8,128)(2,1)}), bf16[16,2,64,256]{3,2,1,0:T(8,128)(2,1)S(1)}, u32[]{:S(2)}, u32[]{:S(2)}) async-start(bf16[16,2,64,256]{3,2,1,0:T(8,128)(2,1)} %copy.70), calls=%async_computation.1 | async-start | bytes 2097152 | tf_op jit(solution)/shard_map/all_to_all | solution.py:182
  172.8 1.6 fusion.57
  174.5 15.2 %all-to-all-done.1 = bf16[16,2,64,256]{3,2,1,0:T(8,128)(2,1)S(1)} async-done(((bf16[16,2,64,256]{3,2,1,0:T(8,128)(2,1)}), bf16[16,2,64,256]{3,2,1,0:T(8,128)(2,1)S(1)}, u32[]{:S(2)}, u32[]{:S(2)}) %all-to-all-start.1) | async-done | bytes 1048608 | tf_op jit(solution)/shard_map/all_to_all | solution.py:182
  191.7 1.7 add.216
  (122 shorter events, 6.8 us)
Async XLA Ops:
  6.5 70.4 %copy-start = (bf16[64,16,704]{2,1,0:T(8,128)(2,1)S(1)}, bf16[64,16,704]{2,1,0:T(8,128)(2,1)}, u32[]{:S(2)}) copy-start(bf16[64,16,704]{2,1,0:T(8,128)(2,1)} %param.27) | copy-start | bytes 4325380
  6.5 10.7 %copy-start.14 = (bf16[256,256]{1,0:T(8,128)(2,1)S(1)}, bf16[256,256]{1,0:T(8,128)(2,1)}, u32[]{:S(2)}) copy-start(bf16[256,256]{1,0:T(8,128)(2,1)} %param.17) | copy-start | bytes 393220
  6.5 7.0 %copy-start.15 = (s32[256,4]{0,1:T(4,128)S(1)}, s32[256,4]{0,1:T(4,128)}, u32[]{:S(2)}) copy-start(s32[256,4]{0,1:T(4,128)} %param.28) | copy-start | bytes 12292
  6.5 96.2 %all-gather.3.cloned.1.call-start = ((), (), s32[]{:S(2)}) async-start(), calls=%async_computation.3 | async-start | bytes 2359296 | tf_op jit(solution)/shard_map/all_gather | solution.py:34
  11.5 126.8 %all-gather.5.cloned.1.call-start = ((), (), s32[]{:S(2)}) async-start(), calls=%async_computation.4 | async-start | bytes 9191424 | tf_op jit(solution)/shard_map/all_gather | solution.py:53
  18.7 24.9 %all-to-all-start = ((bf16[16,2,64,256]{3,2,1,0:T(8,128)(2,1)}), bf16[16,2,64,256]{3,2,1,0:T(8,128)(2,1)S(1)}, u32[]{:S(2)}, u32[]{:S(2)}) async-start(bf16[16,2,64,256]{3,2,1,0:T(8,128)(2,1)} %bitcast.157), calls=%async_computation | async-start | bytes 2097152 | tf_op jit(solution)/shard_map/all_to_all | solution.py:113
  25.8 165.9 %reduce-scatter.2.cloned.1.call-start = ((), (), s32[]{:S(2)}) async-start(), calls=%async_computation.5 | async-start | bytes 2359296 | tf_op jit(solution)/shard_map/reduce_scatter | solution.py:153
  28.4 102.4 %collective-permute-start.9 = (bf16[2,176,256]{2,1,0:T(8,128)(2,1)}, bf16[2,176,256]{2,1,0:T(8,128)(2,1)}, u32[]{:S(2)}, u32[]{:S(2)}) collective-permute-start(bf16[2,176,256]{2,1,0:T(8,128)(2,1)} %get-tuple-element.16), channel_id=1, source_target_pairs={{0,112},{16,0},{32,16},{48,32},{64,48},{80,64},{96,80},{112,96},{1... | collective-permute-start | bytes 540680 | tf_op jit(solution)/shard_map/ppermute | solution.py:90
  31.6 95.7 %collective-permute-start.11 = (bf16[2,176,256]{2,1,0:T(8,128)(2,1)}, bf16[2,176,256]{2,1,0:T(8,128)(2,1)}, u32[]{:S(2)}, u32[]{:S(2)}) collective-permute-start(bf16[2,176,256]{2,1,0:T(8,128)(2,1)} %get-tuple-element.19), channel_id=1, source_target_pairs={{0,32},{16,48},{32,64},{48,80},{64,96},{80,112},{96,0},{112,16},{1... | collective-permute-start | bytes 540680 | tf_op jit(solution)/shard_map/ppermute | solution.py:90
  35.4 14.1 %copy-start.17 = (s32[1,16]{1,0:T(1,128)S(1)}, s32[1,16]{1,0:T(1,128)}, u32[]{:S(2)}) copy-start(s32[1,16]{1,0:T(1,128)} %param.29) | copy-start | bytes 196
  43.6 9.8 %copy-start.8 = (bf16[16,2,64,256]{3,2,1,0:T(8,128)(2,1)}, bf16[16,2,64,256]{3,2,1,0:T(8,128)(2,1)S(1)}, u32[]{:S(2)}) copy-start(bf16[16,2,64,256]{3,2,1,0:T(8,128)(2,1)S(1)} %all-to-all-done) | copy-start | bytes 3145732
  44.7 25.1 %collective-permute-start.1 = (bf16[16,2,64,256]{3,2,0,1:T(8,128)(2,1)}, bf16[16,2,64,256]{3,2,0,1:T(8,128)(2,1)}, u32[]{:S(2)}, u32[]{:S(2)}) collective-permute-start(bf16[16,2,64,256]{3,2,0,1:T(8,128)(2,1)} %copy.66), channel_id=1, source_target_pairs={{0,32},{16,48},{32,64},{48,80},{64,96},{80,112},{96,0},{112,16},{1... | collective-permute-start | bytes 3145736 | tf_op jit(solution)/shard_map/ppermute | solution.py:90
  46.7 25.1 %collective-permute-start.2 = (bf16[16,2,64,256]{3,2,0,1:T(8,128)(2,1)}, bf16[16,2,64,256]{3,2,0,1:T(8,128)(2,1)}, u32[]{:S(2)}, u32[]{:S(2)}) collective-permute-start(bf16[16,2,64,256]{3,2,0,1:T(8,128)(2,1)} %copy.66), channel_id=1, source_target_pairs={{0,96},{16,112},{32,0},{48,16},{64,32},{80,48},{96,64},{112,80},{1... | collective-permute-start | bytes 3145736 | tf_op jit(solution)/shard_map/ppermute | solution.py:90
  63.7 26.8 %collective-permute-start = (bf16[16,2,64,256]{3,2,0,1:T(8,128)(2,1)}, bf16[16,2,64,256]{3,2,0,1:T(8,128)(2,1)}, u32[]{:S(2)}, u32[]{:S(2)}) collective-permute-start(bf16[16,2,64,256]{3,2,0,1:T(8,128)(2,1)} %copy.66), channel_id=1, source_target_pairs={{0,16},{16,0},{32,48},{48,32},{64,80},{80,64},{96,112},{112,96},{1... | collective-permute-start | bytes 3145736 | tf_op jit(solution)/shard_map/ppermute | solution.py:93
  63.8 13.2 %copy-start.16 = (bf16[2048]{0:T(1024)(128)(2,1)S(1)}, bf16[2048]{0:T(1024)(128)(2,1)}, u32[]{:S(2)}) copy-start(bf16[2048]{0:T(1024)(128)(2,1)} %param.19) | copy-start | bytes 12292
  65.1 12.5 %copy-start.7 = (bf16[2,4,256,352]{2,3,0,1:T(8,128)(2,1)S(1)}, bf16[2,4,256,352]{2,3,0,1:T(8,128)(2,1)}, u32[]{:S(2)}) copy-start(bf16[2,4,256,352]{2,3,0,1:T(8,128)(2,1)} %select_bitcast_fusion) | copy-start | bytes 4325380
  71.7 16.1 %collective-permute-start.5 = (bf16[8,2,64,256]{3,2,0,1:T(8,128)(2,1)}, bf16[8,2,64,256]{3,2,0,1:T(8,128)(2,1)}, u32[]{:S(2)}, u32[]{:S(2)}) collective-permute-start(bf16[8,2,64,256]{3,2,0,1:T(8,128)(2,1)} %slice.114), channel_id=1, source_target_pairs={{0,32},{16,48},{32,64},{48,80},{64,96},{80,112},{96,0},{112,16},{1... | collective-permute-start | bytes 1572872 | tf_op jit(solution)/shard_map/ppermute | solution.py:90
  73.7 15.2 %collective-permute-start.6 = (bf16[8,2,64,256]{3,2,0,1:T(8,128)(2,1)}, bf16[8,2,64,256]{3,2,0,1:T(8,128)(2,1)}, u32[]{:S(2)}, u32[]{:S(2)}) collective-permute-start(bf16[8,2,64,256]{3,2,0,1:T(8,128)(2,1)} %slice.115), channel_id=1, source_target_pairs={{0,96},{16,112},{32,0},{48,16},{64,32},{80,48},{96,64},{112,80},{1... | collective-permute-start | bytes 1572872 | tf_op jit(solution)/shard_map/ppermute | solution.py:90
  79.8 4.0 %copy-start.6 = (bf16[2,4,256,352]{2,3,0,1:T(8,128)(2,1)S(1)}, bf16[2,4,256,352]{2,3,0,1:T(8,128)(2,1)}, u32[]{:S(2)}) copy-start(bf16[2,4,256,352]{2,3,0,1:T(8,128)(2,1)} %select_bitcast_fusion.1) | copy-start | bytes 4325380
  84.9 1.9 copy-start.18
  86.8 3.8 %copy-start.9 = (bf16[16,2,64,256]{3,2,1,0:T(8,128)(2,1)S(1)}, bf16[16,2,64,256]{3,2,1,0:T(8,128)(2,1)}, u32[]{:S(2)}) copy-start(bf16[16,2,64,256]{3,2,1,0:T(8,128)(2,1)} %copy-done.8) | copy-start | bytes 3145732
  86.8 3.8 %copy-start.11 = (bf16[2,1024,352,1]{1,2,0,3:T(8,128)(2,1)S(1)}, bf16[2,1024,352,1]{1,2,0,3:T(8,128)(2,1)}, u32[]{:S(2)}) copy-start(bf16[2,1024,352,1]{1,2,0,3:T(8,128)(2,1)} %reshape.137) | copy-start | bytes 4325380
  87.8 6.9 %collective-permute-start.3 = (bf16[16,2,64,256]{3,2,0,1:T(8,128)(2,1)}, bf16[16,2,64,256]{3,2,0,1:T(8,128)(2,1)S(1)}, u32[]{:S(2)}, u32[]{:S(2)}) collective-permute-start(bf16[16,2,64,256]{3,2,0,1:T(8,128)(2,1)} %collective-permute-done.1), channel_id=1, source_target_pairs={{0,16},{16,0},{32,48},{48,32},{64,80},{80,64},{96,112},{112,96},{1... | collective-permute-start | bytes 3145736 | tf_op jit(solution)/shard_map/ppermute | solution.py:93
  88.9 5.8 %collective-permute-start.4 = (bf16[16,2,64,256]{3,2,0,1:T(8,128)(2,1)}, bf16[16,2,64,256]{3,2,0,1:T(8,128)(2,1)S(1)}, u32[]{:S(2)}, u32[]{:S(2)}) collective-permute-start(bf16[16,2,64,256]{3,2,0,1:T(8,128)(2,1)} %collective-permute-done.2), channel_id=1, source_target_pairs={{0,16},{16,0},{32,48},{48,32},{64,80},{80,64},{96,112},{112,96},{1... | collective-permute-start | bytes 3145736 | tf_op jit(solution)/shard_map/ppermute | solution.py:93
  90.5 4.2 %copy-start.10 = (bf16[2,1024,352,1]{1,2,0,3:T(8,128)(2,1)S(1)}, bf16[2,1024,352,1]{1,2,0,3:T(8,128)(2,1)}, u32[]{:S(2)}) copy-start(bf16[2,1024,352,1]{1,2,0,3:T(8,128)(2,1)} %reshape.138) | copy-start | bytes 4325380
  90.6 4.2 %collective-permute-start.7 = (bf16[16,2,64,256]{3,2,0,1:T(8,128)(2,1)S(1)}, bf16[16,2,64,256]{3,2,0,1:T(8,128)(2,1)S(1)}, u32[]{:S(2)}, u32[]{:S(2)}) collective-permute-start(bf16[16,2,64,256]{3,2,0,1:T(8,128)(2,1)S(1)} %constant_dynamic-update-slice_fusion), channel_id=1, source_target_pairs={{0,16},{16,0},{32,48},{48,32},{64,80},{80,64},{96,112},{112,96},{1... | collective-permute-start | bytes 3145736 | tf_op jit(solution)/shard_map/ppermute | solution.py:93
  98.0 25.5 %collective-permute-start.16 = (bf16[16,2,64,176]{3,2,0,1:T(8,128)(2,1)S(1)}, bf16[16,2,64,176]{3,2,0,1:T(8,128)(2,1)S(1)}, u32[]{:S(2)}, u32[]{:S(2)}) collective-permute-start(bf16[16,2,64,176]{3,2,0,1:T(8,128)(2,1)S(1)} %fusion.19), channel_id=1, source_target_pairs={{0,96},{16,112},{32,0},{48,16},{64,32},{80,48},{96,64},{112,80},{1... | collective-permute-start | bytes 2162696 | tf_op jit(solution)/shard_map/ppermute | solution.py:90
  98.6 26.7 %collective-permute-start.12 = (bf16[16,2,64,176]{3,2,0,1:T(8,128)(2,1)S(1)}, bf16[16,2,64,176]{3,2,0,1:T(8,128)(2,1)}, u32[]{:S(2)}, u32[]{:S(2)}) collective-permute-start(bf16[16,2,64,176]{3,2,0,1:T(8,128)(2,1)S(1)} %fusion.19), channel_id=1, source_target_pairs={{0,32},{16,48},{32,64},{48,80},{64,96},{80,112},{96,0},{112,16},{1... | collective-permute-start | bytes 2162696 | tf_op jit(solution)/shard_map/ppermute | solution.py:90
  100.1 35.1 %collective-permute-start.10 = (bf16[16,2,64,176]{3,2,0,1:T(8,128)(2,1)S(1)}, bf16[16,2,64,176]{3,2,0,1:T(8,128)(2,1)}, u32[]{:S(2)}, u32[]{:S(2)}) collective-permute-start(bf16[16,2,64,176]{3,2,0,1:T(8,128)(2,1)S(1)} %fusion.19), channel_id=1, source_target_pairs={{0,16},{16,0},{32,48},{48,32},{64,80},{80,64},{96,112},{112,96},{1... | collective-permute-start | bytes 2162696 | tf_op jit(solution)/shard_map/ppermute | solution.py:93
  102.7 20.8 %copy-start.12 = (bf16[2,176,256]{2,1,0:T(8,128)(2,1)S(1)}, bf16[2,176,256]{2,1,0:T(8,128)(2,1)}, u32[]{:S(2)}) copy-start(bf16[2,176,256]{2,1,0:T(8,128)(2,1)} %get-tuple-element.17) | copy-start | bytes 540676
  102.7 2.3 %copy-start.19 = (bf16[512,2048]{1,0:T(8,128)(2,1)S(1)}, bf16[512,2048]{1,0:T(8,128)(2,1)}, u32[]{:S(2)}) copy-start(bf16[512,2048]{1,0:T(8,128)(2,1)} %all-gather.3.cloned.1.call-done) | copy-start | bytes 6291460
  105.0 22.3 %copy-start.13 = (bf16[2,176,256]{2,1,0:T(8,128)(2,1)S(1)}, bf16[2,176,256]{2,1,0:T(8,128)(2,1)}, u32[]{:S(2)}) copy-start(bf16[2,176,256]{2,1,0:T(8,128)(2,1)} %get-tuple-element.20) | copy-start | bytes 540676
  123.5 29.0 %collective-permute-start.15 = (bf16[2,176,256]{2,1,0:T(8,128)(2,1)S(1)}, bf16[2,176,256]{2,1,0:T(8,128)(2,1)}, u32[]{:S(2)}, u32[]{:S(2)}) collective-permute-start(bf16[2,176,256]{2,1,0:T(8,128)(2,1)S(1)} %copy-done.12), channel_id=1, source_target_pairs={{0,96},{16,112},{32,0},{48,16},{64,32},{80,48},{96,64},{112,80},{1... | collective-permute-start | bytes 540680 | tf_op jit(solution)/shard_map/ppermute | solution.py:90
  125.3 30.0 %collective-permute-start.13 = (bf16[2,176,256]{2,1,0:T(8,128)(2,1)}, bf16[2,176,256]{2,1,0:T(8,128)(2,1)S(1)}, u32[]{:S(2)}, u32[]{:S(2)}) collective-permute-start(bf16[2,176,256]{2,1,0:T(8,128)(2,1)} %get-tuple-element.18), channel_id=1, source_target_pairs={{0,48},{16,64},{32,80},{48,96},{64,112},{80,0},{96,16},{112,32},{1... | collective-permute-start | bytes 540680 | tf_op jit(solution)/shard_map/ppermute | solution.py:90
  127.3 7.8 %collective-permute-start.8 = (bf16[2,176,256]{2,1,0:T(8,128)(2,1)S(1)}, bf16[2,176,256]{2,1,0:T(8,128)(2,1)S(1)}, u32[]{:S(2)}, u32[]{:S(2)}) collective-permute-start(bf16[2,176,256]{2,1,0:T(8,128)(2,1)S(1)} %copy-done.13), channel_id=1, source_target_pairs={{0,16},{16,32},{32,48},{48,64},{64,80},{80,96},{96,112},{112,0},{1... | collective-permute-start | bytes 540680 | tf_op jit(solution)/shard_map/ppermute | solution.py:90
  130.8 18.4 %collective-permute-start.21 = (bf16[8,2,64,176]{3,2,0,1:T(8,128)(2,1)S(1)}, bf16[8,2,64,176]{3,2,0,1:T(8,128)(2,1)}, u32[]{:S(2)}, u32[]{:S(2)}) collective-permute-start(bf16[8,2,64,176]{3,2,0,1:T(8,128)(2,1)S(1)} %slice.123), channel_id=1, source_target_pairs={{0,96},{16,112},{32,0},{48,16},{64,32},{80,48},{96,64},{112,80},{1... | collective-permute-start | bytes 1081352 | tf_op jit(solution)/shard_map/ppermute | solution.py:90
  135.1 15.0 %collective-permute-start.20 = (bf16[8,2,64,176]{3,2,0,1:T(8,128)(2,1)}, bf16[8,2,64,176]{3,2,0,1:T(8,128)(2,1)}, u32[]{:S(2)}, u32[]{:S(2)}) collective-permute-start(bf16[8,2,64,176]{3,2,0,1:T(8,128)(2,1)} %slice.122), channel_id=1, source_target_pairs={{0,32},{16,48},{32,64},{48,80},{64,96},{80,112},{96,0},{112,16},{1... | collective-permute-start | bytes 1081352 | tf_op jit(solution)/shard_map/ppermute | solution.py:90
  135.1 20.6 %collective-permute-start.14 = (bf16[16,2,64,176]{3,2,0,1:T(8,128)(2,1)}, bf16[16,2,64,176]{3,2,0,1:T(8,128)(2,1)S(1)}, u32[]{:S(2)}, u32[]{:S(2)}) collective-permute-start(bf16[16,2,64,176]{3,2,0,1:T(8,128)(2,1)} %collective-permute-done.12), channel_id=1, source_target_pairs={{0,16},{16,0},{32,48},{48,32},{64,80},{80,64},{96,112},{112,96},{1... | collective-permute-start | bytes 2162696 | tf_op jit(solution)/shard_map/ppermute | solution.py:93
  149.2 13.1 %collective-permute-start.19 = (bf16[2,176,256]{2,1,0:T(8,128)(2,1)}, bf16[2,176,256]{2,1,0:T(8,128)(2,1)S(1)}, u32[]{:S(2)}, u32[]{:S(2)}) collective-permute-start(bf16[2,176,256]{2,1,0:T(8,128)(2,1)} %get-tuple-element.21), channel_id=1, source_target_pairs={{0,64},{16,80},{32,96},{48,112},{64,0},{80,16},{96,32},{112,48},{1... | collective-permute-start | bytes 540680 | tf_op jit(solution)/shard_map/ppermute | solution.py:90
  150.1 11.5 %collective-permute-start.17 = (bf16[2,176,256]{2,1,0:T(8,128)(2,1)}, bf16[2,176,256]{2,1,0:T(8,128)(2,1)S(1)}, u32[]{:S(2)}, u32[]{:S(2)}) collective-permute-start(bf16[2,176,256]{2,1,0:T(8,128)(2,1)} %get-tuple-element.22), channel_id=1, source_target_pairs={{0,80},{16,96},{32,112},{48,0},{64,16},{80,32},{96,48},{112,64},{1... | collective-permute-start | bytes 540680 | tf_op jit(solution)/shard_map/ppermute | solution.py:90
  152.5 9.2 %collective-permute-start.22 = (bf16[8,2,64,176]{3,2,0,1:T(8,128)(2,1)}, bf16[8,2,64,176]{3,2,0,1:T(8,128)(2,1)S(1)}, u32[]{:S(2)}, u32[]{:S(2)}) collective-permute-start(bf16[8,2,64,176]{3,2,0,1:T(8,128)(2,1)} %collective-permute-done.20), channel_id=1, source_target_pairs={{0,16},{16,0},{32,48},{48,32},{64,80},{80,64},{96,112},{112,96},{1... | collective-permute-start | bytes 1081352 | tf_op jit(solution)/shard_map/ppermute | solution.py:93
  155.3 10.4 %collective-permute-start.18 = (bf16[16,2,64,176]{3,2,0,1:T(8,128)(2,1)S(1)}, bf16[16,2,64,176]{3,2,0,1:T(8,128)(2,1)S(1)}, u32[]{:S(2)}, u32[]{:S(2)}) collective-permute-start(bf16[16,2,64,176]{3,2,0,1:T(8,128)(2,1)S(1)} %collective-permute-done.16), channel_id=1, source_target_pairs={{0,16},{16,0},{32,48},{48,32},{64,80},{80,64},{96,112},{112,96},{1... | collective-permute-start | bytes 2162696 | tf_op jit(solution)/shard_map/ppermute | solution.py:93
  155.8 6.2 %collective-permute-start.23 = (bf16[8,2,64,176]{3,2,0,1:T(8,128)(2,1)}, bf16[8,2,64,176]{3,2,0,1:T(8,128)(2,1)S(1)}, u32[]{:S(2)}, u32[]{:S(2)}) collective-permute-start(bf16[8,2,64,176]{3,2,0,1:T(8,128)(2,1)} %collective-permute-done.21), channel_id=1, source_target_pairs={{0,16},{16,0},{32,48},{48,32},{64,80},{80,64},{96,112},{112,96},{1... | collective-permute-start | bytes 1081352 | tf_op jit(solution)/shard_map/ppermute | solution.py:93
  161.7 4.1 %copy-start.5 = (f32[2,256,16,64]{1,3,2,0:T(8,128)S(1)}, f32[2,256,16,64]{1,3,2,0:T(8,128)}, u32[]{:S(2)}) copy-start(f32[2,256,16,64]{1,3,2,0:T(8,128)} %fusion.62) | copy-start | bytes 6291460
  162.0 3.7 %copy-start.4 = (f32[2,256,16,64]{1,3,2,0:T(8,128)S(1)}, f32[2,256,16,64]{1,3,2,0:T(8,128)}, u32[]{:S(2)}) copy-start(f32[2,256,16,64]{1,3,2,0:T(8,128)} %fusion.68) | copy-start | bytes 6291460
  162.3 3.4 %copy-start.3 = (f32[2,256,16,64]{1,3,2,0:T(8,128)S(1)}, f32[2,256,16,64]{1,3,2,0:T(8,128)}, u32[]{:S(2)}) copy-start(f32[2,256,16,64]{1,3,2,0:T(8,128)} %fusion.66) | copy-start | bytes 6291460
  164.2 1.9 copy-start.2
  167.1 5.6 %copy-start.20 = (bf16[2048,32]{0,1:T(8,128)(2,1)S(1)}, bf16[2048,32]{0,1:T(8,128)(2,1)}, u32[]{:S(2)}) copy-start(bf16[2048,32]{0,1:T(8,128)(2,1)} %param.18) | copy-start | bytes 393220
  168.2 21.5 %all-to-all-start.1 = ((bf16[16,2,64,256]{3,2,1,0:T(8,128)(2,1)}), bf16[16,2,64,256]{3,2,1,0:T(8,128)(2,1)S(1)}, u32[]{:S(2)}, u32[]{:S(2)}) async-start(bf16[16,2,64,256]{3,2,1,0:T(8,128)(2,1)} %copy.70), calls=%async_computation.1 | async-start | bytes 2097152 | tf_op jit(solution)/shard_map/all_to_all | solution.py:182
  190.7 2.7 %copy-start.1 = (bf16[64,16,704]{2,1,0:T(8,128)(2,1)S(1)}, bf16[64,16,704]{2,1,0:T(8,128)(2,1)}, u32[]{:S(2)}) copy-start(bf16[64,16,704]{2,1,0:T(8,128)(2,1)} %param.27) | copy-start | bytes 4325380
Sparse Core Ops, SparseCore 0:
  11.7 32.8 all-gather.2
  46.6 78.4 all-gather.4
  155.4 33.2 reduce-scatter.1
